TPU v7x, 32 devices: a whole 2x2x4 slice. The times are simulated.
32 devices in a mesh: attn: 8 (over z, y), exp: 4 (over x, core).
Axes of the slice: x: 2, y: 2, z: 4, core: 2. Of those that a mesh axis runs over, the one named last changes fastest.
Arguments:
- q_latent: bfloat16 [16, 128, 512], P('attn'), may hold values from -6 to 6
- q_rope: bfloat16 [16, 64, 128], P('attn'), may hold values from -8 to 8
- cache_latent: bfloat16 [16, 4096, 512], P('attn', 'exp'), may hold values from -6 to 6
- cache_rope: bfloat16 [16, 64, 4096], P('attn', None, 'exp'), may hold values from -8 to 8
- lengths: int32 [16], P('attn'), may hold values from 2 to 4096, as said below
- tokens: bfloat16 [256, 7168], P(('attn', 'exp')), may hold values from -6 to 6
- route_ids: int32 [256, 4], P(('attn', 'exp')), may hold values from 0 to 7, all different within a row; in each aligned block of 8 rows (0 to 7, 8 to 15, ...) at most 8 rows name the same one
- route_gates: float32 [256, 4], P(('attn', 'exp')), may hold values from 0.2 to 1
- w_gate: bfloat16 [8, 7168, 1024], P('attn', None, 'exp'), may hold values from -0.0625 to 0.0625
- w_up: bfloat16 [8, 7168, 1024], P('attn', None, 'exp'), may hold values from -0.0625 to 0.0625
- w_down: bfloat16 [8, 1024, 7168], P('attn', 'exp'), may hold values from -0.1875 to 0.1875
Outputs:
- attn_out: bfloat16 [16, 128, 512], P('attn', 'exp')
- moe_out: bfloat16 [256, 7168], P(('attn', 'exp'))
Inputs may be any that keep to these rules, and one draw needn't show every extreme that they name: `route_ids`: within the rows of one device (aligned blocks of 8 rows) an expert is named at most 8 times; a token names 4 distinct experts. `lengths`: some request has length exactly 4096.
All inputs are finite; a program needn't handle non-finite values.
Results may differ from a plain program's by a relative error of at most 0.0058.
Values may be sent and summed in bfloat16 or wider, within the bound.
No kernel may reach another device: no remote copies, remote signals or barrier semaphores. Data moves between devices by JAX's collectives and lax.ppermute only.
A program may use at most 128 MiB of HBM per device.

v0:
```python
import math

import jax
import jax.numpy as jnp
from jax import lax
from jax.sharding import PartitionSpec as P

score_scale = 1.0 / math.sqrt(192.0)
neg_fill = -1e30


def expert_part(row_block, gate_slice, up_slice, down_slice):
    gate_value = jnp.dot(row_block, gate_slice, preferred_element_type=jnp.float32)
    upward = jnp.dot(row_block, up_slice, preferred_element_type=jnp.float32)
    hidden = (jax.nn.silu(gate_value) * upward).astype(jnp.bfloat16)
    return jnp.dot(hidden, down_slice, preferred_element_type=jnp.float32)


def per_device(
    q_latent,
    q_rope,
    cache_latent,
    cache_rope,
    lengths,
    tokens,
    route_ids,
    route_gates,
    w_gate,
    w_up,
    w_down,
):
    n_exp = lax.axis_size("exp")
    n_attn = lax.axis_size("attn")
    positions = cache_latent.shape[1]
    scores = jnp.einsum("rhl,rpl->rhp", q_latent, cache_latent, preferred_element_type=jnp.float32)
    scores = scores + jnp.einsum(
        "rdh,rdp->rhp", q_rope, cache_rope, preferred_element_type=jnp.float32
    )
    scores = score_scale * scores
    global_pos = lax.axis_index("exp") * positions + jnp.arange(positions, dtype=jnp.int32)
    is_live = global_pos[None, None, :] < lengths[:, None, None]
    masked = jnp.where(is_live, scores, neg_fill)
    block_max = jnp.max(masked, axis=2)
    weights = jnp.where(is_live, jnp.exp(masked - block_max[:, :, None]), 0.0)
    block_sum = jnp.sum(weights, axis=2)
    block_out = jnp.einsum(
        "rhp,rpl->rhl",
        weights.astype(jnp.bfloat16),
        cache_latent,
        preferred_element_type=jnp.float32,
    )
    row_top = lax.pmax(block_max, "exp")
    factor = jnp.exp(block_max - row_top)
    numerator, denominator = (
        lax.psum_scatter(block_out * factor[:, :, None], "exp", scatter_dimension=1, tiled=True),
        lax.psum_scatter(block_sum * factor, "exp", scatter_dimension=1, tiled=True),
    )
    attn_out = (numerator / denominator[:, :, None]).astype(jnp.bfloat16)
    tok_count, model_width = tokens.shape
    top_k = route_ids.shape[1]
    capacity = max(2, 2 * tok_count * top_k // n_attn)
    expert_ids = route_ids.reshape(-1)
    hit_table = (expert_ids[:, None] == jnp.arange(n_attn, dtype=jnp.int32)[None, :]).astype(
        jnp.int32
    )
    earlier = jnp.cumsum(hit_table, axis=0) - hit_table
    slot_index = jnp.sum(earlier * hit_table, axis=1)
    target_tok = (expert_ids * capacity + slot_index).reshape(tok_count, top_k)
    slot_ids = jnp.arange(n_attn * capacity, dtype=jnp.int32)
    select = jnp.any(target_tok[None, :, :] == slot_ids[:, None, None], axis=2).astype(jnp.bfloat16)
    outgoing = jnp.dot(select, tokens, preferred_element_type=jnp.float32).astype(jnp.bfloat16)
    gate_slice = w_gate[0]
    up_slice = w_up[0]
    down_slice = w_down[0]
    copies = jnp.broadcast_to(
        outgoing.reshape(n_attn, 1, capacity, model_width), (n_attn, n_exp, capacity, model_width)
    )
    copies = copies.reshape(n_attn * n_exp, capacity, model_width)
    piece_rows = lax.all_to_all(copies, ("attn", "exp"), split_axis=0, concat_axis=0, tiled=True)
    lead_shape = piece_rows.shape[:-1]
    flat_rows = piece_rows.reshape(-1, model_width)
    returned = lax.all_to_all(
        expert_part(flat_rows, gate_slice, up_slice, down_slice).reshape(
            lead_shape + (model_width,)
        ),
        ("attn", "exp"),
        split_axis=0,
        concat_axis=0,
        tiled=True,
    )
    summed = jnp.sum(returned.reshape(n_attn, n_exp, capacity, model_width), axis=1)
    results = lax.optimization_barrier(summed.astype(jnp.bfloat16))
    flat_results = results.reshape(n_attn * capacity, model_width)
    picked = flat_results[target_tok]
    moe_out = jnp.sum(route_gates[:, :, None] * picked.astype(jnp.float32), axis=1).astype(
        jnp.bfloat16
    )
    return (attn_out, moe_out)


def solution(mesh):
    return jax.shard_map(
        per_device,
        mesh=mesh,
        in_specs=(
            P("attn", None, None),
            P("attn", None, None),
            P("attn", "exp", None),
            P("attn", None, "exp"),
            P("attn"),
            P(("attn", "exp"), None),
            P(("attn", "exp"), None),
            P(("attn", "exp"), None),
            P("attn", None, "exp"),
            P("attn", None, "exp"),
            P("attn", "exp", None),
        ),
        out_specs=(P("attn", "exp", None), P(("attn", "exp"), None)),
        check_vma=False,
    )
```

profile of v0, /device:TPU:0, one launch (start us, length us, event | category | flops | bytes accessed | tf_op | source)
XLA Modules:
  0.0 294.9 jit_solution(10543547195808210691)
XLA Ops:
  7.2 0.9 copy.23
  8.1 0.1 eq.28
  8.2 0.1 fusion.42
  8.3 0.2 select_reduce_fusion
  8.5 0.1 reduce_sum.40
  8.6 0.1 copy.25
  8.7 0.1 fusion.43
  8.7 1.4 fusion
  10.1 0.4 broadcast_in_dim.40
  10.5 90.1 %all_to_all.10 = bf16[32,8,7168]{2,1,0:T(8,128)(2,1)S(1)} all-to-all(bf16[32,8,7168]{2,1,0:T(8,128)(2,1)S(1)} %bitcast.51), channel_id=1, replica_groups=mesh['attn'=8,'exp'=4] {'attn','exp'}, dimensions={0} | all-to-all | bytes 7340032 | tf_op jit(solution)/shard_map/all_to_all | solution.py:79
  100.6 1.9 copy-done.1
  102.5 1.1 fusion.5
  103.6 11.2 %fusion.1 = f32[32,8,7168]{2,1,0:T(8,128)} fusion(bf16[1,256,7168]{2,1,0:T(8,128)(2,1)} %param.21, bf16[1,7168,256]{2,1,0:T(8,128)(2,1)} %param.20, bf16[32,8,7168]{2,1,0:T(8,128)(2,1)} %copy-done.1, f32[256,256]{1,0:T(8,128)S(1)} %fusion.5), kind=kOutput, calls=%fused_computation.4 | convolution fusion | flops 1879441408 | bytes 18612224 | tf_op jit(solution)/shard_map/dot_general | solution.py:16
  114.8 3.8 %all-to-all-start.1 = ((f32[32,8,7168]{2,1,0:T(8,128)}), f32[32,8,7168]{2,1,0:T(8,128)}, u32[]{:S(2)}, u32[]{:S(2)}) async-start(f32[32,8,7168]{2,1,0:T(8,128)} %fusion.1), calls=%async_computation.2 | async-start | bytes 14680064 | tf_op jit(solution)/shard_map/all_to_all | solution.py:82
  118.7 0.1 broadcast_compare_fusion
  118.7 0.8 fusion.48
  119.6 0.4 fusion.47
  120.0 50.0 %pmax.7 = f32[2,128]{1,0:T(2,128)S(1)} all-reduce(f32[2,128]{1,0:T(2,128)S(1)} %get-tuple-element.6), channel_id=1, replica_groups=mesh['attn'=8,'exp'=4] {'exp'}, use_global_device_ids=true, to_apply=%region_1.2 | all-reduce | flops 256 | bytes 2048 | tf_op jit(solution)/shard_map/pmax | solution.py:52
  170.0 0.3 fusion.30
  170.3 0.7 copy.26
  171.2 1.4 convolution_multiply_fusion
  172.6 0.1 reshape.73
  172.6 0.1 copy.22
  172.7 30.3 %reduce-scatter.7.cloned.1.call-done = f32[32,2]{1,0:T(8,128)} async-done(((f32[128,2]{1,0:T(8,128)}), f32[32,2]{1,0:T(8,128)}) %reduce-scatter.7.cloned.1.call-update) | async-done | bytes 272
  203.1 0.8 copy.27
  203.8 22.6 %reduce-scatter.5.cloned.1.call-done = f32[2,32,512]{2,1,0:T(8,128)} async-done(((f32[2,128,512]{2,1,0:T(8,128)}), f32[2,32,512]{2,1,0:T(8,128)}) %reduce-scatter.5.cloned.1.call-update) | async-done | bytes 131088 | tf_op jit(solution)/shard_map/reduce_scatter | solution.py:55
  226.4 1.6 divide_convert_fusion
  228.1 53.6 %all-to-all-done.1 = f32[32,8,7168]{2,1,0:T(8,128)} async-done(((f32[32,8,7168]{2,1,0:T(8,128)}), f32[32,8,7168]{2,1,0:T(8,128)}, u32[]{:S(2)}, u32[]{:S(2)}) %all-to-all-start.1) | async-done | bytes 7340064 | tf_op jit(solution)/shard_map/all_to_all | solution.py:82
  281.7 3.9 %bitcast_reduce_fusion = bf16[8,8,7168]{2,1,0:T(8,128)(2,1)S(1)} fusion(f32[32,8,7168]{2,1,0:T(8,128)} %all-to-all-done.1), kind=kLoop, calls=%fused_computation.3 | loop fusion | flops 1376256 | bytes 8257536 | tf_op jit(solution)/shard_map/reduce_sum | solution.py:91
  285.6 0.8 gather_fusion
  286.5 0.3 reshape.81
  286.8 1.3 multiply_reduce_fusion
  (24 shorter events, 0.2 us)
Async XLA Ops:
  7.2 111.6 %copy-start = (bf16[2,1024,512]{2,1,0:T(8,128)(2,1)S(1)}, bf16[2,1024,512]{2,1,0:T(8,128)(2,1)}, u32[]{:S(2)}) copy-start(bf16[2,1024,512]{2,1,0:T(8,128)(2,1)} %param.13) | copy-start | bytes 6291460
  10.5 92.0 %copy-start.7 = (bf16[1,7168,256]{2,1,0:T(8,128)(2,1)S(1)}, bf16[1,7168,256]{2,1,0:T(8,128)(2,1)}, u32[]{:S(2)}) copy-start(bf16[1,7168,256]{2,1,0:T(8,128)(2,1)} %param.19) | copy-start | bytes 11010052
  100.6 1.9 copy-start.1
  114.8 3.9 %copy-start.6 = (s32[2]{0:T(128)S(1)}, s32[2]{0:T(128)}, u32[]{:S(2)}) copy-start(s32[2]{0:T(128)} %param.15) | copy-start | bytes 28
  114.8 4.0 %copy-start.3 = (bf16[2,128,512]{2,1,0:T(8,128)(2,1)S(1)}, bf16[2,128,512]{2,1,0:T(8,128)(2,1)}, u32[]{:S(2)}) copy-start(bf16[2,128,512]{2,1,0:T(8,128)(2,1)} %param.11) | copy-start | bytes 786436
  114.8 4.8 %copy-start.2 = (bf16[2,64,1024]{2,1,0:T(8,128)(2,1)S(1)}, bf16[2,64,1024]{2,1,0:T(8,128)(2,1)}, u32[]{:S(2)}) copy-start(bf16[2,64,1024]{2,1,0:T(8,128)(2,1)} %param.14) | copy-start | bytes 786436
  114.8 4.8 %copy-start.4 = (bf16[2,64,128]{2,1,0:T(8,128)(2,1)S(1)}, bf16[2,64,128]{2,1,0:T(8,128)(2,1)}, u32[]{:S(2)}) copy-start(bf16[2,64,128]{2,1,0:T(8,128)(2,1)} %param.12) | copy-start | bytes 98308
  114.8 166.9 %all-to-all-start.1 = ((f32[32,8,7168]{2,1,0:T(8,128)}), f32[32,8,7168]{2,1,0:T(8,128)}, u32[]{:S(2)}, u32[]{:S(2)}) async-start(f32[32,8,7168]{2,1,0:T(8,128)} %fusion.1), calls=%async_computation.2 | async-start | bytes 14680064 | tf_op jit(solution)/shard_map/all_to_all | solution.py:82
  118.6 84.5 %reduce-scatter.7.cloned.1.call-start = ((), (), s32[]{:S(2)}) async-start(), calls=%async_computation.5 | async-start | bytes 81920
  119.6 53.1 %copy-start.5 = (f32[8,4]{0,1:T(4,128)S(1)}, f32[8,4]{0,1:T(4,128)}, u32[]{:S(2)}) copy-start(f32[8,4]{0,1:T(4,128)} %param.18) | copy-start | bytes 388
  171.1 55.3 %reduce-scatter.5.cloned.1.call-start = ((), (), s32[]{:S(2)}) async-start(), calls=%async_computation.4 | async-start | bytes 655360 | tf_op jit(solution)/shard_map/reduce_scatter | solution.py:55
Sparse Core Ops, SparseCore 0:
  171.2 31.7 reduce-scatter.6
  205.7 20.7 reduce-scatter.4
where the time goes:
time: 295 us
  blocking collectives  140 us (47%)
  waiting for transfers between devices  107 us (36%)
  matrix products  16.2 us (5%)
  between operations  14.2 us (5%)
  other arithmetic  7.65 us (3%)
  local copies, waits for them, and re-layouts  6.34 us (2%)
  starting transfers between devices  3.87 us (1%)
    all_to_all x1, blocking collectives, per_device(): lax.all_to_all(copies, ('attn', 'exp'), split_axis=0, concat_axis=0, tile...  90.1 us
    all_to_all x1, waiting for transfers between devices, per_device(): lax.all_to_all(expert_part(flat_rows, gate_slice, up_slice, down_slice).r...  53.6 us
    pmax x1, blocking collectives, per_device(): row_top = lax.pmax(block_max, 'exp')  50 us
    unnamed x3, waiting for transfers between devices  30.4 us
    reduce_scatter x1, waiting for transfers between devices, per_device(): lax.psum_scatter(block_out * factor[:, :, None], 'exp', scatter_dimension...  22.6 us
    dot_general x1, matrix products, expert_part(): return jnp.dot(hidden, down_slice, preferred_element_type=jnp.float32)  11.2 us
  transfers between devices with their start and end apart: 3, of which 3 were waited for; matrix products, arithmetic and copies ran while one was open for 2% of the time, Pallas kernels for 0%

commit v1 on v0

--- a/solution.py
+++ b/solution.py
@@ -56,43 +56,18 @@
         lax.psum_scatter(block_sum * factor, "exp", scatter_dimension=1, tiled=True),
     )
     attn_out = (numerator / denominator[:, :, None]).astype(jnp.bfloat16)
-    tok_count, model_width = tokens.shape
-    top_k = route_ids.shape[1]
-    capacity = max(2, 2 * tok_count * top_k // n_attn)
-    expert_ids = route_ids.reshape(-1)
-    hit_table = (expert_ids[:, None] == jnp.arange(n_attn, dtype=jnp.int32)[None, :]).astype(
-        jnp.int32
-    )
-    earlier = jnp.cumsum(hit_table, axis=0) - hit_table
-    slot_index = jnp.sum(earlier * hit_table, axis=1)
-    target_tok = (expert_ids * capacity + slot_index).reshape(tok_count, top_k)
-    slot_ids = jnp.arange(n_attn * capacity, dtype=jnp.int32)
-    select = jnp.any(target_tok[None, :, :] == slot_ids[:, None, None], axis=2).astype(jnp.bfloat16)
-    outgoing = jnp.dot(select, tokens, preferred_element_type=jnp.float32).astype(jnp.bfloat16)
-    gate_slice = w_gate[0]
-    up_slice = w_up[0]
-    down_slice = w_down[0]
-    copies = jnp.broadcast_to(
-        outgoing.reshape(n_attn, 1, capacity, model_width), (n_attn, n_exp, capacity, model_width)
-    )
-    copies = copies.reshape(n_attn * n_exp, capacity, model_width)
-    piece_rows = lax.all_to_all(copies, ("attn", "exp"), split_axis=0, concat_axis=0, tiled=True)
-    lead_shape = piece_rows.shape[:-1]
-    flat_rows = piece_rows.reshape(-1, model_width)
-    returned = lax.all_to_all(
-        expert_part(flat_rows, gate_slice, up_slice, down_slice).reshape(
-            lead_shape + (model_width,)
-        ),
-        ("attn", "exp"),
-        split_axis=0,
-        concat_axis=0,
-        tiled=True,
-    )
-    summed = jnp.sum(returned.reshape(n_attn, n_exp, capacity, model_width), axis=1)
-    results = lax.optimization_barrier(summed.astype(jnp.bfloat16))
-    flat_results = results.reshape(n_attn * capacity, model_width)
-    picked = flat_results[target_tok]
-    moe_out = jnp.sum(route_gates[:, :, None] * picked.astype(jnp.float32), axis=1).astype(
+    n_local = w_gate.shape[0]
+    all_axes = ("attn", "exp")
+    tok_all = lax.all_gather(tokens, all_axes, axis=0, tiled=True)
+    ids_all = lax.all_gather(route_ids, all_axes, axis=0, tiled=True)
+    gates_all = lax.all_gather(route_gates, all_axes, axis=0, tiled=True)
+    first_expert = lax.axis_index("attn") * n_local
+    partial = None
+    for i in range(n_local):
+        weight = jnp.sum(jnp.where(ids_all == first_expert + i, gates_all, 0.0), axis=1)
+        piece = expert_part(tok_all, w_gate[i], w_up[i], w_down[i]) * weight[:, None]
+        partial = piece if partial is None else partial + piece
+    moe_out = lax.psum_scatter(partial, all_axes, scatter_dimension=0, tiled=True).astype(
         jnp.bfloat16
     )
     return (attn_out, moe_out)

time: 295 us -> 271 us (0.919)
  blocking collectives: 140 us -> 86.2 us
  waiting for transfers between devices: 107 us -> 142 us
  local copies, waits for them, and re-layouts: 6.34 us -> 1.69 us
  starting transfers between devices: 3.87 us -> 0.17 us
  matrix products: 16.2 us -> 19.8 us
  other arithmetic: 7.65 us -> 4.34 us
    reduce_scatter x0 -> x1, waiting for transfers between devices: none -> 142 us  [per_device(): lax.psum_scatter(partial, all_axes, scatter_dimension=0, tiled=True)]
    all_to_all x1 -> x0, blocking collectives: 90.1 us -> none  [per_device(): lax.all_to_all(copies, ('attn', 'exp'), split_axis=0, concat_axis=0, tile...]
    all_gather x0 -> x2, blocking collectives: none -> 77.9 us  [the longest x1 41.1 us: per_device(): ids_all = lax.all_gather(route_ids, all_axes, axis=0, tiled=True)]
    all_to_all x1 -> x0, waiting for transfers between devices: 53.6 us -> none  [per_device(): lax.all_to_all(expert_part(flat_rows, gate_slice, up_slice, down_slice).r...]
    pmax x1, blocking collectives: 50 us -> 8.33 us  [per_device(): row_top = lax.pmax(block_max, 'exp')]
    unnamed x3 -> x5, waiting for transfers between devices: 30.4 us -> 0.76 us
    reduce_scatter x1, waiting for transfers between devices: 22.6 us -> 0.01 us  [per_device(): lax.psum_scatter(block_out * factor[:, :, None], 'exp', scatter_dimension...]
    reduce_sum x3 -> x1, other arithmetic: 5.39 us -> 0.05 us  [per_device(): jnp.sum(jnp.where(ids_all == first_expert + i, gates_all, 0.0), axis=1)]
  transfers between devices with their start and end apart: 3 -> 4, of which waited for: 3 -> 1; matrix products, arithmetic and copies ran while one was open for 2% -> 9% of each run, Pallas kernels for 0% -> 0%
where the time goes in v1:
time: 271 us; the launch traced here: 270 us
  waiting for transfers between devices  142 us (52%)
  blocking collectives  86.2 us (32%)
  matrix products  19.8 us (7%)
  between operations  15.8 us (6%)
  other arithmetic  4.34 us (2%)
    reduce_scatter x1, waiting for transfers between devices, per_device(): lax.psum_scatter(partial, all_axes, scatter_dimension=0, tiled=True)  142 us
    all_gather x1, blocking collectives, per_device(): ids_all = lax.all_gather(route_ids, all_axes, axis=0, tiled=True)  41.1 us
    all_gather x1, blocking collectives, per_device(): gates_all = lax.all_gather(route_gates, all_axes, axis=0, tiled=True)  36.8 us
    dot_general x1, matrix products, expert_part(): return jnp.dot(hidden, down_slice, preferred_element_type=jnp.float32)  11.2 us
    pmax x1, blocking collectives, per_device(): row_top = lax.pmax(block_max, 'exp')  8.33 us
  transfers between devices with their start and end apart: 4, of which 1 were waited for; matrix products, arithmetic and copies ran while one was open for 9% of the time, Pallas kernels for 0%

profile of v1, /device:TPU:0, one launch (start us, length us, event | category | flops | bytes accessed | tf_op | source)
XLA Modules:
  0.0 270.4 jit_solution(11026204819615197221)
XLA Ops:
  8.0 0.0 copy-start
  8.0 0.0 copy-start.1
  8.0 0.0 all-gather.4.cloned.1.call-start
  8.1 0.7 all-gather.4.cloned.1.call-update
  8.8 0.0 reduce-scatter.10.cloned.1.call-start
  8.8 0.7 broadcast_compare_fusion
  9.6 0.0 copy-done
  9.6 1.8 fusion.31
  11.4 0.0 copy-start.2
  11.4 0.0 copy-start.3
  11.4 1.2 fusion.30
  12.6 8.3 %pmax.7 = f32[2,128]{1,0:T(2,128)S(1)} all-reduce(f32[2,128]{1,0:T(2,128)S(1)} %get-tuple-element.4), channel_id=1, replica_groups=mesh['attn'=8,'exp'=4] {'exp'}, use_global_device_ids=true, to_apply=%region_1.2 | all-reduce | flops 256 | bytes 2048 | tf_op jit(solution)/shard_map/pmax | solution.py:52
  20.9 0.3 fusion.15
  21.3 0.7 copy.13
  22.0 0.0 reduce-scatter.10.cloned.1.call-update
  22.0 0.0 reduce-scatter.6.cloned.1.call-start
  22.1 1.4 convolution_multiply_fusion.1
  23.5 0.0 reduce-scatter.6.cloned.1.call-update
  23.5 0.0 reduce-scatter.8.cloned.1.call-start
  23.6 41.1 %all-gather = s32[32,8,4]{1,2,0:T(4,128)S(1)} all-gather(s32[1,8,4]{1,2,0:T(4,128)S(1)} %bitcast.28), channel_id=1, replica_groups=mesh['attn'=8,'exp'=4] {'attn','exp'}, dimensions={0}, use_global_device_ids=true | all-gather | bytes 4224 | tf_op jit(solution)/shard_map/all_gather | solution.py:62
  64.7 36.8 %all-gather.1 = f32[32,8,4]{1,2,0:T(4,128)S(1)} all-gather(f32[1,8,4]{1,2,0:T(4,128)S(1)} %bitcast.29), channel_id=1, replica_groups=mesh['attn'=8,'exp'=4] {'attn','exp'}, dimensions={0}, use_global_device_ids=true | all-gather | bytes 4224 | tf_op jit(solution)/shard_map/all_gather | solution.py:63
  101.5 0.1 select_reduce_fusion
  101.5 0.1 reshape.49
  101.6 0.0 all-gather.4.cloned.1.call-done
  101.6 4.3 %fusion.3 = f32[256,256]{1,0:T(8,128)S(1)} fusion(bf16[256,7168]{1,0:T(8,128)(2,1)} %all-gather.4.cloned.1.call-done, bf16[1,7168,256]{2,1,0:T(8,128)(2,1)} %param.19), kind=kOutput, calls=%fused_computation.4 | convolution fusion | flops 939524096 | bytes 7602176 | tf_op jit(solution)/shard_map/dot_general | solution.py:13
  105.9 11.2 %convolution_multiply_fusion = f32[256,7168]{1,0:T(8,128)} fusion(bf16[1,256,7168]{2,1,0:T(8,128)(2,1)} %param.21, f32[256]{0:T(256)S(1)} %reshape.49, bf16[256,7168]{1,0:T(8,128)(2,1)} %all-gather.4.cloned.1.call-done, bf16[1,7168,256]{2,1,0:T(8,128)(2,1)} %param.20, f32[256,256]{1,0:T(8,128)S(1)} %fusion.3), kind=kOutput, calls=%fused_computation | convolution fusion | flops 1881276416 | bytes 18613248 | tf_op jit(solution)/shard_map/dot_general | solution.py:16
  117.1 0.0 reduce-scatter.8.cloned.1.call-update
  117.1 0.0 reduce-scatter.10.cloned.1.call-done
  117.1 0.8 copy.14
  117.9 1.6 divide_convert_fusion
  119.6 141.6 %reduce-scatter.8.cloned.1.call-done = f32[8,7168]{1,0:T(8,128)} async-done(((f32[256,7168]{1,0:T(8,128)}), f32[8,7168]{1,0:T(8,128)}) %reduce-scatter.8.cloned.1.call-update) | async-done | bytes 229392 | tf_op jit(solution)/shard_map/reduce_scatter | solution.py:70
  261.2 1.6 convert_element_type.15
  (6 shorter events, 0.0 us)
Async XLA Ops:
  8.0 1.6 copy-start
  8.0 3.3 %copy-start.1 = (bf16[2,64,1024]{2,1,0:T(8,128)(2,1)S(1)}, bf16[2,64,1024]{2,1,0:T(8,128)(2,1)}, u32[]{:S(2)}) copy-start(bf16[2,64,1024]{2,1,0:T(8,128)(2,1)} %param.14) | copy-start | bytes 786436
  8.0 93.6 %all-gather.4.cloned.1.call-start = ((), (), s32[]{:S(2)}) async-start(), calls=%async_computation.4 | async-start | bytes 3784704 | tf_op jit(solution)/shard_map/all_gather | solution.py:61
  8.8 108.4 %reduce-scatter.10.cloned.1.call-start = ((), (), s32[]{:S(2)}) async-start(), calls=%async_computation.6 | async-start | bytes 81920
  11.4 12.2 %copy-start.2 = (s32[8,4]{0,1:T(4,128)S(1)}, s32[8,4]{0,1:T(4,128)}, u32[]{:S(2)}) copy-start(s32[8,4]{0,1:T(4,128)} %param.17) | copy-start | bytes 388
  11.4 53.3 %copy-start.3 = (f32[8,4]{0,1:T(4,128)S(1)}, f32[8,4]{0,1:T(4,128)}, u32[]{:S(2)}) copy-start(f32[8,4]{0,1:T(4,128)} %param.18) | copy-start | bytes 388
  22.0 95.9 %reduce-scatter.6.cloned.1.call-start = ((), (), s32[]{:S(2)}) async-start(), calls=%async_computation.3 | async-start | bytes 655360 | tf_op jit(solution)/shard_map/reduce_scatter | solution.py:55
  23.5 237.7 %reduce-scatter.8.cloned.1.call-start = ((), (), s32[]{:S(2)}) async-start(), calls=%async_computation.5 | async-start | bytes 7569408 | tf_op jit(solution)/shard_map/reduce_scatter | solution.py:70
Sparse Core Ops, SparseCore 0:
  11.7 63.1 all-gather.3
Sparse Core Ops, SparseCore 1:
  22.1 19.7 reduce-scatter.9
  44.4 25.2 reduce-scatter.5
  117.2 144.0 reduce-scatter.7

commit v2 on v1

--- a/solution.py
+++ b/solution.py
@@ -14,6 +14,66 @@
     upward = jnp.dot(row_block, up_slice, preferred_element_type=jnp.float32)
     hidden = (jax.nn.silu(gate_value) * upward).astype(jnp.bfloat16)
     return jnp.dot(hidden, down_slice, preferred_element_type=jnp.float32)
+
+
+def shift_gather(x, axis, n):
+    pieces = [x]
+    for k in range(1, n):
+        pieces.append(lax.ppermute(x, axis, [(i, (i + k) % n) for i in range(n)]))
+    return jnp.stack(pieces)
+
+
+def shift_scatter_sum(q, axis, n):
+    total = q[0]
+    for k in range(1, n):
+        total = total + lax.ppermute(q[k], axis, [(i, (i - k) % n) for i in range(n)])
+    return total
+
+
+def bit_gather(x, axis, bit, n):
+    other = lax.ppermute(x, axis, [(i, i ^ bit) for i in range(n)])
+    return jnp.stack([x, other])
+
+
+def bit_reduce(x, axis, bit, n):
+    return x[0] + lax.ppermute(x[1], axis, [(i, i ^ bit) for i in range(n)])
+
+
+def routed_experts(tokens, route_ids, route_gates, w_gate, w_up, w_down):
+    n_exp = lax.axis_size("exp")
+    n_attn = lax.axis_size("attn")
+    n_local = w_gate.shape[0]
+    n_experts = n_attn * n_local
+    tok_count, model_width = tokens.shape
+    bits = []
+    b = n_exp // 2
+    while b >= 1:
+        bits.append(b)
+        b //= 2
+    hit = route_ids[:, :, None] == jnp.arange(n_experts, dtype=jnp.int32)[None, None, :]
+    wmat = jnp.sum(jnp.where(hit, route_gates[:, :, None], 0.0), axis=1)
+    rows = shift_gather(tokens, "attn", n_attn)
+    wrows = shift_gather(wmat, "attn", n_attn)
+    for bit in bits:
+        rows = bit_gather(rows, "exp", bit, n_exp)
+        wrows = bit_gather(wrows, "exp", bit, n_exp)
+    lead_shape = rows.shape[:-1]
+    flat_rows = rows.reshape(-1, model_width)
+    flat_w = wrows.reshape(-1, n_experts)
+    first_expert = lax.axis_index("attn") * n_local
+    result = None
+    for i in range(n_local):
+        partial = expert_part(flat_rows, w_gate[i], w_up[i], w_down[i])
+        partial = partial.reshape(lead_shape + (model_width,))
+        for bit in reversed(bits):
+            partial = bit_reduce(partial, "exp", bit, n_exp)
+        weight = lax.dynamic_index_in_dim(flat_w, first_expert + i, axis=1, keepdims=False)
+        weight = weight.reshape(lead_shape)
+        for _ in bits:
+            weight = weight[0]
+        piece = partial.astype(jnp.bfloat16).astype(jnp.float32) * weight[..., None]
+        result = piece if result is None else result + piece
+    return shift_scatter_sum(result, "attn", n_attn).astype(jnp.bfloat16)
 
 
 def per_device(
@@ -56,20 +116,7 @@
         lax.psum_scatter(block_sum * factor, "exp", scatter_dimension=1, tiled=True),
     )
     attn_out = (numerator / denominator[:, :, None]).astype(jnp.bfloat16)
-    n_local = w_gate.shape[0]
-    all_axes = ("attn", "exp")
-    tok_all = lax.all_gather(tokens, all_axes, axis=0, tiled=True)
-    ids_all = lax.all_gather(route_ids, all_axes, axis=0, tiled=True)
-    gates_all = lax.all_gather(route_gates, all_axes, axis=0, tiled=True)
-    first_expert = lax.axis_index("attn") * n_local
-    partial = None
-    for i in range(n_local):
-        weight = jnp.sum(jnp.where(ids_all == first_expert + i, gates_all, 0.0), axis=1)
-        piece = expert_part(tok_all, w_gate[i], w_up[i], w_down[i]) * weight[:, None]
-        partial = piece if partial is None else partial + piece
-    moe_out = lax.psum_scatter(partial, all_axes, scatter_dimension=0, tiled=True).astype(
-        jnp.bfloat16
-    )
+    moe_out = routed_experts(tokens, route_ids, route_gates, w_gate, w_up, w_down)
     return (attn_out, moe_out)
 
 

time: 271 us -> 207 us (0.76)
  blocking collectives: 86.2 us -> 5.98 us
  starting transfers between devices: 0.17 us -> 41.4 us
  waiting for transfers between devices: 142 us -> 101 us
  local copies, waits for them, and re-layouts: 1.69 us -> 18.1 us
  other arithmetic: 4.34 us -> 10.8 us
  matrix products: 19.8 us -> 14.9 us
    reduce_scatter x1 -> x0, waiting for transfers between devices: 142 us -> none  [per_device(): lax.psum_scatter(partial, all_axes, scatter_dimension=0, tiled=True)]
    ppermute x0 -> x27, waiting for transfers between devices: none -> 100 us  [the longest x4 62.7 us: bit_gather(): other = lax.ppermute(x, axis, [(i, i ^ bit) for i in range(n)])]
    all_gather x2 -> x0, blocking collectives: 77.9 us -> none  [the longest x1 41.1 us: per_device(): ids_all = lax.all_gather(route_ids, all_axes, axis=0, tiled=True)]
    ppermute x0 -> x27, starting transfers between devices: none -> 41.3 us  [the longest x14 31 us: shift_gather(): pieces.append(lax.ppermute(x, axis, [(i, (i + k) % n) for i in range(n)]))]
    unnamed x10 -> x41, local copies, waits for them, and re-layouts: 1.6 us -> 9.5 us
    slice x0 -> x1, local copies, waits for them, and re-layouts: none -> 7 us  [bit_reduce(): return x[0] + lax.ppermute(x[1], axis, [(i, i ^ bit) for i in range(n)])]
    add x0 -> x1, other arithmetic: none -> 3.55 us  [bit_reduce(): return x[0] + lax.ppermute(x[1], axis, [(i, i ^ bit) for i in range(n)])]
    dot_general x1, matrix products: 4.27 us -> 1.11 us  [expert_part(): upward = jnp.dot(row_block, up_slice, preferred_element_type=jnp.float32)]
  transfers between devices with their start and end apart: 4 -> 29, of which waited for: 1 -> 11; matrix products, arithmetic and copies ran while one was open for 9% -> 7% of each run, Pallas kernels for 0% -> 0%
where the time goes in v2:
time: 207 us
  waiting for transfers between devices  101 us (49%)
  starting transfers between devices  41.4 us (20%)
  local copies, waits for them, and re-layouts  18.1 us (9%)
  matrix products  14.9 us (7%)
  between operations  14.3 us (7%)
  other arithmetic  10.8 us (5%)
  blocking collectives  5.98 us (3%)
    ppermute x4, waiting for transfers between devices, bit_gather(): other = lax.ppermute(x, axis, [(i, i ^ bit) for i in range(n)])  62.7 us
    ppermute x7, waiting for transfers between devices, shift_scatter_sum(): lax.ppermute(q[k], axis, [(i, (i - k) % n) for i in range(n)])  32.3 us
    ppermute x14, starting transfers between devices, shift_gather(): pieces.append(lax.ppermute(x, axis, [(i, (i + k) % n) for i in range(n)]))  31 us
    dot_general x1, matrix products, expert_part(): return jnp.dot(hidden, down_slice, preferred_element_type=jnp.float32)  11.1 us
    unnamed x41, local copies, waits for them, and re-layouts  9.5 us
    slice x1, local copies, waits for them, and re-layouts, bit_reduce(): return x[0] + lax.ppermute(x[1], axis, [(i, i ^ bit) for i in range(n)])  7 us
    ppermute x7, starting transfers between devices, shift_scatter_sum(): lax.ppermute(q[k], axis, [(i, (i - k) % n) for i in range(n)])  6.41 us
    pmax x1, blocking collectives, per_device(): row_top = lax.pmax(block_max, 'exp')  5.98 us
  transfers between devices with their start and end apart: 29, of which 11 were waited for; matrix products, arithmetic and copies ran while one was open for 7% of the time, Pallas kernels for 0%

profile of v2, /device:TPU:0, one launch (start us, length us, event | category | flops | bytes accessed | tf_op | source)
XLA Modules:
  0.0 206.8 jit_solution(5492339786473106389)
XLA Ops:
  7.2 3.0 %collective-permute-start = (bf16[8,7168]{1,0:T(8,128)(2,1)}, bf16[8,7168]{1,0:T(8,128)(2,1)S(1)}, u32[]{:S(2)}, u32[]{:S(2)}) collective-permute-start(bf16[8,7168]{1,0:T(8,128)(2,1)} %param.16), channel_id=1, source_target_pairs={{0,4},{4,8},{8,12},{12,16},{16,20},{20,24},{24,28},{28,0},{1,5},{5... | collective-permute-start | bytes 344072 | tf_op jit(solution)/shard_map/ppermute | solution.py:22
  10.2 1.6 collective-permute-start.1
  11.8 2.5 %collective-permute-start.2 = (bf16[8,7168]{1,0:T(8,128)(2,1)}, bf16[8,7168]{1,0:T(8,128)(2,1)S(1)}, u32[]{:S(2)}, u32[]{:S(2)}) collective-permute-start(bf16[8,7168]{1,0:T(8,128)(2,1)} %param.16), channel_id=1, source_target_pairs={{0,12},{4,16},{8,20},{12,24},{16,28},{20,0},{24,4},{28,8},{1,13},{... | collective-permute-start | bytes 344072 | tf_op jit(solution)/shard_map/ppermute | solution.py:22
  15.6 2.6 %collective-permute-start.4 = (bf16[8,7168]{1,0:T(8,128)(2,1)}, bf16[8,7168]{1,0:T(8,128)(2,1)S(1)}, u32[]{:S(2)}, u32[]{:S(2)}) collective-permute-start(bf16[8,7168]{1,0:T(8,128)(2,1)} %param.16), channel_id=1, source_target_pairs={{0,20},{4,24},{8,28},{12,0},{16,4},{20,8},{24,12},{28,16},{1,21},{... | collective-permute-start | bytes 344072 | tf_op jit(solution)/shard_map/ppermute | solution.py:22
  19.2 1.4 collective-permute-start.5
  20.6 1.5 collective-permute-start.6
  22.1 4.5 %collective-permute-done.2 = bf16[8,7168]{1,0:T(8,128)(2,1)S(1)} collective-permute-done((bf16[8,7168]{1,0:T(8,128)(2,1)}, bf16[8,7168]{1,0:T(8,128)(2,1)S(1)}, u32[]{:S(2)}, u32[]{:S(2)}) %collective-permute-start.2) | collective-permute-done | bytes 114720 | tf_op jit(solution)/shard_map/ppermute | solution.py:22
  27.5 1.5 collective-permute-start.7
  29.0 20.4 %collective-permute-done.7 = bf16[8,8,7168]{2,1,0:T(8,128)(2,1)S(1)} collective-permute-done((bf16[8,8,7168]{2,1,0:T(8,128)(2,1)S(1)}, bf16[8,8,7168]{2,1,0:T(8,128)(2,1)S(1)}, u32[]{:S(2)}, u32[]{:S(2)}) %collective-permute-start.7) | collective-permute-done | bytes 917536 | tf_op jit(solution)/shard_map/ppermute | solution.py:34
  49.6 3.8 %collective-permute-done.8 = bf16[2,8,8,7168]{3,2,1,0:T(8,128)(2,1)S(1)} collective-permute-done((bf16[2,8,8,7168]{3,2,1,0:T(8,128)(2,1)S(1)}, bf16[2,8,8,7168]{3,2,1,0:T(8,128)(2,1)S(1)}, u32[]{:S(2)}, u32[]{:S(2)}) %collective-permute-start.8) | collective-permute-done | bytes 1835040 | tf_op jit(solution)/shard_map/ppermute | solution.py:34
  53.8 1.9 copy-done.1
  57.9 11.1 %fusion = f32[256,7168]{1,0:T(8,128)} fusion(bf16[1,256,7168]{2,1,0:T(8,128)(2,1)} %param.21, f32[256,256]{1,0:T(8,128)S(1)} %fusion.2, bf16[256,7168]{1,0:T(8,128)(2,1)} %bitcast.112, bf16[1,7168,256]{2,1,0:T(8,128)(2,1)} %param.19), kind=kOutput, calls=%fused_computation.1 | convolution fusion | flops 1879441408 | bytes 18612224 | tf_op jit(solution)/shard_map/dot_general | solution.py:16
  69.1 7.0 %fusion.34 = (f32[128,7168]{1,0:T(8,128)}, f32[128,7168]{1,0:T(8,128)}) fusion(f32[256,7168]{1,0:T(8,128)} %fusion), kind=kLoop, calls=%fused_computation.71 | loop fusion | bytes 14680064 | tf_op jit(solution)/shard_map/slice | solution.py:39
  76.3 4.0 %collective-permute-start.11 = (f32[8,8]{1,0:T(8,128)S(1)}, f32[8,8]{1,0:T(8,128)S(1)}, u32[]{:S(2)}, u32[]{:S(2)}) collective-permute-start(f32[8,8]{1,0:T(8,128)S(1)} %select_reduce_fusion), channel_id=1, source_target_pairs={{0,4},{4,8},{8,12},{12,16},{16,20},{20,24},{24,28},{28,0},{1,5},{5... | collective-permute-start | bytes 776 | tf_op jit(solution)/shard_map/ppermute | solution.py:22
  80.3 5.1 %collective-permute-start.12 = (f32[8,8]{1,0:T(8,128)S(1)}, f32[8,8]{1,0:T(8,128)S(1)}, u32[]{:S(2)}, u32[]{:S(2)}) collective-permute-start(f32[8,8]{1,0:T(8,128)S(1)} %select_reduce_fusion), channel_id=1, source_target_pairs={{0,8},{4,12},{8,16},{12,20},{16,24},{20,28},{24,0},{28,4},{1,9},{5... | collective-permute-start | bytes 776 | tf_op jit(solution)/shard_map/ppermute | solution.py:22
  85.4 1.7 collective-permute-start.14
  88.8 6.0 %pmax.7 = f32[2,128]{1,0:T(2,128)S(1)} all-reduce(f32[2,128]{1,0:T(2,128)S(1)} %get-tuple-element.17), channel_id=1, replica_groups=mesh['attn'=8,'exp'=4] {'exp'}, use_global_device_ids=true, to_apply=%region_1.2 | all-reduce | flops 256 | bytes 2048 | tf_op jit(solution)/shard_map/pmax | solution.py:112
  94.8 2.5 %collective-permute-start.15 = (f32[8,8]{1,0:T(8,128)S(1)}, f32[8,8]{1,0:T(8,128)S(1)}, u32[]{:S(2)}, u32[]{:S(2)}) collective-permute-start(f32[8,8]{1,0:T(8,128)S(1)} %select_reduce_fusion), channel_id=1, source_target_pairs={{0,20},{4,24},{8,28},{12,0},{16,4},{20,8},{24,12},{28,16},{1,21},{... | collective-permute-start | bytes 776 | tf_op jit(solution)/shard_map/ppermute | solution.py:22
  97.3 2.4 %collective-permute-start.16 = (f32[8,8]{1,0:T(8,128)S(1)}, f32[8,8]{1,0:T(8,128)S(1)}, u32[]{:S(2)}, u32[]{:S(2)}) collective-permute-start(f32[8,8]{1,0:T(8,128)S(1)} %select_reduce_fusion), channel_id=1, source_target_pairs={{0,24},{4,28},{8,0},{12,4},{16,8},{20,12},{24,16},{28,20},{1,25},{... | collective-permute-start | bytes 776 | tf_op jit(solution)/shard_map/ppermute | solution.py:22
  99.7 1.5 collective-permute-start.17
  101.2 3.6 %add.56 = f32[2,8,8,7168]{3,2,1,0:T(8,128)S(1)} add(f32[2,8,8,7168]{3,2,1,0:T(8,128)} %bitcast.110, f32[2,8,8,7168]{3,2,1,0:T(8,128)} %collective-permute-done.9) | non-fusion elementwise | flops 917504 | bytes 11010048 | tf_op jit(solution)/shard_map/add | solution.py:39
  104.8 1.8 copy-done.2
  106.5 1.4 slice_bitcast_fusion
  110.9 38.6 %collective-permute-done.18 = f32[8,8,8]{2,1,0:T(8,128)S(1)} collective-permute-done((f32[8,8,8]{2,1,0:T(8,128)S(1)}, f32[8,8,8]{2,1,0:T(8,128)S(1)}, u32[]{:S(2)}, u32[]{:S(2)}) %collective-permute-start.18) | collective-permute-done | bytes 2080 | tf_op jit(solution)/shard_map/ppermute | solution.py:34
  151.3 2.3 %convert_multiply_fusion = f32[8,8,7168]{2,1,0:T(8,128)S(1)} fusion(f32[8,8,7168]{2,1,0:T(8,128)} %collective-permute-done.10, f32[2,8,8,7168]{3,2,1,0:T(8,128)} %copy-done.2, f32[8,8]{1,0:T(8,128)S(1)} %mul.45), kind=kLoop, calls=%fused_computation.12 | loop fusion | flops 1835008 | bytes 5505280 | tf_op jit(solution)/shard_map/mul | solution.py:74
  155.0 2.0 collective-permute-start.20
  157.6 2.6 %collective-permute-start.23 = (f32[8,7168]{1,0:T(8,128)S(1)}, f32[8,7168]{1,0:T(8,128)}, u32[]{:S(2)}, u32[]{:S(2)}) collective-permute-start(f32[8,7168]{1,0:T(8,128)S(1)} %get-tuple-element.10), channel_id=1, source_target_pairs={{0,16},{4,20},{8,24},{12,28},{16,0},{20,4},{24,8},{28,12},{1,17},{... | collective-permute-start | bytes 688136 | tf_op jit(solution)/shard_map/ppermute | solution.py:29
  161.4 1.6 collective-permute-done.20
  163.0 6.1 %collective-permute-done.21 = f32[8,7168]{1,0:T(8,128)S(1)} collective-permute-done((f32[8,7168]{1,0:T(8,128)S(1)}, f32[8,7168]{1,0:T(8,128)S(1)}, u32[]{:S(2)}, u32[]{:S(2)}) %collective-permute-start.21) | collective-permute-done | bytes 229408 | tf_op jit(solution)/shard_map/ppermute | solution.py:29
  171.6 1.6 divide_convert_fusion
  173.2 23.5 %collective-permute-done.23 = f32[8,7168]{1,0:T(8,128)} collective-permute-done((f32[8,7168]{1,0:T(8,128)S(1)}, f32[8,7168]{1,0:T(8,128)}, u32[]{:S(2)}, u32[]{:S(2)}) %collective-permute-start.23) | collective-permute-done | bytes 229408 | tf_op jit(solution)/shard_map/ppermute | solution.py:29
  197.8 2.2 %fusion.23 = bf16[8,7168]{1,0:T(8,128)(2,1)} fusion(f32[8,7168]{1,0:T(8,128)} %collective-permute-done.26, f32[8,7168]{1,0:T(8,128)} %collective-permute-done.25, f32[8,7168]{1,0:T(8,128)} %collective-permute-done.24, f32[8,7168]{1,0:T(8,128)} %collective-permute-done.23, f32[8,7168]{1,0:T(8,128)} %collective-permute-done.22, f32[8,7168]{1,0:T(8,128)} %copy-done.6, ...), kind=kLoop, calls=%fused_computation.39 | loop fusion | flops 458752 | bytes 1949696 | tf_op jit(solution)/shard_map/convert_element_type | solution.py:76
  (94 shorter events, 19.2 us)
Async XLA Ops:
  7.2 80.0 %copy-start = (bf16[2,1024,512]{2,1,0:T(8,128)(2,1)S(1)}, bf16[2,1024,512]{2,1,0:T(8,128)(2,1)}, u32[]{:S(2)}) copy-start(bf16[2,1024,512]{2,1,0:T(8,128)(2,1)} %param.13) | copy-start | bytes 6291460
  7.2 162.6 %reduce-scatter.7.cloned.1.call-start = ((), (), s32[]{:S(2)}) async-start(), calls=%async_computation.3 | async-start | bytes 81920
  7.2 12.0 %collective-permute-start = (bf16[8,7168]{1,0:T(8,128)(2,1)}, bf16[8,7168]{1,0:T(8,128)(2,1)S(1)}, u32[]{:S(2)}, u32[]{:S(2)}) collective-permute-start(bf16[8,7168]{1,0:T(8,128)(2,1)} %param.16), channel_id=1, source_target_pairs={{0,4},{4,8},{8,12},{12,16},{16,20},{20,24},{24,28},{28,0},{1,5},{5... | collective-permute-start | bytes 344072 | tf_op jit(solution)/shard_map/ppermute | solution.py:22
  10.2 10.4 %collective-permute-start.1 = (bf16[8,7168]{1,0:T(8,128)(2,1)}, bf16[8,7168]{1,0:T(8,128)(2,1)S(1)}, u32[]{:S(2)}, u32[]{:S(2)}) collective-permute-start(bf16[8,7168]{1,0:T(8,128)(2,1)} %param.16), channel_id=1, source_target_pairs={{0,8},{4,12},{8,16},{12,20},{16,24},{20,28},{24,0},{28,4},{1,9},{5... | collective-permute-start | bytes 344072 | tf_op jit(solution)/shard_map/ppermute | solution.py:22
  11.8 14.8 %collective-permute-start.2 = (bf16[8,7168]{1,0:T(8,128)(2,1)}, bf16[8,7168]{1,0:T(8,128)(2,1)S(1)}, u32[]{:S(2)}, u32[]{:S(2)}) collective-permute-start(bf16[8,7168]{1,0:T(8,128)(2,1)} %param.16), channel_id=1, source_target_pairs={{0,12},{4,16},{8,20},{12,24},{16,28},{20,0},{24,4},{28,8},{1,13},{... | collective-permute-start | bytes 344072 | tf_op jit(solution)/shard_map/ppermute | solution.py:22
  14.4 12.7 %collective-permute-start.3 = (bf16[8,7168]{1,0:T(8,128)(2,1)}, bf16[8,7168]{1,0:T(8,128)(2,1)S(1)}, u32[]{:S(2)}, u32[]{:S(2)}) collective-permute-start(bf16[8,7168]{1,0:T(8,128)(2,1)} %param.16), channel_id=1, source_target_pairs={{0,16},{4,20},{8,24},{12,28},{16,0},{20,4},{24,8},{28,12},{1,17},{... | collective-permute-start | bytes 344072 | tf_op jit(solution)/shard_map/ppermute | solution.py:22
  15.6 11.5 %collective-permute-start.4 = (bf16[8,7168]{1,0:T(8,128)(2,1)}, bf16[8,7168]{1,0:T(8,128)(2,1)S(1)}, u32[]{:S(2)}, u32[]{:S(2)}) collective-permute-start(bf16[8,7168]{1,0:T(8,128)(2,1)} %param.16), channel_id=1, source_target_pairs={{0,20},{4,24},{8,28},{12,0},{16,4},{20,8},{24,12},{28,16},{1,21},{... | collective-permute-start | bytes 344072 | tf_op jit(solution)/shard_map/ppermute | solution.py:22
  19.2 7.9 %collective-permute-start.5 = (bf16[8,7168]{1,0:T(8,128)(2,1)}, bf16[8,7168]{1,0:T(8,128)(2,1)S(1)}, u32[]{:S(2)}, u32[]{:S(2)}) collective-permute-start(bf16[8,7168]{1,0:T(8,128)(2,1)} %param.16), channel_id=1, source_target_pairs={{0,24},{4,28},{8,0},{12,4},{16,8},{20,12},{24,16},{28,20},{1,25},{... | collective-permute-start | bytes 344072 | tf_op jit(solution)/shard_map/ppermute | solution.py:22
  20.6 6.9 %collective-permute-start.6 = (bf16[8,7168]{1,0:T(8,128)(2,1)}, bf16[8,7168]{1,0:T(8,128)(2,1)S(1)}, u32[]{:S(2)}, u32[]{:S(2)}) collective-permute-start(bf16[8,7168]{1,0:T(8,128)(2,1)} %param.16), channel_id=1, source_target_pairs={{0,28},{4,0},{8,4},{12,8},{16,12},{20,16},{24,20},{28,24},{1,29},{... | collective-permute-start | bytes 344072 | tf_op jit(solution)/shard_map/ppermute | solution.py:22
  27.5 21.8 %collective-permute-start.7 = (bf16[8,8,7168]{2,1,0:T(8,128)(2,1)S(1)}, bf16[8,8,7168]{2,1,0:T(8,128)(2,1)S(1)}, u32[]{:S(2)}, u32[]{:S(2)}) collective-permute-start(bf16[8,8,7168]{2,1,0:T(8,128)(2,1)S(1)} %bitcast_dynamic-update-slice_fusion), channel_id=1, source_target_pairs={{0,2},{1,3},{2,0},{3,1},{4,6},{5,7},{6,4},{7,5},{8,10},{9,11},{10,... | collective-permute-start | bytes 2752520 | tf_op jit(solution)/shard_map/ppermute | solution.py:34
  49.6 3.9 %collective-permute-start.8 = (bf16[2,8,8,7168]{3,2,1,0:T(8,128)(2,1)S(1)}, bf16[2,8,8,7168]{3,2,1,0:T(8,128)(2,1)S(1)}, u32[]{:S(2)}, u32[]{:S(2)}) collective-permute-start(bf16[2,8,8,7168]{3,2,1,0:T(8,128)(2,1)S(1)} %get-tuple-element.14), channel_id=1, source_target_pairs={{0,1},{1,0},{2,3},{3,2},{4,5},{5,4},{6,7},{7,6},{8,9},{9,8},{10,11... | collective-permute-start | bytes 5505032 | tf_op jit(solution)/shard_map/ppermute | solution.py:34
  69.0 19.0 %copy-start.4 = (bf16[2,64,1024]{2,1,0:T(8,128)(2,1)S(1)}, bf16[2,64,1024]{2,1,0:T(8,128)(2,1)}, u32[]{:S(2)}) copy-start(bf16[2,64,1024]{2,1,0:T(8,128)(2,1)} %param.14) | copy-start | bytes 786436
  69.1 19.0 %copy-start.7 = (bf16[2,64,128]{2,1,0:T(8,128)(2,1)S(1)}, bf16[2,64,128]{2,1,0:T(8,128)(2,1)}, u32[]{:S(2)}) copy-start(bf16[2,64,128]{2,1,0:T(8,128)(2,1)} %param.12) | copy-start | bytes 98308
  76.1 23.6 %collective-permute-start.9 = (f32[2,8,8,7168]{3,2,1,0:T(8,128)}, f32[2,8,8,7168]{3,2,1,0:T(8,128)}, u32[]{:S(2)}, u32[]{:S(2)}) collective-permute-start(f32[2,8,8,7168]{3,2,1,0:T(8,128)} %bitcast.17), channel_id=1, source_target_pairs={{0,1},{1,0},{2,3},{3,2},{4,5},{5,4},{6,7},{7,6},{8,9},{9,8},{10,11... | collective-permute-start | bytes 11010056 | tf_op jit(solution)/shard_map/ppermute | solution.py:39
  76.3 18.5 %collective-permute-start.11 = (f32[8,8]{1,0:T(8,128)S(1)}, f32[8,8]{1,0:T(8,128)S(1)}, u32[]{:S(2)}, u32[]{:S(2)}) collective-permute-start(f32[8,8]{1,0:T(8,128)S(1)} %select_reduce_fusion), channel_id=1, source_target_pairs={{0,4},{4,8},{8,12},{12,16},{16,20},{20,24},{24,28},{28,0},{1,5},{5... | collective-permute-start | bytes 776 | tf_op jit(solution)/shard_map/ppermute | solution.py:22
  80.3 17.0 %collective-permute-start.12 = (f32[8,8]{1,0:T(8,128)S(1)}, f32[8,8]{1,0:T(8,128)S(1)}, u32[]{:S(2)}, u32[]{:S(2)}) collective-permute-start(f32[8,8]{1,0:T(8,128)S(1)} %select_reduce_fusion), channel_id=1, source_target_pairs={{0,8},{4,12},{8,16},{12,20},{16,24},{20,28},{24,0},{28,4},{1,9},{5... | collective-permute-start | bytes 776 | tf_op jit(solution)/shard_map/ppermute | solution.py:22
  85.4 22.5 %collective-permute-start.13 = (f32[8,8]{1,0:T(8,128)S(1)}, f32[8,8]{1,0:T(8,128)S(1)}, u32[]{:S(2)}, u32[]{:S(2)}) collective-permute-start(f32[8,8]{1,0:T(8,128)S(1)} %select_reduce_fusion), channel_id=1, source_target_pairs={{0,12},{4,16},{8,20},{12,24},{16,28},{20,0},{24,4},{28,8},{1,13},{... | collective-permute-start | bytes 776 | tf_op jit(solution)/shard_map/ppermute | solution.py:22
  85.4 23.6 %collective-permute-start.14 = (f32[8,8]{1,0:T(8,128)S(1)}, f32[8,8]{1,0:T(8,128)S(1)}, u32[]{:S(2)}, u32[]{:S(2)}) collective-permute-start(f32[8,8]{1,0:T(8,128)S(1)} %select_reduce_fusion), channel_id=1, source_target_pairs={{0,16},{4,20},{8,24},{12,28},{16,0},{20,4},{24,8},{28,12},{1,17},{... | collective-permute-start | bytes 776 | tf_op jit(solution)/shard_map/ppermute | solution.py:22
  94.8 14.2 %collective-permute-start.15 = (f32[8,8]{1,0:T(8,128)S(1)}, f32[8,8]{1,0:T(8,128)S(1)}, u32[]{:S(2)}, u32[]{:S(2)}) collective-permute-start(f32[8,8]{1,0:T(8,128)S(1)} %select_reduce_fusion), channel_id=1, source_target_pairs={{0,20},{4,24},{8,28},{12,0},{16,4},{20,8},{24,12},{28,16},{1,21},{... | collective-permute-start | bytes 776 | tf_op jit(solution)/shard_map/ppermute | solution.py:22
  97.3 11.8 %collective-permute-start.16 = (f32[8,8]{1,0:T(8,128)S(1)}, f32[8,8]{1,0:T(8,128)S(1)}, u32[]{:S(2)}, u32[]{:S(2)}) collective-permute-start(f32[8,8]{1,0:T(8,128)S(1)} %select_reduce_fusion), channel_id=1, source_target_pairs={{0,24},{4,28},{8,0},{12,4},{16,8},{20,12},{24,16},{28,20},{1,25},{... | collective-permute-start | bytes 776 | tf_op jit(solution)/shard_map/ppermute | solution.py:22
  99.7 9.4 %collective-permute-start.17 = (f32[8,8]{1,0:T(8,128)S(1)}, f32[8,8]{1,0:T(8,128)S(1)}, u32[]{:S(2)}, u32[]{:S(2)}) collective-permute-start(f32[8,8]{1,0:T(8,128)S(1)} %select_reduce_fusion), channel_id=1, source_target_pairs={{0,28},{4,0},{8,4},{12,8},{16,12},{20,16},{24,20},{28,24},{1,29},{... | collective-permute-start | bytes 776 | tf_op jit(solution)/shard_map/ppermute | solution.py:22
  107.9 43.4 %collective-permute-start.10 = (f32[8,8,7168]{2,1,0:T(8,128)}, f32[8,8,7168]{2,1,0:T(8,128)}, u32[]{:S(2)}, u32[]{:S(2)}) collective-permute-start(f32[8,8,7168]{2,1,0:T(8,128)} %slice_bitcast_fusion), channel_id=1, source_target_pairs={{0,2},{1,3},{2,0},{3,1},{4,6},{5,7},{6,4},{7,5},{8,10},{9,11},{10,... | collective-permute-start | bytes 5505032 | tf_op jit(solution)/shard_map/ppermute | solution.py:39
  109.1 40.4 %collective-permute-start.18 = (f32[8,8,8]{2,1,0:T(8,128)S(1)}, f32[8,8,8]{2,1,0:T(8,128)S(1)}, u32[]{:S(2)}, u32[]{:S(2)}) collective-permute-start(f32[8,8,8]{2,1,0:T(8,128)S(1)} %constant_dynamic-update-slice_fusion), channel_id=1, source_target_pairs={{0,2},{1,3},{2,0},{3,1},{4,6},{5,7},{6,4},{7,5},{8,10},{9,11},{10,... | collective-permute-start | bytes 6152 | tf_op jit(solution)/shard_map/ppermute | solution.py:34
  110.8 60.8 %reduce-scatter.5.cloned.1.call-start = ((), (), s32[]{:S(2)}) async-start(), calls=%async_computation.2 | async-start | bytes 655360 | tf_op jit(solution)/shard_map/reduce_scatter | solution.py:115
  149.5 1.5 collective-permute-start.19
  155.0 8.1 %collective-permute-start.20 = (f32[8,7168]{1,0:T(8,128)S(1)}, f32[8,7168]{1,0:T(8,128)S(1)}, u32[]{:S(2)}, u32[]{:S(2)}) collective-permute-start(f32[8,7168]{1,0:T(8,128)S(1)} %get-tuple-element.6), channel_id=1, source_target_pairs={{0,28},{4,0},{8,4},{12,8},{16,12},{20,16},{24,20},{28,24},{1,29},{... | collective-permute-start | bytes 688136 | tf_op jit(solution)/shard_map/ppermute | solution.py:29
  157.0 12.1 %collective-permute-start.21 = (f32[8,7168]{1,0:T(8,128)S(1)}, f32[8,7168]{1,0:T(8,128)S(1)}, u32[]{:S(2)}, u32[]{:S(2)}) collective-permute-start(f32[8,7168]{1,0:T(8,128)S(1)} %get-tuple-element.12), channel_id=1, source_target_pairs={{0,24},{4,28},{8,0},{12,4},{16,8},{20,12},{24,16},{28,20},{1,25},{... | collective-permute-start | bytes 688136 | tf_op jit(solution)/shard_map/ppermute | solution.py:29
  157.3 15.9 %collective-permute-start.22 = (f32[8,7168]{1,0:T(8,128)S(1)}, f32[8,7168]{1,0:T(8,128)}, u32[]{:S(2)}, u32[]{:S(2)}) collective-permute-start(f32[8,7168]{1,0:T(8,128)S(1)} %get-tuple-element.11), channel_id=1, source_target_pairs={{0,20},{4,24},{8,28},{12,0},{16,4},{20,8},{24,12},{28,16},{1,21},{... | collective-permute-start | bytes 688136 | tf_op jit(solution)/shard_map/ppermute | solution.py:29
  157.6 39.1 %collective-permute-start.23 = (f32[8,7168]{1,0:T(8,128)S(1)}, f32[8,7168]{1,0:T(8,128)}, u32[]{:S(2)}, u32[]{:S(2)}) collective-permute-start(f32[8,7168]{1,0:T(8,128)S(1)} %get-tuple-element.10), channel_id=1, source_target_pairs={{0,16},{4,20},{8,24},{12,28},{16,0},{20,4},{24,8},{28,12},{1,17},{... | collective-permute-start | bytes 688136 | tf_op jit(solution)/shard_map/ppermute | solution.py:29
  160.2 37.6 %collective-permute-start.24 = (f32[8,7168]{1,0:T(8,128)S(1)}, f32[8,7168]{1,0:T(8,128)}, u32[]{:S(2)}, u32[]{:S(2)}) collective-permute-start(f32[8,7168]{1,0:T(8,128)S(1)} %get-tuple-element.9), channel_id=1, source_target_pairs={{0,12},{4,16},{8,20},{12,24},{16,28},{20,0},{24,4},{28,8},{1,13},{... | collective-permute-start | bytes 688136 | tf_op jit(solution)/shard_map/ppermute | solution.py:29
  163.0 34.7 %collective-permute-start.25 = (f32[8,7168]{1,0:T(8,128)S(1)}, f32[8,7168]{1,0:T(8,128)}, u32[]{:S(2)}, u32[]{:S(2)}) collective-permute-start(f32[8,7168]{1,0:T(8,128)S(1)} %get-tuple-element.8), channel_id=1, source_target_pairs={{0,8},{4,12},{8,16},{12,20},{16,24},{20,28},{24,0},{28,4},{1,9},{5... | collective-permute-start | bytes 688136 | tf_op jit(solution)/shard_map/ppermute | solution.py:29
  169.8 28.0 %collective-permute-start.26 = (f32[8,7168]{1,0:T(8,128)S(1)}, f32[8,7168]{1,0:T(8,128)}, u32[]{:S(2)}, u32[]{:S(2)}) collective-permute-start(f32[8,7168]{1,0:T(8,128)S(1)} %get-tuple-element.7), channel_id=1, source_target_pairs={{0,4},{4,8},{8,12},{12,16},{16,20},{20,24},{24,28},{28,0},{1,5},{5... | collective-permute-start | bytes 688136 | tf_op jit(solution)/shard_map/ppermute | solution.py:29
  (9 other events, 59.6 us)
Sparse Core Ops, SparseCore 0:
  111.0 17.7 reduce-scatter.6
  151.1 20.4 reduce-scatter.4

commit v3 on v2

--- a/solution.py
+++ b/solution.py
@@ -53,28 +53,28 @@
     hit = route_ids[:, :, None] == jnp.arange(n_experts, dtype=jnp.int32)[None, None, :]
     wmat = jnp.sum(jnp.where(hit, route_gates[:, :, None], 0.0), axis=1)
     rows = shift_gather(tokens, "attn", n_attn)
-    wrows = shift_gather(wmat, "attn", n_attn)
     for bit in bits:
         rows = bit_gather(rows, "exp", bit, n_exp)
-        wrows = bit_gather(wrows, "exp", bit, n_exp)
     lead_shape = rows.shape[:-1]
     flat_rows = rows.reshape(-1, model_width)
-    flat_w = wrows.reshape(-1, n_experts)
-    first_expert = lax.axis_index("attn") * n_local
-    result = None
+    me = lax.axis_index("attn")
+    owners = (me + jnp.arange(n_attn, dtype=jnp.int32)) % n_attn
+    result = jnp.zeros((tok_count, model_width), jnp.float32)
     for i in range(n_local):
         partial = expert_part(flat_rows, w_gate[i], w_up[i], w_down[i])
         partial = partial.reshape(lead_shape + (model_width,))
         for bit in reversed(bits):
             partial = bit_reduce(partial, "exp", bit, n_exp)
-        weight = lax.dynamic_index_in_dim(flat_w, first_expert + i, axis=1, keepdims=False)
-        weight = weight.reshape(lead_shape)
-        for _ in bits:
-            weight = weight[0]
-        piece = partial.astype(jnp.bfloat16).astype(jnp.float32) * weight[..., None]
-        result = piece if result is None else result + piece
-    return shift_scatter_sum(result, "attn", n_attn).astype(jnp.bfloat16)
-
+        expert_rows = partial.astype(jnp.bfloat16)
+        back = [expert_rows[0]]
+        for k in range(1, n_attn):
+            back.append(
+                lax.ppermute(expert_rows[k], "attn", [(s, (s - k) % n_attn) for s in range(n_attn)])
+            )
+        chosen = jnp.take(wmat, owners * n_local + i, axis=1)
+        for k in range(n_attn):
+            result = result + chosen[:, k : k + 1] * back[k].astype(jnp.float32)
+    return result.astype(jnp.bfloat16)
 
 def per_device(
     q_latent,

time: 207 us -> 195 us (0.942)
  waiting for transfers between devices: 101 us -> 60.2 us
  blocking collectives: 5.98 us -> 42.9 us
  starting transfers between devices: 41.4 us -> 34.4 us
    ppermute x4 -> x2, waiting for transfers between devices: 62.7 us -> 24.1 us  [bit_gather(): other = lax.ppermute(x, axis, [(i, i ^ bit) for i in range(n)])]
    pmax x1, blocking collectives: 5.98 us -> 42.9 us  [per_device(): row_top = lax.pmax(block_max, 'exp')]
    ppermute x7, waiting for transfers between devices: 32.3 us -> 0.02 us  [routed_experts(): lax.ppermute(expert_rows[k], 'attn', [(s, (s - k) % n_attn) for s in rang...]
    ppermute x14 -> x7, starting transfers between devices: 31 us -> 13.9 us  [shift_gather(): pieces.append(lax.ppermute(x, axis, [(i, (i + k) % n) for i in range(n)]))]
    reduce_scatter x1, waiting for transfers between devices: 1.01 us -> 14.3 us  [per_device(): lax.psum_scatter(block_out * factor[:, :, None], 'exp', scatter_dimension...]
    ppermute x7, starting transfers between devices: 6.41 us -> 17.3 us  [routed_experts(): lax.ppermute(expert_rows[k], 'attn', [(s, (s - k) % n_attn) for s in rang...]
    unnamed x3, waiting for transfers between devices: 0.03 us -> 10.6 us
    ppermute x2, waiting for transfers between devices: 0.01 us -> 5.8 us  [bit_reduce(): return x[0] + lax.ppermute(x[1], axis, [(i, i ^ bit) for i in range(n)])]
  transfers between devices with their start and end apart: 29 -> 20, of which waited for: 11 -> 8; matrix products, arithmetic and copies ran while one was open for 7% -> 6% of each run, Pallas kernels for 0% -> 0%
where the time goes in v3:
time: 195 us; the launch traced here: 194 us
  waiting for transfers between devices  60.2 us (31%)
  blocking collectives  42.9 us (22%)
  starting transfers between devices  34.4 us (18%)
  local copies, waits for them, and re-layouts  17.2 us (9%)
  matrix products  14.9 us (8%)
  between operations  14.3 us (7%)
  other arithmetic  10.7 us (5%)
    pmax x1, blocking collectives, per_device(): row_top = lax.pmax(block_max, 'exp')  42.9 us
    ppermute x2, waiting for transfers between devices, bit_gather(): other = lax.ppermute(x, axis, [(i, i ^ bit) for i in range(n)])  24.1 us
    ppermute x7, starting transfers between devices, routed_experts(): lax.ppermute(expert_rows[k], 'attn', [(s, (s - k) % n_attn) for s in rang...  17.3 us
    reduce_scatter x1, waiting for transfers between devices, per_device(): lax.psum_scatter(block_out * factor[:, :, None], 'exp', scatter_dimension...  14.3 us
    ppermute x7, starting transfers between devices, shift_gather(): pieces.append(lax.ppermute(x, axis, [(i, (i + k) % n) for i in range(n)]))  13.9 us
    dot_general x1, matrix products, expert_part(): return jnp.dot(hidden, down_slice, preferred_element_type=jnp.float32)  11.2 us
    unnamed x3, waiting for transfers between devices  10.6 us
    unnamed x29, local copies, waits for them, and re-layouts  7.37 us
  transfers between devices with their start and end apart: 20, of which 8 were waited for; matrix products, arithmetic and copies ran while one was open for 6% of the time, Pallas kernels for 0%

profile of v3, /device:TPU:0, one launch (start us, length us, event | category | flops | bytes accessed | tf_op | source)
XLA Modules:
  0.0 194.4 jit_solution(4280347491924723976)
XLA Ops:
  7.2 3.0 %collective-permute-start = (bf16[8,7168]{1,0:T(8,128)(2,1)}, bf16[8,7168]{1,0:T(8,128)(2,1)S(1)}, u32[]{:S(2)}, u32[]{:S(2)}) collective-permute-start(bf16[8,7168]{1,0:T(8,128)(2,1)} %param.16), channel_id=1, source_target_pairs={{0,4},{4,8},{8,12},{12,16},{16,20},{20,24},{24,28},{28,0},{1,5},{5... | collective-permute-start | bytes 344072 | tf_op jit(solution)/shard_map/ppermute | solution.py:22
  10.2 1.6 collective-permute-start.1
  11.8 2.5 %collective-permute-start.2 = (bf16[8,7168]{1,0:T(8,128)(2,1)}, bf16[8,7168]{1,0:T(8,128)(2,1)S(1)}, u32[]{:S(2)}, u32[]{:S(2)}) collective-permute-start(bf16[8,7168]{1,0:T(8,128)(2,1)} %param.16), channel_id=1, source_target_pairs={{0,12},{4,16},{8,20},{12,24},{16,28},{20,0},{24,4},{28,8},{1,13},{... | collective-permute-start | bytes 344072 | tf_op jit(solution)/shard_map/ppermute | solution.py:22
  14.4 1.2 collective-permute-start.3
  15.6 2.6 %collective-permute-start.4 = (bf16[8,7168]{1,0:T(8,128)(2,1)}, bf16[8,7168]{1,0:T(8,128)(2,1)S(1)}, u32[]{:S(2)}, u32[]{:S(2)}) collective-permute-start(bf16[8,7168]{1,0:T(8,128)(2,1)} %param.16), channel_id=1, source_target_pairs={{0,20},{4,24},{8,28},{12,0},{16,4},{20,8},{24,12},{28,16},{1,21},{... | collective-permute-start | bytes 344072 | tf_op jit(solution)/shard_map/ppermute | solution.py:22
  19.2 1.4 collective-permute-start.5
  20.6 1.5 collective-permute-start.6
  22.1 4.5 %collective-permute-done.2 = bf16[8,7168]{1,0:T(8,128)(2,1)S(1)} collective-permute-done((bf16[8,7168]{1,0:T(8,128)(2,1)}, bf16[8,7168]{1,0:T(8,128)(2,1)S(1)}, u32[]{:S(2)}, u32[]{:S(2)}) %collective-permute-start.2) | collective-permute-done | bytes 114720 | tf_op jit(solution)/shard_map/ppermute | solution.py:22
  27.5 1.5 collective-permute-start.7
  29.0 20.4 %collective-permute-done.7 = bf16[8,8,7168]{2,1,0:T(8,128)(2,1)S(1)} collective-permute-done((bf16[8,8,7168]{2,1,0:T(8,128)(2,1)S(1)}, bf16[8,8,7168]{2,1,0:T(8,128)(2,1)S(1)}, u32[]{:S(2)}, u32[]{:S(2)}) %collective-permute-start.7) | collective-permute-done | bytes 917536 | tf_op jit(solution)/shard_map/ppermute | solution.py:34
  49.6 3.8 %collective-permute-done.8 = bf16[2,8,8,7168]{3,2,1,0:T(8,128)(2,1)S(1)} collective-permute-done((bf16[2,8,8,7168]{3,2,1,0:T(8,128)(2,1)S(1)}, bf16[2,8,8,7168]{3,2,1,0:T(8,128)(2,1)S(1)}, u32[]{:S(2)}, u32[]{:S(2)}) %collective-permute-start.8) | collective-permute-done | bytes 1835040 | tf_op jit(solution)/shard_map/ppermute | solution.py:34
  53.8 1.9 copy-done.2
  56.8 1.1 fusion.2
  57.9 11.2 %fusion = f32[256,7168]{1,0:T(8,128)} fusion(bf16[1,256,7168]{2,1,0:T(8,128)(2,1)} %param.21, f32[256,256]{1,0:T(8,128)S(1)} %fusion.2, bf16[256,7168]{1,0:T(8,128)(2,1)} %bitcast.95, bf16[1,7168,256]{2,1,0:T(8,128)(2,1)} %param.19), kind=kOutput, calls=%fused_computation.2 | convolution fusion | flops 1879441408 | bytes 18612224 | tf_op jit(solution)/shard_map/dot_general | solution.py:16
  69.1 7.0 %fusion.36 = (f32[128,7168]{1,0:T(8,128)}, f32[128,7168]{1,0:T(8,128)}) fusion(f32[256,7168]{1,0:T(8,128)} %fusion), kind=kLoop, calls=%fused_computation.82 | loop fusion | bytes 14680064 | tf_op jit(solution)/shard_map/slice | solution.py:39
  77.0 5.8 %collective-permute-done.9 = f32[2,8,8,7168]{3,2,1,0:T(8,128)} collective-permute-done((f32[2,8,8,7168]{3,2,1,0:T(8,128)}, f32[2,8,8,7168]{3,2,1,0:T(8,128)}, u32[]{:S(2)}, u32[]{:S(2)}) %collective-permute-start.9) | collective-permute-done | bytes 3670048 | tf_op jit(solution)/shard_map/ppermute | solution.py:39
  82.8 3.6 %add.111 = f32[2,8,8,7168]{3,2,1,0:T(8,128)S(1)} add(f32[2,8,8,7168]{3,2,1,0:T(8,128)} %bitcast.93, f32[2,8,8,7168]{3,2,1,0:T(8,128)} %collective-permute-done.9) | non-fusion elementwise | flops 917504 | bytes 11010048 | tf_op jit(solution)/shard_map/add | solution.py:39
  86.4 1.8 copy-done.1
  88.2 1.4 slice_bitcast_fusion
  89.6 1.5 collective-permute-start.10
  91.6 42.9 %pmax.7 = f32[2,128]{1,0:T(2,128)S(1)} all-reduce(f32[2,128]{1,0:T(2,128)S(1)} %get-tuple-element.23), channel_id=1, replica_groups=mesh['attn'=8,'exp'=4] {'exp'}, use_global_device_ids=true, to_apply=%region_1.2 | all-reduce | flops 256 | bytes 2048 | tf_op jit(solution)/shard_map/pmax | solution.py:112
  135.7 1.3 convolution_multiply_fusion
  137.9 2.2 %fusion.7 = bf16[8,8,7168]{2,1,0:T(8,128)(2,1)S(1)} fusion(f32[8,8,7168]{2,1,0:T(8,128)} %collective-permute-done.10, f32[2,8,8,7168]{3,2,1,0:T(8,128)} %copy-done.1), kind=kLoop, calls=%fused_computation.11 | loop fusion | flops 917504 | bytes 4587520 | tf_op jit(solution)/shard_map/convert_element_type | solution.py:68
  140.9 8.1 %collective-permute-start.11 = (bf16[8,7168]{1,0:T(8,128)(2,1)}, bf16[8,7168]{1,0:T(8,128)(2,1)}, u32[]{:S(2)}, u32[]{:S(2)}) collective-permute-start(bf16[8,7168]{1,0:T(8,128)(2,1)} %get-tuple-element.8), channel_id=1, source_target_pairs={{0,28},{4,0},{8,4},{12,8},{16,12},{20,16},{24,20},{28,24},{1,29},{... | collective-permute-start | bytes 344072 | tf_op jit(solution)/shard_map/ppermute | solution.py:72
  149.0 10.5 %reduce-scatter.7.cloned.1.call-done = f32[32,2]{1,0:T(8,128)} async-done(((f32[128,2]{1,0:T(8,128)}), f32[32,2]{1,0:T(8,128)}) %reduce-scatter.7.cloned.1.call-update) | async-done | bytes 272
  160.3 3.3 %collective-permute-start.13 = (bf16[8,7168]{1,0:T(8,128)(2,1)}, bf16[8,7168]{1,0:T(8,128)(2,1)}, u32[]{:S(2)}, u32[]{:S(2)}) collective-permute-start(bf16[8,7168]{1,0:T(8,128)(2,1)} %get-tuple-element.13), channel_id=1, source_target_pairs={{0,20},{4,24},{8,28},{12,0},{16,4},{20,8},{24,12},{28,16},{1,21},{... | collective-permute-start | bytes 344072 | tf_op jit(solution)/shard_map/ppermute | solution.py:72
  164.1 1.5 collective-permute-start.15
  165.6 2.4 %collective-permute-start.16 = (bf16[8,7168]{1,0:T(8,128)(2,1)S(1)}, bf16[8,7168]{1,0:T(8,128)(2,1)}, u32[]{:S(2)}, u32[]{:S(2)}) collective-permute-start(bf16[8,7168]{1,0:T(8,128)(2,1)S(1)} %get-tuple-element.10), channel_id=1, source_target_pairs={{0,8},{4,12},{8,16},{12,20},{16,24},{20,28},{24,0},{28,4},{1,9},{5... | collective-permute-start | bytes 344072 | tf_op jit(solution)/shard_map/ppermute | solution.py:72
  168.0 1.5 collective-permute-start.17
  169.5 14.3 %reduce-scatter.5.cloned.1.call-done = f32[2,32,512]{2,1,0:T(8,128)} async-done(((f32[2,128,512]{2,1,0:T(8,128)}), f32[2,32,512]{2,1,0:T(8,128)}) %reduce-scatter.5.cloned.1.call-update) | async-done | bytes 131088 | tf_op jit(solution)/shard_map/reduce_scatter | solution.py:115
  183.8 1.6 divide_convert_fusion
  185.4 2.1 %fusion.23 = bf16[8,7168]{1,0:T(8,128)(2,1)} fusion(bf16[8,7168]{1,0:T(8,128)(2,1)} %collective-permute-done.17, bf16[8,7168]{1,0:T(8,128)(2,1)} %collective-permute-done.16, bf16[8,7168]{1,0:T(8,128)(2,1)} %collective-permute-done.15, bf16[8,7168]{1,0:T(8,128)(2,1)} %collective-permute-done.14, bf16[8,7168]{1,0:T(8,128)(2,1)} %collective-permute-done.13, ...), kind=kLoop, calls=%fused_computation.32 | loop fusion | flops 1376256 | bytes 1032448 | tf_op jit(solution)/shard_map/convert_element_type | solution.py:77
  (67 shorter events, 9.1 us)
Async XLA Ops:
  7.2 69.0 %copy-start = (bf16[2,1024,512]{2,1,0:T(8,128)(2,1)S(1)}, bf16[2,1024,512]{2,1,0:T(8,128)(2,1)}, u32[]{:S(2)}) copy-start(bf16[2,1024,512]{2,1,0:T(8,128)(2,1)} %param.13) | copy-start | bytes 6291460
  7.2 152.3 %reduce-scatter.7.cloned.1.call-start = ((), (), s32[]{:S(2)}) async-start(), calls=%async_computation.3 | async-start | bytes 81920
  7.2 12.0 %collective-permute-start = (bf16[8,7168]{1,0:T(8,128)(2,1)}, bf16[8,7168]{1,0:T(8,128)(2,1)S(1)}, u32[]{:S(2)}, u32[]{:S(2)}) collective-permute-start(bf16[8,7168]{1,0:T(8,128)(2,1)} %param.16), channel_id=1, source_target_pairs={{0,4},{4,8},{8,12},{12,16},{16,20},{20,24},{24,28},{28,0},{1,5},{5... | collective-permute-start | bytes 344072 | tf_op jit(solution)/shard_map/ppermute | solution.py:22
  10.2 10.4 %collective-permute-start.1 = (bf16[8,7168]{1,0:T(8,128)(2,1)}, bf16[8,7168]{1,0:T(8,128)(2,1)S(1)}, u32[]{:S(2)}, u32[]{:S(2)}) collective-permute-start(bf16[8,7168]{1,0:T(8,128)(2,1)} %param.16), channel_id=1, source_target_pairs={{0,8},{4,12},{8,16},{12,20},{16,24},{20,28},{24,0},{28,4},{1,9},{5... | collective-permute-start | bytes 344072 | tf_op jit(solution)/shard_map/ppermute | solution.py:22
  11.8 14.8 %collective-permute-start.2 = (bf16[8,7168]{1,0:T(8,128)(2,1)}, bf16[8,7168]{1,0:T(8,128)(2,1)S(1)}, u32[]{:S(2)}, u32[]{:S(2)}) collective-permute-start(bf16[8,7168]{1,0:T(8,128)(2,1)} %param.16), channel_id=1, source_target_pairs={{0,12},{4,16},{8,20},{12,24},{16,28},{20,0},{24,4},{28,8},{1,13},{... | collective-permute-start | bytes 344072 | tf_op jit(solution)/shard_map/ppermute | solution.py:22
  14.4 12.7 %collective-permute-start.3 = (bf16[8,7168]{1,0:T(8,128)(2,1)}, bf16[8,7168]{1,0:T(8,128)(2,1)S(1)}, u32[]{:S(2)}, u32[]{:S(2)}) collective-permute-start(bf16[8,7168]{1,0:T(8,128)(2,1)} %param.16), channel_id=1, source_target_pairs={{0,16},{4,20},{8,24},{12,28},{16,0},{20,4},{24,8},{28,12},{1,17},{... | collective-permute-start | bytes 344072 | tf_op jit(solution)/shard_map/ppermute | solution.py:22
  15.6 11.5 %collective-permute-start.4 = (bf16[8,7168]{1,0:T(8,128)(2,1)}, bf16[8,7168]{1,0:T(8,128)(2,1)S(1)}, u32[]{:S(2)}, u32[]{:S(2)}) collective-permute-start(bf16[8,7168]{1,0:T(8,128)(2,1)} %param.16), channel_id=1, source_target_pairs={{0,20},{4,24},{8,28},{12,0},{16,4},{20,8},{24,12},{28,16},{1,21},{... | collective-permute-start | bytes 344072 | tf_op jit(solution)/shard_map/ppermute | solution.py:22
  19.2 7.9 %collective-permute-start.5 = (bf16[8,7168]{1,0:T(8,128)(2,1)}, bf16[8,7168]{1,0:T(8,128)(2,1)S(1)}, u32[]{:S(2)}, u32[]{:S(2)}) collective-permute-start(bf16[8,7168]{1,0:T(8,128)(2,1)} %param.16), channel_id=1, source_target_pairs={{0,24},{4,28},{8,0},{12,4},{16,8},{20,12},{24,16},{28,20},{1,25},{... | collective-permute-start | bytes 344072 | tf_op jit(solution)/shard_map/ppermute | solution.py:22
  20.6 6.9 %collective-permute-start.6 = (bf16[8,7168]{1,0:T(8,128)(2,1)}, bf16[8,7168]{1,0:T(8,128)(2,1)S(1)}, u32[]{:S(2)}, u32[]{:S(2)}) collective-permute-start(bf16[8,7168]{1,0:T(8,128)(2,1)} %param.16), channel_id=1, source_target_pairs={{0,28},{4,0},{8,4},{12,8},{16,12},{20,16},{24,20},{28,24},{1,29},{... | collective-permute-start | bytes 344072 | tf_op jit(solution)/shard_map/ppermute | solution.py:22
  27.5 21.8 %collective-permute-start.7 = (bf16[8,8,7168]{2,1,0:T(8,128)(2,1)S(1)}, bf16[8,8,7168]{2,1,0:T(8,128)(2,1)S(1)}, u32[]{:S(2)}, u32[]{:S(2)}) collective-permute-start(bf16[8,8,7168]{2,1,0:T(8,128)(2,1)S(1)} %bitcast_dynamic-update-slice_fusion), channel_id=1, source_target_pairs={{0,2},{1,3},{2,0},{3,1},{4,6},{5,7},{6,4},{7,5},{8,10},{9,11},{10,... | collective-permute-start | bytes 2752520 | tf_op jit(solution)/shard_map/ppermute | solution.py:34
  49.6 3.9 %collective-permute-start.8 = (bf16[2,8,8,7168]{3,2,1,0:T(8,128)(2,1)S(1)}, bf16[2,8,8,7168]{3,2,1,0:T(8,128)(2,1)S(1)}, u32[]{:S(2)}, u32[]{:S(2)}) collective-permute-start(bf16[2,8,8,7168]{3,2,1,0:T(8,128)(2,1)S(1)} %get-tuple-element.7), channel_id=1, source_target_pairs={{0,1},{1,0},{2,3},{3,2},{4,5},{5,4},{6,7},{7,6},{8,9},{9,8},{10,11... | collective-permute-start | bytes 5505032 | tf_op jit(solution)/shard_map/ppermute | solution.py:34
  53.4 3.4 %copy-start.9 = (bf16[1,7168,256]{2,1,0:T(8,128)(2,1)S(1)}, bf16[1,7168,256]{2,1,0:T(8,128)(2,1)}, u32[]{:S(2)}) copy-start(bf16[1,7168,256]{2,1,0:T(8,128)(2,1)} %param.20) | copy-start | bytes 11010052
  53.7 1.9 copy-start.2
  69.1 7.2 %copy-start.4 = (bf16[2,128,512]{2,1,0:T(8,128)(2,1)S(1)}, bf16[2,128,512]{2,1,0:T(8,128)(2,1)}, u32[]{:S(2)}) copy-start(bf16[2,128,512]{2,1,0:T(8,128)(2,1)} %param.11) | copy-start | bytes 786436
  76.1 6.8 %collective-permute-start.9 = (f32[2,8,8,7168]{3,2,1,0:T(8,128)}, f32[2,8,8,7168]{3,2,1,0:T(8,128)}, u32[]{:S(2)}, u32[]{:S(2)}) collective-permute-start(f32[2,8,8,7168]{3,2,1,0:T(8,128)} %bitcast.20), channel_id=1, source_target_pairs={{0,1},{1,0},{2,3},{3,2},{4,5},{5,4},{6,7},{7,6},{8,9},{9,8},{10,11... | collective-permute-start | bytes 11010056 | tf_op jit(solution)/shard_map/ppermute | solution.py:39
  86.4 1.8 copy-start.1
  88.2 2.9 %copy-start.8 = (s32[2]{0:T(128)S(1)}, s32[2]{0:T(128)}, u32[]{:S(2)}) copy-start(s32[2]{0:T(128)} %param.15) | copy-start | bytes 28
  88.2 3.0 %copy-start.3 = (bf16[2,64,1024]{2,1,0:T(8,128)(2,1)S(1)}, bf16[2,64,1024]{2,1,0:T(8,128)(2,1)}, u32[]{:S(2)}) copy-start(bf16[2,64,1024]{2,1,0:T(8,128)(2,1)} %param.14) | copy-start | bytes 786436
  88.2 3.0 %copy-start.5 = (bf16[2,64,128]{2,1,0:T(8,128)(2,1)S(1)}, bf16[2,64,128]{2,1,0:T(8,128)(2,1)}, u32[]{:S(2)}) copy-start(bf16[2,64,128]{2,1,0:T(8,128)(2,1)} %param.12) | copy-start | bytes 98308
  89.6 48.3 %collective-permute-start.10 = (f32[8,8,7168]{2,1,0:T(8,128)}, f32[8,8,7168]{2,1,0:T(8,128)}, u32[]{:S(2)}, u32[]{:S(2)}) collective-permute-start(f32[8,8,7168]{2,1,0:T(8,128)} %slice_bitcast_fusion), channel_id=1, source_target_pairs={{0,2},{1,3},{2,0},{3,1},{4,6},{5,7},{6,4},{7,5},{8,10},{9,11},{10,... | collective-permute-start | bytes 5505032 | tf_op jit(solution)/shard_map/ppermute | solution.py:39
  91.2 45.9 %copy-start.6 = (f32[8,4]{0,1:T(4,128)S(1)}, f32[8,4]{0,1:T(4,128)}, u32[]{:S(2)}) copy-start(f32[8,4]{0,1:T(4,128)} %param.18) | copy-start | bytes 388
  91.2 45.9 %copy-start.7 = (s32[8,4]{0,1:T(4,128)S(1)}, s32[8,4]{0,1:T(4,128)}, u32[]{:S(2)}) copy-start(s32[8,4]{0,1:T(4,128)} %param.17) | copy-start | bytes 388
  135.6 48.2 %reduce-scatter.5.cloned.1.call-start = ((), (), s32[]{:S(2)}) async-start(), calls=%async_computation.2 | async-start | bytes 655360 | tf_op jit(solution)/shard_map/reduce_scatter | solution.py:115
  140.9 24.8 %collective-permute-start.11 = (bf16[8,7168]{1,0:T(8,128)(2,1)}, bf16[8,7168]{1,0:T(8,128)(2,1)}, u32[]{:S(2)}, u32[]{:S(2)}) collective-permute-start(bf16[8,7168]{1,0:T(8,128)(2,1)} %get-tuple-element.8), channel_id=1, source_target_pairs={{0,28},{4,0},{8,4},{12,8},{16,12},{20,16},{24,20},{28,24},{1,29},{... | collective-permute-start | bytes 344072 | tf_op jit(solution)/shard_map/ppermute | solution.py:72
  148.9 19.1 %collective-permute-start.12 = (bf16[8,7168]{1,0:T(8,128)(2,1)}, bf16[8,7168]{1,0:T(8,128)(2,1)}, u32[]{:S(2)}, u32[]{:S(2)}) collective-permute-start(bf16[8,7168]{1,0:T(8,128)(2,1)} %get-tuple-element.14), channel_id=1, source_target_pairs={{0,24},{4,28},{8,0},{12,4},{16,8},{20,12},{24,16},{28,20},{1,25},{... | collective-permute-start | bytes 344072 | tf_op jit(solution)/shard_map/ppermute | solution.py:72
  160.3 25.1 %collective-permute-start.13 = (bf16[8,7168]{1,0:T(8,128)(2,1)}, bf16[8,7168]{1,0:T(8,128)(2,1)}, u32[]{:S(2)}, u32[]{:S(2)}) collective-permute-start(bf16[8,7168]{1,0:T(8,128)(2,1)} %get-tuple-element.13), channel_id=1, source_target_pairs={{0,20},{4,24},{8,28},{12,0},{16,4},{20,8},{24,12},{28,16},{1,21},{... | collective-permute-start | bytes 344072 | tf_op jit(solution)/shard_map/ppermute | solution.py:72
  163.6 21.8 %collective-permute-start.14 = (bf16[8,7168]{1,0:T(8,128)(2,1)S(1)}, bf16[8,7168]{1,0:T(8,128)(2,1)}, u32[]{:S(2)}, u32[]{:S(2)}) collective-permute-start(bf16[8,7168]{1,0:T(8,128)(2,1)S(1)} %get-tuple-element.12), channel_id=1, source_target_pairs={{0,16},{4,20},{8,24},{12,28},{16,0},{20,4},{24,8},{28,12},{1,17},{... | collective-permute-start | bytes 344072 | tf_op jit(solution)/shard_map/ppermute | solution.py:72
  164.1 21.3 %collective-permute-start.15 = (bf16[8,7168]{1,0:T(8,128)(2,1)S(1)}, bf16[8,7168]{1,0:T(8,128)(2,1)}, u32[]{:S(2)}, u32[]{:S(2)}) collective-permute-start(bf16[8,7168]{1,0:T(8,128)(2,1)S(1)} %get-tuple-element.11), channel_id=1, source_target_pairs={{0,12},{4,16},{8,20},{12,24},{16,28},{20,0},{24,4},{28,8},{1,13},{... | collective-permute-start | bytes 344072 | tf_op jit(solution)/shard_map/ppermute | solution.py:72
  165.6 19.8 %collective-permute-start.16 = (bf16[8,7168]{1,0:T(8,128)(2,1)S(1)}, bf16[8,7168]{1,0:T(8,128)(2,1)}, u32[]{:S(2)}, u32[]{:S(2)}) collective-permute-start(bf16[8,7168]{1,0:T(8,128)(2,1)S(1)} %get-tuple-element.10), channel_id=1, source_target_pairs={{0,8},{4,12},{8,16},{12,20},{16,24},{20,28},{24,0},{28,4},{1,9},{5... | collective-permute-start | bytes 344072 | tf_op jit(solution)/shard_map/ppermute | solution.py:72
  168.0 17.4 %collective-permute-start.17 = (bf16[8,7168]{1,0:T(8,128)(2,1)S(1)}, bf16[8,7168]{1,0:T(8,128)(2,1)}, u32[]{:S(2)}, u32[]{:S(2)}) collective-permute-start(bf16[8,7168]{1,0:T(8,128)(2,1)S(1)} %get-tuple-element.9), channel_id=1, source_target_pairs={{0,4},{4,8},{8,12},{12,16},{16,20},{20,24},{24,28},{28,0},{1,5},{5... | collective-permute-start | bytes 344072 | tf_op jit(solution)/shard_map/ppermute | solution.py:72
Sparse Core Ops, SparseCore 0:
  135.8 23.7 reduce-scatter.6
  162.1 21.6 reduce-scatter.4

commit v4 on v3

--- a/solution.py
+++ b/solution.py
@@ -39,7 +39,7 @@
     return x[0] + lax.ppermute(x[1], axis, [(i, i ^ bit) for i in range(n)])
 
 
-def routed_experts(tokens, route_ids, route_gates, w_gate, w_up, w_down):
+def routed_experts(tokens, route_ids, route_gates, w_gate, w_up, w_down, earlier):
     n_exp = lax.axis_size("exp")
     n_attn = lax.axis_size("attn")
     n_local = w_gate.shape[0]
@@ -53,6 +53,7 @@
     hit = route_ids[:, :, None] == jnp.arange(n_experts, dtype=jnp.int32)[None, None, :]
     wmat = jnp.sum(jnp.where(hit, route_gates[:, :, None], 0.0), axis=1)
     rows = shift_gather(tokens, "attn", n_attn)
+    rows, _ = lax.optimization_barrier((rows, earlier))
     for bit in bits:
         rows = bit_gather(rows, "exp", bit, n_exp)
     lead_shape = rows.shape[:-1]
@@ -109,14 +110,13 @@
         cache_latent,
         preferred_element_type=jnp.float32,
     )
-    row_top = lax.pmax(block_max, "exp")
+    row_top = jnp.max(lax.all_gather(block_max, "exp", axis=0), axis=0)
     factor = jnp.exp(block_max - row_top)
-    numerator, denominator = (
-        lax.psum_scatter(block_out * factor[:, :, None], "exp", scatter_dimension=1, tiled=True),
-        lax.psum_scatter(block_sum * factor, "exp", scatter_dimension=1, tiled=True),
-    )
+    packed = jnp.concatenate([block_out * factor[:, :, None], (block_sum * factor)[:, :, None]], axis=2)
+    reduced = lax.psum_scatter(packed, "exp", scatter_dimension=1, tiled=True)
+    numerator, denominator = reduced[:, :, :-1], reduced[:, :, -1]
     attn_out = (numerator / denominator[:, :, None]).astype(jnp.bfloat16)
-    moe_out = routed_experts(tokens, route_ids, route_gates, w_gate, w_up, w_down)
+    moe_out = routed_experts(tokens, route_ids, route_gates, w_gate, w_up, w_down, attn_out)
     return (attn_out, moe_out)
 
 

time: 195 us -> 188 us (0.964)
  waiting for transfers between devices: 60.2 us -> 103 us
  blocking collectives: 42.9 us -> 5.07 us
  starting transfers between devices: 34.4 us -> 25.1 us
  local copies, waits for them, and re-layouts: 17.2 us -> 14.6 us
    pmax x1 -> x0, blocking collectives: 42.9 us -> none  [per_device(): row_top = lax.pmax(block_max, 'exp')]
    ppermute x2, waiting for transfers between devices: 5.8 us -> 47.4 us  [bit_reduce(): return x[0] + lax.ppermute(x[1], axis, [(i, i ^ bit) for i in range(n)])]
    ppermute x7, waiting for transfers between devices: 0.02 us -> 15.1 us  [routed_experts(): lax.ppermute(expert_rows[k], 'attn', [(s, (s - k) % n_attn) for s in rang...]
    unnamed x3 -> x1, waiting for transfers between devices: 10.6 us -> 0.02 us
    ppermute x7, starting transfers between devices: 17.3 us -> 10.1 us  [routed_experts(): lax.ppermute(expert_rows[k], 'attn', [(s, (s - k) % n_attn) for s in rang...]
    all_gather x0 -> x1, blocking collectives: none -> 5.07 us  [per_device(): row_top = jnp.max(lax.all_gather(block_max, 'exp', axis=0), axis=0)]
    ppermute x7, waiting for transfers between devices: 5.32 us -> 1.79 us  [shift_gather(): pieces.append(lax.ppermute(x, axis, [(i, (i + k) % n) for i in range(n)]))]
    slice x1, local copies, waits for them, and re-layouts: 7.01 us -> 3.94 us  [bit_reduce(): return x[0] + lax.ppermute(x[1], axis, [(i, i ^ bit) for i in range(n)])]
  transfers between devices with their start and end apart: 20 -> 19, of which waited for: 8 -> 12; matrix products, arithmetic and copies ran while one was open for 6% -> 6% of each run, Pallas kernels for 0% -> 0%
where the time goes in v4:
time: 188 us
  waiting for transfers between devices  103 us (55%)
  starting transfers between devices  25.1 us (13%)
  matrix products  16.8 us (9%)
  local copies, waits for them, and re-layouts  14.6 us (8%)
  between operations  14.2 us (8%)
  other arithmetic  9.04 us (5%)
  blocking collectives  5.07 us (3%)
    ppermute x2, waiting for transfers between devices, bit_reduce(): return x[0] + lax.ppermute(x[1], axis, [(i, i ^ bit) for i in range(n)])  47.4 us
    ppermute x2, waiting for transfers between devices, bit_gather(): other = lax.ppermute(x, axis, [(i, i ^ bit) for i in range(n)])  25.6 us
    ppermute x7, waiting for transfers between devices, routed_experts(): lax.ppermute(expert_rows[k], 'attn', [(s, (s - k) % n_attn) for s in rang...  15.1 us
    ppermute x7, starting transfers between devices, shift_gather(): pieces.append(lax.ppermute(x, axis, [(i, (i + k) % n) for i in range(n)]))  13.9 us
    reduce_scatter x1, waiting for transfers between devices, per_device(): reduced = lax.psum_scatter(packed, 'exp', scatter_dimension=1, tiled=True)  13.2 us
    dot_general x1, matrix products, expert_part(): return jnp.dot(hidden, down_slice, preferred_element_type=jnp.float32)  11.2 us
    ppermute x7, starting transfers between devices, routed_experts(): lax.ppermute(expert_rows[k], 'attn', [(s, (s - k) % n_attn) for s in rang...  10.1 us
    unnamed x21, local copies, waits for them, and re-layouts  7.6 us
  transfers between devices with their start and end apart: 19, of which 12 were waited for; matrix products, arithmetic and copies ran while one was open for 6% of the time, Pallas kernels for 0%

profile of v4, /device:TPU:0, one launch (start us, length us, event | category | flops | bytes accessed | tf_op | source)
XLA Modules:
  0.0 187.8 jit_solution(8172415831278345690)
XLA Ops:
  7.2 3.0 %collective-permute-start = (bf16[8,7168]{1,0:T(8,128)(2,1)}, bf16[8,7168]{1,0:T(8,128)(2,1)}, u32[]{:S(2)}, u32[]{:S(2)}) collective-permute-start(bf16[8,7168]{1,0:T(8,128)(2,1)} %param.16), channel_id=1, source_target_pairs={{0,4},{4,8},{8,12},{12,16},{16,20},{20,24},{24,28},{28,0},{1,5},{5... | collective-permute-start | bytes 344072 | tf_op jit(solution)/shard_map/ppermute | solution.py:22
  10.2 1.6 collective-permute-start.1
  11.8 2.5 %collective-permute-start.2 = (bf16[8,7168]{1,0:T(8,128)(2,1)}, bf16[8,7168]{1,0:T(8,128)(2,1)}, u32[]{:S(2)}, u32[]{:S(2)}) collective-permute-start(bf16[8,7168]{1,0:T(8,128)(2,1)} %param.16), channel_id=1, source_target_pairs={{0,12},{4,16},{8,20},{12,24},{16,28},{20,0},{24,4},{28,8},{1,13},{... | collective-permute-start | bytes 344072 | tf_op jit(solution)/shard_map/ppermute | solution.py:22
  14.4 1.2 collective-permute-start.3
  15.6 2.6 %collective-permute-start.4 = (bf16[8,7168]{1,0:T(8,128)(2,1)}, bf16[8,7168]{1,0:T(8,128)(2,1)S(1)}, u32[]{:S(2)}, u32[]{:S(2)}) collective-permute-start(bf16[8,7168]{1,0:T(8,128)(2,1)} %param.16), channel_id=1, source_target_pairs={{0,20},{4,24},{8,28},{12,0},{16,4},{20,8},{24,12},{28,16},{1,21},{... | collective-permute-start | bytes 344072 | tf_op jit(solution)/shard_map/ppermute | solution.py:22
  19.0 1.8 fusion.38
  20.7 1.4 fusion.37
  22.5 5.1 %all-gather.1 = f32[4,2,128]{2,1,0:T(2,128)S(1)} all-gather(f32[1,2,128]{2,1,0:T(2,128)S(1)} %bitcast.101), channel_id=2, replica_groups=mesh['attn'=8,'exp'=4] {'exp'}, dimensions={0}, use_global_device_ids=true | all-gather | bytes 5120 | tf_op jit(solution)/shard_map/all_gather | solution.py:113
  27.6 1.4 convolution_multiply_fusion
  29.1 1.9 %pad_maximum_fusion.2 = f32[2,128,513]{2,1,0:T(8,128)} fusion(f32[2,128,1]{2,1,0:T(8,128)S(1)} %copy.21, f32[2,128,512]{2,1,0:T(8,128)} %convolution_multiply_fusion), kind=kLoop, calls=%fused_computation.20 | loop fusion | flops 131328 | bytes 1050624 | tf_op jit(solution)/shard_map/concatenate | solution.py:115
  31.1 1.4 collective-permute-start.5
  33.4 1.5 collective-permute-start.6
  36.8 1.7 collective-permute-done.6
  38.6 13.2 %reduce-scatter.2.cloned.1.call-done = f32[2,32,513]{2,1,0:T(8,128)} async-done(((f32[2,128,513]{2,1,0:T(8,128)}), f32[2,32,513]{2,1,0:T(8,128)}) %reduce-scatter.2.cloned.1.call-update) | async-done | bytes 131344 | tf_op jit(solution)/shard_map/reduce_scatter | solution.py:116
  52.6 1.6 fusion.28
  54.5 21.8 %collective-permute-done.7 = bf16[8,8,7168]{2,1,0:T(8,128)(2,1)S(1)} collective-permute-done((bf16[8,8,7168]{2,1,0:T(8,128)(2,1)S(1)}, bf16[8,8,7168]{2,1,0:T(8,128)(2,1)S(1)}, u32[]{:S(2)}, u32[]{:S(2)}) %collective-permute-start.7) | collective-permute-done | bytes 917536 | tf_op jit(solution)/shard_map/ppermute | solution.py:34
  76.6 3.8 %collective-permute-done.8 = bf16[2,8,8,7168]{3,2,1,0:T(8,128)(2,1)S(1)} collective-permute-done((bf16[2,8,8,7168]{3,2,1,0:T(8,128)(2,1)S(1)}, bf16[2,8,8,7168]{3,2,1,0:T(8,128)(2,1)S(1)}, u32[]{:S(2)}, u32[]{:S(2)}) %collective-permute-start.8) | collective-permute-done | bytes 1835040 | tf_op jit(solution)/shard_map/ppermute | solution.py:34
  80.8 1.9 %copy-done.2 = bf16[2,2,8,8,7168]{4,3,2,1,0:T(8,128)(2,1)} copy-done((bf16[2,2,8,8,7168]{4,3,2,1,0:T(8,128)(2,1)}, bf16[2,2,8,8,7168]{4,3,2,1,0:T(8,128)(2,1)S(1)}, u32[]{:S(2)}) %copy-start.2) | copy-done | bytes 3670040
  82.6 1.1 copy-done.6
  84.9 11.2 %fusion = f32[256,7168]{1,0:T(8,128)} fusion(bf16[1,256,7168]{2,1,0:T(8,128)(2,1)} %param.21, f32[256,256]{1,0:T(8,128)S(1)} %fusion.2, bf16[256,7168]{1,0:T(8,128)(2,1)} %bitcast.96, bf16[1,7168,256]{2,1,0:T(8,128)(2,1)} %param.19), kind=kOutput, calls=%fused_computation.2 | convolution fusion | flops 1879441408 | bytes 18612224 | tf_op jit(solution)/shard_map/dot_general | solution.py:16
  96.1 3.9 %fusion.36 = (f32[128,7168]{1,0:T(8,128)S(1)}, f32[128,7168]{1,0:T(8,128)S(1)}) fusion(f32[256,7168]{1,0:T(8,128)} %fusion), kind=kLoop, calls=%fused_computation.85 | loop fusion | bytes 14680064 | tf_op jit(solution)/shard_map/slice | solution.py:39
  100.2 6.3 %collective-permute-done.9 = f32[2,8,8,7168]{3,2,1,0:T(8,128)S(1)} collective-permute-done((f32[2,8,8,7168]{3,2,1,0:T(8,128)S(1)}, f32[2,8,8,7168]{3,2,1,0:T(8,128)S(1)}, u32[]{:S(2)}, u32[]{:S(2)}) %collective-permute-start.9) | collective-permute-done | bytes 3670048 | tf_op jit(solution)/shard_map/ppermute | solution.py:39
  107.0 1.8 copy-done.1
  108.8 1.4 slice_bitcast_fusion
  111.4 41.1 %collective-permute-done.10 = f32[8,8,7168]{2,1,0:T(8,128)} collective-permute-done((f32[8,8,7168]{2,1,0:T(8,128)}, f32[8,8,7168]{2,1,0:T(8,128)}, u32[]{:S(2)}, u32[]{:S(2)}) %collective-permute-start.10) | collective-permute-done | bytes 1835040 | tf_op jit(solution)/shard_map/ppermute | solution.py:39
  152.6 2.2 %fusion.7 = bf16[8,8,7168]{2,1,0:T(8,128)(2,1)S(1)} fusion(f32[8,8,7168]{2,1,0:T(8,128)} %collective-permute-done.10, f32[2,8,8,7168]{3,2,1,0:T(8,128)} %copy-done.1), kind=kLoop, calls=%fused_computation.11 | loop fusion | flops 917504 | bytes 4587520 | tf_op jit(solution)/shard_map/convert_element_type | solution.py:69
  154.8 4.3 %collective-permute-start.11 = (bf16[8,7168]{1,0:T(8,128)(2,1)S(1)}, bf16[8,7168]{1,0:T(8,128)(2,1)S(1)}, u32[]{:S(2)}, u32[]{:S(2)}) collective-permute-start(bf16[8,7168]{1,0:T(8,128)(2,1)S(1)} %get-tuple-element.10), channel_id=1, source_target_pairs={{0,28},{4,0},{8,4},{12,8},{16,12},{20,16},{24,20},{28,24},{1,29},{... | collective-permute-start | bytes 344072 | tf_op jit(solution)/shard_map/ppermute | solution.py:73
  159.8 2.9 %collective-permute-start.14 = (bf16[8,7168]{1,0:T(8,128)(2,1)S(1)}, bf16[8,7168]{1,0:T(8,128)(2,1)S(1)}, u32[]{:S(2)}, u32[]{:S(2)}) collective-permute-start(bf16[8,7168]{1,0:T(8,128)(2,1)S(1)} %get-tuple-element.14), channel_id=1, source_target_pairs={{0,16},{4,20},{8,24},{12,28},{16,0},{20,4},{24,8},{28,12},{1,17},{... | collective-permute-start | bytes 344072 | tf_op jit(solution)/shard_map/ppermute | solution.py:73
  162.8 1.9 %collective-permute-start.16 = (bf16[8,7168]{1,0:T(8,128)(2,1)S(1)}, bf16[8,7168]{1,0:T(8,128)(2,1)S(1)}, u32[]{:S(2)}, u32[]{:S(2)}) collective-permute-start(bf16[8,7168]{1,0:T(8,128)(2,1)S(1)} %get-tuple-element.12), channel_id=1, source_target_pairs={{0,8},{4,12},{8,16},{12,20},{16,24},{20,28},{24,0},{28,4},{1,9},{5... | collective-permute-start | bytes 344072 | tf_op jit(solution)/shard_map/ppermute | solution.py:73
  165.6 2.1 %collective-permute-done.13 = bf16[8,7168]{1,0:T(8,128)(2,1)S(1)} collective-permute-done((bf16[8,7168]{1,0:T(8,128)(2,1)S(1)}, bf16[8,7168]{1,0:T(8,128)(2,1)S(1)}, u32[]{:S(2)}, u32[]{:S(2)}) %collective-permute-start.13) | collective-permute-done | bytes 114720 | tf_op jit(solution)/shard_map/ppermute | solution.py:73
  167.7 10.6 %collective-permute-done.14 = bf16[8,7168]{1,0:T(8,128)(2,1)S(1)} collective-permute-done((bf16[8,7168]{1,0:T(8,128)(2,1)S(1)}, bf16[8,7168]{1,0:T(8,128)(2,1)S(1)}, u32[]{:S(2)}, u32[]{:S(2)}) %collective-permute-start.14) | collective-permute-done | bytes 114720 | tf_op jit(solution)/shard_map/ppermute | solution.py:73
  178.3 1.8 collective-permute-done.15
  (60 shorter events, 11.6 us)
Async XLA Ops:
  7.2 11.8 %copy-start = (bf16[2,1024,512]{2,1,0:T(8,128)(2,1)S(1)}, bf16[2,1024,512]{2,1,0:T(8,128)(2,1)}, u32[]{:S(2)}) copy-start(bf16[2,1024,512]{2,1,0:T(8,128)(2,1)} %param.13) | copy-start | bytes 6291460
  7.2 44.6 %reduce-scatter.2.cloned.1.call-start = ((), (), s32[]{:S(2)}) async-start(), calls=%async_computation.1 | async-start | bytes 819200 | tf_op jit(solution)/shard_map/reduce_scatter | solution.py:116
  7.2 23.9 %collective-permute-start = (bf16[8,7168]{1,0:T(8,128)(2,1)}, bf16[8,7168]{1,0:T(8,128)(2,1)}, u32[]{:S(2)}, u32[]{:S(2)}) collective-permute-start(bf16[8,7168]{1,0:T(8,128)(2,1)} %param.16), channel_id=1, source_target_pairs={{0,4},{4,8},{8,12},{12,16},{16,20},{20,24},{24,28},{28,0},{1,5},{5... | collective-permute-start | bytes 344072 | tf_op jit(solution)/shard_map/ppermute | solution.py:22
  10.2 23.2 %collective-permute-start.1 = (bf16[8,7168]{1,0:T(8,128)(2,1)}, bf16[8,7168]{1,0:T(8,128)(2,1)}, u32[]{:S(2)}, u32[]{:S(2)}) collective-permute-start(bf16[8,7168]{1,0:T(8,128)(2,1)} %param.16), channel_id=1, source_target_pairs={{0,8},{4,12},{8,16},{12,20},{16,24},{20,28},{24,0},{28,4},{1,9},{5... | collective-permute-start | bytes 344072 | tf_op jit(solution)/shard_map/ppermute | solution.py:22
  11.8 24.0 %collective-permute-start.2 = (bf16[8,7168]{1,0:T(8,128)(2,1)}, bf16[8,7168]{1,0:T(8,128)(2,1)}, u32[]{:S(2)}, u32[]{:S(2)}) collective-permute-start(bf16[8,7168]{1,0:T(8,128)(2,1)} %param.16), channel_id=1, source_target_pairs={{0,12},{4,16},{8,20},{12,24},{16,28},{20,0},{24,4},{28,8},{1,13},{... | collective-permute-start | bytes 344072 | tf_op jit(solution)/shard_map/ppermute | solution.py:22
  14.4 22.4 %collective-permute-start.3 = (bf16[8,7168]{1,0:T(8,128)(2,1)}, bf16[8,7168]{1,0:T(8,128)(2,1)S(1)}, u32[]{:S(2)}, u32[]{:S(2)}) collective-permute-start(bf16[8,7168]{1,0:T(8,128)(2,1)} %param.16), channel_id=1, source_target_pairs={{0,16},{4,20},{8,24},{12,28},{16,0},{20,4},{24,8},{28,12},{1,17},{... | collective-permute-start | bytes 344072 | tf_op jit(solution)/shard_map/ppermute | solution.py:22
  15.6 21.1 %collective-permute-start.4 = (bf16[8,7168]{1,0:T(8,128)(2,1)}, bf16[8,7168]{1,0:T(8,128)(2,1)S(1)}, u32[]{:S(2)}, u32[]{:S(2)}) collective-permute-start(bf16[8,7168]{1,0:T(8,128)(2,1)} %param.16), channel_id=1, source_target_pairs={{0,20},{4,24},{8,28},{12,0},{16,4},{20,8},{24,12},{28,16},{1,21},{... | collective-permute-start | bytes 344072 | tf_op jit(solution)/shard_map/ppermute | solution.py:22
  22.2 8.9 %copy-start.3 = (bf16[8,7168]{1,0:T(8,128)(2,1)S(1)}, bf16[8,7168]{1,0:T(8,128)(2,1)}, u32[]{:S(2)}) copy-start(bf16[8,7168]{1,0:T(8,128)(2,1)} %param.16) | copy-start | bytes 344068
  31.1 5.7 %collective-permute-start.5 = (bf16[8,7168]{1,0:T(8,128)(2,1)S(1)}, bf16[8,7168]{1,0:T(8,128)(2,1)S(1)}, u32[]{:S(2)}, u32[]{:S(2)}) collective-permute-start(bf16[8,7168]{1,0:T(8,128)(2,1)S(1)} %copy-done.3), channel_id=1, source_target_pairs={{0,24},{4,28},{8,0},{12,4},{16,8},{20,12},{24,16},{28,20},{1,25},{... | collective-permute-start | bytes 344072 | tf_op jit(solution)/shard_map/ppermute | solution.py:22
  33.4 5.1 %collective-permute-start.6 = (bf16[8,7168]{1,0:T(8,128)(2,1)S(1)}, bf16[8,7168]{1,0:T(8,128)(2,1)S(1)}, u32[]{:S(2)}, u32[]{:S(2)}) collective-permute-start(bf16[8,7168]{1,0:T(8,128)(2,1)S(1)} %copy-done.3), channel_id=1, source_target_pairs={{0,28},{4,0},{8,4},{12,8},{16,12},{20,16},{24,20},{28,24},{1,29},{... | collective-permute-start | bytes 344072 | tf_op jit(solution)/shard_map/ppermute | solution.py:22
  54.2 22.1 %collective-permute-start.7 = (bf16[8,8,7168]{2,1,0:T(8,128)(2,1)S(1)}, bf16[8,8,7168]{2,1,0:T(8,128)(2,1)S(1)}, u32[]{:S(2)}, u32[]{:S(2)}) collective-permute-start(bf16[8,8,7168]{2,1,0:T(8,128)(2,1)S(1)} %bitcast_dynamic-update-slice_fusion), channel_id=1, source_target_pairs={{0,2},{1,3},{2,0},{3,1},{4,6},{5,7},{6,4},{7,5},{8,10},{9,11},{10,... | collective-permute-start | bytes 2752520 | tf_op jit(solution)/shard_map/ppermute | solution.py:34
  76.6 3.9 %collective-permute-start.8 = (bf16[2,8,8,7168]{3,2,1,0:T(8,128)(2,1)S(1)}, bf16[2,8,8,7168]{3,2,1,0:T(8,128)(2,1)S(1)}, u32[]{:S(2)}, u32[]{:S(2)}) collective-permute-start(bf16[2,8,8,7168]{3,2,1,0:T(8,128)(2,1)S(1)} %get-tuple-element.9), channel_id=1, source_target_pairs={{0,1},{1,0},{2,3},{3,2},{4,5},{5,4},{6,7},{7,6},{8,9},{9,8},{10,11... | collective-permute-start | bytes 5505032 | tf_op jit(solution)/shard_map/ppermute | solution.py:34
  80.4 3.4 %copy-start.6 = (bf16[1,7168,256]{2,1,0:T(8,128)(2,1)S(1)}, bf16[1,7168,256]{2,1,0:T(8,128)(2,1)}, u32[]{:S(2)}) copy-start(bf16[1,7168,256]{2,1,0:T(8,128)(2,1)} %param.20) | copy-start | bytes 11010052
  80.8 1.9 %copy-start.2 = (bf16[2,2,8,8,7168]{4,3,2,1,0:T(8,128)(2,1)}, bf16[2,2,8,8,7168]{4,3,2,1,0:T(8,128)(2,1)S(1)}, u32[]{:S(2)}) copy-start(bf16[2,2,8,8,7168]{4,3,2,1,0:T(8,128)(2,1)S(1)} %pad_maximum_fusion) | copy-start | bytes 11010052
  100.0 6.5 %collective-permute-start.9 = (f32[2,8,8,7168]{3,2,1,0:T(8,128)S(1)}, f32[2,8,8,7168]{3,2,1,0:T(8,128)S(1)}, u32[]{:S(2)}, u32[]{:S(2)}) collective-permute-start(f32[2,8,8,7168]{3,2,1,0:T(8,128)S(1)} %bitcast.97), channel_id=1, source_target_pairs={{0,1},{1,0},{2,3},{3,2},{4,5},{5,4},{6,7},{7,6},{8,9},{9,8},{10,11... | collective-permute-start | bytes 11010056 | tf_op jit(solution)/shard_map/ppermute | solution.py:39
  107.0 1.8 copy-start.1
  108.8 1.9 copy-start.4
  108.8 1.9 copy-start.5
  110.2 42.4 %collective-permute-start.10 = (f32[8,8,7168]{2,1,0:T(8,128)}, f32[8,8,7168]{2,1,0:T(8,128)}, u32[]{:S(2)}, u32[]{:S(2)}) collective-permute-start(f32[8,8,7168]{2,1,0:T(8,128)} %slice_bitcast_fusion), channel_id=1, source_target_pairs={{0,2},{1,3},{2,0},{3,1},{4,6},{5,7},{6,4},{7,5},{8,10},{9,11},{10,... | collective-permute-start | bytes 5505032 | tf_op jit(solution)/shard_map/ppermute | solution.py:39
  154.8 7.9 %collective-permute-start.11 = (bf16[8,7168]{1,0:T(8,128)(2,1)S(1)}, bf16[8,7168]{1,0:T(8,128)(2,1)S(1)}, u32[]{:S(2)}, u32[]{:S(2)}) collective-permute-start(bf16[8,7168]{1,0:T(8,128)(2,1)S(1)} %get-tuple-element.10), channel_id=1, source_target_pairs={{0,28},{4,0},{8,4},{12,8},{16,12},{20,16},{24,20},{28,24},{1,29},{... | collective-permute-start | bytes 344072 | tf_op jit(solution)/shard_map/ppermute | solution.py:73
  159.1 6.1 %collective-permute-start.12 = (bf16[8,7168]{1,0:T(8,128)(2,1)S(1)}, bf16[8,7168]{1,0:T(8,128)(2,1)S(1)}, u32[]{:S(2)}, u32[]{:S(2)}) collective-permute-start(bf16[8,7168]{1,0:T(8,128)(2,1)S(1)} %get-tuple-element.16), channel_id=1, source_target_pairs={{0,24},{4,28},{8,0},{12,4},{16,8},{20,12},{24,16},{28,20},{1,25},{... | collective-permute-start | bytes 344072 | tf_op jit(solution)/shard_map/ppermute | solution.py:73
  159.8 7.9 %collective-permute-start.13 = (bf16[8,7168]{1,0:T(8,128)(2,1)S(1)}, bf16[8,7168]{1,0:T(8,128)(2,1)S(1)}, u32[]{:S(2)}, u32[]{:S(2)}) collective-permute-start(bf16[8,7168]{1,0:T(8,128)(2,1)S(1)} %get-tuple-element.15), channel_id=1, source_target_pairs={{0,20},{4,24},{8,28},{12,0},{16,4},{20,8},{24,12},{28,16},{1,21},{... | collective-permute-start | bytes 344072 | tf_op jit(solution)/shard_map/ppermute | solution.py:73
  159.8 18.5 %collective-permute-start.14 = (bf16[8,7168]{1,0:T(8,128)(2,1)S(1)}, bf16[8,7168]{1,0:T(8,128)(2,1)S(1)}, u32[]{:S(2)}, u32[]{:S(2)}) collective-permute-start(bf16[8,7168]{1,0:T(8,128)(2,1)S(1)} %get-tuple-element.14), channel_id=1, source_target_pairs={{0,16},{4,20},{8,24},{12,28},{16,0},{20,4},{24,8},{28,12},{1,17},{... | collective-permute-start | bytes 344072 | tf_op jit(solution)/shard_map/ppermute | solution.py:73
  162.7 17.4 %collective-permute-start.15 = (bf16[8,7168]{1,0:T(8,128)(2,1)S(1)}, bf16[8,7168]{1,0:T(8,128)(2,1)S(1)}, u32[]{:S(2)}, u32[]{:S(2)}) collective-permute-start(bf16[8,7168]{1,0:T(8,128)(2,1)S(1)} %get-tuple-element.13), channel_id=1, source_target_pairs={{0,12},{4,16},{8,20},{12,24},{16,28},{20,0},{24,4},{28,8},{1,13},{... | collective-permute-start | bytes 344072 | tf_op jit(solution)/shard_map/ppermute | solution.py:73
  162.8 17.3 %collective-permute-start.16 = (bf16[8,7168]{1,0:T(8,128)(2,1)S(1)}, bf16[8,7168]{1,0:T(8,128)(2,1)S(1)}, u32[]{:S(2)}, u32[]{:S(2)}) collective-permute-start(bf16[8,7168]{1,0:T(8,128)(2,1)S(1)} %get-tuple-element.12), channel_id=1, source_target_pairs={{0,8},{4,12},{8,16},{12,20},{16,24},{20,28},{24,0},{28,4},{1,9},{5... | collective-permute-start | bytes 344072 | tf_op jit(solution)/shard_map/ppermute | solution.py:73
  165.2 14.9 %collective-permute-start.17 = (bf16[8,7168]{1,0:T(8,128)(2,1)S(1)}, bf16[8,7168]{1,0:T(8,128)(2,1)S(1)}, u32[]{:S(2)}, u32[]{:S(2)}) collective-permute-start(bf16[8,7168]{1,0:T(8,128)(2,1)S(1)} %get-tuple-element.11), channel_id=1, source_target_pairs={{0,4},{4,8},{8,12},{12,16},{16,20},{20,24},{24,28},{28,0},{1,5},{5... | collective-permute-start | bytes 344072 | tf_op jit(solution)/shard_map/ppermute | solution.py:73
Sparse Core Ops, SparseCore 0:
  31.2 20.5 reduce-scatter.1

commit v5 on v4

--- a/solution.py
+++ b/solution.py
@@ -35,8 +35,9 @@
     return jnp.stack([x, other])
 
 
-def bit_reduce(x, axis, bit, n):
-    return x[0] + lax.ppermute(x[1], axis, [(i, i ^ bit) for i in range(n)])
+def bit_reduce(x, axis, bit, n, wire=None):
+    sent = x[1] if wire is None else x[1].astype(wire)
+    return x[0] + lax.ppermute(sent, axis, [(i, i ^ bit) for i in range(n)]).astype(x.dtype)
 
 
 def routed_experts(tokens, route_ids, route_gates, w_gate, w_up, w_down, earlier):
@@ -65,7 +66,8 @@
         partial = expert_part(flat_rows, w_gate[i], w_up[i], w_down[i])
         partial = partial.reshape(lead_shape + (model_width,))
         for bit in reversed(bits):
-            partial = bit_reduce(partial, "exp", bit, n_exp)
+            wire = jnp.bfloat16 if bit == bits[0] else None
+            partial = bit_reduce(partial, "exp", bit, n_exp, wire)
         expert_rows = partial.astype(jnp.bfloat16)
         back = [expert_rows[0]]
         for k in range(1, n_attn):

time: 188 us -> 168 us (0.89)
  waiting for transfers between devices: 103 us -> 83.3 us
    ppermute x2, waiting for transfers between devices: 47.4 us -> 27.6 us  [bit_reduce(): lax.ppermute(sent, axis, [(i, i ^ bit) for i in range(n)]).astype(x.dtype)]
  transfers between devices with their start and end apart: 19 -> 19, of which waited for: 12 -> 12; matrix products, arithmetic and copies ran while one was open for 6% -> 7% of each run, Pallas kernels for 0% -> 0%
where the time goes in v5:
time: 168 us; the launch traced here: 167 us
  waiting for transfers between devices  83.3 us (50%)
  starting transfers between devices  25.1 us (15%)
  matrix products  16.8 us (10%)
  local copies, waits for them, and re-layouts  14.3 us (9%)
  between operations  14.2 us (8%)
  other arithmetic  8.48 us (5%)
  blocking collectives  5.07 us (3%)
    ppermute x2, waiting for transfers between devices, bit_reduce(): lax.ppermute(sent, axis, [(i, i ^ bit) for i in range(n)]).astype(x.dtype)  27.6 us
    ppermute x2, waiting for transfers between devices, bit_gather(): other = lax.ppermute(x, axis, [(i, i ^ bit) for i in range(n)])  25.6 us
    ppermute x7, waiting for transfers between devices, routed_experts(): lax.ppermute(expert_rows[k], 'attn', [(s, (s - k) % n_attn) for s in rang...  15.1 us
    ppermute x7, starting transfers between devices, shift_gather(): pieces.append(lax.ppermute(x, axis, [(i, (i + k) % n) for i in range(n)]))  13.9 us
    reduce_scatter x1, waiting for transfers between devices, per_device(): reduced = lax.psum_scatter(packed, 'exp', scatter_dimension=1, tiled=True)  13.2 us
    dot_general x1, matrix products, expert_part(): return jnp.dot(hidden, down_slice, preferred_element_type=jnp.float32)  11.2 us
    ppermute x7, starting transfers between devices, routed_experts(): lax.ppermute(expert_rows[k], 'attn', [(s, (s - k) % n_attn) for s in rang...  10.1 us
    unnamed x21, local copies, waits for them, and re-layouts  7.6 us
  transfers between devices with their start and end apart: 19, of which 12 were waited for; matrix products, arithmetic and copies ran while one was open for 7% of the time, Pallas kernels for 0%

profile of v5, /device:TPU:0, one launch (start us, length us, event | category | flops | bytes accessed | tf_op | source)
XLA Modules:
  0.0 167.2 jit_solution(9622860262087351717)
XLA Ops:
  7.2 3.0 %collective-permute-start = (bf16[8,7168]{1,0:T(8,128)(2,1)}, bf16[8,7168]{1,0:T(8,128)(2,1)}, u32[]{:S(2)}, u32[]{:S(2)}) collective-permute-start(bf16[8,7168]{1,0:T(8,128)(2,1)} %param.16), channel_id=1, source_target_pairs={{0,4},{4,8},{8,12},{12,16},{16,20},{20,24},{24,28},{28,0},{1,5},{5... | collective-permute-start | bytes 344072 | tf_op jit(solution)/shard_map/ppermute | solution.py:22
  10.2 1.6 collective-permute-start.1
  11.8 2.5 %collective-permute-start.2 = (bf16[8,7168]{1,0:T(8,128)(2,1)}, bf16[8,7168]{1,0:T(8,128)(2,1)}, u32[]{:S(2)}, u32[]{:S(2)}) collective-permute-start(bf16[8,7168]{1,0:T(8,128)(2,1)} %param.16), channel_id=1, source_target_pairs={{0,12},{4,16},{8,20},{12,24},{16,28},{20,0},{24,4},{28,8},{1,13},{... | collective-permute-start | bytes 344072 | tf_op jit(solution)/shard_map/ppermute | solution.py:22
  14.4 1.2 collective-permute-start.3
  15.6 2.6 %collective-permute-start.4 = (bf16[8,7168]{1,0:T(8,128)(2,1)}, bf16[8,7168]{1,0:T(8,128)(2,1)S(1)}, u32[]{:S(2)}, u32[]{:S(2)}) collective-permute-start(bf16[8,7168]{1,0:T(8,128)(2,1)} %param.16), channel_id=1, source_target_pairs={{0,20},{4,24},{8,28},{12,0},{16,4},{20,8},{24,12},{28,16},{1,21},{... | collective-permute-start | bytes 344072 | tf_op jit(solution)/shard_map/ppermute | solution.py:22
  19.0 1.8 %fusion.39 = f32[2,128,1024]{2,1,0:T(8,128)S(1)} fusion(bf16[2,128,512]{2,1,0:T(8,128)(2,1)} %param.11, bf16[2,1024,512]{2,1,0:T(8,128)(2,1)S(1)} %copy-done), kind=kOutput, calls=%fused_computation.88 | convolution fusion | flops 268435456 | bytes 3407872 | tf_op jit(solution)/shard_map/rhl,rpl->rhp/dot_general | solution.py:98
  20.7 1.4 fusion.38
  22.5 5.1 %all-gather.1 = f32[4,2,128]{2,1,0:T(2,128)S(1)} all-gather(f32[1,2,128]{2,1,0:T(2,128)S(1)} %bitcast.101), channel_id=2, replica_groups=mesh['attn'=8,'exp'=4] {'exp'}, dimensions={0}, use_global_device_ids=true | all-gather | bytes 5120 | tf_op jit(solution)/shard_map/all_gather | solution.py:115
  27.6 1.4 convolution_multiply_fusion
  29.1 1.9 %pad_maximum_fusion.2 = f32[2,128,513]{2,1,0:T(8,128)} fusion(f32[2,128,1]{2,1,0:T(8,128)S(1)} %copy.21, f32[2,128,512]{2,1,0:T(8,128)} %convolution_multiply_fusion), kind=kLoop, calls=%fused_computation.21 | loop fusion | flops 131328 | bytes 1050624 | tf_op jit(solution)/shard_map/concatenate | solution.py:117
  31.1 1.4 collective-permute-start.5
  33.4 1.5 collective-permute-start.6
  36.8 1.7 %collective-permute-done.6 = bf16[8,7168]{1,0:T(8,128)(2,1)S(1)} collective-permute-done((bf16[8,7168]{1,0:T(8,128)(2,1)S(1)}, bf16[8,7168]{1,0:T(8,128)(2,1)S(1)}, u32[]{:S(2)}, u32[]{:S(2)}) %collective-permute-start.6) | collective-permute-done | bytes 114720 | tf_op jit(solution)/shard_map/ppermute | solution.py:22
  38.6 13.2 %reduce-scatter.2.cloned.1.call-done = f32[2,32,513]{2,1,0:T(8,128)} async-done(((f32[2,128,513]{2,1,0:T(8,128)}), f32[2,32,513]{2,1,0:T(8,128)}) %reduce-scatter.2.cloned.1.call-update) | async-done | bytes 131344 | tf_op jit(solution)/shard_map/reduce_scatter | solution.py:118
  52.6 1.6 fusion.29
  54.5 21.8 %collective-permute-done.7 = bf16[8,8,7168]{2,1,0:T(8,128)(2,1)S(1)} collective-permute-done((bf16[8,8,7168]{2,1,0:T(8,128)(2,1)S(1)}, bf16[8,8,7168]{2,1,0:T(8,128)(2,1)S(1)}, u32[]{:S(2)}, u32[]{:S(2)}) %collective-permute-start.7) | collective-permute-done | bytes 917536 | tf_op jit(solution)/shard_map/ppermute | solution.py:34
  76.6 3.8 %collective-permute-done.8 = bf16[2,8,8,7168]{3,2,1,0:T(8,128)(2,1)S(1)} collective-permute-done((bf16[2,8,8,7168]{3,2,1,0:T(8,128)(2,1)S(1)}, bf16[2,8,8,7168]{3,2,1,0:T(8,128)(2,1)S(1)}, u32[]{:S(2)}, u32[]{:S(2)}) %collective-permute-start.8) | collective-permute-done | bytes 1835040 | tf_op jit(solution)/shard_map/ppermute | solution.py:34
  80.8 1.9 %copy-done.1 = bf16[2,2,8,8,7168]{4,3,2,1,0:T(8,128)(2,1)} copy-done((bf16[2,2,8,8,7168]{4,3,2,1,0:T(8,128)(2,1)}, bf16[2,2,8,8,7168]{4,3,2,1,0:T(8,128)(2,1)S(1)}, u32[]{:S(2)}) %copy-start.1) | copy-done | bytes 3670040
  82.6 1.1 copy-done.6
  83.8 1.1 fusion.2
  84.9 11.2 %fusion = f32[256,7168]{1,0:T(8,128)} fusion(bf16[1,256,7168]{2,1,0:T(8,128)(2,1)} %param.21, f32[256,256]{1,0:T(8,128)S(1)} %fusion.2, bf16[256,7168]{1,0:T(8,128)(2,1)} %bitcast.96, bf16[1,7168,256]{2,1,0:T(8,128)(2,1)} %param.19), kind=kOutput, calls=%fused_computation.2 | convolution fusion | flops 1879441408 | bytes 18612224 | tf_op jit(solution)/shard_map/dot_general | solution.py:16
  96.1 3.9 %fusion.37 = (f32[128,7168]{1,0:T(8,128)S(1)}, f32[128,7168]{1,0:T(8,128)S(1)}) fusion(f32[256,7168]{1,0:T(8,128)} %fusion), kind=kLoop, calls=%fused_computation.86 | loop fusion | bytes 14680064 | tf_op jit(solution)/shard_map/slice | solution.py:39
  100.2 6.3 %collective-permute-done.9 = f32[2,8,8,7168]{3,2,1,0:T(8,128)S(1)} collective-permute-done((f32[2,8,8,7168]{3,2,1,0:T(8,128)S(1)}, f32[2,8,8,7168]{3,2,1,0:T(8,128)S(1)}, u32[]{:S(2)}, u32[]{:S(2)}) %collective-permute-start.9) | collective-permute-done | bytes 3670048 | tf_op jit(solution)/shard_map/ppermute | solution.py:40
  107.0 1.8 %copy-done.2 = f32[2,8,8,7168]{3,2,1,0:T(8,128)} copy-done((f32[2,8,8,7168]{3,2,1,0:T(8,128)}, f32[2,8,8,7168]{3,2,1,0:T(8,128)S(1)}, u32[]{:S(2)}) %copy-start.2) | copy-done | bytes 3670040
  111.1 21.4 %collective-permute-done.10 = bf16[8,8,7168]{2,1,0:T(8,128)(2,1)S(1)} collective-permute-done((bf16[8,8,7168]{2,1,0:T(8,128)(2,1)}, bf16[8,8,7168]{2,1,0:T(8,128)(2,1)S(1)}, u32[]{:S(2)}, u32[]{:S(2)}) %collective-permute-start.10) | collective-permute-done | bytes 917536 | tf_op jit(solution)/shard_map/ppermute | solution.py:40
  132.5 1.7 fusion.7
  134.2 4.3 %collective-permute-start.11 = (bf16[8,7168]{1,0:T(8,128)(2,1)S(1)}, bf16[8,7168]{1,0:T(8,128)(2,1)S(1)}, u32[]{:S(2)}, u32[]{:S(2)}) collective-permute-start(bf16[8,7168]{1,0:T(8,128)(2,1)S(1)} %get-tuple-element.10), channel_id=1, source_target_pairs={{0,28},{4,0},{8,4},{12,8},{16,12},{20,16},{24,20},{28,24},{1,29},{... | collective-permute-start | bytes 344072 | tf_op jit(solution)/shard_map/ppermute | solution.py:75
  139.1 2.9 %collective-permute-start.14 = (bf16[8,7168]{1,0:T(8,128)(2,1)S(1)}, bf16[8,7168]{1,0:T(8,128)(2,1)S(1)}, u32[]{:S(2)}, u32[]{:S(2)}) collective-permute-start(bf16[8,7168]{1,0:T(8,128)(2,1)S(1)} %get-tuple-element.14), channel_id=1, source_target_pairs={{0,16},{4,20},{8,24},{12,28},{16,0},{20,4},{24,8},{28,12},{1,17},{... | collective-permute-start | bytes 344072 | tf_op jit(solution)/shard_map/ppermute | solution.py:75
  142.1 1.9 %collective-permute-start.16 = (bf16[8,7168]{1,0:T(8,128)(2,1)S(1)}, bf16[8,7168]{1,0:T(8,128)(2,1)S(1)}, u32[]{:S(2)}, u32[]{:S(2)}) collective-permute-start(bf16[8,7168]{1,0:T(8,128)(2,1)S(1)} %get-tuple-element.12), channel_id=1, source_target_pairs={{0,8},{4,12},{8,16},{12,20},{16,24},{20,28},{24,0},{28,4},{1,9},{5... | collective-permute-start | bytes 344072 | tf_op jit(solution)/shard_map/ppermute | solution.py:75
  145.0 2.1 %collective-permute-done.13 = bf16[8,7168]{1,0:T(8,128)(2,1)S(1)} collective-permute-done((bf16[8,7168]{1,0:T(8,128)(2,1)S(1)}, bf16[8,7168]{1,0:T(8,128)(2,1)S(1)}, u32[]{:S(2)}, u32[]{:S(2)}) %collective-permute-start.13) | collective-permute-done | bytes 114720 | tf_op jit(solution)/shard_map/ppermute | solution.py:75
  147.0 10.6 %collective-permute-done.14 = bf16[8,7168]{1,0:T(8,128)(2,1)S(1)} collective-permute-done((bf16[8,7168]{1,0:T(8,128)(2,1)S(1)}, bf16[8,7168]{1,0:T(8,128)(2,1)S(1)}, u32[]{:S(2)}, u32[]{:S(2)}) %collective-permute-start.14) | collective-permute-done | bytes 114720 | tf_op jit(solution)/shard_map/ppermute | solution.py:75
  157.6 1.8 %collective-permute-done.15 = bf16[8,7168]{1,0:T(8,128)(2,1)S(1)} collective-permute-done((bf16[8,7168]{1,0:T(8,128)(2,1)S(1)}, bf16[8,7168]{1,0:T(8,128)(2,1)S(1)}, u32[]{:S(2)}, u32[]{:S(2)}) %collective-permute-start.15) | collective-permute-done | bytes 114720 | tf_op jit(solution)/shard_map/ppermute | solution.py:75
  (60 shorter events, 11.6 us)
Async XLA Ops:
  7.2 11.8 %copy-start = (bf16[2,1024,512]{2,1,0:T(8,128)(2,1)S(1)}, bf16[2,1024,512]{2,1,0:T(8,128)(2,1)}, u32[]{:S(2)}) copy-start(bf16[2,1024,512]{2,1,0:T(8,128)(2,1)} %param.13) | copy-start | bytes 6291460
  7.2 44.6 %reduce-scatter.2.cloned.1.call-start = ((), (), s32[]{:S(2)}) async-start(), calls=%async_computation.1 | async-start | bytes 819200 | tf_op jit(solution)/shard_map/reduce_scatter | solution.py:118
  7.2 23.9 %collective-permute-start = (bf16[8,7168]{1,0:T(8,128)(2,1)}, bf16[8,7168]{1,0:T(8,128)(2,1)}, u32[]{:S(2)}, u32[]{:S(2)}) collective-permute-start(bf16[8,7168]{1,0:T(8,128)(2,1)} %param.16), channel_id=1, source_target_pairs={{0,4},{4,8},{8,12},{12,16},{16,20},{20,24},{24,28},{28,0},{1,5},{5... | collective-permute-start | bytes 344072 | tf_op jit(solution)/shard_map/ppermute | solution.py:22
  10.2 23.2 %collective-permute-start.1 = (bf16[8,7168]{1,0:T(8,128)(2,1)}, bf16[8,7168]{1,0:T(8,128)(2,1)}, u32[]{:S(2)}, u32[]{:S(2)}) collective-permute-start(bf16[8,7168]{1,0:T(8,128)(2,1)} %param.16), channel_id=1, source_target_pairs={{0,8},{4,12},{8,16},{12,20},{16,24},{20,28},{24,0},{28,4},{1,9},{5... | collective-permute-start | bytes 344072 | tf_op jit(solution)/shard_map/ppermute | solution.py:22
  11.8 24.0 %collective-permute-start.2 = (bf16[8,7168]{1,0:T(8,128)(2,1)}, bf16[8,7168]{1,0:T(8,128)(2,1)}, u32[]{:S(2)}, u32[]{:S(2)}) collective-permute-start(bf16[8,7168]{1,0:T(8,128)(2,1)} %param.16), channel_id=1, source_target_pairs={{0,12},{4,16},{8,20},{12,24},{16,28},{20,0},{24,4},{28,8},{1,13},{... | collective-permute-start | bytes 344072 | tf_op jit(solution)/shard_map/ppermute | solution.py:22
  14.4 22.4 %collective-permute-start.3 = (bf16[8,7168]{1,0:T(8,128)(2,1)}, bf16[8,7168]{1,0:T(8,128)(2,1)S(1)}, u32[]{:S(2)}, u32[]{:S(2)}) collective-permute-start(bf16[8,7168]{1,0:T(8,128)(2,1)} %param.16), channel_id=1, source_target_pairs={{0,16},{4,20},{8,24},{12,28},{16,0},{20,4},{24,8},{28,12},{1,17},{... | collective-permute-start | bytes 344072 | tf_op jit(solution)/shard_map/ppermute | solution.py:22
  15.6 21.1 %collective-permute-start.4 = (bf16[8,7168]{1,0:T(8,128)(2,1)}, bf16[8,7168]{1,0:T(8,128)(2,1)S(1)}, u32[]{:S(2)}, u32[]{:S(2)}) collective-permute-start(bf16[8,7168]{1,0:T(8,128)(2,1)} %param.16), channel_id=1, source_target_pairs={{0,20},{4,24},{8,28},{12,0},{16,4},{20,8},{24,12},{28,16},{1,21},{... | collective-permute-start | bytes 344072 | tf_op jit(solution)/shard_map/ppermute | solution.py:22
  22.2 8.9 %copy-start.3 = (bf16[8,7168]{1,0:T(8,128)(2,1)S(1)}, bf16[8,7168]{1,0:T(8,128)(2,1)}, u32[]{:S(2)}) copy-start(bf16[8,7168]{1,0:T(8,128)(2,1)} %param.16) | copy-start | bytes 344068
  31.1 5.7 %collective-permute-start.5 = (bf16[8,7168]{1,0:T(8,128)(2,1)S(1)}, bf16[8,7168]{1,0:T(8,128)(2,1)S(1)}, u32[]{:S(2)}, u32[]{:S(2)}) collective-permute-start(bf16[8,7168]{1,0:T(8,128)(2,1)S(1)} %copy-done.3), channel_id=1, source_target_pairs={{0,24},{4,28},{8,0},{12,4},{16,8},{20,12},{24,16},{28,20},{1,25},{... | collective-permute-start | bytes 344072 | tf_op jit(solution)/shard_map/ppermute | solution.py:22
  33.4 5.1 %collective-permute-start.6 = (bf16[8,7168]{1,0:T(8,128)(2,1)S(1)}, bf16[8,7168]{1,0:T(8,128)(2,1)S(1)}, u32[]{:S(2)}, u32[]{:S(2)}) collective-permute-start(bf16[8,7168]{1,0:T(8,128)(2,1)S(1)} %copy-done.3), channel_id=1, source_target_pairs={{0,28},{4,0},{8,4},{12,8},{16,12},{20,16},{24,20},{28,24},{1,29},{... | collective-permute-start | bytes 344072 | tf_op jit(solution)/shard_map/ppermute | solution.py:22
  54.2 22.1 %collective-permute-start.7 = (bf16[8,8,7168]{2,1,0:T(8,128)(2,1)S(1)}, bf16[8,8,7168]{2,1,0:T(8,128)(2,1)S(1)}, u32[]{:S(2)}, u32[]{:S(2)}) collective-permute-start(bf16[8,8,7168]{2,1,0:T(8,128)(2,1)S(1)} %bitcast_dynamic-update-slice_fusion), channel_id=1, source_target_pairs={{0,2},{1,3},{2,0},{3,1},{4,6},{5,7},{6,4},{7,5},{8,10},{9,11},{10,... | collective-permute-start | bytes 2752520 | tf_op jit(solution)/shard_map/ppermute | solution.py:34
  76.6 3.9 %collective-permute-start.8 = (bf16[2,8,8,7168]{3,2,1,0:T(8,128)(2,1)S(1)}, bf16[2,8,8,7168]{3,2,1,0:T(8,128)(2,1)S(1)}, u32[]{:S(2)}, u32[]{:S(2)}) collective-permute-start(bf16[2,8,8,7168]{3,2,1,0:T(8,128)(2,1)S(1)} %get-tuple-element.9), channel_id=1, source_target_pairs={{0,1},{1,0},{2,3},{3,2},{4,5},{5,4},{6,7},{7,6},{8,9},{9,8},{10,11... | collective-permute-start | bytes 5505032 | tf_op jit(solution)/shard_map/ppermute | solution.py:34
  80.4 3.4 %copy-start.6 = (bf16[1,7168,256]{2,1,0:T(8,128)(2,1)S(1)}, bf16[1,7168,256]{2,1,0:T(8,128)(2,1)}, u32[]{:S(2)}) copy-start(bf16[1,7168,256]{2,1,0:T(8,128)(2,1)} %param.20) | copy-start | bytes 11010052
  80.8 1.9 %copy-start.1 = (bf16[2,2,8,8,7168]{4,3,2,1,0:T(8,128)(2,1)}, bf16[2,2,8,8,7168]{4,3,2,1,0:T(8,128)(2,1)S(1)}, u32[]{:S(2)}) copy-start(bf16[2,2,8,8,7168]{4,3,2,1,0:T(8,128)(2,1)S(1)} %pad_maximum_fusion) | copy-start | bytes 11010052
  100.0 6.5 %collective-permute-start.9 = (f32[2,8,8,7168]{3,2,1,0:T(8,128)S(1)}, f32[2,8,8,7168]{3,2,1,0:T(8,128)S(1)}, u32[]{:S(2)}, u32[]{:S(2)}) collective-permute-start(f32[2,8,8,7168]{3,2,1,0:T(8,128)S(1)} %bitcast.97), channel_id=1, source_target_pairs={{0,1},{1,0},{2,3},{3,2},{4,5},{5,4},{6,7},{7,6},{8,9},{9,8},{10,11... | collective-permute-start | bytes 11010056 | tf_op jit(solution)/shard_map/ppermute | solution.py:40
  106.5 3.9 %copy-start.4 = (f32[8,4]{0,1:T(4,128)S(1)}, f32[8,4]{0,1:T(4,128)}, u32[]{:S(2)}) copy-start(f32[8,4]{0,1:T(4,128)} %param.18) | copy-start | bytes 388
  106.5 3.9 %copy-start.5 = (s32[8,4]{0,1:T(4,128)S(1)}, s32[8,4]{0,1:T(4,128)}, u32[]{:S(2)}) copy-start(s32[8,4]{0,1:T(4,128)} %param.17) | copy-start | bytes 388
  107.0 1.8 %copy-start.2 = (f32[2,8,8,7168]{3,2,1,0:T(8,128)}, f32[2,8,8,7168]{3,2,1,0:T(8,128)S(1)}, u32[]{:S(2)}) copy-start(f32[2,8,8,7168]{3,2,1,0:T(8,128)S(1)} %add.109) | copy-start | bytes 11010052
  109.9 22.6 %collective-permute-start.10 = (bf16[8,8,7168]{2,1,0:T(8,128)(2,1)}, bf16[8,8,7168]{2,1,0:T(8,128)(2,1)S(1)}, u32[]{:S(2)}, u32[]{:S(2)}) collective-permute-start(bf16[8,8,7168]{2,1,0:T(8,128)(2,1)} %fusion.10), channel_id=1, source_target_pairs={{0,2},{1,3},{2,0},{3,1},{4,6},{5,7},{6,4},{7,5},{8,10},{9,11},{10,... | collective-permute-start | bytes 2752520 | tf_op jit(solution)/shard_map/ppermute | solution.py:40
  134.2 7.9 %collective-permute-start.11 = (bf16[8,7168]{1,0:T(8,128)(2,1)S(1)}, bf16[8,7168]{1,0:T(8,128)(2,1)S(1)}, u32[]{:S(2)}, u32[]{:S(2)}) collective-permute-start(bf16[8,7168]{1,0:T(8,128)(2,1)S(1)} %get-tuple-element.10), channel_id=1, source_target_pairs={{0,28},{4,0},{8,4},{12,8},{16,12},{20,16},{24,20},{28,24},{1,29},{... | collective-permute-start | bytes 344072 | tf_op jit(solution)/shard_map/ppermute | solution.py:75
  138.5 6.1 %collective-permute-start.12 = (bf16[8,7168]{1,0:T(8,128)(2,1)S(1)}, bf16[8,7168]{1,0:T(8,128)(2,1)S(1)}, u32[]{:S(2)}, u32[]{:S(2)}) collective-permute-start(bf16[8,7168]{1,0:T(8,128)(2,1)S(1)} %get-tuple-element.16), channel_id=1, source_target_pairs={{0,24},{4,28},{8,0},{12,4},{16,8},{20,12},{24,16},{28,20},{1,25},{... | collective-permute-start | bytes 344072 | tf_op jit(solution)/shard_map/ppermute | solution.py:75
  139.1 7.9 %collective-permute-start.13 = (bf16[8,7168]{1,0:T(8,128)(2,1)S(1)}, bf16[8,7168]{1,0:T(8,128)(2,1)S(1)}, u32[]{:S(2)}, u32[]{:S(2)}) collective-permute-start(bf16[8,7168]{1,0:T(8,128)(2,1)S(1)} %get-tuple-element.15), channel_id=1, source_target_pairs={{0,20},{4,24},{8,28},{12,0},{16,4},{20,8},{24,12},{28,16},{1,21},{... | collective-permute-start | bytes 344072 | tf_op jit(solution)/shard_map/ppermute | solution.py:75
  139.1 18.5 %collective-permute-start.14 = (bf16[8,7168]{1,0:T(8,128)(2,1)S(1)}, bf16[8,7168]{1,0:T(8,128)(2,1)S(1)}, u32[]{:S(2)}, u32[]{:S(2)}) collective-permute-start(bf16[8,7168]{1,0:T(8,128)(2,1)S(1)} %get-tuple-element.14), channel_id=1, source_target_pairs={{0,16},{4,20},{8,24},{12,28},{16,0},{20,4},{24,8},{28,12},{1,17},{... | collective-permute-start | bytes 344072 | tf_op jit(solution)/shard_map/ppermute | solution.py:75
  142.0 17.4 %collective-permute-start.15 = (bf16[8,7168]{1,0:T(8,128)(2,1)S(1)}, bf16[8,7168]{1,0:T(8,128)(2,1)S(1)}, u32[]{:S(2)}, u32[]{:S(2)}) collective-permute-start(bf16[8,7168]{1,0:T(8,128)(2,1)S(1)} %get-tuple-element.13), channel_id=1, source_target_pairs={{0,12},{4,16},{8,20},{12,24},{16,28},{20,0},{24,4},{28,8},{1,13},{... | collective-permute-start | bytes 344072 | tf_op jit(solution)/shard_map/ppermute | solution.py:75
  142.1 17.3 %collective-permute-start.16 = (bf16[8,7168]{1,0:T(8,128)(2,1)S(1)}, bf16[8,7168]{1,0:T(8,128)(2,1)S(1)}, u32[]{:S(2)}, u32[]{:S(2)}) collective-permute-start(bf16[8,7168]{1,0:T(8,128)(2,1)S(1)} %get-tuple-element.12), channel_id=1, source_target_pairs={{0,8},{4,12},{8,16},{12,20},{16,24},{20,28},{24,0},{28,4},{1,9},{5... | collective-permute-start | bytes 344072 | tf_op jit(solution)/shard_map/ppermute | solution.py:75
  144.6 14.9 %collective-permute-start.17 = (bf16[8,7168]{1,0:T(8,128)(2,1)S(1)}, bf16[8,7168]{1,0:T(8,128)(2,1)S(1)}, u32[]{:S(2)}, u32[]{:S(2)}) collective-permute-start(bf16[8,7168]{1,0:T(8,128)(2,1)S(1)} %get-tuple-element.11), channel_id=1, source_target_pairs={{0,4},{4,8},{8,12},{12,16},{16,20},{20,24},{24,28},{28,0},{1,5},{5... | collective-permute-start | bytes 344072 | tf_op jit(solution)/shard_map/ppermute | solution.py:75
Sparse Core Ops, SparseCore 0:
  31.2 20.5 reduce-scatter.1

commit v6 on v5

--- a/solution.py
+++ b/solution.py
@@ -40,7 +40,7 @@
     return x[0] + lax.ppermute(sent, axis, [(i, i ^ bit) for i in range(n)]).astype(x.dtype)
 
 
-def routed_experts(tokens, route_ids, route_gates, w_gate, w_up, w_down, earlier):
+def routed_experts(tokens, route_ids, route_gates, w_gate, w_up, w_down, packed):
     n_exp = lax.axis_size("exp")
     n_attn = lax.axis_size("attn")
     n_local = w_gate.shape[0]
@@ -54,9 +54,12 @@
     hit = route_ids[:, :, None] == jnp.arange(n_experts, dtype=jnp.int32)[None, None, :]
     wmat = jnp.sum(jnp.where(hit, route_gates[:, :, None], 0.0), axis=1)
     rows = shift_gather(tokens, "attn", n_attn)
-    rows, _ = lax.optimization_barrier((rows, earlier))
     for bit in bits:
         rows = bit_gather(rows, "exp", bit, n_exp)
+    rows, packed = lax.optimization_barrier((rows, packed))
+    reduced = lax.psum_scatter(packed, "exp", scatter_dimension=1, tiled=True)
+    numerator, denominator = reduced[:, :, :-1], reduced[:, :, -1]
+    attn_out = (numerator / denominator[:, :, None]).astype(jnp.bfloat16)
     lead_shape = rows.shape[:-1]
     flat_rows = rows.reshape(-1, model_width)
     me = lax.axis_index("attn")
@@ -66,6 +69,8 @@
         partial = expert_part(flat_rows, w_gate[i], w_up[i], w_down[i])
         partial = partial.reshape(lead_shape + (model_width,))
         for bit in reversed(bits):
+            if bit == bits[0]:
+                partial, attn_out = lax.optimization_barrier((partial, attn_out))
             wire = jnp.bfloat16 if bit == bits[0] else None
             partial = bit_reduce(partial, "exp", bit, n_exp, wire)
         expert_rows = partial.astype(jnp.bfloat16)
@@ -77,7 +82,7 @@
         chosen = jnp.take(wmat, owners * n_local + i, axis=1)
         for k in range(n_attn):
             result = result + chosen[:, k : k + 1] * back[k].astype(jnp.float32)
-    return result.astype(jnp.bfloat16)
+    return result.astype(jnp.bfloat16), attn_out
 
 def per_device(
     q_latent,
@@ -115,10 +120,7 @@
     row_top = jnp.max(lax.all_gather(block_max, "exp", axis=0), axis=0)
     factor = jnp.exp(block_max - row_top)
     packed = jnp.concatenate([block_out * factor[:, :, None], (block_sum * factor)[:, :, None]], axis=2)
-    reduced = lax.psum_scatter(packed, "exp", scatter_dimension=1, tiled=True)
-    numerator, denominator = reduced[:, :, :-1], reduced[:, :, -1]
-    attn_out = (numerator / denominator[:, :, None]).astype(jnp.bfloat16)
-    moe_out = routed_experts(tokens, route_ids, route_gates, w_gate, w_up, w_down, attn_out)
+    moe_out, attn_out = routed_experts(tokens, route_ids, route_gates, w_gate, w_up, w_down, packed)
     return (attn_out, moe_out)
 
 

time: 168 us -> 183 us (1.089)
  the two profiles are of different devices: /device:TPU:0 before, /device:TPU:13 now
where the time goes in v6:
time: 183 us
  waiting for transfers between devices  98 us (54%)
  starting transfers between devices  23.1 us (13%)
  local copies, waits for them, and re-layouts  14.4 us (8%)
  between operations  14.3 us (8%)
  matrix products  14 us (8%)
  other arithmetic  13.8 us (8%)
  blocking collectives  4.9 us (3%)
    reduce_scatter x1, waiting for transfers between devices, routed_experts(): reduced = lax.psum_scatter(packed, 'exp', scatter_dimension=1, tiled=True)  23.2 us
    ppermute x2, waiting for transfers between devices, bit_reduce(): lax.ppermute(sent, axis, [(i, i ^ bit) for i in range(n)]).astype(x.dtype)  20.4 us
    ppermute x7, waiting for transfers between devices, shift_gather(): pieces.append(lax.ppermute(x, axis, [(i, (i + k) % n) for i in range(n)]))  20.2 us
    ppermute x2, waiting for transfers between devices, bit_gather(): other = lax.ppermute(x, axis, [(i, i ^ bit) for i in range(n)])  18.2 us
    ppermute x7, waiting for transfers between devices, routed_experts(): lax.ppermute(expert_rows[k], 'attn', [(s, (s - k) % n_attn) for s in rang...  16 us
    dot_general x1, matrix products, expert_part(): return jnp.dot(hidden, down_slice, preferred_element_type=jnp.float32)  11.1 us
    ppermute x7, starting transfers between devices, routed_experts(): lax.ppermute(expert_rows[k], 'attn', [(s, (s - k) % n_attn) for s in rang...  11.1 us
    slice x1, local copies, waits for them, and re-layouts, bit_reduce(): sent = x[1] if wire is None else x[1].astype(wire)  6.97 us
  transfers between devices with their start and end apart: 19, of which 8 were waited for; matrix products, arithmetic and copies ran while one was open for 4% of the time, Pallas kernels for 0%

profile of v6, /device:TPU:13, one launch (start us, length us, event | category | flops | bytes accessed | tf_op | source)
XLA Modules:
  0.0 182.6 jit_solution(13198022290750902394)
XLA Ops:
  7.3 2.4 %collective-permute-start.3 = (bf16[8,7168]{1,0:T(8,128)(2,1)}, bf16[8,7168]{1,0:T(8,128)(2,1)S(1)}, u32[]{:S(2)}, u32[]{:S(2)}) collective-permute-start(bf16[8,7168]{1,0:T(8,128)(2,1)} %param.16), channel_id=1, source_target_pairs={{0,16},{4,20},{8,24},{12,28},{16,0},{20,4},{24,8},{28,12},{1,17},{... | collective-permute-start | bytes 344072 | tf_op jit(solution)/shard_map/ppermute | solution.py:22
  9.7 3.2 %collective-permute-start.2 = (bf16[8,7168]{1,0:T(8,128)(2,1)}, bf16[8,7168]{1,0:T(8,128)(2,1)S(1)}, u32[]{:S(2)}, u32[]{:S(2)}) collective-permute-start(bf16[8,7168]{1,0:T(8,128)(2,1)} %param.16), channel_id=1, source_target_pairs={{0,12},{4,16},{8,20},{12,24},{16,28},{20,0},{24,4},{28,8},{1,13},{... | collective-permute-start | bytes 344072 | tf_op jit(solution)/shard_map/ppermute | solution.py:22
  12.9 1.1 collective-permute-start
  14.0 0.9 bitcast_dynamic-update-slice_fusion.7
  14.9 14.2 %collective-permute-done = bf16[8,7168]{1,0:T(8,128)(2,1)S(1)} collective-permute-done((bf16[8,7168]{1,0:T(8,128)(2,1)}, bf16[8,7168]{1,0:T(8,128)(2,1)S(1)}, u32[]{:S(2)}, u32[]{:S(2)}) %collective-permute-start) | collective-permute-done | bytes 114720 | tf_op jit(solution)/shard_map/ppermute | solution.py:22
  29.4 6.0 %collective-permute-done.5 = bf16[8,7168]{1,0:T(8,128)(2,1)S(1)} collective-permute-done((bf16[8,7168]{1,0:T(8,128)(2,1)}, bf16[8,7168]{1,0:T(8,128)(2,1)S(1)}, u32[]{:S(2)}, u32[]{:S(2)}) %collective-permute-start.5) | collective-permute-done | bytes 114720 | tf_op jit(solution)/shard_map/ppermute | solution.py:22
  35.4 1.3 collective-permute-start.7
  36.7 18.2 %collective-permute-done.7 = bf16[8,8,7168]{2,1,0:T(8,128)(2,1)S(1)} collective-permute-done((bf16[8,8,7168]{2,1,0:T(8,128)(2,1)S(1)}, bf16[8,8,7168]{2,1,0:T(8,128)(2,1)S(1)}, u32[]{:S(2)}, u32[]{:S(2)}) %collective-permute-start.7) | collective-permute-done | bytes 917536 | tf_op jit(solution)/shard_map/ppermute | solution.py:34
  54.9 2.0 %fusion.44 = (bf16[1,2,8,8,7168]{4,3,2,1,0:T(8,128)(2,1)}, bf16[2,8,8,7168]{3,2,1,0:T(8,128)(2,1)}) fusion(bf16[1,8,8,7168]{3,2,1,0:T(8,128)(2,1)S(1)} %bitcast.98, bf16[1,8,8,7168]{3,2,1,0:T(8,128)(2,1)S(1)} %bitcast.97), kind=kLoop, calls=%fused_computation.90 | loop fusion | flops 917504 | bytes 5505024 | tf_op jit(solution)/shard_map/stack | solution.py:35
  56.9 3.4 %collective-permute-start.8 = (bf16[2,8,8,7168]{3,2,1,0:T(8,128)(2,1)}, bf16[2,8,8,7168]{3,2,1,0:T(8,128)(2,1)}, u32[]{:S(2)}, u32[]{:S(2)}) collective-permute-start(bf16[2,8,8,7168]{3,2,1,0:T(8,128)(2,1)} %get-tuple-element.15), channel_id=1, source_target_pairs={{0,1},{1,0},{2,3},{3,2},{4,5},{5,4},{6,7},{7,6},{8,9},{9,8},{10,11... | collective-permute-start | bytes 5505032 | tf_op jit(solution)/shard_map/ppermute | solution.py:34
  61.6 4.9 %all-gather.1 = f32[4,2,128]{2,1,0:T(2,128)S(1)} all-gather(f32[1,2,128]{2,1,0:T(2,128)S(1)} %bitcast.99), channel_id=2, replica_groups=mesh['attn'=8,'exp'=4] {'exp'}, dimensions={0}, use_global_device_ids=true | all-gather | bytes 5120 | tf_op jit(solution)/shard_map/all_gather | solution.py:120
  68.5 2.5 %pad_maximum_fusion = bf16[2,2,8,8,7168]{4,3,2,1,0:T(8,128)(2,1)S(1)} fusion(bf16[1,2,8,8,7168]{4,3,2,1,0:T(8,128)(2,1)} %bitcast.11, bf16[1,2,8,8,7168]{4,3,2,1,0:T(8,128)(2,1)} %get-tuple-element.14), kind=kLoop, calls=%fused_computation.1 | loop fusion | flops 1835008 | bytes 7340032 | tf_op jit(solution)/shard_map/stack | solution.py:35
  71.1 1.9 %copy-done.1 = bf16[2,2,8,8,7168]{4,3,2,1,0:T(8,128)(2,1)} copy-done((bf16[2,2,8,8,7168]{4,3,2,1,0:T(8,128)(2,1)}, bf16[2,2,8,8,7168]{4,3,2,1,0:T(8,128)(2,1)S(1)}, u32[]{:S(2)}) %copy-start.1) | copy-done | bytes 3670040
  73.0 1.1 fusion.4
  74.1 11.1 %fusion = f32[256,7168]{1,0:T(8,128)} fusion(bf16[1,256,7168]{2,1,0:T(8,128)(2,1)} %param.21, bf16[256,7168]{1,0:T(8,128)(2,1)} %bitcast.96, bf16[1,7168,256]{2,1,0:T(8,128)(2,1)} %param.20, f32[256,256]{1,0:T(8,128)S(1)} %fusion.4), kind=kOutput, calls=%fused_computation.2 | convolution fusion | flops 1879441408 | bytes 18612224 | tf_op jit(solution)/shard_map/dot_general | solution.py:16
  85.2 7.0 %fusion.45 = (f32[128,7168]{1,0:T(8,128)}, f32[128,7168]{1,0:T(8,128)}) fusion(f32[256,7168]{1,0:T(8,128)} %fusion), kind=kLoop, calls=%fused_computation.91 | loop fusion | bytes 14680064 | tf_op jit(solution)/shard_map/slice | solution.py:39
  92.4 23.2 %reduce-scatter.2.cloned.1.call-done = f32[2,32,513]{2,1,0:T(8,128)} async-done(((f32[2,128,513]{2,1,0:T(8,128)}), f32[2,32,513]{2,1,0:T(8,128)}) %reduce-scatter.2.cloned.1.call-update) | async-done | bytes 131344 | tf_op jit(solution)/shard_map/reduce_scatter | solution.py:60
  116.5 1.6 fusion.37
  118.1 3.6 %add.101 = f32[2,8,8,7168]{3,2,1,0:T(8,128)S(1)} add(f32[2,8,8,7168]{3,2,1,0:T(8,128)} %bitcast.94, f32[2,8,8,7168]{3,2,1,0:T(8,128)} %collective-permute-done.9) | non-fusion elementwise | flops 917504 | bytes 11010048 | tf_op jit(solution)/shard_map/add | solution.py:40
  121.7 1.8 copy-done.2
  123.5 1.0 fusion.17
  125.5 20.4 %collective-permute-done.10 = bf16[8,8,7168]{2,1,0:T(8,128)(2,1)S(1)} collective-permute-done((bf16[8,8,7168]{2,1,0:T(8,128)(2,1)}, bf16[8,8,7168]{2,1,0:T(8,128)(2,1)S(1)}, u32[]{:S(2)}, u32[]{:S(2)}) %collective-permute-start.10) | collective-permute-done | bytes 917536 | tf_op jit(solution)/shard_map/ppermute | solution.py:40
  145.9 1.7 fusion.6
  148.0 2.1 %collective-permute-start.17 = (bf16[8,7168]{1,0:T(8,128)(2,1)S(1)}, bf16[8,7168]{1,0:T(8,128)(2,1)S(1)}, u32[]{:S(2)}, u32[]{:S(2)}) collective-permute-start(bf16[8,7168]{1,0:T(8,128)(2,1)S(1)} %get-tuple-element.17), channel_id=1, source_target_pairs={{0,4},{4,8},{8,12},{12,16},{16,20},{20,24},{24,28},{28,0},{1,5},{5... | collective-permute-start | bytes 344072 | tf_op jit(solution)/shard_map/ppermute | solution.py:80
  150.1 1.2 collective-permute-start.16
  151.4 2.7 %collective-permute-start.15 = (bf16[8,7168]{1,0:T(8,128)(2,1)S(1)}, bf16[8,7168]{1,0:T(8,128)(2,1)S(1)}, u32[]{:S(2)}, u32[]{:S(2)}) collective-permute-start(bf16[8,7168]{1,0:T(8,128)(2,1)S(1)} %get-tuple-element.19), channel_id=1, source_target_pairs={{0,12},{4,16},{8,20},{12,24},{16,28},{20,0},{24,4},{28,8},{1,13},{... | collective-permute-start | bytes 344072 | tf_op jit(solution)/shard_map/ppermute | solution.py:80
  154.2 2.3 %collective-permute-start.13 = (bf16[8,7168]{1,0:T(8,128)(2,1)S(1)}, bf16[8,7168]{1,0:T(8,128)(2,1)S(1)}, u32[]{:S(2)}, u32[]{:S(2)}) collective-permute-start(bf16[8,7168]{1,0:T(8,128)(2,1)S(1)} %get-tuple-element.21), channel_id=1, source_target_pairs={{0,20},{4,24},{8,28},{12,0},{16,4},{20,8},{24,12},{28,16},{1,21},{... | collective-permute-start | bytes 344072 | tf_op jit(solution)/shard_map/ppermute | solution.py:80
  156.5 2.4 %collective-permute-start.12 = (bf16[8,7168]{1,0:T(8,128)(2,1)S(1)}, bf16[8,7168]{1,0:T(8,128)(2,1)S(1)}, u32[]{:S(2)}, u32[]{:S(2)}) collective-permute-start(bf16[8,7168]{1,0:T(8,128)(2,1)S(1)} %get-tuple-element.22), channel_id=1, source_target_pairs={{0,24},{4,28},{8,0},{12,4},{16,8},{20,12},{24,16},{28,20},{1,25},{... | collective-permute-start | bytes 344072 | tf_op jit(solution)/shard_map/ppermute | solution.py:80
  158.8 7.4 %collective-permute-done.15 = bf16[8,7168]{1,0:T(8,128)(2,1)S(1)} collective-permute-done((bf16[8,7168]{1,0:T(8,128)(2,1)S(1)}, bf16[8,7168]{1,0:T(8,128)(2,1)S(1)}, u32[]{:S(2)}, u32[]{:S(2)}) %collective-permute-start.15) | collective-permute-done | bytes 114720 | tf_op jit(solution)/shard_map/ppermute | solution.py:80
  166.3 2.5 %collective-permute-done.14 = bf16[8,7168]{1,0:T(8,128)(2,1)S(1)} collective-permute-done((bf16[8,7168]{1,0:T(8,128)(2,1)S(1)}, bf16[8,7168]{1,0:T(8,128)(2,1)S(1)}, u32[]{:S(2)}, u32[]{:S(2)}) %collective-permute-start.14) | collective-permute-done | bytes 114720 | tf_op jit(solution)/shard_map/ppermute | solution.py:80
  168.7 6.1 %collective-permute-done.12 = bf16[8,7168]{1,0:T(8,128)(2,1)S(1)} collective-permute-done((bf16[8,7168]{1,0:T(8,128)(2,1)S(1)}, bf16[8,7168]{1,0:T(8,128)(2,1)S(1)}, u32[]{:S(2)}, u32[]{:S(2)}) %collective-permute-start.12) | collective-permute-done | bytes 114720 | tf_op jit(solution)/shard_map/ppermute | solution.py:80
  174.8 0.9 fusion.36
  (66 shorter events, 6.1 us)
Async XLA Ops:
  7.2 53.2 %copy-start = (bf16[2,1024,512]{2,1,0:T(8,128)(2,1)S(1)}, bf16[2,1024,512]{2,1,0:T(8,128)(2,1)}, u32[]{:S(2)}) copy-start(bf16[2,1024,512]{2,1,0:T(8,128)(2,1)} %param.13) | copy-start | bytes 6291460
  7.2 53.1 %copy-start.8 = (s32[2]{0:T(128)S(1)}, s32[2]{0:T(128)}, u32[]{:S(2)}) copy-start(s32[2]{0:T(128)} %param.15) | copy-start | bytes 28
  7.2 53.2 %copy-start.4 = (bf16[2,128,512]{2,1,0:T(8,128)(2,1)S(1)}, bf16[2,128,512]{2,1,0:T(8,128)(2,1)}, u32[]{:S(2)}) copy-start(bf16[2,128,512]{2,1,0:T(8,128)(2,1)} %param.11) | copy-start | bytes 786436
  7.2 108.4 %reduce-scatter.2.cloned.1.call-start = ((), (), s32[]{:S(2)}) async-start(), calls=%async_computation.1 | async-start | bytes 819200 | tf_op jit(solution)/shard_map/reduce_scatter | solution.py:60
  7.2 22.1 %collective-permute-start.4 = (bf16[8,7168]{1,0:T(8,128)(2,1)}, bf16[8,7168]{1,0:T(8,128)(2,1)S(1)}, u32[]{:S(2)}, u32[]{:S(2)}) collective-permute-start(bf16[8,7168]{1,0:T(8,128)(2,1)} %param.16), channel_id=1, source_target_pairs={{0,20},{4,24},{8,28},{12,0},{16,4},{20,8},{24,12},{28,16},{1,21},{... | collective-permute-start | bytes 344072 | tf_op jit(solution)/shard_map/ppermute | solution.py:22
  7.3 22.0 %collective-permute-start.3 = (bf16[8,7168]{1,0:T(8,128)(2,1)}, bf16[8,7168]{1,0:T(8,128)(2,1)S(1)}, u32[]{:S(2)}, u32[]{:S(2)}) collective-permute-start(bf16[8,7168]{1,0:T(8,128)(2,1)} %param.16), channel_id=1, source_target_pairs={{0,16},{4,20},{8,24},{12,28},{16,0},{20,4},{24,8},{28,12},{1,17},{... | collective-permute-start | bytes 344072 | tf_op jit(solution)/shard_map/ppermute | solution.py:22
  9.7 19.6 %collective-permute-start.2 = (bf16[8,7168]{1,0:T(8,128)(2,1)}, bf16[8,7168]{1,0:T(8,128)(2,1)S(1)}, u32[]{:S(2)}, u32[]{:S(2)}) collective-permute-start(bf16[8,7168]{1,0:T(8,128)(2,1)} %param.16), channel_id=1, source_target_pairs={{0,12},{4,16},{8,20},{12,24},{16,28},{20,0},{24,4},{28,8},{1,13},{... | collective-permute-start | bytes 344072 | tf_op jit(solution)/shard_map/ppermute | solution.py:22
  12.9 16.3 %collective-permute-start.1 = (bf16[8,7168]{1,0:T(8,128)(2,1)}, bf16[8,7168]{1,0:T(8,128)(2,1)S(1)}, u32[]{:S(2)}, u32[]{:S(2)}) collective-permute-start(bf16[8,7168]{1,0:T(8,128)(2,1)} %param.16), channel_id=1, source_target_pairs={{0,8},{4,12},{8,16},{12,20},{16,24},{20,28},{24,0},{28,4},{1,9},{5... | collective-permute-start | bytes 344072 | tf_op jit(solution)/shard_map/ppermute | solution.py:22
  12.9 16.3 %collective-permute-start = (bf16[8,7168]{1,0:T(8,128)(2,1)}, bf16[8,7168]{1,0:T(8,128)(2,1)S(1)}, u32[]{:S(2)}, u32[]{:S(2)}) collective-permute-start(bf16[8,7168]{1,0:T(8,128)(2,1)} %param.16), channel_id=1, source_target_pairs={{0,4},{4,8},{8,12},{12,16},{16,20},{20,24},{24,28},{28,0},{1,5},{5... | collective-permute-start | bytes 344072 | tf_op jit(solution)/shard_map/ppermute | solution.py:22
  29.2 6.2 %collective-permute-start.6 = (bf16[8,7168]{1,0:T(8,128)(2,1)}, bf16[8,7168]{1,0:T(8,128)(2,1)S(1)}, u32[]{:S(2)}, u32[]{:S(2)}) collective-permute-start(bf16[8,7168]{1,0:T(8,128)(2,1)} %param.16), channel_id=1, source_target_pairs={{0,28},{4,0},{8,4},{12,8},{16,12},{20,16},{24,20},{28,24},{1,29},{... | collective-permute-start | bytes 344072 | tf_op jit(solution)/shard_map/ppermute | solution.py:22
  29.2 6.2 %collective-permute-start.5 = (bf16[8,7168]{1,0:T(8,128)(2,1)}, bf16[8,7168]{1,0:T(8,128)(2,1)S(1)}, u32[]{:S(2)}, u32[]{:S(2)}) collective-permute-start(bf16[8,7168]{1,0:T(8,128)(2,1)} %param.16), channel_id=1, source_target_pairs={{0,24},{4,28},{8,0},{12,4},{16,8},{20,12},{24,16},{28,20},{1,25},{... | collective-permute-start | bytes 344072 | tf_op jit(solution)/shard_map/ppermute | solution.py:22
  35.4 19.5 %collective-permute-start.7 = (bf16[8,8,7168]{2,1,0:T(8,128)(2,1)S(1)}, bf16[8,8,7168]{2,1,0:T(8,128)(2,1)S(1)}, u32[]{:S(2)}, u32[]{:S(2)}) collective-permute-start(bf16[8,8,7168]{2,1,0:T(8,128)(2,1)S(1)} %bitcast_dynamic-update-slice_fusion), channel_id=1, source_target_pairs={{0,2},{1,3},{2,0},{3,1},{4,6},{5,7},{6,4},{7,5},{8,10},{9,11},{10,... | collective-permute-start | bytes 2752520 | tf_op jit(solution)/shard_map/ppermute | solution.py:34
  54.9 6.3 %copy-start.3 = (bf16[2,64,1024]{2,1,0:T(8,128)(2,1)S(1)}, bf16[2,64,1024]{2,1,0:T(8,128)(2,1)}, u32[]{:S(2)}) copy-start(bf16[2,64,1024]{2,1,0:T(8,128)(2,1)} %param.14) | copy-start | bytes 786436
  54.9 6.3 %copy-start.5 = (bf16[2,64,128]{2,1,0:T(8,128)(2,1)S(1)}, bf16[2,64,128]{2,1,0:T(8,128)(2,1)}, u32[]{:S(2)}) copy-start(bf16[2,64,128]{2,1,0:T(8,128)(2,1)} %param.12) | copy-start | bytes 98308
  56.9 11.6 %collective-permute-start.8 = (bf16[2,8,8,7168]{3,2,1,0:T(8,128)(2,1)}, bf16[2,8,8,7168]{3,2,1,0:T(8,128)(2,1)}, u32[]{:S(2)}, u32[]{:S(2)}) collective-permute-start(bf16[2,8,8,7168]{3,2,1,0:T(8,128)(2,1)} %get-tuple-element.15), channel_id=1, source_target_pairs={{0,1},{1,0},{2,3},{3,2},{4,5},{5,4},{6,7},{7,6},{8,9},{9,8},{10,11... | collective-permute-start | bytes 5505032 | tf_op jit(solution)/shard_map/ppermute | solution.py:34
  68.5 4.5 %copy-start.9 = (bf16[1,7168,256]{2,1,0:T(8,128)(2,1)S(1)}, bf16[1,7168,256]{2,1,0:T(8,128)(2,1)}, u32[]{:S(2)}) copy-start(bf16[1,7168,256]{2,1,0:T(8,128)(2,1)} %param.19) | copy-start | bytes 11010052
  71.0 1.9 %copy-start.1 = (bf16[2,2,8,8,7168]{4,3,2,1,0:T(8,128)(2,1)}, bf16[2,2,8,8,7168]{4,3,2,1,0:T(8,128)(2,1)S(1)}, u32[]{:S(2)}) copy-start(bf16[2,2,8,8,7168]{4,3,2,1,0:T(8,128)(2,1)S(1)} %pad_maximum_fusion) | copy-start | bytes 11010052
  92.2 25.9 %collective-permute-start.9 = (f32[2,8,8,7168]{3,2,1,0:T(8,128)}, f32[2,8,8,7168]{3,2,1,0:T(8,128)}, u32[]{:S(2)}, u32[]{:S(2)}) collective-permute-start(f32[2,8,8,7168]{3,2,1,0:T(8,128)} %bitcast.19), channel_id=1, source_target_pairs={{0,1},{1,0},{2,3},{3,2},{4,5},{5,4},{6,7},{7,6},{8,9},{9,8},{10,11... | collective-permute-start | bytes 11010056 | tf_op jit(solution)/shard_map/ppermute | solution.py:40
  118.1 6.7 %copy-start.6 = (f32[8,4]{0,1:T(4,128)S(1)}, f32[8,4]{0,1:T(4,128)}, u32[]{:S(2)}) copy-start(f32[8,4]{0,1:T(4,128)} %param.18) | copy-start | bytes 388
  118.1 6.7 %copy-start.7 = (s32[8,4]{0,1:T(4,128)S(1)}, s32[8,4]{0,1:T(4,128)}, u32[]{:S(2)}) copy-start(s32[8,4]{0,1:T(4,128)} %param.17) | copy-start | bytes 388
  121.7 1.8 copy-start.2
  124.5 21.4 %collective-permute-start.10 = (bf16[8,8,7168]{2,1,0:T(8,128)(2,1)}, bf16[8,8,7168]{2,1,0:T(8,128)(2,1)S(1)}, u32[]{:S(2)}, u32[]{:S(2)}) collective-permute-start(bf16[8,8,7168]{2,1,0:T(8,128)(2,1)} %fusion.17), channel_id=1, source_target_pairs={{0,2},{1,3},{2,0},{3,1},{4,6},{5,7},{6,4},{7,5},{8,10},{9,11},{10,... | collective-permute-start | bytes 2752520 | tf_op jit(solution)/shard_map/ppermute | solution.py:40
  147.6 6.5 %collective-permute-start.11 = (bf16[8,7168]{1,0:T(8,128)(2,1)S(1)}, bf16[8,7168]{1,0:T(8,128)(2,1)S(1)}, u32[]{:S(2)}, u32[]{:S(2)}) collective-permute-start(bf16[8,7168]{1,0:T(8,128)(2,1)S(1)} %get-tuple-element.16), channel_id=1, source_target_pairs={{0,28},{4,0},{8,4},{12,8},{16,12},{20,16},{24,20},{28,24},{1,29},{... | collective-permute-start | bytes 344072 | tf_op jit(solution)/shard_map/ppermute | solution.py:80
  148.0 8.5 %collective-permute-start.17 = (bf16[8,7168]{1,0:T(8,128)(2,1)S(1)}, bf16[8,7168]{1,0:T(8,128)(2,1)S(1)}, u32[]{:S(2)}, u32[]{:S(2)}) collective-permute-start(bf16[8,7168]{1,0:T(8,128)(2,1)S(1)} %get-tuple-element.17), channel_id=1, source_target_pairs={{0,4},{4,8},{8,12},{12,16},{16,20},{20,24},{24,28},{28,0},{1,5},{5... | collective-permute-start | bytes 344072 | tf_op jit(solution)/shard_map/ppermute | solution.py:80
  150.1 8.7 %collective-permute-start.16 = (bf16[8,7168]{1,0:T(8,128)(2,1)S(1)}, bf16[8,7168]{1,0:T(8,128)(2,1)S(1)}, u32[]{:S(2)}, u32[]{:S(2)}) collective-permute-start(bf16[8,7168]{1,0:T(8,128)(2,1)S(1)} %get-tuple-element.18), channel_id=1, source_target_pairs={{0,8},{4,12},{8,16},{12,20},{16,24},{20,28},{24,0},{28,4},{1,9},{5... | collective-permute-start | bytes 344072 | tf_op jit(solution)/shard_map/ppermute | solution.py:80
  151.4 14.9 %collective-permute-start.15 = (bf16[8,7168]{1,0:T(8,128)(2,1)S(1)}, bf16[8,7168]{1,0:T(8,128)(2,1)S(1)}, u32[]{:S(2)}, u32[]{:S(2)}) collective-permute-start(bf16[8,7168]{1,0:T(8,128)(2,1)S(1)} %get-tuple-element.19), channel_id=1, source_target_pairs={{0,12},{4,16},{8,20},{12,24},{16,28},{20,0},{24,4},{28,8},{1,13},{... | collective-permute-start | bytes 344072 | tf_op jit(solution)/shard_map/ppermute | solution.py:80
  154.1 14.6 %collective-permute-start.14 = (bf16[8,7168]{1,0:T(8,128)(2,1)S(1)}, bf16[8,7168]{1,0:T(8,128)(2,1)S(1)}, u32[]{:S(2)}, u32[]{:S(2)}) collective-permute-start(bf16[8,7168]{1,0:T(8,128)(2,1)S(1)} %get-tuple-element.20), channel_id=1, source_target_pairs={{0,16},{4,20},{8,24},{12,28},{16,0},{20,4},{24,8},{28,12},{1,17},{... | collective-permute-start | bytes 344072 | tf_op jit(solution)/shard_map/ppermute | solution.py:80
  154.2 14.6 %collective-permute-start.13 = (bf16[8,7168]{1,0:T(8,128)(2,1)S(1)}, bf16[8,7168]{1,0:T(8,128)(2,1)S(1)}, u32[]{:S(2)}, u32[]{:S(2)}) collective-permute-start(bf16[8,7168]{1,0:T(8,128)(2,1)S(1)} %get-tuple-element.21), channel_id=1, source_target_pairs={{0,20},{4,24},{8,28},{12,0},{16,4},{20,8},{24,12},{28,16},{1,21},{... | collective-permute-start | bytes 344072 | tf_op jit(solution)/shard_map/ppermute | solution.py:80
  156.5 18.4 %collective-permute-start.12 = (bf16[8,7168]{1,0:T(8,128)(2,1)S(1)}, bf16[8,7168]{1,0:T(8,128)(2,1)S(1)}, u32[]{:S(2)}, u32[]{:S(2)}) collective-permute-start(bf16[8,7168]{1,0:T(8,128)(2,1)S(1)} %get-tuple-element.22), channel_id=1, source_target_pairs={{0,24},{4,28},{8,0},{12,4},{16,8},{20,12},{24,16},{28,20},{1,25},{... | collective-permute-start | bytes 344072 | tf_op jit(solution)/shard_map/ppermute | solution.py:80
Sparse Core Ops, SparseCore 0:
  92.5 23.0 reduce-scatter.1

commit v7 on v5

--- a/solution.py
+++ b/solution.py
@@ -53,10 +53,20 @@
         b //= 2
     hit = route_ids[:, :, None] == jnp.arange(n_experts, dtype=jnp.int32)[None, None, :]
     wmat = jnp.sum(jnp.where(hit, route_gates[:, :, None], 0.0), axis=1)
-    rows = shift_gather(tokens, "attn", n_attn)
-    rows, _ = lax.optimization_barrier((rows, earlier))
-    for bit in bits:
-        rows = bit_gather(rows, "exp", bit, n_exp)
+    n_chunks = 2 if n_attn % 2 == 0 else 1
+    per_chunk = n_attn // n_chunks
+    pieces = [tokens]
+    for k in range(1, n_attn):
+        pieces.append(lax.ppermute(tokens, "attn", [(s, (s + k) % n_attn) for s in range(n_attn)]))
+    blocks = []
+    for c in range(n_chunks):
+        block = jnp.stack(pieces[c * per_chunk : (c + 1) * per_chunk])
+        if c == 0:
+            block, _ = lax.optimization_barrier((block, earlier))
+        for bit in bits:
+            block = bit_gather(block, "exp", bit, n_exp)
+        blocks.append(block)
+    rows = jnp.stack(blocks)
     lead_shape = rows.shape[:-1]
     flat_rows = rows.reshape(-1, model_width)
     me = lax.axis_index("attn")
@@ -65,18 +75,22 @@
     for i in range(n_local):
         partial = expert_part(flat_rows, w_gate[i], w_up[i], w_down[i])
         partial = partial.reshape(lead_shape + (model_width,))
-        for bit in reversed(bits):
-            wire = jnp.bfloat16 if bit == bits[0] else None
-            partial = bit_reduce(partial, "exp", bit, n_exp, wire)
-        expert_rows = partial.astype(jnp.bfloat16)
-        back = [expert_rows[0]]
-        for k in range(1, n_attn):
-            back.append(
-                lax.ppermute(expert_rows[k], "attn", [(s, (s - k) % n_attn) for s in range(n_attn)])
-            )
         chosen = jnp.take(wmat, owners * n_local + i, axis=1)
-        for k in range(n_attn):
-            result = result + chosen[:, k : k + 1] * back[k].astype(jnp.float32)
+        for c in range(n_chunks):
+            part = partial[c]
+            for bit in reversed(bits):
+                wire = jnp.bfloat16 if bit == bits[0] else None
+                part = bit_reduce(part, "exp", bit, n_exp, wire)
+            expert_rows = part.astype(jnp.bfloat16)
+            for kk in range(per_chunk):
+                k = c * per_chunk + kk
+                if k == 0:
+                    back = expert_rows[kk]
+                else:
+                    back = lax.ppermute(
+                        expert_rows[kk], "attn", [(s, (s - k) % n_attn) for s in range(n_attn)]
+                    )
+                result = result + chosen[:, k : k + 1] * back.astype(jnp.float32)
     return result.astype(jnp.bfloat16)
 
 def per_device(

time: 168 us -> 146 us (0.87)
  waiting for transfers between devices: 83.3 us -> 57.8 us
  other arithmetic: 8.48 us -> 14.1 us
  local copies, waits for them, and re-layouts: 14.3 us -> 11 us
  starting transfers between devices: 25.1 us -> 27.6 us
    ppermute x2 -> x4, waiting for transfers between devices: 25.6 us -> 13 us  [bit_gather(): other = lax.ppermute(x, axis, [(i, i ^ bit) for i in range(n)])]
    ppermute x2 -> x4, waiting for transfers between devices: 27.6 us -> 16.3 us  [bit_reduce(): lax.ppermute(sent, axis, [(i, i ^ bit) for i in range(n)]).astype(x.dtype)]
    reduce_scatter x1, waiting for transfers between devices: 13.2 us -> 7.83 us  [per_device(): reduced = lax.psum_scatter(packed, 'exp', scatter_dimension=1, tiled=True)]
    unnamed x21 -> x18, local copies, waits for them, and re-layouts: 7.6 us -> 3.04 us
    ppermute x14, waiting for transfers between devices: 16.9 us -> 20.7 us  [the longest x7 12.6 us: routed_experts(): lax.ppermute(expert_rows[kk], 'attn', [(s, (s - k) % n_attn) for s in ran...]
    add x1 -> x2, other arithmetic: 0.53 us -> 4.11 us  [bit_reduce(): x[0]]
    slice x1, local copies, waits for them, and re-layouts: 3.94 us -> 6.25 us  [bit_reduce(): sent = x[1] if wire is None else x[1].astype(wire)]
    ppermute x2 -> x4, starting transfers between devices: 0.69 us -> 2.73 us  [bit_reduce(): lax.ppermute(sent, axis, [(i, i ^ bit) for i in range(n)]).astype(x.dtype)]
  transfers between devices with their start and end apart: 19 -> 23, of which waited for: 12 -> 10; matrix products, arithmetic and copies ran while one was open for 7% -> 12% of each run, Pallas kernels for 0% -> 0%
where the time goes in v7:
time: 146 us
  waiting for transfers between devices  57.8 us (40%)
  starting transfers between devices  27.6 us (19%)
  matrix products  15.8 us (11%)
  between operations  14.3 us (10%)
  other arithmetic  14.1 us (10%)
  local copies, waits for them, and re-layouts  11 us (8%)
  blocking collectives  5.07 us (3%)
    ppermute x4, waiting for transfers between devices, bit_reduce(): lax.ppermute(sent, axis, [(i, i ^ bit) for i in range(n)]).astype(x.dtype)  16.3 us
    ppermute x4, waiting for transfers between devices, bit_gather(): other = lax.ppermute(x, axis, [(i, i ^ bit) for i in range(n)])  13 us
    ppermute x7, waiting for transfers between devices, routed_experts(): lax.ppermute(expert_rows[kk], 'attn', [(s, (s - k) % n_attn) for s in ran...  12.6 us
    ppermute x7, starting transfers between devices, routed_experts(): lax.ppermute(tokens, 'attn', [(s, (s + k) % n_attn) for s in range(n_attn)])  12 us
    dot_general x1, matrix products, expert_part(): return jnp.dot(hidden, down_slice, preferred_element_type=jnp.float32)  11.1 us
    ppermute x7, starting transfers between devices, routed_experts(): lax.ppermute(expert_rows[kk], 'attn', [(s, (s - k) % n_attn) for s in ran...  10.8 us
    ppermute x7, waiting for transfers between devices, routed_experts(): lax.ppermute(tokens, 'attn', [(s, (s + k) % n_attn) for s in range(n_attn)])  8.14 us
    reduce_scatter x1, waiting for transfers between devices, per_device(): reduced = lax.psum_scatter(packed, 'exp', scatter_dimension=1, tiled=True)  7.83 us
  transfers between devices with their start and end apart: 23, of which 10 were waited for; matrix products, arithmetic and copies ran while one was open for 12% of the time, Pallas kernels for 0%

profile of v7, /device:TPU:0, one launch (start us, length us, event | category | flops | bytes accessed | tf_op | source)
XLA Modules:
  0.0 145.7 jit_solution(17745006903357269521)
XLA Ops:
  7.2 3.0 %collective-permute-start = (bf16[8,7168]{1,0:T(8,128)(2,1)}, bf16[8,7168]{1,0:T(8,128)(2,1)}, u32[]{:S(2)}, u32[]{:S(2)}) collective-permute-start(bf16[8,7168]{1,0:T(8,128)(2,1)} %param.16), channel_id=1, source_target_pairs={{0,4},{4,8},{8,12},{12,16},{16,20},{20,24},{24,28},{28,0},{1,5},{5... | collective-permute-start | bytes 344072 | tf_op jit(solution)/shard_map/ppermute | solution.py:60
  10.3 2.6 %collective-permute-start.5 = (bf16[8,7168]{1,0:T(8,128)(2,1)}, bf16[8,7168]{1,0:T(8,128)(2,1)S(1)}, u32[]{:S(2)}, u32[]{:S(2)}) collective-permute-start(bf16[8,7168]{1,0:T(8,128)(2,1)} %param.16), channel_id=1, source_target_pairs={{0,16},{4,20},{8,24},{12,28},{16,0},{20,4},{24,8},{28,12},{1,17},{... | collective-permute-start | bytes 344072 | tf_op jit(solution)/shard_map/ppermute | solution.py:60
  12.8 1.3 collective-permute-start.6
  14.1 2.2 %collective-permute-start.7 = (bf16[8,7168]{1,0:T(8,128)(2,1)}, bf16[8,7168]{1,0:T(8,128)(2,1)}, u32[]{:S(2)}, u32[]{:S(2)}) collective-permute-start(bf16[8,7168]{1,0:T(8,128)(2,1)} %param.16), channel_id=1, source_target_pairs={{0,24},{4,28},{8,0},{12,4},{16,8},{20,12},{24,16},{28,20},{1,25},{... | collective-permute-start | bytes 344072 | tf_op jit(solution)/shard_map/ppermute | solution.py:60
  16.3 1.9 %collective-permute-start.8 = (bf16[8,7168]{1,0:T(8,128)(2,1)}, bf16[8,7168]{1,0:T(8,128)(2,1)}, u32[]{:S(2)}, u32[]{:S(2)}) collective-permute-start(bf16[8,7168]{1,0:T(8,128)(2,1)} %param.16), channel_id=1, source_target_pairs={{0,28},{4,0},{8,4},{12,8},{16,12},{20,16},{24,20},{28,24},{1,29},{... | collective-permute-start | bytes 344072 | tf_op jit(solution)/shard_map/ppermute | solution.py:60
  19.0 1.8 %fusion.53 = f32[2,128,1024]{2,1,0:T(8,128)S(1)} fusion(bf16[2,128,512]{2,1,0:T(8,128)(2,1)} %param.11, bf16[2,1024,512]{2,1,0:T(8,128)(2,1)S(1)} %copy-done), kind=kOutput, calls=%fused_computation.98 | convolution fusion | flops 268435456 | bytes 3407872 | tf_op jit(solution)/shard_map/rhl,rpl->rhp/dot_general | solution.py:112
  21.6 5.1 %all-gather.1 = f32[4,2,128]{2,1,0:T(2,128)S(1)} all-gather(f32[1,2,128]{2,1,0:T(2,128)S(1)} %bitcast.120), channel_id=2, replica_groups=mesh['attn'=8,'exp'=4] {'exp'}, dimensions={0}, use_global_device_ids=true | all-gather | bytes 5120 | tf_op jit(solution)/shard_map/all_gather | solution.py:129
  26.7 1.4 convolution_multiply_fusion
  28.2 2.0 %pad_maximum_fusion.3 = f32[2,128,513]{2,1,0:T(8,128)} fusion(f32[2,128,1]{2,1,0:T(8,128)S(1)} %copy.21, f32[2,128,512]{2,1,0:T(8,128)} %convolution_multiply_fusion), kind=kLoop, calls=%fused_computation.29 | loop fusion | flops 131328 | bytes 1050624 | tf_op jit(solution)/shard_map/concatenate | solution.py:131
  31.2 1.1 fusion.50
  32.3 1.6 %collective-permute-start.9 = (bf16[4,8,7168]{2,1,0:T(8,128)(2,1)S(1)}, bf16[4,8,7168]{2,1,0:T(8,128)(2,1)}, u32[]{:S(2)}, u32[]{:S(2)}) collective-permute-start(bf16[4,8,7168]{2,1,0:T(8,128)(2,1)S(1)} %get-tuple-element.22), channel_id=1, source_target_pairs={{0,2},{1,3},{2,0},{3,1},{4,6},{5,7},{6,4},{7,5},{8,10},{9,11},{10,... | collective-permute-start | bytes 1376264 | tf_op jit(solution)/shard_map/ppermute | solution.py:34
  33.9 4.3 %collective-permute-done.1 = bf16[8,7168]{1,0:T(8,128)(2,1)S(1)} collective-permute-done((bf16[8,7168]{1,0:T(8,128)(2,1)}, bf16[8,7168]{1,0:T(8,128)(2,1)S(1)}, u32[]{:S(2)}, u32[]{:S(2)}) %collective-permute-start.1) | collective-permute-done | bytes 114720 | tf_op jit(solution)/shard_map/ppermute | solution.py:60
  38.2 3.8 %collective-permute-done.2 = bf16[8,7168]{1,0:T(8,128)(2,1)S(1)} collective-permute-done((bf16[8,7168]{1,0:T(8,128)(2,1)}, bf16[8,7168]{1,0:T(8,128)(2,1)S(1)}, u32[]{:S(2)}, u32[]{:S(2)}) %collective-permute-start.2) | collective-permute-done | bytes 114720 | tf_op jit(solution)/shard_map/ppermute | solution.py:60
  43.0 7.8 %reduce-scatter.2.cloned.1.call-done = f32[2,32,513]{2,1,0:T(8,128)} async-done(((f32[2,128,513]{2,1,0:T(8,128)}), f32[2,32,513]{2,1,0:T(8,128)}) %reduce-scatter.2.cloned.1.call-update) | async-done | bytes 131344 | tf_op jit(solution)/shard_map/reduce_scatter | solution.py:132
  51.7 1.6 %fusion.41 = bf16[2,32,512]{2,1,0:T(8,128)(2,1)} fusion(f32[2,32,513]{2,1,0:T(8,128)} %reduce-scatter.2.cloned.1.call-done, f32[2,32]{1,0:T(2,128)S(1)} %slice_reduce_fusion), kind=kLoop, calls=%fused_computation.52 | loop fusion | flops 65536 | bytes 196864 | tf_op jit(solution)/shard_map/convert_element_type | solution.py:134
  53.7 1.1 fusion.48
  54.9 10.7 %collective-permute-done.3 = bf16[4,8,7168]{2,1,0:T(8,128)(2,1)S(1)} collective-permute-done((bf16[4,8,7168]{2,1,0:T(8,128)(2,1)S(1)}, bf16[4,8,7168]{2,1,0:T(8,128)(2,1)S(1)}, u32[]{:S(2)}, u32[]{:S(2)}) %collective-permute-start.3) | collective-permute-done | bytes 458784 | tf_op jit(solution)/shard_map/ppermute | solution.py:34
  66.0 2.3 %collective-permute-done.4 = bf16[2,4,8,7168]{3,2,1,0:T(8,128)(2,1)S(1)} collective-permute-done((bf16[2,4,8,7168]{3,2,1,0:T(8,128)(2,1)S(1)}, bf16[2,4,8,7168]{3,2,1,0:T(8,128)(2,1)S(1)}, u32[]{:S(2)}, u32[]{:S(2)}) %collective-permute-start.4) | collective-permute-done | bytes 917536 | tf_op jit(solution)/shard_map/ppermute | solution.py:34
  68.8 1.9 %copy-done.1 = bf16[2,2,2,4,8,7168]{5,4,3,2,1,0:T(8,128)(2,1)} copy-done((bf16[2,2,2,4,8,7168]{5,4,3,2,1,0:T(8,128)(2,1)}, bf16[2,2,2,4,8,7168]{5,4,3,2,1,0:T(8,128)(2,1)S(1)}, u32[]{:S(2)}) %copy-start.1) | copy-done | bytes 3670040
  72.9 11.1 %fusion = f32[256,7168]{1,0:T(8,128)} fusion(bf16[1,256,7168]{2,1,0:T(8,128)(2,1)} %param.21, bf16[256,7168]{1,0:T(8,128)(2,1)} %bitcast.109, bf16[1,7168,256]{2,1,0:T(8,128)(2,1)} %param.20, f32[256,256]{1,0:T(8,128)S(1)} %fusion.4), kind=kOutput, calls=%fused_computation.2 | convolution fusion | flops 1879441408 | bytes 18612224 | tf_op jit(solution)/shard_map/dot_general | solution.py:16
  84.1 6.2 %fusion.51 = (f32[64,7168]{1,0:T(8,128)}, f32[64,7168]{1,0:T(8,128)}, f32[64,7168]{1,0:T(8,128)}, f32[64,7168]{1,0:T(8,128)}) fusion(f32[256,7168]{1,0:T(8,128)} %fusion), kind=kLoop, calls=%fused_computation.96 | loop fusion | bytes 14680064 | tf_op jit(solution)/shard_map/slice | solution.py:39
  91.7 2.7 %collective-permute-done.11 = f32[2,4,8,7168]{3,2,1,0:T(8,128)} collective-permute-done((f32[2,4,8,7168]{3,2,1,0:T(8,128)}, f32[2,4,8,7168]{3,2,1,0:T(8,128)}, u32[]{:S(2)}, u32[]{:S(2)}) %collective-permute-start.11) | collective-permute-done | bytes 1835040 | tf_op jit(solution)/shard_map/ppermute | solution.py:40
  94.4 2.4 %add.115 = f32[2,4,8,7168]{3,2,1,0:T(8,128)S(1)} add(f32[2,4,8,7168]{3,2,1,0:T(8,128)} %bitcast.111, f32[2,4,8,7168]{3,2,1,0:T(8,128)} %collective-permute-done.11) | non-fusion elementwise | flops 458752 | bytes 5505024 | tf_op jit(solution)/shard_map/add | solution.py:40
  97.4 1.7 %add.120 = f32[2,4,8,7168]{3,2,1,0:T(8,128)S(1)} add(f32[2,4,8,7168]{3,2,1,0:T(8,128)S(1)} %bitcast.110, f32[2,4,8,7168]{3,2,1,0:T(8,128)} %collective-permute-done.16) | non-fusion elementwise | flops 458752 | bytes 5505024 | tf_op jit(solution)/shard_map/add | solution.py:40
  99.2 1.6 %collective-permute-start.17 = (bf16[4,8,7168]{2,1,0:T(8,128)(2,1)S(1)}, bf16[4,8,7168]{2,1,0:T(8,128)(2,1)S(1)}, u32[]{:S(2)}, u32[]{:S(2)}) collective-permute-start(bf16[4,8,7168]{2,1,0:T(8,128)(2,1)S(1)} %fusion.27), channel_id=1, source_target_pairs={{0,2},{1,3},{2,0},{3,1},{4,6},{5,7},{6,4},{7,5},{8,10},{9,11},{10,... | collective-permute-start | bytes 1376264 | tf_op jit(solution)/shard_map/ppermute | solution.py:40
  100.8 9.5 %collective-permute-done.12 = bf16[4,8,7168]{2,1,0:T(8,128)(2,1)S(1)} collective-permute-done((bf16[4,8,7168]{2,1,0:T(8,128)(2,1)S(1)}, bf16[4,8,7168]{2,1,0:T(8,128)(2,1)S(1)}, u32[]{:S(2)}, u32[]{:S(2)}) %collective-permute-start.12) | collective-permute-done | bytes 458784 | tf_op jit(solution)/shard_map/ppermute | solution.py:40
  110.4 4.3 %collective-permute-start.13 = (bf16[8,7168]{1,0:T(8,128)(2,1)S(1)}, bf16[8,7168]{1,0:T(8,128)(2,1)S(1)}, u32[]{:S(2)}, u32[]{:S(2)}) collective-permute-start(bf16[8,7168]{1,0:T(8,128)(2,1)S(1)} %get-tuple-element.14), channel_id=1, source_target_pairs={{0,28},{4,0},{8,4},{12,8},{16,12},{20,16},{24,20},{28,24},{1,29},{... | collective-permute-start | bytes 344072 | tf_op jit(solution)/shard_map/ppermute | solution.py:90
  115.3 4.1 %collective-permute-done.17 = bf16[4,8,7168]{2,1,0:T(8,128)(2,1)S(1)} collective-permute-done((bf16[4,8,7168]{2,1,0:T(8,128)(2,1)S(1)}, bf16[4,8,7168]{2,1,0:T(8,128)(2,1)S(1)}, u32[]{:S(2)}, u32[]{:S(2)}) %collective-permute-start.17) | collective-permute-done | bytes 458784 | tf_op jit(solution)/shard_map/ppermute | solution.py:40
  119.5 2.5 %collective-permute-start.18 = (bf16[8,7168]{1,0:T(8,128)(2,1)S(1)}, bf16[8,7168]{1,0:T(8,128)(2,1)S(1)}, u32[]{:S(2)}, u32[]{:S(2)}) collective-permute-start(bf16[8,7168]{1,0:T(8,128)(2,1)S(1)} %get-tuple-element.17), channel_id=1, source_target_pairs={{0,16},{4,20},{8,24},{12,28},{16,0},{20,4},{24,8},{28,12},{1,17},{... | collective-permute-start | bytes 344072 | tf_op jit(solution)/shard_map/ppermute | solution.py:90
  121.9 2.4 %collective-permute-start.19 = (bf16[8,7168]{1,0:T(8,128)(2,1)S(1)}, bf16[8,7168]{1,0:T(8,128)(2,1)S(1)}, u32[]{:S(2)}, u32[]{:S(2)}) collective-permute-start(bf16[8,7168]{1,0:T(8,128)(2,1)S(1)} %get-tuple-element.20), channel_id=1, source_target_pairs={{0,12},{4,16},{8,20},{12,24},{16,28},{20,0},{24,4},{28,8},{1,13},{... | collective-permute-start | bytes 344072 | tf_op jit(solution)/shard_map/ppermute | solution.py:90
  125.4 7.8 %collective-permute-done.18 = bf16[8,7168]{1,0:T(8,128)(2,1)S(1)} collective-permute-done((bf16[8,7168]{1,0:T(8,128)(2,1)S(1)}, bf16[8,7168]{1,0:T(8,128)(2,1)S(1)}, u32[]{:S(2)}, u32[]{:S(2)}) %collective-permute-start.18) | collective-permute-done | bytes 114720 | tf_op jit(solution)/shard_map/ppermute | solution.py:90
  133.2 4.8 %collective-permute-done.19 = bf16[8,7168]{1,0:T(8,128)(2,1)S(1)} collective-permute-done((bf16[8,7168]{1,0:T(8,128)(2,1)S(1)}, bf16[8,7168]{1,0:T(8,128)(2,1)S(1)}, u32[]{:S(2)}, u32[]{:S(2)}) %collective-permute-start.19) | collective-permute-done | bytes 114720 | tf_op jit(solution)/shard_map/ppermute | solution.py:90
  (73 shorter events, 12.9 us)
Async XLA Ops:
  7.2 11.8 %copy-start = (bf16[2,1024,512]{2,1,0:T(8,128)(2,1)S(1)}, bf16[2,1024,512]{2,1,0:T(8,128)(2,1)}, u32[]{:S(2)}) copy-start(bf16[2,1024,512]{2,1,0:T(8,128)(2,1)} %param.13) | copy-start | bytes 6291460
  7.2 13.6 %copy-start.3 = (bf16[2,64,1024]{2,1,0:T(8,128)(2,1)S(1)}, bf16[2,64,1024]{2,1,0:T(8,128)(2,1)}, u32[]{:S(2)}) copy-start(bf16[2,64,1024]{2,1,0:T(8,128)(2,1)} %param.14) | copy-start | bytes 786436
  7.2 43.7 %reduce-scatter.2.cloned.1.call-start = ((), (), s32[]{:S(2)}) async-start(), calls=%async_computation.1 | async-start | bytes 819200 | tf_op jit(solution)/shard_map/reduce_scatter | solution.py:132
  7.2 26.7 %collective-permute-start = (bf16[8,7168]{1,0:T(8,128)(2,1)}, bf16[8,7168]{1,0:T(8,128)(2,1)}, u32[]{:S(2)}, u32[]{:S(2)}) collective-permute-start(bf16[8,7168]{1,0:T(8,128)(2,1)} %param.16), channel_id=1, source_target_pairs={{0,4},{4,8},{8,12},{12,16},{16,20},{20,24},{24,28},{28,0},{1,5},{5... | collective-permute-start | bytes 344072 | tf_op jit(solution)/shard_map/ppermute | solution.py:60
  10.3 19.9 %collective-permute-start.5 = (bf16[8,7168]{1,0:T(8,128)(2,1)}, bf16[8,7168]{1,0:T(8,128)(2,1)S(1)}, u32[]{:S(2)}, u32[]{:S(2)}) collective-permute-start(bf16[8,7168]{1,0:T(8,128)(2,1)} %param.16), channel_id=1, source_target_pairs={{0,16},{4,20},{8,24},{12,28},{16,0},{20,4},{24,8},{28,12},{1,17},{... | collective-permute-start | bytes 344072 | tf_op jit(solution)/shard_map/ppermute | solution.py:60
  12.8 17.4 %collective-permute-start.6 = (bf16[8,7168]{1,0:T(8,128)(2,1)}, bf16[8,7168]{1,0:T(8,128)(2,1)}, u32[]{:S(2)}, u32[]{:S(2)}) collective-permute-start(bf16[8,7168]{1,0:T(8,128)(2,1)} %param.16), channel_id=1, source_target_pairs={{0,20},{4,24},{8,28},{12,0},{16,4},{20,8},{24,12},{28,16},{1,21},{... | collective-permute-start | bytes 344072 | tf_op jit(solution)/shard_map/ppermute | solution.py:60
  14.1 17.0 %collective-permute-start.7 = (bf16[8,7168]{1,0:T(8,128)(2,1)}, bf16[8,7168]{1,0:T(8,128)(2,1)}, u32[]{:S(2)}, u32[]{:S(2)}) collective-permute-start(bf16[8,7168]{1,0:T(8,128)(2,1)} %param.16), channel_id=1, source_target_pairs={{0,24},{4,28},{8,0},{12,4},{16,8},{20,12},{24,16},{28,20},{1,25},{... | collective-permute-start | bytes 344072 | tf_op jit(solution)/shard_map/ppermute | solution.py:60
  16.3 14.9 %collective-permute-start.8 = (bf16[8,7168]{1,0:T(8,128)(2,1)}, bf16[8,7168]{1,0:T(8,128)(2,1)}, u32[]{:S(2)}, u32[]{:S(2)}) collective-permute-start(bf16[8,7168]{1,0:T(8,128)(2,1)} %param.16), channel_id=1, source_target_pairs={{0,28},{4,0},{8,4},{12,8},{16,12},{20,16},{24,20},{28,24},{1,29},{... | collective-permute-start | bytes 344072 | tf_op jit(solution)/shard_map/ppermute | solution.py:60
  18.2 2.5 %copy-start.5 = (bf16[2,64,128]{2,1,0:T(8,128)(2,1)S(1)}, bf16[2,64,128]{2,1,0:T(8,128)(2,1)}, u32[]{:S(2)}) copy-start(bf16[2,64,128]{2,1,0:T(8,128)(2,1)} %param.12) | copy-start | bytes 98308
  30.1 1.0 copy-start.4
  30.2 8.0 %collective-permute-start.1 = (bf16[8,7168]{1,0:T(8,128)(2,1)}, bf16[8,7168]{1,0:T(8,128)(2,1)S(1)}, u32[]{:S(2)}, u32[]{:S(2)}) collective-permute-start(bf16[8,7168]{1,0:T(8,128)(2,1)} %param.16), channel_id=1, source_target_pairs={{0,8},{4,12},{8,16},{12,20},{16,24},{20,28},{24,0},{28,4},{1,9},{5... | collective-permute-start | bytes 344072 | tf_op jit(solution)/shard_map/ppermute | solution.py:60
  30.2 11.8 %collective-permute-start.2 = (bf16[8,7168]{1,0:T(8,128)(2,1)}, bf16[8,7168]{1,0:T(8,128)(2,1)S(1)}, u32[]{:S(2)}, u32[]{:S(2)}) collective-permute-start(bf16[8,7168]{1,0:T(8,128)(2,1)} %param.16), channel_id=1, source_target_pairs={{0,12},{4,16},{8,20},{12,24},{16,28},{20,0},{24,4},{28,8},{1,13},{... | collective-permute-start | bytes 344072 | tf_op jit(solution)/shard_map/ppermute | solution.py:60
  32.3 21.3 %collective-permute-start.9 = (bf16[4,8,7168]{2,1,0:T(8,128)(2,1)S(1)}, bf16[4,8,7168]{2,1,0:T(8,128)(2,1)}, u32[]{:S(2)}, u32[]{:S(2)}) collective-permute-start(bf16[4,8,7168]{2,1,0:T(8,128)(2,1)S(1)} %get-tuple-element.22), channel_id=1, source_target_pairs={{0,2},{1,3},{2,0},{3,1},{4,6},{5,7},{6,4},{7,5},{8,10},{9,11},{10,... | collective-permute-start | bytes 1376264 | tf_op jit(solution)/shard_map/ppermute | solution.py:34
  53.3 12.3 %collective-permute-start.3 = (bf16[4,8,7168]{2,1,0:T(8,128)(2,1)S(1)}, bf16[4,8,7168]{2,1,0:T(8,128)(2,1)S(1)}, u32[]{:S(2)}, u32[]{:S(2)}) collective-permute-start(bf16[4,8,7168]{2,1,0:T(8,128)(2,1)S(1)} %pad_maximum_fusion.4), channel_id=1, source_target_pairs={{0,2},{1,3},{2,0},{3,1},{4,6},{5,7},{6,4},{7,5},{8,10},{9,11},{10,... | collective-permute-start | bytes 1376264 | tf_op jit(solution)/shard_map/ppermute | solution.py:34
  54.8 11.0 %collective-permute-start.10 = (bf16[2,4,8,7168]{3,2,1,0:T(8,128)(2,1)S(1)}, bf16[2,4,8,7168]{3,2,1,0:T(8,128)(2,1)S(1)}, u32[]{:S(2)}, u32[]{:S(2)}) collective-permute-start(bf16[2,4,8,7168]{3,2,1,0:T(8,128)(2,1)S(1)} %get-tuple-element.13), channel_id=1, source_target_pairs={{0,1},{1,0},{2,3},{3,2},{4,5},{5,4},{6,7},{7,6},{8,9},{9,8},{10,11... | collective-permute-start | bytes 2752520 | tf_op jit(solution)/shard_map/ppermute | solution.py:34
  65.7 2.5 %collective-permute-start.4 = (bf16[2,4,8,7168]{3,2,1,0:T(8,128)(2,1)S(1)}, bf16[2,4,8,7168]{3,2,1,0:T(8,128)(2,1)S(1)}, u32[]{:S(2)}, u32[]{:S(2)}) collective-permute-start(bf16[2,4,8,7168]{3,2,1,0:T(8,128)(2,1)S(1)} %get-tuple-element.11), channel_id=1, source_target_pairs={{0,1},{1,0},{2,3},{3,2},{4,5},{5,4},{6,7},{7,6},{8,9},{9,8},{10,11... | collective-permute-start | bytes 2752520 | tf_op jit(solution)/shard_map/ppermute | solution.py:34
  68.4 3.4 %copy-start.8 = (bf16[1,7168,256]{2,1,0:T(8,128)(2,1)S(1)}, bf16[1,7168,256]{2,1,0:T(8,128)(2,1)}, u32[]{:S(2)}) copy-start(bf16[1,7168,256]{2,1,0:T(8,128)(2,1)} %param.19) | copy-start | bytes 11010052
  68.8 1.9 %copy-start.1 = (bf16[2,2,2,4,8,7168]{5,4,3,2,1,0:T(8,128)(2,1)}, bf16[2,2,2,4,8,7168]{5,4,3,2,1,0:T(8,128)(2,1)S(1)}, u32[]{:S(2)}) copy-start(bf16[2,2,2,4,8,7168]{5,4,3,2,1,0:T(8,128)(2,1)S(1)} %pad_maximum_fusion) | copy-start | bytes 11010052
  84.1 6.4 %copy-start.6 = (f32[8,4]{0,1:T(4,128)S(1)}, f32[8,4]{0,1:T(4,128)}, u32[]{:S(2)}) copy-start(f32[8,4]{0,1:T(4,128)} %param.18) | copy-start | bytes 388
  84.1 6.4 %copy-start.7 = (s32[8,4]{0,1:T(4,128)S(1)}, s32[8,4]{0,1:T(4,128)}, u32[]{:S(2)}) copy-start(s32[8,4]{0,1:T(4,128)} %param.17) | copy-start | bytes 388
  90.3 4.1 %collective-permute-start.11 = (f32[2,4,8,7168]{3,2,1,0:T(8,128)}, f32[2,4,8,7168]{3,2,1,0:T(8,128)}, u32[]{:S(2)}, u32[]{:S(2)}) collective-permute-start(f32[2,4,8,7168]{3,2,1,0:T(8,128)} %bitcast.28), channel_id=1, source_target_pairs={{0,1},{1,0},{2,3},{3,2},{4,5},{5,4},{6,7},{7,6},{8,9},{9,8},{10,11... | collective-permute-start | bytes 5505032 | tf_op jit(solution)/shard_map/ppermute | solution.py:40
  90.6 6.8 %collective-permute-start.16 = (f32[2,4,8,7168]{3,2,1,0:T(8,128)}, f32[2,4,8,7168]{3,2,1,0:T(8,128)}, u32[]{:S(2)}, u32[]{:S(2)}) collective-permute-start(f32[2,4,8,7168]{3,2,1,0:T(8,128)} %bitcast.112), channel_id=1, source_target_pairs={{0,1},{1,0},{2,3},{3,2},{4,5},{5,4},{6,7},{7,6},{8,9},{9,8},{10,11... | collective-permute-start | bytes 5505032 | tf_op jit(solution)/shard_map/ppermute | solution.py:40
  94.4 3.0 %copy-start.2 = (f32[64,7168]{1,0:T(8,128)S(1)}, f32[64,7168]{1,0:T(8,128)}, u32[]{:S(2)}) copy-start(f32[64,7168]{1,0:T(8,128)} %get-tuple-element.8) | copy-start | bytes 5505028
  96.9 13.4 %collective-permute-start.12 = (bf16[4,8,7168]{2,1,0:T(8,128)(2,1)S(1)}, bf16[4,8,7168]{2,1,0:T(8,128)(2,1)S(1)}, u32[]{:S(2)}, u32[]{:S(2)}) collective-permute-start(bf16[4,8,7168]{2,1,0:T(8,128)(2,1)S(1)} %fusion.26), channel_id=1, source_target_pairs={{0,2},{1,3},{2,0},{3,1},{4,6},{5,7},{6,4},{7,5},{8,10},{9,11},{10,... | collective-permute-start | bytes 1376264 | tf_op jit(solution)/shard_map/ppermute | solution.py:40
  99.2 20.1 %collective-permute-start.17 = (bf16[4,8,7168]{2,1,0:T(8,128)(2,1)S(1)}, bf16[4,8,7168]{2,1,0:T(8,128)(2,1)S(1)}, u32[]{:S(2)}, u32[]{:S(2)}) collective-permute-start(bf16[4,8,7168]{2,1,0:T(8,128)(2,1)S(1)} %fusion.27), channel_id=1, source_target_pairs={{0,2},{1,3},{2,0},{3,1},{4,6},{5,7},{6,4},{7,5},{8,10},{9,11},{10,... | collective-permute-start | bytes 1376264 | tf_op jit(solution)/shard_map/ppermute | solution.py:40
  110.4 13.9 %collective-permute-start.13 = (bf16[8,7168]{1,0:T(8,128)(2,1)S(1)}, bf16[8,7168]{1,0:T(8,128)(2,1)S(1)}, u32[]{:S(2)}, u32[]{:S(2)}) collective-permute-start(bf16[8,7168]{1,0:T(8,128)(2,1)S(1)} %get-tuple-element.14), channel_id=1, source_target_pairs={{0,28},{4,0},{8,4},{12,8},{16,12},{20,16},{24,20},{28,24},{1,29},{... | collective-permute-start | bytes 344072 | tf_op jit(solution)/shard_map/ppermute | solution.py:90
  114.7 9.7 %collective-permute-start.14 = (bf16[8,7168]{1,0:T(8,128)(2,1)S(1)}, bf16[8,7168]{1,0:T(8,128)(2,1)S(1)}, u32[]{:S(2)}, u32[]{:S(2)}) collective-permute-start(bf16[8,7168]{1,0:T(8,128)(2,1)S(1)} %get-tuple-element.16), channel_id=1, source_target_pairs={{0,24},{4,28},{8,0},{12,4},{16,8},{20,12},{24,16},{28,20},{1,25},{... | collective-permute-start | bytes 344072 | tf_op jit(solution)/shard_map/ppermute | solution.py:90
  115.2 10.2 %collective-permute-start.15 = (bf16[8,7168]{1,0:T(8,128)(2,1)S(1)}, bf16[8,7168]{1,0:T(8,128)(2,1)S(1)}, u32[]{:S(2)}, u32[]{:S(2)}) collective-permute-start(bf16[8,7168]{1,0:T(8,128)(2,1)S(1)} %get-tuple-element.15), channel_id=1, source_target_pairs={{0,20},{4,24},{8,28},{12,0},{16,4},{20,8},{24,12},{28,16},{1,21},{... | collective-permute-start | bytes 344072 | tf_op jit(solution)/shard_map/ppermute | solution.py:90
  119.5 13.8 %collective-permute-start.18 = (bf16[8,7168]{1,0:T(8,128)(2,1)S(1)}, bf16[8,7168]{1,0:T(8,128)(2,1)S(1)}, u32[]{:S(2)}, u32[]{:S(2)}) collective-permute-start(bf16[8,7168]{1,0:T(8,128)(2,1)S(1)} %get-tuple-element.17), channel_id=1, source_target_pairs={{0,16},{4,20},{8,24},{12,28},{16,0},{20,4},{24,8},{28,12},{1,17},{... | collective-permute-start | bytes 344072 | tf_op jit(solution)/shard_map/ppermute | solution.py:90
  121.9 16.0 %collective-permute-start.19 = (bf16[8,7168]{1,0:T(8,128)(2,1)S(1)}, bf16[8,7168]{1,0:T(8,128)(2,1)S(1)}, u32[]{:S(2)}, u32[]{:S(2)}) collective-permute-start(bf16[8,7168]{1,0:T(8,128)(2,1)S(1)} %get-tuple-element.20), channel_id=1, source_target_pairs={{0,12},{4,16},{8,20},{12,24},{16,28},{20,0},{24,4},{28,8},{1,13},{... | collective-permute-start | bytes 344072 | tf_op jit(solution)/shard_map/ppermute | solution.py:90
  124.4 13.6 %collective-permute-start.20 = (bf16[8,7168]{1,0:T(8,128)(2,1)S(1)}, bf16[8,7168]{1,0:T(8,128)(2,1)S(1)}, u32[]{:S(2)}, u32[]{:S(2)}) collective-permute-start(bf16[8,7168]{1,0:T(8,128)(2,1)S(1)} %get-tuple-element.19), channel_id=1, source_target_pairs={{0,8},{4,12},{8,16},{12,20},{16,24},{20,28},{24,0},{28,4},{1,9},{5... | collective-permute-start | bytes 344072 | tf_op jit(solution)/shard_map/ppermute | solution.py:90
  124.4 13.6 %collective-permute-start.21 = (bf16[8,7168]{1,0:T(8,128)(2,1)S(1)}, bf16[8,7168]{1,0:T(8,128)(2,1)S(1)}, u32[]{:S(2)}, u32[]{:S(2)}) collective-permute-start(bf16[8,7168]{1,0:T(8,128)(2,1)S(1)} %get-tuple-element.18), channel_id=1, source_target_pairs={{0,4},{4,8},{8,12},{12,16},{16,20},{20,24},{24,28},{28,0},{1,5},{5... | collective-permute-start | bytes 344072 | tf_op jit(solution)/shard_map/ppermute | solution.py:90
Sparse Core Ops, SparseCore 0:
  30.3 20.5 reduce-scatter.1

commit v8 on v7

--- a/solution.py
+++ b/solution.py
@@ -66,18 +66,15 @@
         for bit in bits:
             block = bit_gather(block, "exp", bit, n_exp)
         blocks.append(block)
-    rows = jnp.stack(blocks)
-    lead_shape = rows.shape[:-1]
-    flat_rows = rows.reshape(-1, model_width)
     me = lax.axis_index("attn")
     owners = (me + jnp.arange(n_attn, dtype=jnp.int32)) % n_attn
     result = jnp.zeros((tok_count, model_width), jnp.float32)
     for i in range(n_local):
-        partial = expert_part(flat_rows, w_gate[i], w_up[i], w_down[i])
-        partial = partial.reshape(lead_shape + (model_width,))
         chosen = jnp.take(wmat, owners * n_local + i, axis=1)
         for c in range(n_chunks):
-            part = partial[c]
+            block = blocks[c]
+            part = expert_part(block.reshape(-1, model_width), w_gate[i], w_up[i], w_down[i])
+            part = part.reshape(block.shape[:-1] + (model_width,))
             for bit in reversed(bits):
                 wire = jnp.bfloat16 if bit == bits[0] else None
                 part = bit_reduce(part, "exp", bit, n_exp, wire)

time: 146 us -> 136 us (0.932)
  waiting for transfers between devices: 57.8 us -> 40.3 us
  matrix products: 15.8 us -> 20.1 us
  other arithmetic: 14.1 us -> 17.1 us
  local copies, waits for them, and re-layouts: 11 us -> 8.86 us
    ppermute x7, waiting for transfers between devices: 12.6 us -> 5.27 us  [routed_experts(): lax.ppermute(expert_rows[kk], 'attn', [(s, (s - k) % n_attn) for s in ran...]
    another operation x3 -> x5, other arithmetic: 2.4 us -> 9.08 us  [bit_gather(): return jnp.stack([x, other])]
    ppermute x7, waiting for transfers between devices: 8.14 us -> 1.6 us  [routed_experts(): lax.ppermute(tokens, 'attn', [(s, (s + k) % n_attn) for s in range(n_attn)])]
    dot_general x1 -> x2, matrix products: 11.1 us -> 15.3 us  [expert_part(): return jnp.dot(hidden, down_slice, preferred_element_type=jnp.float32)]
    ppermute x4, waiting for transfers between devices: 13 us -> 10.2 us  [bit_gather(): other = lax.ppermute(x, axis, [(i, i ^ bit) for i in range(n)])]
    slice x1 -> x2, local copies, waits for them, and re-layouts: 6.25 us -> 4.56 us  [bit_reduce(): sent = x[1] if wire is None else x[1].astype(wire)]
    unnamed x18 -> x26, local copies, waits for them, and re-layouts: 3.04 us -> 2.54 us
  transfers between devices with their start and end apart: 23 -> 23, of which waited for: 10 -> 9; matrix products, arithmetic and copies ran while one was open for 12% -> 28% of each run, Pallas kernels for 0% -> 0%
where the time goes in v8:
time: 136 us; the launch traced here: 134 us
  waiting for transfers between devices  40.3 us (30%)
  starting transfers between devices  28.7 us (21%)
  matrix products  20.1 us (15%)
  other arithmetic  17.1 us (13%)
  between operations  14.3 us (11%)
  local copies, waits for them, and re-layouts  8.86 us (7%)
  blocking collectives  5.07 us (4%)
    dot_general x2, matrix products, expert_part(): return jnp.dot(hidden, down_slice, preferred_element_type=jnp.float32)  15.3 us
    ppermute x4, waiting for transfers between devices, bit_reduce(): lax.ppermute(sent, axis, [(i, i ^ bit) for i in range(n)]).astype(x.dtype)  15.2 us
    ppermute x7, starting transfers between devices, routed_experts(): lax.ppermute(tokens, 'attn', [(s, (s + k) % n_attn) for s in range(n_attn)])  12.5 us
    ppermute x7, starting transfers between devices, routed_experts(): lax.ppermute(expert_rows[kk], 'attn', [(s, (s - k) % n_attn) for s in ran...  12.2 us
    ppermute x4, waiting for transfers between devices, bit_gather(): other = lax.ppermute(x, axis, [(i, i ^ bit) for i in range(n)])  10.2 us
    another operation x5, other arithmetic, bit_gather(): return jnp.stack([x, other])  9.08 us
    reduce_scatter x1, waiting for transfers between devices, per_device(): reduced = lax.psum_scatter(packed, 'exp', scatter_dimension=1, tiled=True)  8.09 us
    ppermute x7, waiting for transfers between devices, routed_experts(): lax.ppermute(expert_rows[kk], 'attn', [(s, (s - k) % n_attn) for s in ran...  5.27 us
  transfers between devices with their start and end apart: 23, of which 9 were waited for; matrix products, arithmetic and copies ran while one was open for 28% of the time, Pallas kernels for 0%

profile of v8, /device:TPU:0, one launch (start us, length us, event | category | flops | bytes accessed | tf_op | source)
XLA Modules:
  0.0 134.5 jit_solution(3548951624275983760)
XLA Ops:
  7.2 6.1 %collective-permute-start.13 = (bf16[8,7168]{1,0:T(8,128)(2,1)}, bf16[8,7168]{1,0:T(8,128)(2,1)S(1)}, u32[]{:S(2)}, u32[]{:S(2)}) collective-permute-start(bf16[8,7168]{1,0:T(8,128)(2,1)} %param.16), channel_id=1, source_target_pairs={{0,28},{4,0},{8,4},{12,8},{16,12},{20,16},{24,20},{28,24},{1,29},{... | collective-permute-start | bytes 344072 | tf_op jit(solution)/shard_map/ppermute | solution.py:60
  13.8 3.0 %collective-permute-start.10 = (bf16[8,7168]{1,0:T(8,128)(2,1)}, bf16[8,7168]{1,0:T(8,128)(2,1)}, u32[]{:S(2)}, u32[]{:S(2)}) collective-permute-start(bf16[8,7168]{1,0:T(8,128)(2,1)} %param.16), channel_id=1, source_target_pairs={{0,16},{4,20},{8,24},{12,28},{16,0},{20,4},{24,8},{28,12},{1,17},{... | collective-permute-start | bytes 344072 | tf_op jit(solution)/shard_map/ppermute | solution.py:60
  16.8 1.8 %fusion.57 = f32[2,128,1024]{2,1,0:T(8,128)S(1)} fusion(bf16[2,128,512]{2,1,0:T(8,128)(2,1)} %param.11, bf16[2,1024,512]{2,1,0:T(8,128)(2,1)S(1)} %copy-done), kind=kOutput, calls=%fused_computation.101 | convolution fusion | flops 268435456 | bytes 3407872 | tf_op jit(solution)/shard_map/rhl,rpl->rhp/dot_general | solution.py:109
  19.4 5.1 %all-gather.1 = f32[4,2,128]{2,1,0:T(2,128)S(1)} all-gather(f32[1,2,128]{2,1,0:T(2,128)S(1)} %bitcast.124), channel_id=2, replica_groups=mesh['attn'=8,'exp'=4] {'exp'}, dimensions={0}, use_global_device_ids=true | all-gather | bytes 5120 | tf_op jit(solution)/shard_map/all_gather | solution.py:126
  24.5 1.4 %convolution_multiply_fusion = f32[2,128,512]{2,1,0:T(8,128)} fusion(bf16[2,1024,512]{2,1,0:T(8,128)(2,1)S(1)} %copy-done, f32[2,128,1024]{2,1,0:T(8,128)S(1)} %get-tuple-element.32, f32[2,128]{1,0:T(2,128)S(1)} %get-tuple-element.31, pred[2,1024]{1,0:T(4,128)(4,1)S(1)} %broadcast_compare_fusion, f32[2,128]{1,0:T(2,128)S(1)} %get-tuple-element.5), kind=kOutput, calls=%fused_computation.18 | convolution fusion | flops 269352960 | bytes 3674112 | tf_op jit(solution)/shard_map/rhp,rpl->rhl/dot_general | solution.py:120
  26.0 1.9 %collective-permute-start.1 = (bf16[8,7168]{1,0:T(8,128)(2,1)}, bf16[8,7168]{1,0:T(8,128)(2,1)}, u32[]{:S(2)}, u32[]{:S(2)}) collective-permute-start(bf16[8,7168]{1,0:T(8,128)(2,1)} %param.16), channel_id=1, source_target_pairs={{0,8},{4,12},{8,16},{12,20},{16,24},{20,28},{24,0},{28,4},{1,9},{5... | collective-permute-start | bytes 344072 | tf_op jit(solution)/shard_map/ppermute | solution.py:60
  29.1 1.6 %collective-permute-done.10 = bf16[8,7168]{1,0:T(8,128)(2,1)} collective-permute-done((bf16[8,7168]{1,0:T(8,128)(2,1)}, bf16[8,7168]{1,0:T(8,128)(2,1)}, u32[]{:S(2)}, u32[]{:S(2)}) %collective-permute-start.10) | collective-permute-done | bytes 114720 | tf_op jit(solution)/shard_map/ppermute | solution.py:60
  30.7 1.9 %fusion.53 = (bf16[1,4,8,7168]{3,2,1,0:T(8,128)(2,1)S(1)}, bf16[4,8,7168]{2,1,0:T(8,128)(2,1)}) fusion(bf16[1,8,7168]{2,1,0:T(8,128)(2,1)} %bitcast.123, bf16[1,8,7168]{2,1,0:T(8,128)(2,1)} %bitcast.31, bf16[1,8,7168]{2,1,0:T(8,128)(2,1)} %bitcast.30, bf16[1,8,7168]{2,1,0:T(8,128)(2,1)} %bitcast.29), kind=kLoop, calls=%fused_computation.97 | loop fusion | flops 688128 | bytes 1376256 | tf_op jit(solution)/shard_map/stack | solution.py:35
  32.6 1.5 %collective-permute-start.14 = (bf16[4,8,7168]{2,1,0:T(8,128)(2,1)}, bf16[4,8,7168]{2,1,0:T(8,128)(2,1)}, u32[]{:S(2)}, u32[]{:S(2)}) collective-permute-start(bf16[4,8,7168]{2,1,0:T(8,128)(2,1)} %get-tuple-element.22), channel_id=1, source_target_pairs={{0,2},{1,3},{2,0},{3,1},{4,6},{5,7},{6,4},{7,5},{8,10},{9,11},{10,... | collective-permute-start | bytes 1376264 | tf_op jit(solution)/shard_map/ppermute | solution.py:34
  35.1 9.2 %collective-permute-done.14 = bf16[4,8,7168]{2,1,0:T(8,128)(2,1)} collective-permute-done((bf16[4,8,7168]{2,1,0:T(8,128)(2,1)}, bf16[4,8,7168]{2,1,0:T(8,128)(2,1)}, u32[]{:S(2)}, u32[]{:S(2)}) %collective-permute-start.14) | collective-permute-done | bytes 458784 | tf_op jit(solution)/shard_map/ppermute | solution.py:34
  44.3 2.1 %fusion.51 = (bf16[1,2,4,8,7168]{4,3,2,1,0:T(8,128)(2,1)S(1)}, bf16[2,4,8,7168]{3,2,1,0:T(8,128)(2,1)}) fusion(bf16[1,4,8,7168]{3,2,1,0:T(8,128)(2,1)} %bitcast.34, bf16[1,4,8,7168]{3,2,1,0:T(8,128)(2,1)S(1)} %get-tuple-element.21), kind=kLoop, calls=%fused_computation.95 | loop fusion | flops 458752 | bytes 2752512 | tf_op jit(solution)/shard_map/stack | solution.py:35
  46.4 1.1 pad_maximum_fusion.5
  47.5 8.1 %reduce-scatter.2.cloned.1.call-done = f32[2,32,513]{2,1,0:T(8,128)} async-done(((f32[2,128,513]{2,1,0:T(8,128)}), f32[2,32,513]{2,1,0:T(8,128)}) %reduce-scatter.2.cloned.1.call-update) | async-done | bytes 131344 | tf_op jit(solution)/shard_map/reduce_scatter | solution.py:129
  56.5 1.6 %fusion.34 = bf16[2,32,512]{2,1,0:T(8,128)(2,1)} fusion(f32[2,32,513]{2,1,0:T(8,128)} %reduce-scatter.2.cloned.1.call-done, f32[2,32]{1,0:T(2,128)S(1)} %slice_reduce_fusion), kind=kLoop, calls=%fused_computation.50 | loop fusion | flops 65536 | bytes 196864 | tf_op jit(solution)/shard_map/convert_element_type | solution.py:131
  58.4 1.5 %pad_maximum_fusion.1 = bf16[2,2,4,8,7168]{4,3,2,1,0:T(8,128)(2,1)S(1)} fusion(bf16[1,2,4,8,7168]{4,3,2,1,0:T(8,128)(2,1)} %bitcast.36, bf16[1,2,4,8,7168]{4,3,2,1,0:T(8,128)(2,1)S(1)} %get-tuple-element.12), kind=kLoop, calls=%fused_computation.14 | loop fusion | flops 917504 | bytes 3670016 | tf_op jit(solution)/shard_map/stack | solution.py:35
  59.9 1.3 copy-done.1
  61.8 7.6 %fusion = f32[128,7168]{1,0:T(8,128)} fusion(bf16[1,256,7168]{2,1,0:T(8,128)(2,1)} %param.21, f32[128,256]{1,0:T(8,128)S(1)} %fusion.4, bf16[128,7168]{1,0:T(8,128)(2,1)} %bitcast.116, bf16[1,7168,256]{2,1,0:T(8,128)(2,1)} %param.19), kind=kOutput, calls=%fused_computation.1 | convolution fusion | flops 939720704 | bytes 12976128 | tf_op jit(solution)/shard_map/dot_general | solution.py:16
  70.5 2.1 %fusion.52 = (bf16[1,2,4,8,7168]{4,3,2,1,0:T(8,128)(2,1)S(1)}, bf16[2,4,8,7168]{3,2,1,0:T(8,128)(2,1)}) fusion(bf16[1,4,8,7168]{3,2,1,0:T(8,128)(2,1)} %bitcast.10, bf16[1,4,8,7168]{3,2,1,0:T(8,128)(2,1)S(1)} %bitcast.122), kind=kLoop, calls=%fused_computation.96 | loop fusion | flops 458752 | bytes 2752512 | tf_op jit(solution)/shard_map/stack | solution.py:35
  72.5 4.2 %fusion.55 = (f32[64,7168]{1,0:T(8,128)}, f32[64,7168]{1,0:T(8,128)}) fusion(f32[128,7168]{1,0:T(8,128)} %fusion), kind=kLoop, calls=%fused_computation.99 | loop fusion | bytes 7340032 | tf_op jit(solution)/shard_map/slice | solution.py:39
  77.9 1.5 %pad_maximum_fusion = bf16[2,2,4,8,7168]{4,3,2,1,0:T(8,128)(2,1)S(1)} fusion(bf16[1,2,4,8,7168]{4,3,2,1,0:T(8,128)(2,1)} %bitcast.12, bf16[1,2,4,8,7168]{4,3,2,1,0:T(8,128)(2,1)S(1)} %get-tuple-element.10), kind=kLoop, calls=%fused_computation.13 | loop fusion | flops 917504 | bytes 3670016 | tf_op jit(solution)/shard_map/stack | solution.py:35
  79.4 1.2 copy-done.2
  81.3 7.6 %fusion.2 = f32[128,7168]{1,0:T(8,128)} fusion(bf16[1,256,7168]{2,1,0:T(8,128)(2,1)} %param.21, f32[128,256]{1,0:T(8,128)S(1)} %fusion.6, bf16[128,7168]{1,0:T(8,128)(2,1)} %bitcast.118, bf16[1,7168,256]{2,1,0:T(8,128)(2,1)} %param.19), kind=kOutput, calls=%fused_computation.3 | convolution fusion | flops 939720704 | bytes 12976128 | tf_op jit(solution)/shard_map/dot_general | solution.py:16
  89.0 2.4 %add.124 = f32[2,4,8,7168]{3,2,1,0:T(8,128)S(1)} add(f32[2,4,8,7168]{3,2,1,0:T(8,128)} %bitcast.119, f32[2,4,8,7168]{3,2,1,0:T(8,128)} %collective-permute-done.16) | non-fusion elementwise | flops 458752 | bytes 5505024 | tf_op jit(solution)/shard_map/add | solution.py:40
  92.7 11.2 %collective-permute-done.17 = bf16[4,8,7168]{2,1,0:T(8,128)(2,1)S(1)} collective-permute-done((bf16[4,8,7168]{2,1,0:T(8,128)(2,1)S(1)}, bf16[4,8,7168]{2,1,0:T(8,128)(2,1)S(1)}, u32[]{:S(2)}, u32[]{:S(2)}) %collective-permute-start.17) | collective-permute-done | bytes 458784 | tf_op jit(solution)/shard_map/ppermute | solution.py:40
  105.2 1.5 %collective-permute-start.21 = (bf16[8,7168]{1,0:T(8,128)(2,1)S(1)}, bf16[8,7168]{1,0:T(8,128)(2,1)S(1)}, u32[]{:S(2)}, u32[]{:S(2)}) collective-permute-start(bf16[8,7168]{1,0:T(8,128)(2,1)S(1)} %get-tuple-element.18), channel_id=1, source_target_pairs={{0,4},{4,8},{8,12},{12,16},{16,20},{20,24},{24,28},{28,0},{1,5},{5... | collective-permute-start | bytes 344072 | tf_op jit(solution)/shard_map/ppermute | solution.py:87
  106.7 1.5 %collective-permute-start.20 = (bf16[8,7168]{1,0:T(8,128)(2,1)S(1)}, bf16[8,7168]{1,0:T(8,128)(2,1)S(1)}, u32[]{:S(2)}, u32[]{:S(2)}) collective-permute-start(bf16[8,7168]{1,0:T(8,128)(2,1)S(1)} %get-tuple-element.19), channel_id=1, source_target_pairs={{0,8},{4,12},{8,16},{12,20},{16,24},{20,28},{24,0},{28,4},{1,9},{5... | collective-permute-start | bytes 344072 | tf_op jit(solution)/shard_map/ppermute | solution.py:87
  108.2 2.4 %collective-permute-start.19 = (bf16[8,7168]{1,0:T(8,128)(2,1)S(1)}, bf16[8,7168]{1,0:T(8,128)(2,1)S(1)}, u32[]{:S(2)}, u32[]{:S(2)}) collective-permute-start(bf16[8,7168]{1,0:T(8,128)(2,1)S(1)} %get-tuple-element.20), channel_id=1, source_target_pairs={{0,12},{4,16},{8,20},{12,24},{16,28},{20,0},{24,4},{28,8},{1,13},{... | collective-permute-start | bytes 344072 | tf_op jit(solution)/shard_map/ppermute | solution.py:87
  110.6 1.4 %collective-permute-start.18 = (bf16[8,7168]{1,0:T(8,128)(2,1)S(1)}, bf16[8,7168]{1,0:T(8,128)(2,1)S(1)}, u32[]{:S(2)}, u32[]{:S(2)}) collective-permute-start(bf16[8,7168]{1,0:T(8,128)(2,1)S(1)} %get-tuple-element.17), channel_id=1, source_target_pairs={{0,16},{4,20},{8,24},{12,28},{16,0},{20,4},{24,8},{28,12},{1,17},{... | collective-permute-start | bytes 344072 | tf_op jit(solution)/shard_map/ppermute | solution.py:87
  112.0 4.0 %collective-permute-done.6 = bf16[4,8,7168]{2,1,0:T(8,128)(2,1)S(1)} collective-permute-done((bf16[4,8,7168]{2,1,0:T(8,128)(2,1)S(1)}, bf16[4,8,7168]{2,1,0:T(8,128)(2,1)S(1)}, u32[]{:S(2)}, u32[]{:S(2)}) %collective-permute-start.6) | collective-permute-done | bytes 458784 | tf_op jit(solution)/shard_map/ppermute | solution.py:40
  116.1 3.4 %collective-permute-start.9 = (bf16[8,7168]{1,0:T(8,128)(2,1)S(1)}, bf16[8,7168]{1,0:T(8,128)(2,1)S(1)}, u32[]{:S(2)}, u32[]{:S(2)}) collective-permute-start(bf16[8,7168]{1,0:T(8,128)(2,1)S(1)} %get-tuple-element.15), channel_id=1, source_target_pairs={{0,20},{4,24},{8,28},{12,0},{16,4},{20,8},{24,12},{28,16},{1,21},{... | collective-permute-start | bytes 344072 | tf_op jit(solution)/shard_map/ppermute | solution.py:87
  119.5 1.5 %collective-permute-start.8 = (bf16[8,7168]{1,0:T(8,128)(2,1)S(1)}, bf16[8,7168]{1,0:T(8,128)(2,1)S(1)}, u32[]{:S(2)}, u32[]{:S(2)}) collective-permute-start(bf16[8,7168]{1,0:T(8,128)(2,1)S(1)} %get-tuple-element.16), channel_id=1, source_target_pairs={{0,24},{4,28},{8,0},{12,4},{16,8},{20,12},{24,16},{28,20},{1,25},{... | collective-permute-start | bytes 344072 | tf_op jit(solution)/shard_map/ppermute | solution.py:87
  121.9 4.7 %collective-permute-done.9 = bf16[8,7168]{1,0:T(8,128)(2,1)S(1)} collective-permute-done((bf16[8,7168]{1,0:T(8,128)(2,1)S(1)}, bf16[8,7168]{1,0:T(8,128)(2,1)S(1)}, u32[]{:S(2)}, u32[]{:S(2)}) %collective-permute-start.9) | collective-permute-done | bytes 114720 | tf_op jit(solution)/shard_map/ppermute | solution.py:87
  (83 shorter events, 13.0 us)
Async XLA Ops:
  7.2 9.6 %copy-start = (bf16[2,1024,512]{2,1,0:T(8,128)(2,1)S(1)}, bf16[2,1024,512]{2,1,0:T(8,128)(2,1)}, u32[]{:S(2)}) copy-start(bf16[2,1024,512]{2,1,0:T(8,128)(2,1)} %param.13) | copy-start | bytes 6291460
  7.2 11.3 %copy-start.12 = (s32[2]{0:T(128)S(1)}, s32[2]{0:T(128)}, u32[]{:S(2)}) copy-start(s32[2]{0:T(128)} %param.15) | copy-start | bytes 28
  7.2 11.4 %copy-start.7 = (bf16[2,64,1024]{2,1,0:T(8,128)(2,1)S(1)}, bf16[2,64,1024]{2,1,0:T(8,128)(2,1)}, u32[]{:S(2)}) copy-start(bf16[2,64,1024]{2,1,0:T(8,128)(2,1)} %param.14) | copy-start | bytes 786436
  7.2 48.4 %reduce-scatter.2.cloned.1.call-start = ((), (), s32[]{:S(2)}) async-start(), calls=%async_computation.1 | async-start | bytes 819200 | tf_op jit(solution)/shard_map/reduce_scatter | solution.py:129
  7.2 18.8 %collective-permute-start.13 = (bf16[8,7168]{1,0:T(8,128)(2,1)}, bf16[8,7168]{1,0:T(8,128)(2,1)S(1)}, u32[]{:S(2)}, u32[]{:S(2)}) collective-permute-start(bf16[8,7168]{1,0:T(8,128)(2,1)} %param.16), channel_id=1, source_target_pairs={{0,28},{4,0},{8,4},{12,8},{16,12},{20,16},{24,20},{28,24},{1,29},{... | collective-permute-start | bytes 344072 | tf_op jit(solution)/shard_map/ppermute | solution.py:60
  13.3 14.6 %collective-permute-start.12 = (bf16[8,7168]{1,0:T(8,128)(2,1)}, bf16[8,7168]{1,0:T(8,128)(2,1)}, u32[]{:S(2)}, u32[]{:S(2)}) collective-permute-start(bf16[8,7168]{1,0:T(8,128)(2,1)} %param.16), channel_id=1, source_target_pairs={{0,24},{4,28},{8,0},{12,4},{16,8},{20,12},{24,16},{28,20},{1,25},{... | collective-permute-start | bytes 344072 | tf_op jit(solution)/shard_map/ppermute | solution.py:60
  13.8 15.3 %collective-permute-start.11 = (bf16[8,7168]{1,0:T(8,128)(2,1)}, bf16[8,7168]{1,0:T(8,128)(2,1)}, u32[]{:S(2)}, u32[]{:S(2)}) collective-permute-start(bf16[8,7168]{1,0:T(8,128)(2,1)} %param.16), channel_id=1, source_target_pairs={{0,20},{4,24},{8,28},{12,0},{16,4},{20,8},{24,12},{28,16},{1,21},{... | collective-permute-start | bytes 344072 | tf_op jit(solution)/shard_map/ppermute | solution.py:60
  13.8 16.9 %collective-permute-start.10 = (bf16[8,7168]{1,0:T(8,128)(2,1)}, bf16[8,7168]{1,0:T(8,128)(2,1)}, u32[]{:S(2)}, u32[]{:S(2)}) collective-permute-start(bf16[8,7168]{1,0:T(8,128)(2,1)} %param.16), channel_id=1, source_target_pairs={{0,16},{4,20},{8,24},{12,28},{16,0},{20,4},{24,8},{28,12},{1,17},{... | collective-permute-start | bytes 344072 | tf_op jit(solution)/shard_map/ppermute | solution.py:60
  16.7 29.7 %collective-permute-start.2 = (bf16[8,7168]{1,0:T(8,128)(2,1)}, bf16[8,7168]{1,0:T(8,128)(2,1)}, u32[]{:S(2)}, u32[]{:S(2)}) collective-permute-start(bf16[8,7168]{1,0:T(8,128)(2,1)} %param.16), channel_id=1, source_target_pairs={{0,12},{4,16},{8,20},{12,24},{16,28},{20,0},{24,4},{28,8},{1,13},{... | collective-permute-start | bytes 344072 | tf_op jit(solution)/shard_map/ppermute | solution.py:60
  25.9 8.2 %copy-start.6 = (f32[2,128,512]{2,1,0:T(8,128)S(1)}, f32[2,128,512]{2,1,0:T(8,128)}, u32[]{:S(2)}) copy-start(f32[2,128,512]{2,1,0:T(8,128)} %convolution_multiply_fusion) | copy-start | bytes 1572868
  25.9 9.1 %copy-start.10 = (f32[8,4]{0,1:T(4,128)S(1)}, f32[8,4]{0,1:T(4,128)}, u32[]{:S(2)}) copy-start(f32[8,4]{0,1:T(4,128)} %param.18) | copy-start | bytes 388
  25.9 9.2 %copy-start.11 = (s32[8,4]{0,1:T(4,128)S(1)}, s32[8,4]{0,1:T(4,128)}, u32[]{:S(2)}) copy-start(s32[8,4]{0,1:T(4,128)} %param.17) | copy-start | bytes 388
  26.0 4.6 %copy-start.8 = (bf16[8,7168]{1,0:T(8,128)(2,1)}, bf16[8,7168]{1,0:T(8,128)(2,1)S(1)}, u32[]{:S(2)}) copy-start(bf16[8,7168]{1,0:T(8,128)(2,1)S(1)} %collective-permute-done.13) | copy-start | bytes 344068
  26.0 20.3 %collective-permute-start.1 = (bf16[8,7168]{1,0:T(8,128)(2,1)}, bf16[8,7168]{1,0:T(8,128)(2,1)}, u32[]{:S(2)}, u32[]{:S(2)}) collective-permute-start(bf16[8,7168]{1,0:T(8,128)(2,1)} %param.16), channel_id=1, source_target_pairs={{0,8},{4,12},{8,16},{12,20},{16,24},{20,28},{24,0},{28,4},{1,9},{5... | collective-permute-start | bytes 344072 | tf_op jit(solution)/shard_map/ppermute | solution.py:60
  28.0 18.4 %collective-permute-start = (bf16[8,7168]{1,0:T(8,128)(2,1)}, bf16[8,7168]{1,0:T(8,128)(2,1)}, u32[]{:S(2)}, u32[]{:S(2)}) collective-permute-start(bf16[8,7168]{1,0:T(8,128)(2,1)} %param.16), channel_id=1, source_target_pairs={{0,4},{4,8},{8,12},{12,16},{16,20},{20,24},{24,28},{28,0},{1,5},{5... | collective-permute-start | bytes 344072 | tf_op jit(solution)/shard_map/ppermute | solution.py:60
  32.6 11.7 %collective-permute-start.14 = (bf16[4,8,7168]{2,1,0:T(8,128)(2,1)}, bf16[4,8,7168]{2,1,0:T(8,128)(2,1)}, u32[]{:S(2)}, u32[]{:S(2)}) collective-permute-start(bf16[4,8,7168]{2,1,0:T(8,128)(2,1)} %get-tuple-element.22), channel_id=1, source_target_pairs={{0,2},{1,3},{2,0},{3,1},{4,6},{5,7},{6,4},{7,5},{8,10},{9,11},{10,... | collective-permute-start | bytes 1376264 | tf_op jit(solution)/shard_map/ppermute | solution.py:34
  46.4 12.0 %collective-permute-start.15 = (bf16[2,4,8,7168]{3,2,1,0:T(8,128)(2,1)}, bf16[2,4,8,7168]{3,2,1,0:T(8,128)(2,1)}, u32[]{:S(2)}, u32[]{:S(2)}) collective-permute-start(bf16[2,4,8,7168]{3,2,1,0:T(8,128)(2,1)} %get-tuple-element.13), channel_id=1, source_target_pairs={{0,1},{1,0},{2,3},{3,2},{4,5},{5,4},{6,7},{7,6},{8,9},{9,8},{10,11... | collective-permute-start | bytes 2752520 | tf_op jit(solution)/shard_map/ppermute | solution.py:34
  58.1 12.4 %collective-permute-start.3 = (bf16[4,8,7168]{2,1,0:T(8,128)(2,1)S(1)}, bf16[4,8,7168]{2,1,0:T(8,128)(2,1)}, u32[]{:S(2)}, u32[]{:S(2)}) collective-permute-start(bf16[4,8,7168]{2,1,0:T(8,128)(2,1)S(1)} %pad_maximum_fusion.5), channel_id=1, source_target_pairs={{0,2},{1,3},{2,0},{3,1},{4,6},{5,7},{6,4},{7,5},{8,10},{9,11},{10,... | collective-permute-start | bytes 1376264 | tf_op jit(solution)/shard_map/ppermute | solution.py:34
  58.4 2.8 %copy-start.4 = (bf16[1,7168,256]{2,1,0:T(8,128)(2,1)S(1)}, bf16[1,7168,256]{2,1,0:T(8,128)(2,1)}, u32[]{:S(2)}) copy-start(bf16[1,7168,256]{2,1,0:T(8,128)(2,1)} %param.20) | copy-start | bytes 11010052
  72.5 5.4 %collective-permute-start.4 = (bf16[2,4,8,7168]{3,2,1,0:T(8,128)(2,1)}, bf16[2,4,8,7168]{3,2,1,0:T(8,128)(2,1)}, u32[]{:S(2)}, u32[]{:S(2)}) collective-permute-start(bf16[2,4,8,7168]{3,2,1,0:T(8,128)(2,1)} %get-tuple-element.11), channel_id=1, source_target_pairs={{0,1},{1,0},{2,3},{3,2},{4,5},{5,4},{6,7},{7,6},{8,9},{9,8},{10,11... | collective-permute-start | bytes 2752520 | tf_op jit(solution)/shard_map/ppermute | solution.py:34
  76.8 12.2 %collective-permute-start.16 = (f32[2,4,8,7168]{3,2,1,0:T(8,128)}, f32[2,4,8,7168]{3,2,1,0:T(8,128)}, u32[]{:S(2)}, u32[]{:S(2)}) collective-permute-start(f32[2,4,8,7168]{3,2,1,0:T(8,128)} %bitcast.39), channel_id=1, source_target_pairs={{0,1},{1,0},{2,3},{3,2},{4,5},{5,4},{6,7},{7,6},{8,9},{9,8},{10,11... | collective-permute-start | bytes 5505032 | tf_op jit(solution)/shard_map/ppermute | solution.py:40
  89.0 3.3 %copy-start.3 = (f32[128,7168]{1,0:T(8,128)S(1)}, f32[128,7168]{1,0:T(8,128)}, u32[]{:S(2)}) copy-start(f32[128,7168]{1,0:T(8,128)} %fusion.2) | copy-start | bytes 11010052
  91.4 12.5 %collective-permute-start.17 = (bf16[4,8,7168]{2,1,0:T(8,128)(2,1)S(1)}, bf16[4,8,7168]{2,1,0:T(8,128)(2,1)S(1)}, u32[]{:S(2)}, u32[]{:S(2)}) collective-permute-start(bf16[4,8,7168]{2,1,0:T(8,128)(2,1)S(1)} %fusion.25), channel_id=1, source_target_pairs={{0,2},{1,3},{2,0},{3,1},{4,6},{5,7},{6,4},{7,5},{8,10},{9,11},{10,... | collective-permute-start | bytes 1376264 | tf_op jit(solution)/shard_map/ppermute | solution.py:40
  92.5 11.4 %collective-permute-start.5 = (f32[2,4,8,7168]{3,2,1,0:T(8,128)S(1)}, f32[2,4,8,7168]{3,2,1,0:T(8,128)S(1)}, u32[]{:S(2)}, u32[]{:S(2)}) collective-permute-start(f32[2,4,8,7168]{3,2,1,0:T(8,128)S(1)} %bitcast.121), channel_id=1, source_target_pairs={{0,1},{1,0},{2,3},{3,2},{4,5},{5,4},{6,7},{7,6},{8,9},{9,8},{10,11... | collective-permute-start | bytes 5505032 | tf_op jit(solution)/shard_map/ppermute | solution.py:40
  104.3 11.6 %collective-permute-start.6 = (bf16[4,8,7168]{2,1,0:T(8,128)(2,1)S(1)}, bf16[4,8,7168]{2,1,0:T(8,128)(2,1)S(1)}, u32[]{:S(2)}, u32[]{:S(2)}) collective-permute-start(bf16[4,8,7168]{2,1,0:T(8,128)(2,1)S(1)} %fusion.24), channel_id=1, source_target_pairs={{0,2},{1,3},{2,0},{3,1},{4,6},{5,7},{6,4},{7,5},{8,10},{9,11},{10,... | collective-permute-start | bytes 1376264 | tf_op jit(solution)/shard_map/ppermute | solution.py:40
  105.2 14.3 %collective-permute-start.21 = (bf16[8,7168]{1,0:T(8,128)(2,1)S(1)}, bf16[8,7168]{1,0:T(8,128)(2,1)S(1)}, u32[]{:S(2)}, u32[]{:S(2)}) collective-permute-start(bf16[8,7168]{1,0:T(8,128)(2,1)S(1)} %get-tuple-element.18), channel_id=1, source_target_pairs={{0,4},{4,8},{8,12},{12,16},{16,20},{20,24},{24,28},{28,0},{1,5},{5... | collective-permute-start | bytes 344072 | tf_op jit(solution)/shard_map/ppermute | solution.py:87
  106.7 14.3 %collective-permute-start.20 = (bf16[8,7168]{1,0:T(8,128)(2,1)S(1)}, bf16[8,7168]{1,0:T(8,128)(2,1)S(1)}, u32[]{:S(2)}, u32[]{:S(2)}) collective-permute-start(bf16[8,7168]{1,0:T(8,128)(2,1)S(1)} %get-tuple-element.19), channel_id=1, source_target_pairs={{0,8},{4,12},{8,16},{12,20},{16,24},{20,28},{24,0},{28,4},{1,9},{5... | collective-permute-start | bytes 344072 | tf_op jit(solution)/shard_map/ppermute | solution.py:87
  108.2 13.7 %collective-permute-start.19 = (bf16[8,7168]{1,0:T(8,128)(2,1)S(1)}, bf16[8,7168]{1,0:T(8,128)(2,1)S(1)}, u32[]{:S(2)}, u32[]{:S(2)}) collective-permute-start(bf16[8,7168]{1,0:T(8,128)(2,1)S(1)} %get-tuple-element.20), channel_id=1, source_target_pairs={{0,12},{4,16},{8,20},{12,24},{16,28},{20,0},{24,4},{28,8},{1,13},{... | collective-permute-start | bytes 344072 | tf_op jit(solution)/shard_map/ppermute | solution.py:87
  110.6 11.3 %collective-permute-start.18 = (bf16[8,7168]{1,0:T(8,128)(2,1)S(1)}, bf16[8,7168]{1,0:T(8,128)(2,1)S(1)}, u32[]{:S(2)}, u32[]{:S(2)}) collective-permute-start(bf16[8,7168]{1,0:T(8,128)(2,1)S(1)} %get-tuple-element.17), channel_id=1, source_target_pairs={{0,16},{4,20},{8,24},{12,28},{16,0},{20,4},{24,8},{28,12},{1,17},{... | collective-permute-start | bytes 344072 | tf_op jit(solution)/shard_map/ppermute | solution.py:87
  116.1 10.4 %collective-permute-start.9 = (bf16[8,7168]{1,0:T(8,128)(2,1)S(1)}, bf16[8,7168]{1,0:T(8,128)(2,1)S(1)}, u32[]{:S(2)}, u32[]{:S(2)}) collective-permute-start(bf16[8,7168]{1,0:T(8,128)(2,1)S(1)} %get-tuple-element.15), channel_id=1, source_target_pairs={{0,20},{4,24},{8,28},{12,0},{16,4},{20,8},{24,12},{28,16},{1,21},{... | collective-permute-start | bytes 344072 | tf_op jit(solution)/shard_map/ppermute | solution.py:87
  119.5 7.2 %collective-permute-start.8 = (bf16[8,7168]{1,0:T(8,128)(2,1)S(1)}, bf16[8,7168]{1,0:T(8,128)(2,1)S(1)}, u32[]{:S(2)}, u32[]{:S(2)}) collective-permute-start(bf16[8,7168]{1,0:T(8,128)(2,1)S(1)} %get-tuple-element.16), channel_id=1, source_target_pairs={{0,24},{4,28},{8,0},{12,4},{16,8},{20,12},{24,16},{28,20},{1,25},{... | collective-permute-start | bytes 344072 | tf_op jit(solution)/shard_map/ppermute | solution.py:87
  120.9 5.8 %collective-permute-start.7 = (bf16[8,7168]{1,0:T(8,128)(2,1)S(1)}, bf16[8,7168]{1,0:T(8,128)(2,1)S(1)}, u32[]{:S(2)}, u32[]{:S(2)}) collective-permute-start(bf16[8,7168]{1,0:T(8,128)(2,1)S(1)} %get-tuple-element.14), channel_id=1, source_target_pairs={{0,28},{4,0},{8,4},{12,8},{16,12},{20,16},{24,20},{28,24},{1,29},{... | collective-permute-start | bytes 344072 | tf_op jit(solution)/shard_map/ppermute | solution.py:87
  (4 other events, 7.1 us)
Sparse Core Ops, SparseCore 0:
  35.1 20.4 reduce-scatter.1

commit v9 on v8

--- a/solution.py
+++ b/solution.py
@@ -123,10 +123,27 @@
         cache_latent,
         preferred_element_type=jnp.float32,
     )
-    row_top = jnp.max(lax.all_gather(block_max, "exp", axis=0), axis=0)
+    me_exp = lax.axis_index("exp")
+    row_top = block_max
+    bit = 1
+    while bit < n_exp:
+        row_top = jnp.maximum(
+            row_top, lax.ppermute(row_top, "exp", [(i, i ^ bit) for i in range(n_exp)])
+        )
+        bit *= 2
     factor = jnp.exp(block_max - row_top)
-    packed = jnp.concatenate([block_out * factor[:, :, None], (block_sum * factor)[:, :, None]], axis=2)
-    reduced = lax.psum_scatter(packed, "exp", scatter_dimension=1, tiled=True)
+    reduced = jnp.concatenate([block_out * factor[:, :, None], (block_sum * factor)[:, :, None]], axis=2)
+    rows_n, heads_n, width = reduced.shape
+    bit = 1
+    while bit < n_exp:
+        outer = n_exp // (2 * bit)
+        view = reduced.reshape(rows_n, outer, 2, -1, width)
+        mine = (me_exp // bit) % 2
+        keep = lax.dynamic_index_in_dim(view, mine, axis=2, keepdims=False)
+        sent = lax.dynamic_index_in_dim(view, 1 - mine, axis=2, keepdims=False)
+        got = lax.ppermute(sent, "exp", [(i, i ^ bit) for i in range(n_exp)])
+        reduced = (keep + got).reshape(rows_n, -1, width)
+        bit *= 2
     numerator, denominator = reduced[:, :, :-1], reduced[:, :, -1]
     attn_out = (numerator / denominator[:, :, None]).astype(jnp.bfloat16)
     moe_out = routed_experts(tokens, route_ids, route_gates, w_gate, w_up, w_down, attn_out)

time: 136 us -> 126 us (0.926)
  between operations: 14.3 us -> 0.96 us
  starting transfers between devices: 28.7 us -> 34.4 us
  other arithmetic: 17.1 us -> 11.7 us
  blocking collectives: 5.07 us -> 0 us
  local copies, waits for them, and re-layouts: 8.86 us -> 13.4 us
  waiting for transfers between devices: 40.3 us -> 44.8 us
    ppermute x0 -> x4, waiting for transfers between devices: none -> 13.6 us  [the longest x2 10.9 us: per_device(): got = lax.ppermute(sent, 'exp', [(i, i ^ bit) for i in range(n_exp)])]
    reduce_scatter x1 -> x0, waiting for transfers between devices: 8.09 us -> none  [per_device(): reduced = lax.psum_scatter(packed, 'exp', scatter_dimension=1, tiled=True)]
    another operation x5, other arithmetic: 9.08 us -> 3.97 us  [bit_gather(): return jnp.stack([x, other])]
    all_gather x1 -> x0, blocking collectives: 5.07 us -> none  [per_device(): row_top = jnp.max(lax.all_gather(block_max, 'exp', axis=0), axis=0)]
    ppermute x4, waiting for transfers between devices: 15.2 us -> 11.1 us  [bit_reduce(): lax.ppermute(sent, axis, [(i, i ^ bit) for i in range(n)]).astype(x.dtype)]
    slice x2, local copies, waits for them, and re-layouts: 4.56 us -> 8.53 us  [bit_reduce(): sent = x[1] if wire is None else x[1].astype(wire)]
    ppermute x0 -> x4, starting transfers between devices: none -> 2.15 us  [the longest x2 1.56 us: per_device(): lax.ppermute(row_top, 'exp', [(i, i ^ bit) for i in range(n_exp)])]
    ppermute x7, waiting for transfers between devices: 1.6 us -> 3.36 us  [routed_experts(): lax.ppermute(tokens, 'attn', [(s, (s + k) % n_attn) for s in range(n_attn)])]
  transfers between devices with their start and end apart: 23 -> 26, of which waited for: 9 -> 10; matrix products, arithmetic and copies ran while one was open for 28% -> 32% of each run, Pallas kernels for 0% -> 0%
where the time goes in v9:
time: 126 us; the launch traced here: 125 us
  waiting for transfers between devices  44.8 us (36%)
  starting transfers between devices  34.4 us (27%)
  matrix products  20.1 us (16%)
  local copies, waits for them, and re-layouts  13.4 us (11%)
  other arithmetic  11.7 us (9%)
    dot_general x2, matrix products, expert_part(): return jnp.dot(hidden, down_slice, preferred_element_type=jnp.float32)  15.3 us
    ppermute x7, starting transfers between devices, routed_experts(): lax.ppermute(expert_rows[kk], 'attn', [(s, (s - k) % n_attn) for s in ran...  13.6 us
    ppermute x7, starting transfers between devices, routed_experts(): lax.ppermute(tokens, 'attn', [(s, (s + k) % n_attn) for s in range(n_attn)])  12.5 us
    ppermute x4, waiting for transfers between devices, bit_reduce(): lax.ppermute(sent, axis, [(i, i ^ bit) for i in range(n)]).astype(x.dtype)  11.1 us
    ppermute x2, waiting for transfers between devices, per_device(): got = lax.ppermute(sent, 'exp', [(i, i ^ bit) for i in range(n_exp)])  10.9 us
    ppermute x4, waiting for transfers between devices, bit_gather(): other = lax.ppermute(x, axis, [(i, i ^ bit) for i in range(n)])  10.4 us
    slice x2, local copies, waits for them, and re-layouts, bit_reduce(): sent = x[1] if wire is None else x[1].astype(wire)  8.53 us
    ppermute x7, waiting for transfers between devices, routed_experts(): lax.ppermute(expert_rows[kk], 'attn', [(s, (s - k) % n_attn) for s in ran...  6.37 us
  transfers between devices with their start and end apart: 26, of which 10 were waited for; matrix products, arithmetic and copies ran while one was open for 32% of the time, Pallas kernels for 0%

profile of v9, /device:TPU:0, one launch (start us, length us, event | category | flops | bytes accessed | tf_op | source)
XLA Modules:
  0.0 125.4 jit_solution(3977429194440373594)
XLA Ops:
  0.7 6.1 %collective-permute-start.17 = (bf16[8,7168]{1,0:T(8,128)(2,1)}, bf16[8,7168]{1,0:T(8,128)(2,1)}, u32[]{:S(2)}, u32[]{:S(2)}) collective-permute-start(bf16[8,7168]{1,0:T(8,128)(2,1)} %param.16), channel_id=1, source_target_pairs={{0,28},{4,0},{8,4},{12,8},{16,12},{20,16},{24,20},{28,24},{1,29},{... | collective-permute-start | bytes 344072 | tf_op jit(solution)/shard_map/ppermute | solution.py:60
  7.2 3.0 %collective-permute-start.14 = (bf16[8,7168]{1,0:T(8,128)(2,1)}, bf16[8,7168]{1,0:T(8,128)(2,1)}, u32[]{:S(2)}, u32[]{:S(2)}) collective-permute-start(bf16[8,7168]{1,0:T(8,128)(2,1)} %param.16), channel_id=1, source_target_pairs={{0,16},{4,20},{8,24},{12,28},{16,0},{20,4},{24,8},{28,12},{1,17},{... | collective-permute-start | bytes 344072 | tf_op jit(solution)/shard_map/ppermute | solution.py:60
  10.2 1.8 %fusion.63 = f32[2,128,1024]{2,1,0:T(8,128)S(1)} fusion(bf16[2,128,512]{2,1,0:T(8,128)(2,1)} %param.11, bf16[2,1024,512]{2,1,0:T(8,128)(2,1)S(1)} %copy-done), kind=kOutput, calls=%fused_computation.111 | convolution fusion | flops 268435456 | bytes 3407872 | tf_op jit(solution)/shard_map/rhl,rpl->rhp/dot_general | solution.py:109
  13.7 1.5 %collective-permute-start.1 = (f32[2,128]{1,0:T(2,128)S(1)}, f32[2,128]{1,0:T(2,128)S(1)}, u32[]{:S(2)}, u32[]{:S(2)}) collective-permute-start(f32[2,128]{1,0:T(2,128)S(1)} %max.6), channel_id=1, source_target_pairs={{0,2},{1,3},{2,0},{3,1},{4,6},{5,7},{6,4},{7,5},{8,10},{9,11},{10,... | collective-permute-start | bytes 3080 | tf_op jit(solution)/shard_map/ppermute | solution.py:131
  15.2 2.1 %collective-permute-done.1 = f32[2,128]{1,0:T(2,128)S(1)} collective-permute-done((f32[2,128]{1,0:T(2,128)S(1)}, f32[2,128]{1,0:T(2,128)S(1)}, u32[]{:S(2)}, u32[]{:S(2)}) %collective-permute-start.1) | collective-permute-done | bytes 1056 | tf_op jit(solution)/shard_map/ppermute | solution.py:131
  17.3 1.3 %broadcast_multiply_fusion = f32[2,128,512]{2,1,0:T(8,128)} fusion(f32[2,128]{1,0:T(2,128)S(1)} %get-tuple-element.5, bf16[2,1024,512]{2,1,0:T(8,128)(2,1)S(1)} %copy-done, f32[2,128,1024]{2,1,0:T(8,128)S(1)} %get-tuple-element.34, f32[2,128]{1,0:T(2,128)S(1)} %get-tuple-element.33, pred[2,1024]{1,0:T(4,128)(4,1)S(1)} %broadcast_compare_fusion), kind=kOutput, calls=%fused_computation.47 | convolution fusion | flops 269352960 | bytes 3674112 | tf_op jit(solution)/shard_map/rhp,rpl->rhl/dot_general | solution.py:120
  20.0 1.9 %collective-permute-start.5 = (bf16[8,7168]{1,0:T(8,128)(2,1)S(1)}, bf16[8,7168]{1,0:T(8,128)(2,1)S(1)}, u32[]{:S(2)}, u32[]{:S(2)}) collective-permute-start(bf16[8,7168]{1,0:T(8,128)(2,1)S(1)} %copy-done.7), channel_id=1, source_target_pairs={{0,8},{4,12},{8,16},{12,20},{16,24},{20,28},{24,0},{28,4},{1,9},{5... | collective-permute-start | bytes 344072 | tf_op jit(solution)/shard_map/ppermute | solution.py:60
  24.2 1.6 %collective-permute-start.18 = (bf16[4,8,7168]{2,1,0:T(8,128)(2,1)S(1)}, bf16[4,8,7168]{2,1,0:T(8,128)(2,1)S(1)}, u32[]{:S(2)}, u32[]{:S(2)}) collective-permute-start(bf16[4,8,7168]{2,1,0:T(8,128)(2,1)S(1)} %get-tuple-element.24), channel_id=1, source_target_pairs={{0,2},{1,3},{2,0},{3,1},{4,6},{5,7},{6,4},{7,5},{8,10},{9,11},{10,... | collective-permute-start | bytes 1376264 | tf_op jit(solution)/shard_map/ppermute | solution.py:34
  27.6 2.2 %collective-permute-done.4 = bf16[8,7168]{1,0:T(8,128)(2,1)S(1)} collective-permute-done((bf16[8,7168]{1,0:T(8,128)(2,1)S(1)}, bf16[8,7168]{1,0:T(8,128)(2,1)S(1)}, u32[]{:S(2)}, u32[]{:S(2)}) %collective-permute-start.4) | collective-permute-done | bytes 114720 | tf_op jit(solution)/shard_map/ppermute | solution.py:60
  29.8 10.9 %collective-permute-done.3 = f32[2,1,32,513]{3,2,0,1:T(8,128)S(1)} collective-permute-done((f32[2,1,32,513]{3,2,0,1:T(8,128)S(1)}, f32[2,1,32,513]{3,2,0,1:T(8,128)S(1)}, u32[]{:S(2)}, u32[]{:S(2)}) %collective-permute-start.3) | collective-permute-done | bytes 131360 | tf_op jit(solution)/shard_map/ppermute | solution.py:144
  41.5 1.5 %collective-permute-start.7 = (bf16[4,8,7168]{2,1,0:T(8,128)(2,1)S(1)}, bf16[4,8,7168]{2,1,0:T(8,128)(2,1)S(1)}, u32[]{:S(2)}, u32[]{:S(2)}) collective-permute-start(bf16[4,8,7168]{2,1,0:T(8,128)(2,1)S(1)} %pad_maximum_fusion.4), channel_id=1, source_target_pairs={{0,2},{1,3},{2,0},{3,1},{4,6},{5,7},{6,4},{7,5},{8,10},{9,11},{10,... | collective-permute-start | bytes 1376264 | tf_op jit(solution)/shard_map/ppermute | solution.py:34
  43.2 10.4 %collective-permute-done.7 = bf16[4,8,7168]{2,1,0:T(8,128)(2,1)S(1)} collective-permute-done((bf16[4,8,7168]{2,1,0:T(8,128)(2,1)S(1)}, bf16[4,8,7168]{2,1,0:T(8,128)(2,1)S(1)}, u32[]{:S(2)}, u32[]{:S(2)}) %collective-permute-start.7) | collective-permute-done | bytes 458784 | tf_op jit(solution)/shard_map/ppermute | solution.py:34
  54.9 1.3 %copy-done.1 = bf16[2,2,4,8,7168]{4,3,2,1,0:T(8,128)(2,1)} copy-done((bf16[2,2,4,8,7168]{4,3,2,1,0:T(8,128)(2,1)}, bf16[2,2,4,8,7168]{4,3,2,1,0:T(8,128)(2,1)S(1)}, u32[]{:S(2)}) %copy-start.1) | copy-done | bytes 1835032
  56.2 1.2 copy-done.3
  58.1 7.6 %fusion = f32[128,7168]{1,0:T(8,128)} fusion(bf16[1,256,7168]{2,1,0:T(8,128)(2,1)} %param.21, f32[128,256]{1,0:T(8,128)S(1)} %fusion.4, bf16[128,7168]{1,0:T(8,128)(2,1)} %bitcast.121, bf16[1,7168,256]{2,1,0:T(8,128)(2,1)} %param.19), kind=kOutput, calls=%fused_computation.1 | convolution fusion | flops 939720704 | bytes 12976128 | tf_op jit(solution)/shard_map/dot_general | solution.py:16
  65.7 4.2 %fusion.61 = (f32[64,7168]{1,0:T(8,128)}, f32[64,7168]{1,0:T(8,128)}) fusion(f32[128,7168]{1,0:T(8,128)} %fusion), kind=kLoop, calls=%fused_computation.109 | loop fusion | bytes 7340032 | tf_op jit(solution)/shard_map/slice | solution.py:39
  70.4 1.5 %pad_maximum_fusion = bf16[2,2,4,8,7168]{4,3,2,1,0:T(8,128)(2,1)S(1)} fusion(bf16[1,2,4,8,7168]{4,3,2,1,0:T(8,128)(2,1)} %bitcast.14, bf16[1,2,4,8,7168]{4,3,2,1,0:T(8,128)(2,1)S(1)} %get-tuple-element.10), kind=kLoop, calls=%fused_computation.13 | loop fusion | flops 917504 | bytes 3670016 | tf_op jit(solution)/shard_map/stack | solution.py:35
  71.9 1.2 copy-done.2
  73.8 7.6 %fusion.2 = f32[128,7168]{1,0:T(8,128)} fusion(bf16[1,256,7168]{2,1,0:T(8,128)(2,1)} %param.21, f32[128,256]{1,0:T(8,128)S(1)} %fusion.6, bf16[128,7168]{1,0:T(8,128)(2,1)} %bitcast.123, bf16[1,7168,256]{2,1,0:T(8,128)(2,1)} %param.19), kind=kOutput, calls=%fused_computation.3 | convolution fusion | flops 939720704 | bytes 12976128 | tf_op jit(solution)/shard_map/dot_general | solution.py:16
  81.4 4.3 %fusion.60 = (f32[64,7168]{1,0:T(8,128)}, f32[64,7168]{1,0:T(8,128)}) fusion(f32[128,7168]{1,0:T(8,128)} %fusion.2), kind=kLoop, calls=%fused_computation.108 | loop fusion | bytes 7340032 | tf_op jit(solution)/shard_map/slice | solution.py:39
  86.5 2.4 %add.161 = f32[2,4,8,7168]{3,2,1,0:T(8,128)S(1)} add(f32[2,4,8,7168]{3,2,1,0:T(8,128)} %bitcast.124, f32[2,4,8,7168]{3,2,1,0:T(8,128)} %collective-permute-done.20) | non-fusion elementwise | flops 458752 | bytes 5505024 | tf_op jit(solution)/shard_map/add | solution.py:40
  88.9 1.6 %collective-permute-start.21 = (bf16[4,8,7168]{2,1,0:T(8,128)(2,1)S(1)}, bf16[4,8,7168]{2,1,0:T(8,128)(2,1)S(1)}, u32[]{:S(2)}, u32[]{:S(2)}) collective-permute-start(bf16[4,8,7168]{2,1,0:T(8,128)(2,1)S(1)} %fusion.26), channel_id=1, source_target_pairs={{0,2},{1,3},{2,0},{3,1},{4,6},{5,7},{6,4},{7,5},{8,10},{9,11},{10,... | collective-permute-start | bytes 1376264 | tf_op jit(solution)/shard_map/ppermute | solution.py:40
  90.5 1.7 %add.155 = f32[2,4,8,7168]{3,2,1,0:T(8,128)S(1)} add(f32[2,4,8,7168]{3,2,1,0:T(8,128)S(1)} %bitcast.125, f32[2,4,8,7168]{3,2,1,0:T(8,128)} %collective-permute-done.9) | non-fusion elementwise | flops 458752 | bytes 5505024 | tf_op jit(solution)/shard_map/add | solution.py:40
  93.2 9.1 %collective-permute-done.21 = bf16[4,8,7168]{2,1,0:T(8,128)(2,1)S(1)} collective-permute-done((bf16[4,8,7168]{2,1,0:T(8,128)(2,1)S(1)}, bf16[4,8,7168]{2,1,0:T(8,128)(2,1)S(1)}, u32[]{:S(2)}, u32[]{:S(2)}) %collective-permute-start.21) | collective-permute-done | bytes 458784 | tf_op jit(solution)/shard_map/ppermute | solution.py:40
  102.4 2.0 %collective-permute-start.25 = (bf16[8,7168]{1,0:T(8,128)(2,1)S(1)}, bf16[8,7168]{1,0:T(8,128)(2,1)S(1)}, u32[]{:S(2)}, u32[]{:S(2)}) collective-permute-start(bf16[8,7168]{1,0:T(8,128)(2,1)S(1)} %get-tuple-element.20), channel_id=1, source_target_pairs={{0,4},{4,8},{8,12},{12,16},{16,20},{20,24},{24,28},{28,0},{1,5},{5... | collective-permute-start | bytes 344072 | tf_op jit(solution)/shard_map/ppermute | solution.py:87
  104.4 2.5 %collective-permute-start.24 = (bf16[8,7168]{1,0:T(8,128)(2,1)S(1)}, bf16[8,7168]{1,0:T(8,128)(2,1)S(1)}, u32[]{:S(2)}, u32[]{:S(2)}) collective-permute-start(bf16[8,7168]{1,0:T(8,128)(2,1)S(1)} %get-tuple-element.21), channel_id=1, source_target_pairs={{0,8},{4,12},{8,16},{12,20},{16,24},{20,28},{24,0},{28,4},{1,9},{5... | collective-permute-start | bytes 344072 | tf_op jit(solution)/shard_map/ppermute | solution.py:87
  106.8 2.9 %collective-permute-start.22 = (bf16[8,7168]{1,0:T(8,128)(2,1)S(1)}, bf16[8,7168]{1,0:T(8,128)(2,1)S(1)}, u32[]{:S(2)}, u32[]{:S(2)}) collective-permute-start(bf16[8,7168]{1,0:T(8,128)(2,1)S(1)} %get-tuple-element.19), channel_id=1, source_target_pairs={{0,16},{4,20},{8,24},{12,28},{16,0},{20,4},{24,8},{28,12},{1,17},{... | collective-permute-start | bytes 344072 | tf_op jit(solution)/shard_map/ppermute | solution.py:87
  109.7 2.0 %collective-permute-done.10 = bf16[4,8,7168]{2,1,0:T(8,128)(2,1)S(1)} collective-permute-done((bf16[4,8,7168]{2,1,0:T(8,128)(2,1)S(1)}, bf16[4,8,7168]{2,1,0:T(8,128)(2,1)S(1)}, u32[]{:S(2)}, u32[]{:S(2)}) %collective-permute-start.10) | collective-permute-done | bytes 458784 | tf_op jit(solution)/shard_map/ppermute | solution.py:40
  111.9 3.4 %collective-permute-start.13 = (bf16[8,7168]{1,0:T(8,128)(2,1)S(1)}, bf16[8,7168]{1,0:T(8,128)(2,1)S(1)}, u32[]{:S(2)}, u32[]{:S(2)}) collective-permute-start(bf16[8,7168]{1,0:T(8,128)(2,1)S(1)} %get-tuple-element.17), channel_id=1, source_target_pairs={{0,20},{4,24},{8,28},{12,0},{16,4},{20,8},{24,12},{28,16},{1,21},{... | collective-permute-start | bytes 344072 | tf_op jit(solution)/shard_map/ppermute | solution.py:87
  115.3 2.9 %collective-permute-start.12 = (bf16[8,7168]{1,0:T(8,128)(2,1)S(1)}, bf16[8,7168]{1,0:T(8,128)(2,1)S(1)}, u32[]{:S(2)}, u32[]{:S(2)}) collective-permute-start(bf16[8,7168]{1,0:T(8,128)(2,1)S(1)} %get-tuple-element.18), channel_id=1, source_target_pairs={{0,24},{4,28},{8,0},{12,4},{16,8},{20,12},{24,16},{28,20},{1,25},{... | collective-permute-start | bytes 344072 | tf_op jit(solution)/shard_map/ppermute | solution.py:87
  118.1 1.8 %collective-permute-done.23 = bf16[8,7168]{1,0:T(8,128)(2,1)S(1)} collective-permute-done((bf16[8,7168]{1,0:T(8,128)(2,1)S(1)}, bf16[8,7168]{1,0:T(8,128)(2,1)S(1)}, u32[]{:S(2)}, u32[]{:S(2)}) %collective-permute-start.23) | collective-permute-done | bytes 114720 | tf_op jit(solution)/shard_map/ppermute | solution.py:87
  120.0 4.5 %collective-permute-done.13 = bf16[8,7168]{1,0:T(8,128)(2,1)S(1)} collective-permute-done((bf16[8,7168]{1,0:T(8,128)(2,1)S(1)}, bf16[8,7168]{1,0:T(8,128)(2,1)S(1)}, u32[]{:S(2)}, u32[]{:S(2)}) %collective-permute-start.13) | collective-permute-done | bytes 114720 | tf_op jit(solution)/shard_map/ppermute | solution.py:87
  (89 shorter events, 14.6 us)
Async XLA Ops:
  0.6 9.5 %copy-start = (bf16[2,1024,512]{2,1,0:T(8,128)(2,1)S(1)}, bf16[2,1024,512]{2,1,0:T(8,128)(2,1)}, u32[]{:S(2)}) copy-start(bf16[2,1024,512]{2,1,0:T(8,128)(2,1)} %param.13) | copy-start | bytes 6291460
  0.6 11.3 %copy-start.11 = (s32[2]{0:T(128)S(1)}, s32[2]{0:T(128)}, u32[]{:S(2)}) copy-start(s32[2]{0:T(128)} %param.15) | copy-start | bytes 28
  0.7 11.4 %copy-start.6 = (bf16[2,64,1024]{2,1,0:T(8,128)(2,1)S(1)}, bf16[2,64,1024]{2,1,0:T(8,128)(2,1)}, u32[]{:S(2)}) copy-start(bf16[2,64,1024]{2,1,0:T(8,128)(2,1)} %param.14) | copy-start | bytes 786436
  0.7 19.3 %collective-permute-start.17 = (bf16[8,7168]{1,0:T(8,128)(2,1)}, bf16[8,7168]{1,0:T(8,128)(2,1)}, u32[]{:S(2)}, u32[]{:S(2)}) collective-permute-start(bf16[8,7168]{1,0:T(8,128)(2,1)} %param.16), channel_id=1, source_target_pairs={{0,28},{4,0},{8,4},{12,8},{16,12},{20,16},{24,20},{28,24},{1,29},{... | collective-permute-start | bytes 344072 | tf_op jit(solution)/shard_map/ppermute | solution.py:60
  6.7 15.2 %collective-permute-start.16 = (bf16[8,7168]{1,0:T(8,128)(2,1)}, bf16[8,7168]{1,0:T(8,128)(2,1)}, u32[]{:S(2)}, u32[]{:S(2)}) collective-permute-start(bf16[8,7168]{1,0:T(8,128)(2,1)} %param.16), channel_id=1, source_target_pairs={{0,24},{4,28},{8,0},{12,4},{16,8},{20,12},{24,16},{28,20},{1,25},{... | collective-permute-start | bytes 344072 | tf_op jit(solution)/shard_map/ppermute | solution.py:60
  7.2 15.8 %collective-permute-start.15 = (bf16[8,7168]{1,0:T(8,128)(2,1)}, bf16[8,7168]{1,0:T(8,128)(2,1)}, u32[]{:S(2)}, u32[]{:S(2)}) collective-permute-start(bf16[8,7168]{1,0:T(8,128)(2,1)} %param.16), channel_id=1, source_target_pairs={{0,20},{4,24},{8,28},{12,0},{16,4},{20,8},{24,12},{28,16},{1,21},{... | collective-permute-start | bytes 344072 | tf_op jit(solution)/shard_map/ppermute | solution.py:60
  7.2 15.9 %collective-permute-start.14 = (bf16[8,7168]{1,0:T(8,128)(2,1)}, bf16[8,7168]{1,0:T(8,128)(2,1)}, u32[]{:S(2)}, u32[]{:S(2)}) collective-permute-start(bf16[8,7168]{1,0:T(8,128)(2,1)} %param.16), channel_id=1, source_target_pairs={{0,16},{4,20},{8,24},{12,28},{16,0},{20,4},{24,8},{28,12},{1,17},{... | collective-permute-start | bytes 344072 | tf_op jit(solution)/shard_map/ppermute | solution.py:60
  12.0 5.3 %copy-start.7 = (bf16[8,7168]{1,0:T(8,128)(2,1)S(1)}, bf16[8,7168]{1,0:T(8,128)(2,1)}, u32[]{:S(2)}) copy-start(bf16[8,7168]{1,0:T(8,128)(2,1)} %param.16) | copy-start | bytes 344068
  12.5 1.2 collective-permute-start
  13.7 3.6 %collective-permute-start.1 = (f32[2,128]{1,0:T(2,128)S(1)}, f32[2,128]{1,0:T(2,128)S(1)}, u32[]{:S(2)}, u32[]{:S(2)}) collective-permute-start(f32[2,128]{1,0:T(2,128)S(1)} %max.6), channel_id=1, source_target_pairs={{0,2},{1,3},{2,0},{3,1},{4,6},{5,7},{6,4},{7,5},{8,10},{9,11},{10,... | collective-permute-start | bytes 3080 | tf_op jit(solution)/shard_map/ppermute | solution.py:131
  17.3 9.1 %collective-permute-start.6 = (bf16[8,7168]{1,0:T(8,128)(2,1)S(1)}, bf16[8,7168]{1,0:T(8,128)(2,1)S(1)}, u32[]{:S(2)}, u32[]{:S(2)}) collective-permute-start(bf16[8,7168]{1,0:T(8,128)(2,1)S(1)} %copy-done.7), channel_id=1, source_target_pairs={{0,12},{4,16},{8,20},{12,24},{16,28},{20,0},{24,4},{28,8},{1,13},{... | collective-permute-start | bytes 344072 | tf_op jit(solution)/shard_map/ppermute | solution.py:60
  20.0 7.6 %collective-permute-start.5 = (bf16[8,7168]{1,0:T(8,128)(2,1)S(1)}, bf16[8,7168]{1,0:T(8,128)(2,1)S(1)}, u32[]{:S(2)}, u32[]{:S(2)}) collective-permute-start(bf16[8,7168]{1,0:T(8,128)(2,1)S(1)} %copy-done.7), channel_id=1, source_target_pairs={{0,8},{4,12},{8,16},{12,20},{16,24},{20,28},{24,0},{28,4},{1,9},{5... | collective-permute-start | bytes 344072 | tf_op jit(solution)/shard_map/ppermute | solution.py:60
  21.9 7.9 %collective-permute-start.4 = (bf16[8,7168]{1,0:T(8,128)(2,1)S(1)}, bf16[8,7168]{1,0:T(8,128)(2,1)S(1)}, u32[]{:S(2)}, u32[]{:S(2)}) collective-permute-start(bf16[8,7168]{1,0:T(8,128)(2,1)S(1)} %copy-done.7), channel_id=1, source_target_pairs={{0,4},{4,8},{8,12},{12,16},{16,20},{20,24},{24,28},{28,0},{1,5},{5... | collective-permute-start | bytes 344072 | tf_op jit(solution)/shard_map/ppermute | solution.py:60
  23.0 2.7 %collective-permute-start.2 = (f32[2,2,32,513]{3,2,0,1:T(8,128)S(1)}, f32[2,2,32,513]{3,2,0,1:T(8,128)S(1)}, u32[]{:S(2)}, u32[]{:S(2)}) collective-permute-start(f32[2,2,32,513]{3,2,0,1:T(8,128)S(1)} %bitcast.131), channel_id=1, source_target_pairs={{0,1},{1,0},{2,3},{3,2},{4,5},{5,4},{6,7},{7,6},{8,9},{9,8},{10,11... | collective-permute-start | bytes 787976 | tf_op jit(solution)/shard_map/ppermute | solution.py:144
  24.2 18.8 %collective-permute-start.18 = (bf16[4,8,7168]{2,1,0:T(8,128)(2,1)S(1)}, bf16[4,8,7168]{2,1,0:T(8,128)(2,1)S(1)}, u32[]{:S(2)}, u32[]{:S(2)}) collective-permute-start(bf16[4,8,7168]{2,1,0:T(8,128)(2,1)S(1)} %get-tuple-element.24), channel_id=1, source_target_pairs={{0,2},{1,3},{2,0},{3,1},{4,6},{5,7},{6,4},{7,5},{8,10},{9,11},{10,... | collective-permute-start | bytes 1376264 | tf_op jit(solution)/shard_map/ppermute | solution.py:34
  25.8 14.9 %collective-permute-start.3 = (f32[2,1,32,513]{3,2,0,1:T(8,128)S(1)}, f32[2,1,32,513]{3,2,0,1:T(8,128)S(1)}, u32[]{:S(2)}, u32[]{:S(2)}) collective-permute-start(f32[2,1,32,513]{3,2,0,1:T(8,128)S(1)} %constant_dynamic-slice_fusion), channel_id=1, source_target_pairs={{0,2},{1,3},{2,0},{3,1},{4,6},{5,7},{6,4},{7,5},{8,10},{9,11},{10,... | collective-permute-start | bytes 393992 | tf_op jit(solution)/shard_map/ppermute | solution.py:144
  41.5 12.1 %collective-permute-start.7 = (bf16[4,8,7168]{2,1,0:T(8,128)(2,1)S(1)}, bf16[4,8,7168]{2,1,0:T(8,128)(2,1)S(1)}, u32[]{:S(2)}, u32[]{:S(2)}) collective-permute-start(bf16[4,8,7168]{2,1,0:T(8,128)(2,1)S(1)} %pad_maximum_fusion.4), channel_id=1, source_target_pairs={{0,2},{1,3},{2,0},{3,1},{4,6},{5,7},{6,4},{7,5},{8,10},{9,11},{10,... | collective-permute-start | bytes 1376264 | tf_op jit(solution)/shard_map/ppermute | solution.py:34
  43.1 11.6 %collective-permute-start.19 = (bf16[2,4,8,7168]{3,2,1,0:T(8,128)(2,1)S(1)}, bf16[2,4,8,7168]{3,2,1,0:T(8,128)(2,1)S(1)}, u32[]{:S(2)}, u32[]{:S(2)}) collective-permute-start(bf16[2,4,8,7168]{3,2,1,0:T(8,128)(2,1)S(1)} %get-tuple-element.13), channel_id=1, source_target_pairs={{0,1},{1,0},{2,3},{3,2},{4,5},{5,4},{6,7},{7,6},{8,9},{9,8},{10,11... | collective-permute-start | bytes 2752520 | tf_op jit(solution)/shard_map/ppermute | solution.py:34
  54.7 15.7 %collective-permute-start.8 = (bf16[2,4,8,7168]{3,2,1,0:T(8,128)(2,1)}, bf16[2,4,8,7168]{3,2,1,0:T(8,128)(2,1)}, u32[]{:S(2)}, u32[]{:S(2)}) collective-permute-start(bf16[2,4,8,7168]{3,2,1,0:T(8,128)(2,1)} %get-tuple-element.11), channel_id=1, source_target_pairs={{0,1},{1,0},{2,3},{3,2},{4,5},{5,4},{6,7},{7,6},{8,9},{9,8},{10,11... | collective-permute-start | bytes 2752520 | tf_op jit(solution)/shard_map/ppermute | solution.py:34
  69.9 16.6 %collective-permute-start.20 = (f32[2,4,8,7168]{3,2,1,0:T(8,128)}, f32[2,4,8,7168]{3,2,1,0:T(8,128)}, u32[]{:S(2)}, u32[]{:S(2)}) collective-permute-start(f32[2,4,8,7168]{3,2,1,0:T(8,128)} %bitcast.41), channel_id=1, source_target_pairs={{0,1},{1,0},{2,3},{3,2},{4,5},{5,4},{6,7},{7,6},{8,9},{9,8},{10,11... | collective-permute-start | bytes 5505032 | tf_op jit(solution)/shard_map/ppermute | solution.py:40
  70.4 2.7 %copy-start.4 = (bf16[1,7168,256]{2,1,0:T(8,128)(2,1)S(1)}, bf16[1,7168,256]{2,1,0:T(8,128)(2,1)}, u32[]{:S(2)}) copy-start(bf16[1,7168,256]{2,1,0:T(8,128)(2,1)} %param.20) | copy-start | bytes 11010052
  85.7 4.7 %collective-permute-start.9 = (f32[2,4,8,7168]{3,2,1,0:T(8,128)}, f32[2,4,8,7168]{3,2,1,0:T(8,128)}, u32[]{:S(2)}, u32[]{:S(2)}) collective-permute-start(f32[2,4,8,7168]{3,2,1,0:T(8,128)} %bitcast.20), channel_id=1, source_target_pairs={{0,1},{1,0},{2,3},{3,2},{4,5},{5,4},{6,7},{7,6},{8,9},{9,8},{10,11... | collective-permute-start | bytes 5505032 | tf_op jit(solution)/shard_map/ppermute | solution.py:40
  86.5 4.0 %copy-start.5 = (f32[64,7168]{1,0:T(8,128)S(1)}, f32[64,7168]{1,0:T(8,128)}, u32[]{:S(2)}) copy-start(f32[64,7168]{1,0:T(8,128)} %get-tuple-element.7) | copy-start | bytes 5505028
  88.9 13.4 %collective-permute-start.21 = (bf16[4,8,7168]{2,1,0:T(8,128)(2,1)S(1)}, bf16[4,8,7168]{2,1,0:T(8,128)(2,1)S(1)}, u32[]{:S(2)}, u32[]{:S(2)}) collective-permute-start(bf16[4,8,7168]{2,1,0:T(8,128)(2,1)S(1)} %fusion.26), channel_id=1, source_target_pairs={{0,2},{1,3},{2,0},{3,1},{4,6},{5,7},{6,4},{7,5},{8,10},{9,11},{10,... | collective-permute-start | bytes 1376264 | tf_op jit(solution)/shard_map/ppermute | solution.py:40
  92.3 19.5 %collective-permute-start.10 = (bf16[4,8,7168]{2,1,0:T(8,128)(2,1)S(1)}, bf16[4,8,7168]{2,1,0:T(8,128)(2,1)S(1)}, u32[]{:S(2)}, u32[]{:S(2)}) collective-permute-start(bf16[4,8,7168]{2,1,0:T(8,128)(2,1)S(1)} %fusion.25), channel_id=1, source_target_pairs={{0,2},{1,3},{2,0},{3,1},{4,6},{5,7},{6,4},{7,5},{8,10},{9,11},{10,... | collective-permute-start | bytes 1376264 | tf_op jit(solution)/shard_map/ppermute | solution.py:40
  102.4 12.9 %collective-permute-start.25 = (bf16[8,7168]{1,0:T(8,128)(2,1)S(1)}, bf16[8,7168]{1,0:T(8,128)(2,1)S(1)}, u32[]{:S(2)}, u32[]{:S(2)}) collective-permute-start(bf16[8,7168]{1,0:T(8,128)(2,1)S(1)} %get-tuple-element.20), channel_id=1, source_target_pairs={{0,4},{4,8},{8,12},{12,16},{16,20},{20,24},{24,28},{28,0},{1,5},{5... | collective-permute-start | bytes 344072 | tf_op jit(solution)/shard_map/ppermute | solution.py:87
  104.4 13.7 %collective-permute-start.24 = (bf16[8,7168]{1,0:T(8,128)(2,1)S(1)}, bf16[8,7168]{1,0:T(8,128)(2,1)S(1)}, u32[]{:S(2)}, u32[]{:S(2)}) collective-permute-start(bf16[8,7168]{1,0:T(8,128)(2,1)S(1)} %get-tuple-element.21), channel_id=1, source_target_pairs={{0,8},{4,12},{8,16},{12,20},{16,24},{20,28},{24,0},{28,4},{1,9},{5... | collective-permute-start | bytes 344072 | tf_op jit(solution)/shard_map/ppermute | solution.py:87
  106.8 13.1 %collective-permute-start.23 = (bf16[8,7168]{1,0:T(8,128)(2,1)S(1)}, bf16[8,7168]{1,0:T(8,128)(2,1)S(1)}, u32[]{:S(2)}, u32[]{:S(2)}) collective-permute-start(bf16[8,7168]{1,0:T(8,128)(2,1)S(1)} %get-tuple-element.22), channel_id=1, source_target_pairs={{0,12},{4,16},{8,20},{12,24},{16,28},{20,0},{24,4},{28,8},{1,13},{... | collective-permute-start | bytes 344072 | tf_op jit(solution)/shard_map/ppermute | solution.py:87
  106.8 13.1 %collective-permute-start.22 = (bf16[8,7168]{1,0:T(8,128)(2,1)S(1)}, bf16[8,7168]{1,0:T(8,128)(2,1)S(1)}, u32[]{:S(2)}, u32[]{:S(2)}) collective-permute-start(bf16[8,7168]{1,0:T(8,128)(2,1)S(1)} %get-tuple-element.19), channel_id=1, source_target_pairs={{0,16},{4,20},{8,24},{12,28},{16,0},{20,4},{24,8},{28,12},{1,17},{... | collective-permute-start | bytes 344072 | tf_op jit(solution)/shard_map/ppermute | solution.py:87
  111.9 12.6 %collective-permute-start.13 = (bf16[8,7168]{1,0:T(8,128)(2,1)S(1)}, bf16[8,7168]{1,0:T(8,128)(2,1)S(1)}, u32[]{:S(2)}, u32[]{:S(2)}) collective-permute-start(bf16[8,7168]{1,0:T(8,128)(2,1)S(1)} %get-tuple-element.17), channel_id=1, source_target_pairs={{0,20},{4,24},{8,28},{12,0},{16,4},{20,8},{24,12},{28,16},{1,21},{... | collective-permute-start | bytes 344072 | tf_op jit(solution)/shard_map/ppermute | solution.py:87
  115.3 9.2 %collective-permute-start.12 = (bf16[8,7168]{1,0:T(8,128)(2,1)S(1)}, bf16[8,7168]{1,0:T(8,128)(2,1)S(1)}, u32[]{:S(2)}, u32[]{:S(2)}) collective-permute-start(bf16[8,7168]{1,0:T(8,128)(2,1)S(1)} %get-tuple-element.18), channel_id=1, source_target_pairs={{0,24},{4,28},{8,0},{12,4},{16,8},{20,12},{24,16},{28,20},{1,25},{... | collective-permute-start | bytes 344072 | tf_op jit(solution)/shard_map/ppermute | solution.py:87
  118.1 6.4 %collective-permute-start.11 = (bf16[8,7168]{1,0:T(8,128)(2,1)S(1)}, bf16[8,7168]{1,0:T(8,128)(2,1)S(1)}, u32[]{:S(2)}, u32[]{:S(2)}) collective-permute-start(bf16[8,7168]{1,0:T(8,128)(2,1)S(1)} %get-tuple-element.16), channel_id=1, source_target_pairs={{0,28},{4,0},{8,4},{12,8},{16,12},{20,16},{24,20},{28,24},{1,29},{... | collective-permute-start | bytes 344072 | tf_op jit(solution)/shard_map/ppermute | solution.py:87
  (6 other events, 9.1 us)

commit v10 on v9

--- a/solution.py
+++ b/solution.py
@@ -71,14 +71,22 @@
     result = jnp.zeros((tok_count, model_width), jnp.float32)
     for i in range(n_local):
         chosen = jnp.take(wmat, owners * n_local + i, axis=1)
+        halved = [None] * n_chunks
         for c in range(n_chunks):
             block = blocks[c]
             part = expert_part(block.reshape(-1, model_width), w_gate[i], w_up[i], w_down[i])
             part = part.reshape(block.shape[:-1] + (model_width,))
-            for bit in reversed(bits):
-                wire = jnp.bfloat16 if bit == bits[0] else None
-                part = bit_reduce(part, "exp", bit, n_exp, wire)
-            expert_rows = part.astype(jnp.bfloat16)
+            if c > 0:
+                halved[c - 1], part = lax.optimization_barrier((halved[c - 1], part))
+            for bit in reversed(bits[1:]):
+                part = bit_reduce(part, "exp", bit, n_exp)
+            if c + 1 < n_chunks:
+                part, blocks[c + 1] = lax.optimization_barrier((part, blocks[c + 1]))
+            if bits:
+                part = bit_reduce(part, "exp", bits[0], n_exp, jnp.bfloat16)
+            halved[c] = part
+        for c in range(n_chunks):
+            expert_rows = halved[c].astype(jnp.bfloat16)
             for kk in range(per_chunk):
                 k = c * per_chunk + kk
                 if k == 0:

time: 126 us -> 135 us (1.071)
  waiting for transfers between devices: 44.8 us -> 65 us
  matrix products: 20.1 us -> 13.7 us
  other arithmetic: 11.7 us -> 8.54 us
  local copies, waits for them, and re-layouts: 13.4 us -> 11.8 us
    ppermute x7, waiting for transfers between devices: 3.36 us -> 15.5 us  [routed_experts(): lax.ppermute(tokens, 'attn', [(s, (s + k) % n_attn) for s in range(n_attn)])]
    ppermute x2, waiting for transfers between devices: 10.9 us -> 0.01 us  [per_device(): got = lax.ppermute(sent, 'exp', [(i, i ^ bit) for i in range(n_exp)])]
    ppermute x4, waiting for transfers between devices: 11.1 us -> 19.7 us  [bit_reduce(): lax.ppermute(sent, axis, [(i, i ^ bit) for i in range(n)]).astype(x.dtype)]
    ppermute x7, waiting for transfers between devices: 6.37 us -> 13.6 us  [routed_experts(): lax.ppermute(expert_rows[kk], 'attn', [(s, (s - k) % n_attn) for s in ran...]
    dot_general x2, matrix products: 15.3 us -> 8.27 us  [expert_part(): return jnp.dot(hidden, down_slice, preferred_element_type=jnp.float32)]
    slice x2 -> x1, local copies, waits for them, and re-layouts: 8.53 us -> 2.31 us  [bit_reduce(): sent = x[1] if wire is None else x[1].astype(wire)]
    ppermute x4, waiting for transfers between devices: 10.4 us -> 14.2 us  [bit_gather(): other = lax.ppermute(x, axis, [(i, i ^ bit) for i in range(n)])]
    unnamed x24, local copies, waits for them, and re-layouts: 3.77 us -> 6.97 us
  transfers between devices with their start and end apart: 26 -> 26, of which waited for: 10 -> 13; matrix products, arithmetic and copies ran while one was open for 32% -> 11% of each run, Pallas kernels for 0% -> 0%
where the time goes in v10:
time: 135 us; the launch traced here: 134 us
  waiting for transfers between devices  65 us (48%)
  starting transfers between devices  34.1 us (25%)
  matrix products  13.7 us (10%)
  local copies, waits for them, and re-layouts  11.8 us (9%)
  other arithmetic  8.54 us (6%)
    ppermute x4, waiting for transfers between devices, bit_reduce(): lax.ppermute(sent, axis, [(i, i ^ bit) for i in range(n)]).astype(x.dtype)  19.7 us
    ppermute x7, waiting for transfers between devices, routed_experts(): lax.ppermute(tokens, 'attn', [(s, (s + k) % n_attn) for s in range(n_attn)])  15.5 us
    ppermute x4, waiting for transfers between devices, bit_gather(): other = lax.ppermute(x, axis, [(i, i ^ bit) for i in range(n)])  14.2 us
    ppermute x7, waiting for transfers between devices, routed_experts(): lax.ppermute(expert_rows[kk], 'attn', [(s, (s - k) % n_attn) for s in ran...  13.6 us
    ppermute x7, starting transfers between devices, routed_experts(): lax.ppermute(expert_rows[kk], 'attn', [(s, (s - k) % n_attn) for s in ran...  12.5 us
    ppermute x7, starting transfers between devices, routed_experts(): lax.ppermute(tokens, 'attn', [(s, (s + k) % n_attn) for s in range(n_attn)])  11.6 us
    dot_general x2, matrix products, expert_part(): return jnp.dot(hidden, down_slice, preferred_element_type=jnp.float32)  8.27 us
    unnamed x24, local copies, waits for them, and re-layouts  6.97 us
  transfers between devices with their start and end apart: 26, of which 13 were waited for; matrix products, arithmetic and copies ran while one was open for 11% of the time, Pallas kernels for 0%

profile of v10, /device:TPU:0, one launch (start us, length us, event | category | flops | bytes accessed | tf_op | source)
XLA Modules:
  0.0 134.2 jit_solution(13082964737426885906)
XLA Ops:
  2.2 1.7 %fusion.60 = f32[2,128,1024]{2,1,0:T(8,128)S(1)} fusion(bf16[2,128,512]{2,1,0:T(8,128)(2,1)} %param.11, bf16[2,1024,512]{2,1,0:T(8,128)(2,1)S(1)} %copy-done), kind=kOutput, calls=%fused_computation.109 | convolution fusion | flops 268435456 | bytes 3407872 | tf_op jit(solution)/shard_map/rhl,rpl->rhp/dot_general | solution.py:117
  5.8 2.8 %collective-permute-start.1 = (f32[2,128]{1,0:T(2,128)S(1)}, f32[2,128]{1,0:T(2,128)S(1)}, u32[]{:S(2)}, u32[]{:S(2)}) collective-permute-start(f32[2,128]{1,0:T(2,128)S(1)} %max.6), channel_id=1, source_target_pairs={{0,2},{1,3},{2,0},{3,1},{4,6},{5,7},{6,4},{7,5},{8,10},{9,11},{10,... | collective-permute-start | bytes 3080 | tf_op jit(solution)/shard_map/ppermute | solution.py:139
  8.6 1.5 %collective-permute-done.1 = f32[2,128]{1,0:T(2,128)S(1)} collective-permute-done((f32[2,128]{1,0:T(2,128)S(1)}, f32[2,128]{1,0:T(2,128)S(1)}, u32[]{:S(2)}, u32[]{:S(2)}) %collective-permute-start.1) | collective-permute-done | bytes 1056 | tf_op jit(solution)/shard_map/ppermute | solution.py:139
  10.2 1.4 %broadcast_multiply_fusion = f32[2,128,512]{2,1,0:T(8,128)} fusion(f32[2,128]{1,0:T(2,128)S(1)} %get-tuple-element.13, bf16[2,1024,512]{2,1,0:T(8,128)(2,1)S(1)} %copy-done, f32[2,128,1024]{2,1,0:T(8,128)S(1)} %get-tuple-element.40, f32[2,128]{1,0:T(2,128)S(1)} %get-tuple-element.39, pred[2,1024]{1,0:T(4,128)(4,1)S(1)} %broadcast_compare_fusion), kind=kOutput, calls=%fused_computation.49 | convolution fusion | flops 269352960 | bytes 3674112 | tf_op jit(solution)/shard_map/rhp,rpl->rhl/dot_general | solution.py:128
  12.9 3.1 %collective-permute-start.6 = (bf16[8,7168]{1,0:T(8,128)(2,1)S(1)}, bf16[8,7168]{1,0:T(8,128)(2,1)S(1)}, u32[]{:S(2)}, u32[]{:S(2)}) collective-permute-start(bf16[8,7168]{1,0:T(8,128)(2,1)S(1)} %copy-done.8), channel_id=1, source_target_pairs={{0,12},{4,16},{8,20},{12,24},{16,28},{20,0},{24,4},{28,8},{1,13},{... | collective-permute-start | bytes 344072 | tf_op jit(solution)/shard_map/ppermute | solution.py:60
  16.1 1.5 %collective-permute-start.4 = (bf16[8,7168]{1,0:T(8,128)(2,1)S(1)}, bf16[8,7168]{1,0:T(8,128)(2,1)S(1)}, u32[]{:S(2)}, u32[]{:S(2)}) collective-permute-start(bf16[8,7168]{1,0:T(8,128)(2,1)S(1)} %copy-done.8), channel_id=1, source_target_pairs={{0,4},{4,8},{8,12},{12,16},{16,20},{20,24},{24,28},{28,0},{1,5},{5... | collective-permute-start | bytes 344072 | tf_op jit(solution)/shard_map/ppermute | solution.py:60
  17.6 1.6 %collective-permute-start.5 = (bf16[8,7168]{1,0:T(8,128)(2,1)S(1)}, bf16[8,7168]{1,0:T(8,128)(2,1)S(1)}, u32[]{:S(2)}, u32[]{:S(2)}) collective-permute-start(bf16[8,7168]{1,0:T(8,128)(2,1)S(1)} %copy-done.8), channel_id=1, source_target_pairs={{0,8},{4,12},{8,16},{12,20},{16,24},{20,28},{24,0},{28,4},{1,9},{5... | collective-permute-start | bytes 344072 | tf_op jit(solution)/shard_map/ppermute | solution.py:60
  19.2 1.6 %collective-permute-start.3 = (f32[2,1,32,513]{3,2,0,1:T(8,128)S(1)}, f32[2,1,32,513]{3,2,0,1:T(8,128)S(1)}, u32[]{:S(2)}, u32[]{:S(2)}) collective-permute-start(f32[2,1,32,513]{3,2,0,1:T(8,128)S(1)} %constant_dynamic-slice_fusion), channel_id=1, source_target_pairs={{0,2},{1,3},{2,0},{3,1},{4,6},{5,7},{6,4},{7,5},{8,10},{9,11},{10,... | collective-permute-start | bytes 393992 | tf_op jit(solution)/shard_map/ppermute | solution.py:152
  20.8 7.4 %collective-permute-done.6 = bf16[8,7168]{1,0:T(8,128)(2,1)S(1)} collective-permute-done((bf16[8,7168]{1,0:T(8,128)(2,1)S(1)}, bf16[8,7168]{1,0:T(8,128)(2,1)S(1)}, u32[]{:S(2)}, u32[]{:S(2)}) %collective-permute-start.6) | collective-permute-done | bytes 114720 | tf_op jit(solution)/shard_map/ppermute | solution.py:60
  29.1 1.5 %collective-permute-start.7 = (bf16[4,8,7168]{2,1,0:T(8,128)(2,1)S(1)}, bf16[4,8,7168]{2,1,0:T(8,128)(2,1)S(1)}, u32[]{:S(2)}, u32[]{:S(2)}) collective-permute-start(bf16[4,8,7168]{2,1,0:T(8,128)(2,1)S(1)} %pad_maximum_fusion.4), channel_id=1, source_target_pairs={{0,2},{1,3},{2,0},{3,1},{4,6},{5,7},{6,4},{7,5},{8,10},{9,11},{10,... | collective-permute-start | bytes 1376264 | tf_op jit(solution)/shard_map/ppermute | solution.py:34
  30.6 10.8 %collective-permute-done.7 = bf16[4,8,7168]{2,1,0:T(8,128)(2,1)S(1)} collective-permute-done((bf16[4,8,7168]{2,1,0:T(8,128)(2,1)S(1)}, bf16[4,8,7168]{2,1,0:T(8,128)(2,1)S(1)}, u32[]{:S(2)}, u32[]{:S(2)}) %collective-permute-start.7) | collective-permute-done | bytes 458784 | tf_op jit(solution)/shard_map/ppermute | solution.py:34
  42.0 2.5 %collective-permute-start.11 = (bf16[8,7168]{1,0:T(8,128)(2,1)S(1)}, bf16[8,7168]{1,0:T(8,128)(2,1)S(1)}, u32[]{:S(2)}, u32[]{:S(2)}) collective-permute-start(bf16[8,7168]{1,0:T(8,128)(2,1)S(1)} %copy-done.8), channel_id=1, source_target_pairs={{0,20},{4,24},{8,28},{12,0},{16,4},{20,8},{24,12},{28,16},{1,21},{... | collective-permute-start | bytes 344072 | tf_op jit(solution)/shard_map/ppermute | solution.py:60
  45.3 1.7 %collective-permute-start.13 = (bf16[8,7168]{1,0:T(8,128)(2,1)S(1)}, bf16[8,7168]{1,0:T(8,128)(2,1)S(1)}, u32[]{:S(2)}, u32[]{:S(2)}) collective-permute-start(bf16[8,7168]{1,0:T(8,128)(2,1)S(1)} %copy-done.8), channel_id=1, source_target_pairs={{0,28},{4,0},{8,4},{12,8},{16,12},{20,16},{24,20},{28,24},{1,29},{... | collective-permute-start | bytes 344072 | tf_op jit(solution)/shard_map/ppermute | solution.py:60
  47.0 4.1 %collective-permute-done.10 = bf16[8,7168]{1,0:T(8,128)(2,1)S(1)} collective-permute-done((bf16[8,7168]{1,0:T(8,128)(2,1)S(1)}, bf16[8,7168]{1,0:T(8,128)(2,1)S(1)}, u32[]{:S(2)}, u32[]{:S(2)}) %collective-permute-start.10) | collective-permute-done | bytes 114720 | tf_op jit(solution)/shard_map/ppermute | solution.py:60
  51.1 3.9 %collective-permute-done.12 = bf16[8,7168]{1,0:T(8,128)(2,1)S(1)} collective-permute-done((bf16[8,7168]{1,0:T(8,128)(2,1)S(1)}, bf16[8,7168]{1,0:T(8,128)(2,1)S(1)}, u32[]{:S(2)}, u32[]{:S(2)}) %collective-permute-start.12) | collective-permute-done | bytes 114720 | tf_op jit(solution)/shard_map/ppermute | solution.py:60
  55.1 1.3 %collective-permute-start.14 = (bf16[4,8,7168]{2,1,0:T(8,128)(2,1)S(1)}, bf16[4,8,7168]{2,1,0:T(8,128)(2,1)}, u32[]{:S(2)}, u32[]{:S(2)}) collective-permute-start(bf16[4,8,7168]{2,1,0:T(8,128)(2,1)S(1)} %get-tuple-element.30), channel_id=1, source_target_pairs={{0,2},{1,3},{2,0},{3,1},{4,6},{5,7},{6,4},{7,5},{8,10},{9,11},{10,... | collective-permute-start | bytes 1376264 | tf_op jit(solution)/shard_map/ppermute | solution.py:34
  56.6 1.3 copy-done.1
  59.8 7.6 %fusion.2 = f32[128,7168]{1,0:T(8,128)} fusion(bf16[1,256,7168]{2,1,0:T(8,128)(2,1)} %param.21, f32[128,256]{1,0:T(8,128)S(1)} %fusion.6, bf16[128,7168]{1,0:T(8,128)(2,1)} %bitcast.127, bf16[1,7168,256]{2,1,0:T(8,128)(2,1)} %param.19), kind=kOutput, calls=%fused_computation.3 | convolution fusion | flops 939720704 | bytes 12976128 | tf_op jit(solution)/shard_map/dot_general | solution.py:16
  67.4 2.3 %fusion.58 = (f32[64,7168]{1,0:T(8,128)S(1)}, f32[64,7168]{1,0:T(8,128)S(1)}) fusion(f32[128,7168]{1,0:T(8,128)} %fusion.2), kind=kLoop, calls=%fused_computation.107 | loop fusion | bytes 7340032 | tf_op jit(solution)/shard_map/slice | solution.py:39
  71.5 3.4 %collective-permute-done.15 = bf16[2,4,8,7168]{3,2,1,0:T(8,128)(2,1)S(1)} collective-permute-done((bf16[2,4,8,7168]{3,2,1,0:T(8,128)(2,1)S(1)}, bf16[2,4,8,7168]{3,2,1,0:T(8,128)(2,1)S(1)}, u32[]{:S(2)}, u32[]{:S(2)}) %collective-permute-start.15) | collective-permute-done | bytes 917536 | tf_op jit(solution)/shard_map/ppermute | solution.py:34
  75.3 1.8 %copy-done.3 = bf16[1,7168,256]{2,1,0:T(8,128)(2,1)S(1)} copy-done((bf16[1,7168,256]{2,1,0:T(8,128)(2,1)S(1)}, bf16[1,7168,256]{2,1,0:T(8,128)(2,1)}, u32[]{:S(2)}) %copy-start.3) | copy-done | bytes 3670040
  77.8 1.4 %copy-done.5 = bf16[1,7168,256]{2,1,0:T(8,128)(2,1)S(1)} copy-done((bf16[1,7168,256]{2,1,0:T(8,128)(2,1)S(1)}, bf16[1,7168,256]{2,1,0:T(8,128)(2,1)}, u32[]{:S(2)}) %copy-start.5) | copy-done | bytes 3670040
  81.9 10.6 %collective-permute-done.16 = bf16[4,8,7168]{2,1,0:T(8,128)(2,1)S(1)} collective-permute-done((bf16[4,8,7168]{2,1,0:T(8,128)(2,1)S(1)}, bf16[4,8,7168]{2,1,0:T(8,128)(2,1)S(1)}, u32[]{:S(2)}, u32[]{:S(2)}) %collective-permute-start.16) | collective-permute-done | bytes 458784 | tf_op jit(solution)/shard_map/ppermute | solution.py:40
  92.6 1.4 %slice_bitcast_fusion = f32[2,4,8,7168]{3,2,1,0:T(8,128)} fusion(f32[2,2,4,8,7168]{4,3,2,1,0:T(8,128)S(1)} %fusion), kind=kLoop, calls=%fused_computation.16 | loop fusion | bytes 3670016 | tf_op jit(solution)/shard_map/squeeze | solution.py:39
  94.9 3.3 %collective-permute-done.20 = f32[2,4,8,7168]{3,2,1,0:T(8,128)} collective-permute-done((f32[2,4,8,7168]{3,2,1,0:T(8,128)}, f32[2,4,8,7168]{3,2,1,0:T(8,128)}, u32[]{:S(2)}, u32[]{:S(2)}) %collective-permute-start.20) | collective-permute-done | bytes 1835040 | tf_op jit(solution)/shard_map/ppermute | solution.py:40
  98.1 2.2 %bitcast_add_fusion = f32[2,4,8,7168]{3,2,1,0:T(8,128)S(1)} fusion(f32[2,4,8,7168]{3,2,1,0:T(8,128)} %collective-permute-done.20, f32[2,2,4,8,7168]{4,3,2,1,0:T(8,128)} %copy-done.6), kind=kLoop, calls=%fused_computation.15 | loop fusion | flops 458752 | bytes 5505024 | tf_op jit(solution)/shard_map/add | solution.py:40
  101.3 5.1 %collective-permute-start.17 = (bf16[8,7168]{1,0:T(8,128)(2,1)S(1)}, bf16[8,7168]{1,0:T(8,128)(2,1)S(1)}, u32[]{:S(2)}, u32[]{:S(2)}) collective-permute-start(bf16[8,7168]{1,0:T(8,128)(2,1)S(1)} %get-tuple-element.22), channel_id=1, source_target_pairs={{0,28},{4,0},{8,4},{12,8},{16,12},{20,16},{24,20},{28,24},{1,29},{... | collective-permute-start | bytes 344072 | tf_op jit(solution)/shard_map/ppermute | solution.py:95
  107.2 5.8 %collective-permute-done.21 = bf16[4,8,7168]{2,1,0:T(8,128)(2,1)S(1)} collective-permute-done((bf16[4,8,7168]{2,1,0:T(8,128)(2,1)S(1)}, bf16[4,8,7168]{2,1,0:T(8,128)(2,1)S(1)}, u32[]{:S(2)}, u32[]{:S(2)}) %collective-permute-start.21) | collective-permute-done | bytes 458784 | tf_op jit(solution)/shard_map/ppermute | solution.py:40
  113.2 2.5 %collective-permute-start.22 = (bf16[8,7168]{1,0:T(8,128)(2,1)S(1)}, bf16[8,7168]{1,0:T(8,128)(2,1)S(1)}, u32[]{:S(2)}, u32[]{:S(2)}) collective-permute-start(bf16[8,7168]{1,0:T(8,128)(2,1)S(1)} %get-tuple-element.25), channel_id=1, source_target_pairs={{0,16},{4,20},{8,24},{12,28},{16,0},{20,4},{24,8},{28,12},{1,17},{... | collective-permute-start | bytes 344072 | tf_op jit(solution)/shard_map/ppermute | solution.py:95
  115.7 3.4 %collective-permute-start.23 = (bf16[8,7168]{1,0:T(8,128)(2,1)S(1)}, bf16[8,7168]{1,0:T(8,128)(2,1)S(1)}, u32[]{:S(2)}, u32[]{:S(2)}) collective-permute-start(bf16[8,7168]{1,0:T(8,128)(2,1)S(1)} %get-tuple-element.28), channel_id=1, source_target_pairs={{0,12},{4,16},{8,20},{12,24},{16,28},{20,0},{24,4},{28,8},{1,13},{... | collective-permute-start | bytes 344072 | tf_op jit(solution)/shard_map/ppermute | solution.py:95
  119.7 7.6 %collective-permute-done.22 = bf16[8,7168]{1,0:T(8,128)(2,1)S(1)} collective-permute-done((bf16[8,7168]{1,0:T(8,128)(2,1)S(1)}, bf16[8,7168]{1,0:T(8,128)(2,1)S(1)}, u32[]{:S(2)}, u32[]{:S(2)}) %collective-permute-start.22) | collective-permute-done | bytes 114720 | tf_op jit(solution)/shard_map/ppermute | solution.py:95
  127.3 6.0 %collective-permute-done.23 = bf16[8,7168]{1,0:T(8,128)(2,1)S(1)} collective-permute-done((bf16[8,7168]{1,0:T(8,128)(2,1)S(1)}, bf16[8,7168]{1,0:T(8,128)(2,1)S(1)}, u32[]{:S(2)}, u32[]{:S(2)}) %collective-permute-start.23) | collective-permute-done | bytes 114720 | tf_op jit(solution)/shard_map/ppermute | solution.py:95
  (90 shorter events, 19.0 us)
Async XLA Ops:
  0.6 3.4 %copy-start.9 = (bf16[2,64,128]{2,1,0:T(8,128)(2,1)S(1)}, bf16[2,64,128]{2,1,0:T(8,128)(2,1)}, u32[]{:S(2)}) copy-start(bf16[2,64,128]{2,1,0:T(8,128)(2,1)} %param.12) | copy-start | bytes 98308
  0.7 3.4 %copy-start.7 = (bf16[2,64,1024]{2,1,0:T(8,128)(2,1)S(1)}, bf16[2,64,1024]{2,1,0:T(8,128)(2,1)}, u32[]{:S(2)}) copy-start(bf16[2,64,1024]{2,1,0:T(8,128)(2,1)} %param.14) | copy-start | bytes 786436
  4.5 1.3 collective-permute-start
  5.8 4.4 %collective-permute-start.1 = (f32[2,128]{1,0:T(2,128)S(1)}, f32[2,128]{1,0:T(2,128)S(1)}, u32[]{:S(2)}, u32[]{:S(2)}) collective-permute-start(f32[2,128]{1,0:T(2,128)S(1)} %max.6), channel_id=1, source_target_pairs={{0,2},{1,3},{2,0},{3,1},{4,6},{5,7},{6,4},{7,5},{8,10},{9,11},{10,... | collective-permute-start | bytes 3080 | tf_op jit(solution)/shard_map/ppermute | solution.py:139
  12.8 6.3 %collective-permute-start.2 = (f32[2,2,32,513]{3,2,0,1:T(8,128)S(1)}, f32[2,2,32,513]{3,2,0,1:T(8,128)S(1)}, u32[]{:S(2)}, u32[]{:S(2)}) collective-permute-start(f32[2,2,32,513]{3,2,0,1:T(8,128)S(1)} %bitcast.135), channel_id=1, source_target_pairs={{0,1},{1,0},{2,3},{3,2},{4,5},{5,4},{6,7},{7,6},{8,9},{9,8},{10,11... | collective-permute-start | bytes 787976 | tf_op jit(solution)/shard_map/ppermute | solution.py:152
  12.9 15.3 %collective-permute-start.6 = (bf16[8,7168]{1,0:T(8,128)(2,1)S(1)}, bf16[8,7168]{1,0:T(8,128)(2,1)S(1)}, u32[]{:S(2)}, u32[]{:S(2)}) collective-permute-start(bf16[8,7168]{1,0:T(8,128)(2,1)S(1)} %copy-done.8), channel_id=1, source_target_pairs={{0,12},{4,16},{8,20},{12,24},{16,28},{20,0},{24,4},{28,8},{1,13},{... | collective-permute-start | bytes 344072 | tf_op jit(solution)/shard_map/ppermute | solution.py:60
  16.1 12.1 %collective-permute-start.4 = (bf16[8,7168]{1,0:T(8,128)(2,1)S(1)}, bf16[8,7168]{1,0:T(8,128)(2,1)S(1)}, u32[]{:S(2)}, u32[]{:S(2)}) collective-permute-start(bf16[8,7168]{1,0:T(8,128)(2,1)S(1)} %copy-done.8), channel_id=1, source_target_pairs={{0,4},{4,8},{8,12},{12,16},{16,20},{20,24},{24,28},{28,0},{1,5},{5... | collective-permute-start | bytes 344072 | tf_op jit(solution)/shard_map/ppermute | solution.py:60
  17.6 10.6 %collective-permute-start.5 = (bf16[8,7168]{1,0:T(8,128)(2,1)S(1)}, bf16[8,7168]{1,0:T(8,128)(2,1)S(1)}, u32[]{:S(2)}, u32[]{:S(2)}) collective-permute-start(bf16[8,7168]{1,0:T(8,128)(2,1)S(1)} %copy-done.8), channel_id=1, source_target_pairs={{0,8},{4,12},{8,16},{12,20},{16,24},{20,28},{24,0},{28,4},{1,9},{5... | collective-permute-start | bytes 344072 | tf_op jit(solution)/shard_map/ppermute | solution.py:60
  19.2 9.0 %collective-permute-start.3 = (f32[2,1,32,513]{3,2,0,1:T(8,128)S(1)}, f32[2,1,32,513]{3,2,0,1:T(8,128)S(1)}, u32[]{:S(2)}, u32[]{:S(2)}) collective-permute-start(f32[2,1,32,513]{3,2,0,1:T(8,128)S(1)} %constant_dynamic-slice_fusion), channel_id=1, source_target_pairs={{0,2},{1,3},{2,0},{3,1},{4,6},{5,7},{6,4},{7,5},{8,10},{9,11},{10,... | collective-permute-start | bytes 393992 | tf_op jit(solution)/shard_map/ppermute | solution.py:152
  29.1 12.3 %collective-permute-start.7 = (bf16[4,8,7168]{2,1,0:T(8,128)(2,1)S(1)}, bf16[4,8,7168]{2,1,0:T(8,128)(2,1)S(1)}, u32[]{:S(2)}, u32[]{:S(2)}) collective-permute-start(bf16[4,8,7168]{2,1,0:T(8,128)(2,1)S(1)} %pad_maximum_fusion.4), channel_id=1, source_target_pairs={{0,2},{1,3},{2,0},{3,1},{4,6},{5,7},{6,4},{7,5},{8,10},{9,11},{10,... | collective-permute-start | bytes 1376264 | tf_op jit(solution)/shard_map/ppermute | solution.py:34
  41.5 14.9 %collective-permute-start.8 = (bf16[2,4,8,7168]{3,2,1,0:T(8,128)(2,1)S(1)}, bf16[2,4,8,7168]{3,2,1,0:T(8,128)(2,1)S(1)}, u32[]{:S(2)}, u32[]{:S(2)}) collective-permute-start(bf16[2,4,8,7168]{3,2,1,0:T(8,128)(2,1)S(1)} %get-tuple-element.19), channel_id=1, source_target_pairs={{0,1},{1,0},{2,3},{3,2},{4,5},{5,4},{6,7},{7,6},{8,9},{9,8},{10,11... | collective-permute-start | bytes 2752520 | tf_op jit(solution)/shard_map/ppermute | solution.py:34
  41.6 9.4 %collective-permute-start.10 = (bf16[8,7168]{1,0:T(8,128)(2,1)S(1)}, bf16[8,7168]{1,0:T(8,128)(2,1)S(1)}, u32[]{:S(2)}, u32[]{:S(2)}) collective-permute-start(bf16[8,7168]{1,0:T(8,128)(2,1)S(1)} %copy-done.8), channel_id=1, source_target_pairs={{0,16},{4,20},{8,24},{12,28},{16,0},{20,4},{24,8},{28,12},{1,17},{... | collective-permute-start | bytes 344072 | tf_op jit(solution)/shard_map/ppermute | solution.py:60
  42.0 9.1 %collective-permute-start.11 = (bf16[8,7168]{1,0:T(8,128)(2,1)S(1)}, bf16[8,7168]{1,0:T(8,128)(2,1)S(1)}, u32[]{:S(2)}, u32[]{:S(2)}) collective-permute-start(bf16[8,7168]{1,0:T(8,128)(2,1)S(1)} %copy-done.8), channel_id=1, source_target_pairs={{0,20},{4,24},{8,28},{12,0},{16,4},{20,8},{24,12},{28,16},{1,21},{... | collective-permute-start | bytes 344072 | tf_op jit(solution)/shard_map/ppermute | solution.py:60
  44.6 10.4 %collective-permute-start.12 = (bf16[8,7168]{1,0:T(8,128)(2,1)S(1)}, bf16[8,7168]{1,0:T(8,128)(2,1)S(1)}, u32[]{:S(2)}, u32[]{:S(2)}) collective-permute-start(bf16[8,7168]{1,0:T(8,128)(2,1)S(1)} %copy-done.8), channel_id=1, source_target_pairs={{0,24},{4,28},{8,0},{12,4},{16,8},{20,12},{24,16},{28,20},{1,25},{... | collective-permute-start | bytes 344072 | tf_op jit(solution)/shard_map/ppermute | solution.py:60
  45.3 9.7 %collective-permute-start.13 = (bf16[8,7168]{1,0:T(8,128)(2,1)S(1)}, bf16[8,7168]{1,0:T(8,128)(2,1)S(1)}, u32[]{:S(2)}, u32[]{:S(2)}) collective-permute-start(bf16[8,7168]{1,0:T(8,128)(2,1)S(1)} %copy-done.8), channel_id=1, source_target_pairs={{0,28},{4,0},{8,4},{12,8},{16,12},{20,16},{24,20},{28,24},{1,29},{... | collective-permute-start | bytes 344072 | tf_op jit(solution)/shard_map/ppermute | solution.py:60
  55.1 14.7 %collective-permute-start.14 = (bf16[4,8,7168]{2,1,0:T(8,128)(2,1)S(1)}, bf16[4,8,7168]{2,1,0:T(8,128)(2,1)}, u32[]{:S(2)}, u32[]{:S(2)}) collective-permute-start(bf16[4,8,7168]{2,1,0:T(8,128)(2,1)S(1)} %get-tuple-element.30), channel_id=1, source_target_pairs={{0,2},{1,3},{2,0},{3,1},{4,6},{5,7},{6,4},{7,5},{8,10},{9,11},{10,... | collective-permute-start | bytes 1376264 | tf_op jit(solution)/shard_map/ppermute | solution.py:34
  56.4 2.7 %copy-start.4 = (bf16[1,7168,256]{2,1,0:T(8,128)(2,1)S(1)}, bf16[1,7168,256]{2,1,0:T(8,128)(2,1)}, u32[]{:S(2)}) copy-start(bf16[1,7168,256]{2,1,0:T(8,128)(2,1)} %param.20) | copy-start | bytes 11010052
  69.7 5.3 %collective-permute-start.9 = (f32[2,4,8,7168]{3,2,1,0:T(8,128)S(1)}, f32[2,4,8,7168]{3,2,1,0:T(8,128)S(1)}, u32[]{:S(2)}, u32[]{:S(2)}) collective-permute-start(f32[2,4,8,7168]{3,2,1,0:T(8,128)S(1)} %bitcast.130), channel_id=1, source_target_pairs={{0,1},{1,0},{2,3},{3,2},{4,5},{5,4},{6,7},{7,6},{8,9},{9,8},{10,11... | collective-permute-start | bytes 5505032 | tf_op jit(solution)/shard_map/ppermute | solution.py:40
  71.0 3.9 %collective-permute-start.15 = (bf16[2,4,8,7168]{3,2,1,0:T(8,128)(2,1)S(1)}, bf16[2,4,8,7168]{3,2,1,0:T(8,128)(2,1)S(1)}, u32[]{:S(2)}, u32[]{:S(2)}) collective-permute-start(bf16[2,4,8,7168]{3,2,1,0:T(8,128)(2,1)S(1)} %get-tuple-element.17), channel_id=1, source_target_pairs={{0,1},{1,0},{2,3},{3,2},{4,5},{5,4},{6,7},{7,6},{8,9},{9,8},{10,11... | collective-permute-start | bytes 2752520 | tf_op jit(solution)/shard_map/ppermute | solution.py:34
  75.1 2.0 %copy-start.3 = (bf16[1,7168,256]{2,1,0:T(8,128)(2,1)S(1)}, bf16[1,7168,256]{2,1,0:T(8,128)(2,1)}, u32[]{:S(2)}) copy-start(bf16[1,7168,256]{2,1,0:T(8,128)(2,1)} %param.19) | copy-start | bytes 11010052
  77.1 2.0 %copy-start.5 = (bf16[1,7168,256]{2,1,0:T(8,128)(2,1)S(1)}, bf16[1,7168,256]{2,1,0:T(8,128)(2,1)}, u32[]{:S(2)}) copy-start(bf16[1,7168,256]{2,1,0:T(8,128)(2,1)} %param.20) | copy-start | bytes 11010052
  79.9 12.6 %collective-permute-start.16 = (bf16[4,8,7168]{2,1,0:T(8,128)(2,1)S(1)}, bf16[4,8,7168]{2,1,0:T(8,128)(2,1)S(1)}, u32[]{:S(2)}, u32[]{:S(2)}) collective-permute-start(bf16[4,8,7168]{2,1,0:T(8,128)(2,1)S(1)} %fusion.29), channel_id=1, source_target_pairs={{0,2},{1,3},{2,0},{3,1},{4,6},{5,7},{6,4},{7,5},{8,10},{9,11},{10,... | collective-permute-start | bytes 1376264 | tf_op jit(solution)/shard_map/ppermute | solution.py:40
  81.9 12.2 %copy-start.6 = (f32[2,2,4,8,7168]{4,3,2,1,0:T(8,128)}, f32[2,2,4,8,7168]{4,3,2,1,0:T(8,128)S(1)}, u32[]{:S(2)}) copy-start(f32[2,2,4,8,7168]{4,3,2,1,0:T(8,128)S(1)} %fusion) | copy-start | bytes 11010052
  94.0 4.1 %collective-permute-start.20 = (f32[2,4,8,7168]{3,2,1,0:T(8,128)}, f32[2,4,8,7168]{3,2,1,0:T(8,128)}, u32[]{:S(2)}, u32[]{:S(2)}) collective-permute-start(f32[2,4,8,7168]{3,2,1,0:T(8,128)} %slice_bitcast_fusion), channel_id=1, source_target_pairs={{0,1},{1,0},{2,3},{3,2},{4,5},{5,4},{6,7},{7,6},{8,9},{9,8},{10,11... | collective-permute-start | bytes 5505032 | tf_op jit(solution)/shard_map/ppermute | solution.py:40
  100.4 12.6 %collective-permute-start.21 = (bf16[4,8,7168]{2,1,0:T(8,128)(2,1)S(1)}, bf16[4,8,7168]{2,1,0:T(8,128)(2,1)S(1)}, u32[]{:S(2)}, u32[]{:S(2)}) collective-permute-start(bf16[4,8,7168]{2,1,0:T(8,128)(2,1)S(1)} %fusion.30), channel_id=1, source_target_pairs={{0,2},{1,3},{2,0},{3,1},{4,6},{5,7},{6,4},{7,5},{8,10},{9,11},{10,... | collective-permute-start | bytes 1376264 | tf_op jit(solution)/shard_map/ppermute | solution.py:40
  101.3 17.9 %collective-permute-start.17 = (bf16[8,7168]{1,0:T(8,128)(2,1)S(1)}, bf16[8,7168]{1,0:T(8,128)(2,1)S(1)}, u32[]{:S(2)}, u32[]{:S(2)}) collective-permute-start(bf16[8,7168]{1,0:T(8,128)(2,1)S(1)} %get-tuple-element.22), channel_id=1, source_target_pairs={{0,28},{4,0},{8,4},{12,8},{16,12},{20,16},{24,20},{28,24},{1,29},{... | collective-permute-start | bytes 344072 | tf_op jit(solution)/shard_map/ppermute | solution.py:95
  106.4 12.9 %collective-permute-start.18 = (bf16[8,7168]{1,0:T(8,128)(2,1)S(1)}, bf16[8,7168]{1,0:T(8,128)(2,1)S(1)}, u32[]{:S(2)}, u32[]{:S(2)}) collective-permute-start(bf16[8,7168]{1,0:T(8,128)(2,1)S(1)} %get-tuple-element.23), channel_id=1, source_target_pairs={{0,24},{4,28},{8,0},{12,4},{16,8},{20,12},{24,16},{28,20},{1,25},{... | collective-permute-start | bytes 344072 | tf_op jit(solution)/shard_map/ppermute | solution.py:95
  106.4 13.3 %collective-permute-start.19 = (bf16[8,7168]{1,0:T(8,128)(2,1)S(1)}, bf16[8,7168]{1,0:T(8,128)(2,1)S(1)}, u32[]{:S(2)}, u32[]{:S(2)}) collective-permute-start(bf16[8,7168]{1,0:T(8,128)(2,1)S(1)} %get-tuple-element.24), channel_id=1, source_target_pairs={{0,20},{4,24},{8,28},{12,0},{16,4},{20,8},{24,12},{28,16},{1,21},{... | collective-permute-start | bytes 344072 | tf_op jit(solution)/shard_map/ppermute | solution.py:95
  113.2 14.1 %collective-permute-start.22 = (bf16[8,7168]{1,0:T(8,128)(2,1)S(1)}, bf16[8,7168]{1,0:T(8,128)(2,1)S(1)}, u32[]{:S(2)}, u32[]{:S(2)}) collective-permute-start(bf16[8,7168]{1,0:T(8,128)(2,1)S(1)} %get-tuple-element.25), channel_id=1, source_target_pairs={{0,16},{4,20},{8,24},{12,28},{16,0},{20,4},{24,8},{28,12},{1,17},{... | collective-permute-start | bytes 344072 | tf_op jit(solution)/shard_map/ppermute | solution.py:95
  115.7 17.5 %collective-permute-start.23 = (bf16[8,7168]{1,0:T(8,128)(2,1)S(1)}, bf16[8,7168]{1,0:T(8,128)(2,1)S(1)}, u32[]{:S(2)}, u32[]{:S(2)}) collective-permute-start(bf16[8,7168]{1,0:T(8,128)(2,1)S(1)} %get-tuple-element.28), channel_id=1, source_target_pairs={{0,12},{4,16},{8,20},{12,24},{16,28},{20,0},{24,4},{28,8},{1,13},{... | collective-permute-start | bytes 344072 | tf_op jit(solution)/shard_map/ppermute | solution.py:95
  119.1 14.2 %collective-permute-start.24 = (bf16[8,7168]{1,0:T(8,128)(2,1)S(1)}, bf16[8,7168]{1,0:T(8,128)(2,1)S(1)}, u32[]{:S(2)}, u32[]{:S(2)}) collective-permute-start(bf16[8,7168]{1,0:T(8,128)(2,1)S(1)} %get-tuple-element.27), channel_id=1, source_target_pairs={{0,8},{4,12},{8,16},{12,20},{16,24},{20,28},{24,0},{28,4},{1,9},{5... | collective-permute-start | bytes 344072 | tf_op jit(solution)/shard_map/ppermute | solution.py:95
  119.2 14.1 %collective-permute-start.25 = (bf16[8,7168]{1,0:T(8,128)(2,1)S(1)}, bf16[8,7168]{1,0:T(8,128)(2,1)S(1)}, u32[]{:S(2)}, u32[]{:S(2)}) collective-permute-start(bf16[8,7168]{1,0:T(8,128)(2,1)S(1)} %get-tuple-element.26), channel_id=1, source_target_pairs={{0,4},{4,8},{8,12},{12,16},{16,20},{20,24},{24,28},{28,0},{1,5},{5... | collective-permute-start | bytes 344072 | tf_op jit(solution)/shard_map/ppermute | solution.py:95
  (6 other events, 9.2 us)

commit v11 on v9

--- a/solution.py
+++ b/solution.py
@@ -61,8 +61,6 @@
     blocks = []
     for c in range(n_chunks):
         block = jnp.stack(pieces[c * per_chunk : (c + 1) * per_chunk])
-        if c == 0:
-            block, _ = lax.optimization_barrier((block, earlier))
         for bit in bits:
             block = bit_gather(block, "exp", bit, n_exp)
         blocks.append(block)

time: 126 us -> 119 us (0.944)
  waiting for transfers between devices: 44.8 us -> 38 us
    ppermute x2, waiting for transfers between devices: 10.9 us -> 0.01 us  [per_device(): got = lax.ppermute(sent, 'exp', [(i, i ^ bit) for i in range(n_exp)])]
    ppermute x4, waiting for transfers between devices: 10.4 us -> 13.3 us  [bit_gather(): other = lax.ppermute(x, axis, [(i, i ^ bit) for i in range(n)])]
    add x2, other arithmetic: 4.11 us -> 1.95 us  [bit_reduce(): x[0]]
    slice x2, local copies, waits for them, and re-layouts: 8.53 us -> 6.7 us  [bit_reduce(): sent = x[1] if wire is None else x[1].astype(wire)]
    ppermute x4, waiting for transfers between devices: 11.1 us -> 12.7 us  [bit_reduce(): lax.ppermute(sent, axis, [(i, i ^ bit) for i in range(n)]).astype(x.dtype)]
    another operation x5 -> x6, other arithmetic: 3.97 us -> 4.07 us  [bit_gather(): return jnp.stack([x, other])]
    unnamed x24 -> x28, local copies, waits for them, and re-layouts: 3.77 us -> 3.8 us
  transfers between devices with their start and end apart: 26 -> 26, of which waited for: 10 -> 9; matrix products, arithmetic and copies ran while one was open for 32% -> 33% of each run, Pallas kernels for 0% -> 0%
where the time goes in v11:
time: 119 us; the launch traced here: 118 us
  waiting for transfers between devices  38 us (32%)
  starting transfers between devices  35.4 us (30%)
  matrix products  20.1 us (17%)
  local copies, waits for them, and re-layouts  12.8 us (11%)
  other arithmetic  10.5 us (9%)
    dot_general x2, matrix products, expert_part(): return jnp.dot(hidden, down_slice, preferred_element_type=jnp.float32)  15.3 us
    ppermute x7, starting transfers between devices, routed_experts(): lax.ppermute(expert_rows[kk], 'attn', [(s, (s - k) % n_attn) for s in ran...  13.5 us
    ppermute x4, waiting for transfers between devices, bit_gather(): other = lax.ppermute(x, axis, [(i, i ^ bit) for i in range(n)])  13.3 us
    ppermute x4, waiting for transfers between devices, bit_reduce(): lax.ppermute(sent, axis, [(i, i ^ bit) for i in range(n)]).astype(x.dtype)  12.7 us
    ppermute x7, starting transfers between devices, routed_experts(): lax.ppermute(tokens, 'attn', [(s, (s + k) % n_attn) for s in range(n_attn)])  12.5 us
    slice x2, local copies, waits for them, and re-layouts, bit_reduce(): sent = x[1] if wire is None else x[1].astype(wire)  6.7 us
    ppermute x7, waiting for transfers between devices, routed_experts(): lax.ppermute(expert_rows[kk], 'attn', [(s, (s - k) % n_attn) for s in ran...  5.68 us
    ppermute x7, waiting for transfers between devices, routed_experts(): lax.ppermute(tokens, 'attn', [(s, (s + k) % n_attn) for s in range(n_attn)])  4.31 us
  transfers between devices with their start and end apart: 26, of which 9 were waited for; matrix products, arithmetic and copies ran while one was open for 33% of the time, Pallas kernels for 0%

profile of v11, /device:TPU:0, one launch (start us, length us, event | category | flops | bytes accessed | tf_op | source)
XLA Modules:
  0.0 117.8 jit_solution(2412399110274479630)
XLA Ops:
  0.7 6.1 %collective-permute-start.17 = (bf16[8,7168]{1,0:T(8,128)(2,1)}, bf16[8,7168]{1,0:T(8,128)(2,1)}, u32[]{:S(2)}, u32[]{:S(2)}) collective-permute-start(bf16[8,7168]{1,0:T(8,128)(2,1)} %param.16), channel_id=1, source_target_pairs={{0,28},{4,0},{8,4},{12,8},{16,12},{20,16},{24,20},{28,24},{1,29},{... | collective-permute-start | bytes 344072 | tf_op jit(solution)/shard_map/ppermute | solution.py:60
  7.2 3.0 %collective-permute-start.14 = (bf16[8,7168]{1,0:T(8,128)(2,1)}, bf16[8,7168]{1,0:T(8,128)(2,1)}, u32[]{:S(2)}, u32[]{:S(2)}) collective-permute-start(bf16[8,7168]{1,0:T(8,128)(2,1)} %param.16), channel_id=1, source_target_pairs={{0,16},{4,20},{8,24},{12,28},{16,0},{20,4},{24,8},{28,12},{1,17},{... | collective-permute-start | bytes 344072 | tf_op jit(solution)/shard_map/ppermute | solution.py:60
  10.2 1.8 %fusion.64 = f32[2,128,1024]{2,1,0:T(8,128)S(1)} fusion(bf16[2,128,512]{2,1,0:T(8,128)(2,1)} %param.11, bf16[2,1024,512]{2,1,0:T(8,128)(2,1)S(1)} %copy-done), kind=kOutput, calls=%fused_computation.112 | convolution fusion | flops 268435456 | bytes 3407872 | tf_op jit(solution)/shard_map/rhl,rpl->rhp/dot_general | solution.py:107
  14.3 1.5 %collective-permute-start.1 = (f32[2,128]{1,0:T(2,128)S(1)}, f32[2,128]{1,0:T(2,128)S(1)}, u32[]{:S(2)}, u32[]{:S(2)}) collective-permute-start(f32[2,128]{1,0:T(2,128)S(1)} %max.6), channel_id=1, source_target_pairs={{0,2},{1,3},{2,0},{3,1},{4,6},{5,7},{6,4},{7,5},{8,10},{9,11},{10,... | collective-permute-start | bytes 3080 | tf_op jit(solution)/shard_map/ppermute | solution.py:129
  15.9 2.1 %collective-permute-done.1 = f32[2,128]{1,0:T(2,128)S(1)} collective-permute-done((f32[2,128]{1,0:T(2,128)S(1)}, f32[2,128]{1,0:T(2,128)S(1)}, u32[]{:S(2)}, u32[]{:S(2)}) %collective-permute-start.1) | collective-permute-done | bytes 1056 | tf_op jit(solution)/shard_map/ppermute | solution.py:129
  18.0 1.4 %broadcast_multiply_fusion = f32[2,128,512]{2,1,0:T(8,128)} fusion(f32[2,128]{1,0:T(2,128)S(1)} %get-tuple-element.3, bf16[2,1024,512]{2,1,0:T(8,128)(2,1)S(1)} %copy-done, f32[2,128,1024]{2,1,0:T(8,128)S(1)} %get-tuple-element.34, f32[2,128]{1,0:T(2,128)S(1)} %get-tuple-element.33, pred[2,1024]{1,0:T(4,128)(4,1)S(1)} %broadcast_compare_fusion), kind=kOutput, calls=%fused_computation.47 | convolution fusion | flops 269352960 | bytes 3674112 | tf_op jit(solution)/shard_map/rhp,rpl->rhl/dot_general | solution.py:118
  20.7 1.9 %collective-permute-start.5 = (bf16[8,7168]{1,0:T(8,128)(2,1)S(1)}, bf16[8,7168]{1,0:T(8,128)(2,1)S(1)}, u32[]{:S(2)}, u32[]{:S(2)}) collective-permute-start(bf16[8,7168]{1,0:T(8,128)(2,1)S(1)} %copy-done.7), channel_id=1, source_target_pairs={{0,8},{4,12},{8,16},{12,20},{16,24},{20,28},{24,0},{28,4},{1,9},{5... | collective-permute-start | bytes 344072 | tf_op jit(solution)/shard_map/ppermute | solution.py:60
  24.8 1.6 %collective-permute-start.18 = (bf16[4,8,7168]{2,1,0:T(8,128)(2,1)S(1)}, bf16[4,8,7168]{2,1,0:T(8,128)(2,1)S(1)}, u32[]{:S(2)}, u32[]{:S(2)}) collective-permute-start(bf16[4,8,7168]{2,1,0:T(8,128)(2,1)S(1)} %get-tuple-element.24), channel_id=1, source_target_pairs={{0,2},{1,3},{2,0},{3,1},{4,6},{5,7},{6,4},{7,5},{8,10},{9,11},{10,... | collective-permute-start | bytes 1376264 | tf_op jit(solution)/shard_map/ppermute | solution.py:34
  26.4 1.8 %collective-permute-done.5 = bf16[8,7168]{1,0:T(8,128)(2,1)S(1)} collective-permute-done((bf16[8,7168]{1,0:T(8,128)(2,1)S(1)}, bf16[8,7168]{1,0:T(8,128)(2,1)S(1)}, u32[]{:S(2)}, u32[]{:S(2)}) %collective-permute-start.5) | collective-permute-done | bytes 114720 | tf_op jit(solution)/shard_map/ppermute | solution.py:60
  28.3 2.5 %collective-permute-done.4 = bf16[8,7168]{1,0:T(8,128)(2,1)S(1)} collective-permute-done((bf16[8,7168]{1,0:T(8,128)(2,1)S(1)}, bf16[8,7168]{1,0:T(8,128)(2,1)S(1)}, u32[]{:S(2)}, u32[]{:S(2)}) %collective-permute-start.4) | collective-permute-done | bytes 114720 | tf_op jit(solution)/shard_map/ppermute | solution.py:60
  30.8 1.6 %collective-permute-start.7 = (bf16[4,8,7168]{2,1,0:T(8,128)(2,1)S(1)}, bf16[4,8,7168]{2,1,0:T(8,128)(2,1)S(1)}, u32[]{:S(2)}, u32[]{:S(2)}) collective-permute-start(bf16[4,8,7168]{2,1,0:T(8,128)(2,1)S(1)} %get-tuple-element.18), channel_id=1, source_target_pairs={{0,2},{1,3},{2,0},{3,1},{4,6},{5,7},{6,4},{7,5},{8,10},{9,11},{10,... | collective-permute-start | bytes 1376264 | tf_op jit(solution)/shard_map/ppermute | solution.py:34
  32.4 5.8 %collective-permute-done.18 = bf16[4,8,7168]{2,1,0:T(8,128)(2,1)S(1)} collective-permute-done((bf16[4,8,7168]{2,1,0:T(8,128)(2,1)S(1)}, bf16[4,8,7168]{2,1,0:T(8,128)(2,1)S(1)}, u32[]{:S(2)}, u32[]{:S(2)}) %collective-permute-start.18) | collective-permute-done | bytes 458784 | tf_op jit(solution)/shard_map/ppermute | solution.py:34
  39.1 1.5 %collective-permute-start.3 = (f32[2,1,32,513]{3,2,0,1:T(8,128)}, f32[2,1,32,513]{3,2,0,1:T(8,128)}, u32[]{:S(2)}, u32[]{:S(2)}) collective-permute-start(f32[2,1,32,513]{3,2,0,1:T(8,128)} %constant_dynamic-slice_fusion), channel_id=1, source_target_pairs={{0,2},{1,3},{2,0},{3,1},{4,6},{5,7},{6,4},{7,5},{8,10},{9,11},{10,... | collective-permute-start | bytes 393992 | tf_op jit(solution)/shard_map/ppermute | solution.py:142
  40.6 7.5 %collective-permute-done.7 = bf16[4,8,7168]{2,1,0:T(8,128)(2,1)S(1)} collective-permute-done((bf16[4,8,7168]{2,1,0:T(8,128)(2,1)S(1)}, bf16[4,8,7168]{2,1,0:T(8,128)(2,1)S(1)}, u32[]{:S(2)}, u32[]{:S(2)}) %collective-permute-start.7) | collective-permute-done | bytes 458784 | tf_op jit(solution)/shard_map/ppermute | solution.py:34
  49.3 1.2 %copy-done.1 = bf16[2,2,4,8,7168]{4,3,2,1,0:T(8,128)(2,1)} copy-done((bf16[2,2,4,8,7168]{4,3,2,1,0:T(8,128)(2,1)}, bf16[2,2,4,8,7168]{4,3,2,1,0:T(8,128)(2,1)S(1)}, u32[]{:S(2)}) %copy-start.1) | copy-done | bytes 1835032
  50.6 1.3 %copy-done.3 = bf16[1,7168,256]{2,1,0:T(8,128)(2,1)S(1)} copy-done((bf16[1,7168,256]{2,1,0:T(8,128)(2,1)S(1)}, bf16[1,7168,256]{2,1,0:T(8,128)(2,1)}, u32[]{:S(2)}) %copy-start.3) | copy-done | bytes 3670040
  52.5 7.6 %fusion = f32[128,7168]{1,0:T(8,128)} fusion(bf16[1,256,7168]{2,1,0:T(8,128)(2,1)} %param.21, f32[128,256]{1,0:T(8,128)S(1)} %fusion.4, bf16[128,7168]{1,0:T(8,128)(2,1)} %bitcast.122, bf16[1,7168,256]{2,1,0:T(8,128)(2,1)} %param.19), kind=kOutput, calls=%fused_computation.1 | convolution fusion | flops 939720704 | bytes 12976128 | tf_op jit(solution)/shard_map/dot_general | solution.py:16
  60.1 4.2 %fusion.62 = (f32[64,7168]{1,0:T(8,128)}, f32[64,7168]{1,0:T(8,128)}) fusion(f32[128,7168]{1,0:T(8,128)} %fusion), kind=kLoop, calls=%fused_computation.110 | loop fusion | bytes 7340032 | tf_op jit(solution)/shard_map/slice | solution.py:39
  64.8 1.5 %pad_maximum_fusion = bf16[2,2,4,8,7168]{4,3,2,1,0:T(8,128)(2,1)S(1)} fusion(bf16[1,2,4,8,7168]{4,3,2,1,0:T(8,128)(2,1)} %bitcast.14, bf16[1,2,4,8,7168]{4,3,2,1,0:T(8,128)(2,1)S(1)} %get-tuple-element.8), kind=kLoop, calls=%fused_computation.13 | loop fusion | flops 917504 | bytes 3670016 | tf_op jit(solution)/shard_map/stack | solution.py:35
  66.3 1.2 %copy-done.2 = bf16[2,2,4,8,7168]{4,3,2,1,0:T(8,128)(2,1)} copy-done((bf16[2,2,4,8,7168]{4,3,2,1,0:T(8,128)(2,1)}, bf16[2,2,4,8,7168]{4,3,2,1,0:T(8,128)(2,1)S(1)}, u32[]{:S(2)}) %copy-start.2) | copy-done | bytes 1835032
  68.2 7.6 %fusion.2 = f32[128,7168]{1,0:T(8,128)} fusion(bf16[1,256,7168]{2,1,0:T(8,128)(2,1)} %param.21, f32[128,256]{1,0:T(8,128)S(1)} %fusion.6, bf16[128,7168]{1,0:T(8,128)(2,1)} %bitcast.124, bf16[1,7168,256]{2,1,0:T(8,128)(2,1)} %param.19), kind=kOutput, calls=%fused_computation.3 | convolution fusion | flops 939720704 | bytes 12976128 | tf_op jit(solution)/shard_map/dot_general | solution.py:16
  75.9 2.5 %fusion.61 = (f32[64,7168]{1,0:T(8,128)S(1)}, f32[64,7168]{1,0:T(8,128)S(1)}) fusion(f32[128,7168]{1,0:T(8,128)} %fusion.2), kind=kLoop, calls=%fused_computation.109 | loop fusion | bytes 7340032 | tf_op jit(solution)/shard_map/slice | solution.py:39
  79.5 1.8 %add.161 = f32[2,4,8,7168]{3,2,1,0:T(8,128)S(1)} add(f32[2,4,8,7168]{3,2,1,0:T(8,128)S(1)} %bitcast.125, f32[2,4,8,7168]{3,2,1,0:T(8,128)} %collective-permute-done.20) | non-fusion elementwise | flops 458752 | bytes 5505024 | tf_op jit(solution)/shard_map/add | solution.py:40
  81.3 1.6 %collective-permute-start.21 = (bf16[4,8,7168]{2,1,0:T(8,128)(2,1)S(1)}, bf16[4,8,7168]{2,1,0:T(8,128)(2,1)S(1)}, u32[]{:S(2)}, u32[]{:S(2)}) collective-permute-start(bf16[4,8,7168]{2,1,0:T(8,128)(2,1)S(1)} %fusion.26), channel_id=1, source_target_pairs={{0,2},{1,3},{2,0},{3,1},{4,6},{5,7},{6,4},{7,5},{8,10},{9,11},{10,... | collective-permute-start | bytes 1376264 | tf_op jit(solution)/shard_map/ppermute | solution.py:40
  84.0 10.7 %collective-permute-done.21 = bf16[4,8,7168]{2,1,0:T(8,128)(2,1)S(1)} collective-permute-done((bf16[4,8,7168]{2,1,0:T(8,128)(2,1)S(1)}, bf16[4,8,7168]{2,1,0:T(8,128)(2,1)S(1)}, u32[]{:S(2)}, u32[]{:S(2)}) %collective-permute-start.21) | collective-permute-done | bytes 458784 | tf_op jit(solution)/shard_map/ppermute | solution.py:40
  94.8 2.0 %collective-permute-start.25 = (bf16[8,7168]{1,0:T(8,128)(2,1)S(1)}, bf16[8,7168]{1,0:T(8,128)(2,1)S(1)}, u32[]{:S(2)}, u32[]{:S(2)}) collective-permute-start(bf16[8,7168]{1,0:T(8,128)(2,1)S(1)} %get-tuple-element.20), channel_id=1, source_target_pairs={{0,4},{4,8},{8,12},{12,16},{16,20},{20,24},{24,28},{28,0},{1,5},{5... | collective-permute-start | bytes 344072 | tf_op jit(solution)/shard_map/ppermute | solution.py:85
  96.8 2.5 %collective-permute-start.24 = (bf16[8,7168]{1,0:T(8,128)(2,1)S(1)}, bf16[8,7168]{1,0:T(8,128)(2,1)S(1)}, u32[]{:S(2)}, u32[]{:S(2)}) collective-permute-start(bf16[8,7168]{1,0:T(8,128)(2,1)S(1)} %get-tuple-element.21), channel_id=1, source_target_pairs={{0,8},{4,12},{8,16},{12,20},{16,24},{20,28},{24,0},{28,4},{1,9},{5... | collective-permute-start | bytes 344072 | tf_op jit(solution)/shard_map/ppermute | solution.py:85
  99.4 2.8 %collective-permute-start.22 = (bf16[8,7168]{1,0:T(8,128)(2,1)S(1)}, bf16[8,7168]{1,0:T(8,128)(2,1)S(1)}, u32[]{:S(2)}, u32[]{:S(2)}) collective-permute-start(bf16[8,7168]{1,0:T(8,128)(2,1)S(1)} %get-tuple-element.19), channel_id=1, source_target_pairs={{0,16},{4,20},{8,24},{12,28},{16,0},{20,4},{24,8},{28,12},{1,17},{... | collective-permute-start | bytes 344072 | tf_op jit(solution)/shard_map/ppermute | solution.py:85
  102.1 2.0 %collective-permute-done.10 = bf16[4,8,7168]{2,1,0:T(8,128)(2,1)S(1)} collective-permute-done((bf16[4,8,7168]{2,1,0:T(8,128)(2,1)S(1)}, bf16[4,8,7168]{2,1,0:T(8,128)(2,1)S(1)}, u32[]{:S(2)}, u32[]{:S(2)}) %collective-permute-start.10) | collective-permute-done | bytes 458784 | tf_op jit(solution)/shard_map/ppermute | solution.py:40
  104.3 3.4 %collective-permute-start.13 = (bf16[8,7168]{1,0:T(8,128)(2,1)S(1)}, bf16[8,7168]{1,0:T(8,128)(2,1)S(1)}, u32[]{:S(2)}, u32[]{:S(2)}) collective-permute-start(bf16[8,7168]{1,0:T(8,128)(2,1)S(1)} %get-tuple-element.15), channel_id=1, source_target_pairs={{0,20},{4,24},{8,28},{12,0},{16,4},{20,8},{24,12},{28,16},{1,21},{... | collective-permute-start | bytes 344072 | tf_op jit(solution)/shard_map/ppermute | solution.py:85
  107.7 2.8 %collective-permute-start.12 = (bf16[8,7168]{1,0:T(8,128)(2,1)S(1)}, bf16[8,7168]{1,0:T(8,128)(2,1)S(1)}, u32[]{:S(2)}, u32[]{:S(2)}) collective-permute-start(bf16[8,7168]{1,0:T(8,128)(2,1)S(1)} %get-tuple-element.16), channel_id=1, source_target_pairs={{0,24},{4,28},{8,0},{12,4},{16,8},{20,12},{24,16},{28,20},{1,25},{... | collective-permute-start | bytes 344072 | tf_op jit(solution)/shard_map/ppermute | solution.py:85
  112.4 4.5 %collective-permute-done.13 = bf16[8,7168]{1,0:T(8,128)(2,1)S(1)} collective-permute-done((bf16[8,7168]{1,0:T(8,128)(2,1)S(1)}, bf16[8,7168]{1,0:T(8,128)(2,1)S(1)}, u32[]{:S(2)}, u32[]{:S(2)}) %collective-permute-start.13) | collective-permute-done | bytes 114720 | tf_op jit(solution)/shard_map/ppermute | solution.py:85
  (93 shorter events, 15.9 us)
Async XLA Ops:
  0.6 9.5 %copy-start = (bf16[2,1024,512]{2,1,0:T(8,128)(2,1)S(1)}, bf16[2,1024,512]{2,1,0:T(8,128)(2,1)}, u32[]{:S(2)}) copy-start(bf16[2,1024,512]{2,1,0:T(8,128)(2,1)} %param.13) | copy-start | bytes 6291460
  0.6 11.3 %copy-start.13 = (s32[2]{0:T(128)S(1)}, s32[2]{0:T(128)}, u32[]{:S(2)}) copy-start(s32[2]{0:T(128)} %param.15) | copy-start | bytes 28
  0.7 11.4 %copy-start.6 = (bf16[2,64,1024]{2,1,0:T(8,128)(2,1)S(1)}, bf16[2,64,1024]{2,1,0:T(8,128)(2,1)}, u32[]{:S(2)}) copy-start(bf16[2,64,1024]{2,1,0:T(8,128)(2,1)} %param.14) | copy-start | bytes 786436
  0.7 20.0 %collective-permute-start.17 = (bf16[8,7168]{1,0:T(8,128)(2,1)}, bf16[8,7168]{1,0:T(8,128)(2,1)}, u32[]{:S(2)}, u32[]{:S(2)}) collective-permute-start(bf16[8,7168]{1,0:T(8,128)(2,1)} %param.16), channel_id=1, source_target_pairs={{0,28},{4,0},{8,4},{12,8},{16,12},{20,16},{24,20},{28,24},{1,29},{... | collective-permute-start | bytes 344072 | tf_op jit(solution)/shard_map/ppermute | solution.py:60
  6.7 15.8 %collective-permute-start.16 = (bf16[8,7168]{1,0:T(8,128)(2,1)}, bf16[8,7168]{1,0:T(8,128)(2,1)}, u32[]{:S(2)}, u32[]{:S(2)}) collective-permute-start(bf16[8,7168]{1,0:T(8,128)(2,1)} %param.16), channel_id=1, source_target_pairs={{0,24},{4,28},{8,0},{12,4},{16,8},{20,12},{24,16},{28,20},{1,25},{... | collective-permute-start | bytes 344072 | tf_op jit(solution)/shard_map/ppermute | solution.py:60
  7.2 16.5 %collective-permute-start.15 = (bf16[8,7168]{1,0:T(8,128)(2,1)}, bf16[8,7168]{1,0:T(8,128)(2,1)}, u32[]{:S(2)}, u32[]{:S(2)}) collective-permute-start(bf16[8,7168]{1,0:T(8,128)(2,1)} %param.16), channel_id=1, source_target_pairs={{0,20},{4,24},{8,28},{12,0},{16,4},{20,8},{24,12},{28,16},{1,21},{... | collective-permute-start | bytes 344072 | tf_op jit(solution)/shard_map/ppermute | solution.py:60
  7.2 16.5 %collective-permute-start.14 = (bf16[8,7168]{1,0:T(8,128)(2,1)}, bf16[8,7168]{1,0:T(8,128)(2,1)}, u32[]{:S(2)}, u32[]{:S(2)}) collective-permute-start(bf16[8,7168]{1,0:T(8,128)(2,1)} %param.16), channel_id=1, source_target_pairs={{0,16},{4,20},{8,24},{12,28},{16,0},{20,4},{24,8},{28,12},{1,17},{... | collective-permute-start | bytes 344072 | tf_op jit(solution)/shard_map/ppermute | solution.py:60
  12.0 6.0 %copy-start.7 = (bf16[8,7168]{1,0:T(8,128)(2,1)S(1)}, bf16[8,7168]{1,0:T(8,128)(2,1)}, u32[]{:S(2)}) copy-start(bf16[8,7168]{1,0:T(8,128)(2,1)} %param.16) | copy-start | bytes 344068
  12.5 1.8 %collective-permute-start = (f32[2,128]{1,0:T(2,128)S(1)}, f32[2,128]{1,0:T(2,128)S(1)}, u32[]{:S(2)}, u32[]{:S(2)}) collective-permute-start(f32[2,128]{1,0:T(2,128)S(1)} %get-tuple-element.33), channel_id=1, source_target_pairs={{0,1},{1,0},{2,3},{3,2},{4,5},{5,4},{6,7},{7,6},{8,9},{9,8},{10,11... | collective-permute-start | bytes 3080 | tf_op jit(solution)/shard_map/ppermute | solution.py:129
  14.3 3.6 %collective-permute-start.1 = (f32[2,128]{1,0:T(2,128)S(1)}, f32[2,128]{1,0:T(2,128)S(1)}, u32[]{:S(2)}, u32[]{:S(2)}) collective-permute-start(f32[2,128]{1,0:T(2,128)S(1)} %max.6), channel_id=1, source_target_pairs={{0,2},{1,3},{2,0},{3,1},{4,6},{5,7},{6,4},{7,5},{8,10},{9,11},{10,... | collective-permute-start | bytes 3080 | tf_op jit(solution)/shard_map/ppermute | solution.py:129
  17.9 8.5 %collective-permute-start.6 = (bf16[8,7168]{1,0:T(8,128)(2,1)S(1)}, bf16[8,7168]{1,0:T(8,128)(2,1)S(1)}, u32[]{:S(2)}, u32[]{:S(2)}) collective-permute-start(bf16[8,7168]{1,0:T(8,128)(2,1)S(1)} %copy-done.7), channel_id=1, source_target_pairs={{0,12},{4,16},{8,20},{12,24},{16,28},{20,0},{24,4},{28,8},{1,13},{... | collective-permute-start | bytes 344072 | tf_op jit(solution)/shard_map/ppermute | solution.py:60
  20.7 7.6 %collective-permute-start.5 = (bf16[8,7168]{1,0:T(8,128)(2,1)S(1)}, bf16[8,7168]{1,0:T(8,128)(2,1)S(1)}, u32[]{:S(2)}, u32[]{:S(2)}) collective-permute-start(bf16[8,7168]{1,0:T(8,128)(2,1)S(1)} %copy-done.7), channel_id=1, source_target_pairs={{0,8},{4,12},{8,16},{12,20},{16,24},{20,28},{24,0},{28,4},{1,9},{5... | collective-permute-start | bytes 344072 | tf_op jit(solution)/shard_map/ppermute | solution.py:60
  22.6 8.1 %collective-permute-start.4 = (bf16[8,7168]{1,0:T(8,128)(2,1)S(1)}, bf16[8,7168]{1,0:T(8,128)(2,1)S(1)}, u32[]{:S(2)}, u32[]{:S(2)}) collective-permute-start(bf16[8,7168]{1,0:T(8,128)(2,1)S(1)} %copy-done.7), channel_id=1, source_target_pairs={{0,4},{4,8},{8,12},{12,16},{16,20},{20,24},{24,28},{28,0},{1,5},{5... | collective-permute-start | bytes 344072 | tf_op jit(solution)/shard_map/ppermute | solution.py:60
  23.7 8.7 %collective-permute-start.2 = (f32[2,2,32,513]{3,2,0,1:T(8,128)S(1)}, f32[2,2,32,513]{3,2,0,1:T(8,128)S(1)}, u32[]{:S(2)}, u32[]{:S(2)}) collective-permute-start(f32[2,2,32,513]{3,2,0,1:T(8,128)S(1)} %bitcast.132), channel_id=1, source_target_pairs={{0,1},{1,0},{2,3},{3,2},{4,5},{5,4},{6,7},{7,6},{8,9},{9,8},{10,11... | collective-permute-start | bytes 787976 | tf_op jit(solution)/shard_map/ppermute | solution.py:142
  24.8 13.4 %collective-permute-start.18 = (bf16[4,8,7168]{2,1,0:T(8,128)(2,1)S(1)}, bf16[4,8,7168]{2,1,0:T(8,128)(2,1)S(1)}, u32[]{:S(2)}, u32[]{:S(2)}) collective-permute-start(bf16[4,8,7168]{2,1,0:T(8,128)(2,1)S(1)} %get-tuple-element.24), channel_id=1, source_target_pairs={{0,2},{1,3},{2,0},{3,1},{4,6},{5,7},{6,4},{7,5},{8,10},{9,11},{10,... | collective-permute-start | bytes 1376264 | tf_op jit(solution)/shard_map/ppermute | solution.py:34
  30.8 17.3 %collective-permute-start.7 = (bf16[4,8,7168]{2,1,0:T(8,128)(2,1)S(1)}, bf16[4,8,7168]{2,1,0:T(8,128)(2,1)S(1)}, u32[]{:S(2)}, u32[]{:S(2)}) collective-permute-start(bf16[4,8,7168]{2,1,0:T(8,128)(2,1)S(1)} %get-tuple-element.18), channel_id=1, source_target_pairs={{0,2},{1,3},{2,0},{3,1},{4,6},{5,7},{6,4},{7,5},{8,10},{9,11},{10,... | collective-permute-start | bytes 1376264 | tf_op jit(solution)/shard_map/ppermute | solution.py:34
  38.4 10.8 %collective-permute-start.19 = (bf16[2,4,8,7168]{3,2,1,0:T(8,128)(2,1)S(1)}, bf16[2,4,8,7168]{3,2,1,0:T(8,128)(2,1)S(1)}, u32[]{:S(2)}, u32[]{:S(2)}) collective-permute-start(bf16[2,4,8,7168]{3,2,1,0:T(8,128)(2,1)S(1)} %get-tuple-element.11), channel_id=1, source_target_pairs={{0,1},{1,0},{2,3},{3,2},{4,5},{5,4},{6,7},{7,6},{8,9},{9,8},{10,11... | collective-permute-start | bytes 2752520 | tf_op jit(solution)/shard_map/ppermute | solution.py:34
  39.1 39.3 %collective-permute-start.3 = (f32[2,1,32,513]{3,2,0,1:T(8,128)}, f32[2,1,32,513]{3,2,0,1:T(8,128)}, u32[]{:S(2)}, u32[]{:S(2)}) collective-permute-start(f32[2,1,32,513]{3,2,0,1:T(8,128)} %constant_dynamic-slice_fusion), channel_id=1, source_target_pairs={{0,2},{1,3},{2,0},{3,1},{4,6},{5,7},{6,4},{7,5},{8,10},{9,11},{10,... | collective-permute-start | bytes 393992 | tf_op jit(solution)/shard_map/ppermute | solution.py:142
  49.1 15.7 %collective-permute-start.8 = (bf16[2,4,8,7168]{3,2,1,0:T(8,128)(2,1)}, bf16[2,4,8,7168]{3,2,1,0:T(8,128)(2,1)}, u32[]{:S(2)}, u32[]{:S(2)}) collective-permute-start(bf16[2,4,8,7168]{3,2,1,0:T(8,128)(2,1)} %get-tuple-element.9), channel_id=1, source_target_pairs={{0,1},{1,0},{2,3},{3,2},{4,5},{5,4},{6,7},{7,6},{8,9},{9,8},{10,11... | collective-permute-start | bytes 2752520 | tf_op jit(solution)/shard_map/ppermute | solution.py:34
  64.3 15.2 %collective-permute-start.20 = (f32[2,4,8,7168]{3,2,1,0:T(8,128)}, f32[2,4,8,7168]{3,2,1,0:T(8,128)}, u32[]{:S(2)}, u32[]{:S(2)}) collective-permute-start(f32[2,4,8,7168]{3,2,1,0:T(8,128)} %bitcast.41), channel_id=1, source_target_pairs={{0,1},{1,0},{2,3},{3,2},{4,5},{5,4},{6,7},{7,6},{8,9},{9,8},{10,11... | collective-permute-start | bytes 5505032 | tf_op jit(solution)/shard_map/ppermute | solution.py:40
  78.4 4.5 %collective-permute-start.9 = (f32[2,4,8,7168]{3,2,1,0:T(8,128)S(1)}, f32[2,4,8,7168]{3,2,1,0:T(8,128)S(1)}, u32[]{:S(2)}, u32[]{:S(2)}) collective-permute-start(f32[2,4,8,7168]{3,2,1,0:T(8,128)S(1)} %bitcast.128), channel_id=1, source_target_pairs={{0,1},{1,0},{2,3},{3,2},{4,5},{5,4},{6,7},{7,6},{8,9},{9,8},{10,11... | collective-permute-start | bytes 5505032 | tf_op jit(solution)/shard_map/ppermute | solution.py:40
  81.3 13.4 %collective-permute-start.21 = (bf16[4,8,7168]{2,1,0:T(8,128)(2,1)S(1)}, bf16[4,8,7168]{2,1,0:T(8,128)(2,1)S(1)}, u32[]{:S(2)}, u32[]{:S(2)}) collective-permute-start(bf16[4,8,7168]{2,1,0:T(8,128)(2,1)S(1)} %fusion.26), channel_id=1, source_target_pairs={{0,2},{1,3},{2,0},{3,1},{4,6},{5,7},{6,4},{7,5},{8,10},{9,11},{10,... | collective-permute-start | bytes 1376264 | tf_op jit(solution)/shard_map/ppermute | solution.py:40
  83.1 21.0 %collective-permute-start.10 = (bf16[4,8,7168]{2,1,0:T(8,128)(2,1)S(1)}, bf16[4,8,7168]{2,1,0:T(8,128)(2,1)S(1)}, u32[]{:S(2)}, u32[]{:S(2)}) collective-permute-start(bf16[4,8,7168]{2,1,0:T(8,128)(2,1)S(1)} %fusion.25), channel_id=1, source_target_pairs={{0,2},{1,3},{2,0},{3,1},{4,6},{5,7},{6,4},{7,5},{8,10},{9,11},{10,... | collective-permute-start | bytes 1376264 | tf_op jit(solution)/shard_map/ppermute | solution.py:40
  94.8 22.1 %copy-start.9 = (f32[8]{0:T(128)S(1)}, f32[8]{0:T(128)}, u32[]{:S(2)}) copy-start(f32[8]{0:T(128)} %get-tuple-element.31) | copy-start | bytes 100
  94.8 22.1 %copy-start.10 = (f32[8]{0:T(128)S(1)}, f32[8]{0:T(128)}, u32[]{:S(2)}) copy-start(f32[8]{0:T(128)} %get-tuple-element.32) | copy-start | bytes 100
  94.8 12.8 %collective-permute-start.25 = (bf16[8,7168]{1,0:T(8,128)(2,1)S(1)}, bf16[8,7168]{1,0:T(8,128)(2,1)S(1)}, u32[]{:S(2)}, u32[]{:S(2)}) collective-permute-start(bf16[8,7168]{1,0:T(8,128)(2,1)S(1)} %get-tuple-element.20), channel_id=1, source_target_pairs={{0,4},{4,8},{8,12},{12,16},{16,20},{20,24},{24,28},{28,0},{1,5},{5... | collective-permute-start | bytes 344072 | tf_op jit(solution)/shard_map/ppermute | solution.py:85
  96.8 13.7 %collective-permute-start.24 = (bf16[8,7168]{1,0:T(8,128)(2,1)S(1)}, bf16[8,7168]{1,0:T(8,128)(2,1)S(1)}, u32[]{:S(2)}, u32[]{:S(2)}) collective-permute-start(bf16[8,7168]{1,0:T(8,128)(2,1)S(1)} %get-tuple-element.21), channel_id=1, source_target_pairs={{0,8},{4,12},{8,16},{12,20},{16,24},{20,28},{24,0},{28,4},{1,9},{5... | collective-permute-start | bytes 344072 | tf_op jit(solution)/shard_map/ppermute | solution.py:85
  99.3 13.1 %collective-permute-start.23 = (bf16[8,7168]{1,0:T(8,128)(2,1)S(1)}, bf16[8,7168]{1,0:T(8,128)(2,1)S(1)}, u32[]{:S(2)}, u32[]{:S(2)}) collective-permute-start(bf16[8,7168]{1,0:T(8,128)(2,1)S(1)} %get-tuple-element.22), channel_id=1, source_target_pairs={{0,12},{4,16},{8,20},{12,24},{16,28},{20,0},{24,4},{28,8},{1,13},{... | collective-permute-start | bytes 344072 | tf_op jit(solution)/shard_map/ppermute | solution.py:85
  99.4 13.0 %collective-permute-start.22 = (bf16[8,7168]{1,0:T(8,128)(2,1)S(1)}, bf16[8,7168]{1,0:T(8,128)(2,1)S(1)}, u32[]{:S(2)}, u32[]{:S(2)}) collective-permute-start(bf16[8,7168]{1,0:T(8,128)(2,1)S(1)} %get-tuple-element.19), channel_id=1, source_target_pairs={{0,16},{4,20},{8,24},{12,28},{16,0},{20,4},{24,8},{28,12},{1,17},{... | collective-permute-start | bytes 344072 | tf_op jit(solution)/shard_map/ppermute | solution.py:85
  104.3 12.6 %collective-permute-start.13 = (bf16[8,7168]{1,0:T(8,128)(2,1)S(1)}, bf16[8,7168]{1,0:T(8,128)(2,1)S(1)}, u32[]{:S(2)}, u32[]{:S(2)}) collective-permute-start(bf16[8,7168]{1,0:T(8,128)(2,1)S(1)} %get-tuple-element.15), channel_id=1, source_target_pairs={{0,20},{4,24},{8,28},{12,0},{16,4},{20,8},{24,12},{28,16},{1,21},{... | collective-permute-start | bytes 344072 | tf_op jit(solution)/shard_map/ppermute | solution.py:85
  107.7 9.2 %collective-permute-start.12 = (bf16[8,7168]{1,0:T(8,128)(2,1)S(1)}, bf16[8,7168]{1,0:T(8,128)(2,1)S(1)}, u32[]{:S(2)}, u32[]{:S(2)}) collective-permute-start(bf16[8,7168]{1,0:T(8,128)(2,1)S(1)} %get-tuple-element.16), channel_id=1, source_target_pairs={{0,24},{4,28},{8,0},{12,4},{16,8},{20,12},{24,16},{28,20},{1,25},{... | collective-permute-start | bytes 344072 | tf_op jit(solution)/shard_map/ppermute | solution.py:85
  110.5 6.4 %collective-permute-start.11 = (bf16[8,7168]{1,0:T(8,128)(2,1)S(1)}, bf16[8,7168]{1,0:T(8,128)(2,1)S(1)}, u32[]{:S(2)}, u32[]{:S(2)}) collective-permute-start(bf16[8,7168]{1,0:T(8,128)(2,1)S(1)} %get-tuple-element.14), channel_id=1, source_target_pairs={{0,28},{4,0},{8,4},{12,8},{16,12},{20,16},{24,20},{28,24},{1,29},{... | collective-permute-start | bytes 344072 | tf_op jit(solution)/shard_map/ppermute | solution.py:85
  (8 other events, 15.5 us)

commit v12 on v11

--- a/solution.py
+++ b/solution.py
@@ -53,14 +53,15 @@
         b //= 2
     hit = route_ids[:, :, None] == jnp.arange(n_experts, dtype=jnp.int32)[None, None, :]
     wmat = jnp.sum(jnp.where(hit, route_gates[:, :, None], 0.0), axis=1)
-    n_chunks = 2 if n_attn % 2 == 0 else 1
-    per_chunk = n_attn // n_chunks
+    n_chunks = min(3, n_attn)
+    step = -(-n_attn // n_chunks)
+    bounds = [min(c * step, n_attn) for c in range(n_chunks)] + [n_attn]
     pieces = [tokens]
     for k in range(1, n_attn):
         pieces.append(lax.ppermute(tokens, "attn", [(s, (s + k) % n_attn) for s in range(n_attn)]))
     blocks = []
     for c in range(n_chunks):
-        block = jnp.stack(pieces[c * per_chunk : (c + 1) * per_chunk])
+        block = jnp.stack(pieces[bounds[c] : bounds[c + 1]])
         for bit in bits:
             block = bit_gather(block, "exp", bit, n_exp)
         blocks.append(block)
@@ -77,8 +78,8 @@
                 wire = jnp.bfloat16 if bit == bits[0] else None
                 part = bit_reduce(part, "exp", bit, n_exp, wire)
             expert_rows = part.astype(jnp.bfloat16)
-            for kk in range(per_chunk):
-                k = c * per_chunk + kk
+            for kk in range(bounds[c + 1] - bounds[c]):
+                k = bounds[c] + kk
                 if k == 0:
                     back = expert_rows[kk]
                 else:

time: 119 us -> 137 us (1.15)
  waiting for transfers between devices: 38 us -> 47.3 us
  matrix products: 20.1 us -> 27.5 us
  other arithmetic: 10.5 us -> 14.9 us
  local copies, waits for them, and re-layouts: 12.8 us -> 10 us
    dot_general x2 -> x3, matrix products: 15.3 us -> 20.4 us  [expert_part(): return jnp.dot(hidden, down_slice, preferred_element_type=jnp.float32)]
    ppermute x4 -> x6, waiting for transfers between devices: 13.3 us -> 17.8 us  [bit_gather(): other = lax.ppermute(x, axis, [(i, i ^ bit) for i in range(n)])]
    ppermute x7, waiting for transfers between devices: 5.68 us -> 10.1 us  [routed_experts(): lax.ppermute(expert_rows[kk], 'attn', [(s, (s - k) % n_attn) for s in ran...]
    ppermute x7, waiting for transfers between devices: 4.31 us -> 0.02 us  [routed_experts(): lax.ppermute(tokens, 'attn', [(s, (s + k) % n_attn) for s in range(n_attn)])]
    another operation x6 -> x9, other arithmetic: 4.07 us -> 7.25 us  [bit_gather(): return jnp.stack([x, other])]
    ppermute x2, waiting for transfers between devices: 0.01 us -> 2.91 us  [per_device(): got = lax.ppermute(sent, 'exp', [(i, i ^ bit) for i in range(n_exp)])]
    ppermute x7, starting transfers between devices: 13.5 us -> 11 us  [routed_experts(): lax.ppermute(expert_rows[kk], 'attn', [(s, (s - k) % n_attn) for s in ran...]
    unnamed x28 -> x32, local copies, waits for them, and re-layouts: 3.8 us -> 1.46 us
  transfers between devices with their start and end apart: 26 -> 30, of which waited for: 9 -> 8; matrix products, arithmetic and copies ran while one was open for 33% -> 37% of each run, Pallas kernels for 0% -> 0%
where the time goes in v12:
time: 137 us; the launch traced here: 136 us
  waiting for transfers between devices  47.3 us (35%)
  starting transfers between devices  35.7 us (26%)
  matrix products  27.5 us (20%)
  other arithmetic  14.9 us (11%)
  local copies, waits for them, and re-layouts  10 us (7%)
    dot_general x3, matrix products, expert_part(): return jnp.dot(hidden, down_slice, preferred_element_type=jnp.float32)  20.4 us
    ppermute x6, waiting for transfers between devices, bit_gather(): other = lax.ppermute(x, axis, [(i, i ^ bit) for i in range(n)])  17.8 us
    ppermute x6, waiting for transfers between devices, bit_reduce(): lax.ppermute(sent, axis, [(i, i ^ bit) for i in range(n)]).astype(x.dtype)  14.4 us
    ppermute x7, starting transfers between devices, routed_experts(): lax.ppermute(tokens, 'attn', [(s, (s + k) % n_attn) for s in range(n_attn)])  13.8 us
    ppermute x7, starting transfers between devices, routed_experts(): lax.ppermute(expert_rows[kk], 'attn', [(s, (s - k) % n_attn) for s in ran...  11 us
    ppermute x7, waiting for transfers between devices, routed_experts(): lax.ppermute(expert_rows[kk], 'attn', [(s, (s - k) % n_attn) for s in ran...  10.1 us
    another operation x9, other arithmetic, bit_gather(): return jnp.stack([x, other])  7.25 us
    slice x3, local copies, waits for them, and re-layouts, bit_reduce(): sent = x[1] if wire is None else x[1].astype(wire)  6.85 us
  transfers between devices with their start and end apart: 30, of which 8 were waited for; matrix products, arithmetic and copies ran while one was open for 37% of the time, Pallas kernels for 0%

profile of v12, /device:TPU:0, one launch (start us, length us, event | category | flops | bytes accessed | tf_op | source)
XLA Modules:
  0.0 136.5 jit_solution(13755609379505569024)
XLA Ops:
  0.7 3.0 %collective-permute-start.4 = (bf16[8,7168]{1,0:T(8,128)(2,1)}, bf16[8,7168]{1,0:T(8,128)(2,1)}, u32[]{:S(2)}, u32[]{:S(2)}) collective-permute-start(bf16[8,7168]{1,0:T(8,128)(2,1)} %param.16), channel_id=1, source_target_pairs={{0,4},{4,8},{8,12},{12,16},{16,20},{20,24},{24,28},{28,0},{1,5},{5... | collective-permute-start | bytes 344072 | tf_op jit(solution)/shard_map/ppermute | solution.py:61
  3.7 1.6 %collective-permute-start.5 = (bf16[8,7168]{1,0:T(8,128)(2,1)}, bf16[8,7168]{1,0:T(8,128)(2,1)}, u32[]{:S(2)}, u32[]{:S(2)}) collective-permute-start(bf16[8,7168]{1,0:T(8,128)(2,1)} %param.16), channel_id=1, source_target_pairs={{0,8},{4,12},{8,16},{12,20},{16,24},{20,28},{24,0},{28,4},{1,9},{5... | collective-permute-start | bytes 344072 | tf_op jit(solution)/shard_map/ppermute | solution.py:61
  5.3 2.5 %collective-permute-start.12 = (bf16[8,7168]{1,0:T(8,128)(2,1)}, bf16[8,7168]{1,0:T(8,128)(2,1)}, u32[]{:S(2)}, u32[]{:S(2)}) collective-permute-start(bf16[8,7168]{1,0:T(8,128)(2,1)} %param.16), channel_id=1, source_target_pairs={{0,12},{4,16},{8,20},{12,24},{16,28},{20,0},{24,4},{28,8},{1,13},{... | collective-permute-start | bytes 344072 | tf_op jit(solution)/shard_map/ppermute | solution.py:61
  9.8 1.8 %fusion.91 = f32[2,128,1024]{2,1,0:T(8,128)S(1)} fusion(bf16[2,128,512]{2,1,0:T(8,128)(2,1)} %param.11, bf16[2,1024,512]{2,1,0:T(8,128)(2,1)S(1)} %copy-done), kind=kOutput, calls=%fused_computation.138 | convolution fusion | flops 268435456 | bytes 3407872 | tf_op jit(solution)/shard_map/rhl,rpl->rhp/dot_general | solution.py:108
  13.9 1.6 %collective-permute-start.1 = (f32[2,128]{1,0:T(2,128)S(1)}, f32[2,128]{1,0:T(2,128)S(1)}, u32[]{:S(2)}, u32[]{:S(2)}) collective-permute-start(f32[2,128]{1,0:T(2,128)S(1)} %max.6), channel_id=1, source_target_pairs={{0,2},{1,3},{2,0},{3,1},{4,6},{5,7},{6,4},{7,5},{8,10},{9,11},{10,... | collective-permute-start | bytes 3080 | tf_op jit(solution)/shard_map/ppermute | solution.py:130
  15.5 2.1 %collective-permute-done.1 = f32[2,128]{1,0:T(2,128)S(1)} collective-permute-done((f32[2,128]{1,0:T(2,128)S(1)}, f32[2,128]{1,0:T(2,128)S(1)}, u32[]{:S(2)}, u32[]{:S(2)}) %collective-permute-start.1) | collective-permute-done | bytes 1056 | tf_op jit(solution)/shard_map/ppermute | solution.py:130
  17.6 2.7 %collective-permute-start.14 = (bf16[8,7168]{1,0:T(8,128)(2,1)S(1)}, bf16[8,7168]{1,0:T(8,128)(2,1)S(1)}, u32[]{:S(2)}, u32[]{:S(2)}) collective-permute-start(bf16[8,7168]{1,0:T(8,128)(2,1)S(1)} %copy-done.10), channel_id=1, source_target_pairs={{0,20},{4,24},{8,28},{12,0},{16,4},{20,8},{24,12},{28,16},{1,21},{... | collective-permute-start | bytes 344072 | tf_op jit(solution)/shard_map/ppermute | solution.py:61
  20.2 1.4 broadcast_multiply_fusion
  22.9 1.4 %collective-permute-start.22 = (bf16[8,7168]{1,0:T(8,128)(2,1)S(1)}, bf16[8,7168]{1,0:T(8,128)(2,1)S(1)}, u32[]{:S(2)}, u32[]{:S(2)}) collective-permute-start(bf16[8,7168]{1,0:T(8,128)(2,1)S(1)} %copy-done.10), channel_id=1, source_target_pairs={{0,24},{4,28},{8,0},{12,4},{16,8},{20,12},{24,16},{28,20},{1,25},{... | collective-permute-start | bytes 344072 | tf_op jit(solution)/shard_map/ppermute | solution.py:61
  24.3 1.4 %collective-permute-start.23 = (bf16[8,7168]{1,0:T(8,128)(2,1)S(1)}, bf16[8,7168]{1,0:T(8,128)(2,1)S(1)}, u32[]{:S(2)}, u32[]{:S(2)}) collective-permute-start(bf16[8,7168]{1,0:T(8,128)(2,1)S(1)} %copy-done.10), channel_id=1, source_target_pairs={{0,28},{4,0},{8,4},{12,8},{16,12},{20,16},{24,20},{28,24},{1,29},{... | collective-permute-start | bytes 344072 | tf_op jit(solution)/shard_map/ppermute | solution.py:61
  26.9 1.6 %collective-permute-start.6 = (bf16[3,8,7168]{2,1,0:T(8,128)(2,1)S(1)}, bf16[3,8,7168]{2,1,0:T(8,128)(2,1)S(1)}, u32[]{:S(2)}, u32[]{:S(2)}) collective-permute-start(bf16[3,8,7168]{2,1,0:T(8,128)(2,1)S(1)} %get-tuple-element.21), channel_id=1, source_target_pairs={{0,2},{1,3},{2,0},{3,1},{4,6},{5,7},{6,4},{7,5},{8,10},{9,11},{10,... | collective-permute-start | bytes 1032200 | tf_op jit(solution)/shard_map/ppermute | solution.py:34
  30.1 1.6 %collective-permute-start.24 = (bf16[2,8,7168]{2,1,0:T(8,128)(2,1)S(1)}, bf16[2,8,7168]{2,1,0:T(8,128)(2,1)S(1)}, u32[]{:S(2)}, u32[]{:S(2)}) collective-permute-start(bf16[2,8,7168]{2,1,0:T(8,128)(2,1)S(1)} %get-tuple-element.30), channel_id=1, source_target_pairs={{0,2},{1,3},{2,0},{3,1},{4,6},{5,7},{6,4},{7,5},{8,10},{9,11},{10,... | collective-permute-start | bytes 688136 | tf_op jit(solution)/shard_map/ppermute | solution.py:34
  32.3 17.8 %collective-permute-done.24 = bf16[2,8,7168]{2,1,0:T(8,128)(2,1)S(1)} collective-permute-done((bf16[2,8,7168]{2,1,0:T(8,128)(2,1)S(1)}, bf16[2,8,7168]{2,1,0:T(8,128)(2,1)S(1)}, u32[]{:S(2)}, u32[]{:S(2)}) %collective-permute-start.24) | collective-permute-done | bytes 229408 | tf_op jit(solution)/shard_map/ppermute | solution.py:34
  50.2 2.9 %collective-permute-done.3 = f32[2,1,32,513]{3,2,0,1:T(8,128)S(1)} collective-permute-done((f32[2,1,32,513]{3,2,0,1:T(8,128)S(1)}, f32[2,1,32,513]{3,2,0,1:T(8,128)S(1)}, u32[]{:S(2)}, u32[]{:S(2)}) %collective-permute-start.3) | collective-permute-done | bytes 131360 | tf_op jit(solution)/shard_map/ppermute | solution.py:143
  58.4 6.7 %fusion = f32[64,7168]{1,0:T(8,128)} fusion(bf16[1,256,7168]{2,1,0:T(8,128)(2,1)} %param.21, bf16[64,7168]{1,0:T(8,128)(2,1)S(1)} %bitcast.157, bf16[1,7168,256]{2,1,0:T(8,128)(2,1)} %param.20, f32[64,256]{1,0:T(8,128)S(1)} %fusion.12), kind=kOutput, calls=%fused_computation.1 | convolution fusion | flops 469860352 | bytes 10158080 | tf_op jit(solution)/shard_map/dot_general | solution.py:16
  65.1 3.0 %fusion.89 = (f32[32,7168]{1,0:T(8,128)}, f32[32,7168]{1,0:T(8,128)}) fusion(f32[64,7168]{1,0:T(8,128)} %fusion), kind=kLoop, calls=%fused_computation.136 | loop fusion | bytes 3670016 | tf_op jit(solution)/shard_map/slice | solution.py:39
  68.2 1.4 %pad_maximum_fusion = bf16[2,2,3,8,7168]{4,3,2,1,0:T(8,128)(2,1)S(1)} fusion(bf16[1,2,3,8,7168]{4,3,2,1,0:T(8,128)(2,1)} %bitcast.13, bf16[1,2,3,8,7168]{4,3,2,1,0:T(8,128)(2,1)} %get-tuple-element.10), kind=kLoop, calls=%fused_computation.19 | loop fusion | flops 688128 | bytes 2752512 | tf_op jit(solution)/shard_map/stack | solution.py:35
  69.6 1.4 %fusion.10 = f32[96,256]{1,0:T(8,128)} fusion(bf16[96,7168]{1,0:T(8,128)(2,1)S(1)} %bitcast.152, bf16[1,7168,256]{2,1,0:T(8,128)(2,1)S(1)} %copy-done.1), kind=kOutput, calls=%fused_computation.11 | convolution fusion | flops 352321536 | bytes 5144576 | tf_op jit(solution)/shard_map/dot_general | solution.py:14
  71.0 6.8 %fusion.4 = f32[96,7168]{1,0:T(8,128)} fusion(bf16[1,256,7168]{2,1,0:T(8,128)(2,1)} %param.21, f32[96,256]{1,0:T(8,128)} %fusion.10, bf16[96,7168]{1,0:T(8,128)(2,1)S(1)} %bitcast.153, bf16[1,7168,256]{2,1,0:T(8,128)(2,1)} %param.19), kind=kOutput, calls=%fused_computation.5 | convolution fusion | flops 704790528 | bytes 11567104 | tf_op jit(solution)/shard_map/dot_general | solution.py:16
  77.8 3.6 %fusion.87 = (f32[48,7168]{1,0:T(8,128)}, f32[48,7168]{1,0:T(8,128)}) fusion(f32[96,7168]{1,0:T(8,128)} %fusion.4), kind=kLoop, calls=%fused_computation.134 | loop fusion | bytes 5505024 | tf_op jit(solution)/shard_map/slice | solution.py:39
  83.2 1.4 %fusion.8 = f32[96,256]{1,0:T(8,128)} fusion(bf16[96,7168]{1,0:T(8,128)(2,1)S(1)} %bitcast.154, bf16[1,7168,256]{2,1,0:T(8,128)(2,1)S(1)} %copy-done.2), kind=kOutput, calls=%fused_computation.9 | convolution fusion | flops 352321536 | bytes 5144576 | tf_op jit(solution)/shard_map/dot_general | solution.py:14
  84.6 6.8 %fusion.2 = f32[96,7168]{1,0:T(8,128)} fusion(bf16[1,256,7168]{2,1,0:T(8,128)(2,1)} %param.21, f32[96,256]{1,0:T(8,128)} %fusion.8, bf16[96,7168]{1,0:T(8,128)(2,1)S(1)} %bitcast.155, bf16[1,7168,256]{2,1,0:T(8,128)(2,1)} %param.19), kind=kOutput, calls=%fused_computation.3 | convolution fusion | flops 704790528 | bytes 11567104 | tf_op jit(solution)/shard_map/dot_general | solution.py:16
  91.5 1.7 %add.176 = f32[2,2,8,7168]{3,2,1,0:T(8,128)S(1)} add(f32[2,2,8,7168]{3,2,1,0:T(8,128)} %bitcast.160, f32[2,2,8,7168]{3,2,1,0:T(8,128)} %collective-permute-done.26) | non-fusion elementwise | flops 229376 | bytes 2752512 | tf_op jit(solution)/shard_map/add | solution.py:40
  93.2 1.6 %collective-permute-start.27 = (bf16[2,8,7168]{2,1,0:T(8,128)(2,1)S(1)}, bf16[2,8,7168]{2,1,0:T(8,128)(2,1)S(1)}, u32[]{:S(2)}, u32[]{:S(2)}) collective-permute-start(bf16[2,8,7168]{2,1,0:T(8,128)(2,1)S(1)} %fusion.45), channel_id=1, source_target_pairs={{0,2},{1,3},{2,0},{3,1},{4,6},{5,7},{6,4},{7,5},{8,10},{9,11},{10,... | collective-permute-start | bytes 688136 | tf_op jit(solution)/shard_map/ppermute | solution.py:40
  95.1 5.7 %collective-permute-done.27 = bf16[2,8,7168]{2,1,0:T(8,128)(2,1)S(1)} collective-permute-done((bf16[2,8,7168]{2,1,0:T(8,128)(2,1)S(1)}, bf16[2,8,7168]{2,1,0:T(8,128)(2,1)S(1)}, u32[]{:S(2)}, u32[]{:S(2)}) %collective-permute-start.27) | collective-permute-done | bytes 229408 | tf_op jit(solution)/shard_map/ppermute | solution.py:40
  102.2 1.5 %add.165 = f32[2,3,8,7168]{3,2,1,0:T(8,128)S(1)} add(f32[2,3,8,7168]{3,2,1,0:T(8,128)S(1)} %bitcast.158, f32[2,3,8,7168]{3,2,1,0:T(8,128)} %collective-permute-done.8) | non-fusion elementwise | flops 344064 | bytes 4128768 | tf_op jit(solution)/shard_map/add | solution.py:40
  103.8 1.6 %collective-permute-start.9 = (bf16[3,8,7168]{2,1,0:T(8,128)(2,1)S(1)}, bf16[3,8,7168]{2,1,0:T(8,128)(2,1)S(1)}, u32[]{:S(2)}, u32[]{:S(2)}) collective-permute-start(bf16[3,8,7168]{2,1,0:T(8,128)(2,1)S(1)} %fusion.41), channel_id=1, source_target_pairs={{0,2},{1,3},{2,0},{3,1},{4,6},{5,7},{6,4},{7,5},{8,10},{9,11},{10,... | collective-permute-start | bytes 1032200 | tf_op jit(solution)/shard_map/ppermute | solution.py:40
  106.3 8.6 %collective-permute-done.9 = bf16[3,8,7168]{2,1,0:T(8,128)(2,1)S(1)} collective-permute-done((bf16[3,8,7168]{2,1,0:T(8,128)(2,1)S(1)}, bf16[3,8,7168]{2,1,0:T(8,128)(2,1)S(1)}, u32[]{:S(2)}, u32[]{:S(2)}) %collective-permute-start.9) | collective-permute-done | bytes 344096 | tf_op jit(solution)/shard_map/ppermute | solution.py:40
  115.0 4.2 %collective-permute-start.10 = (bf16[8,7168]{1,0:T(8,128)(2,1)S(1)}, bf16[8,7168]{1,0:T(8,128)(2,1)S(1)}, u32[]{:S(2)}, u32[]{:S(2)}) collective-permute-start(bf16[8,7168]{1,0:T(8,128)(2,1)S(1)} %get-tuple-element.18), channel_id=1, source_target_pairs={{0,28},{4,0},{8,4},{12,8},{16,12},{20,16},{24,20},{28,24},{1,29},{... | collective-permute-start | bytes 344072 | tf_op jit(solution)/shard_map/ppermute | solution.py:86
  120.6 3.4 %collective-permute-start.19 = (bf16[8,7168]{1,0:T(8,128)(2,1)S(1)}, bf16[8,7168]{1,0:T(8,128)(2,1)S(1)}, u32[]{:S(2)}, u32[]{:S(2)}) collective-permute-start(bf16[8,7168]{1,0:T(8,128)(2,1)S(1)} %get-tuple-element.22), channel_id=1, source_target_pairs={{0,20},{4,24},{8,28},{12,0},{16,4},{20,8},{24,12},{28,16},{1,21},{... | collective-permute-start | bytes 344072 | tf_op jit(solution)/shard_map/ppermute | solution.py:86
  125.5 2.1 %collective-permute-done.19 = bf16[8,7168]{1,0:T(8,128)(2,1)S(1)} collective-permute-done((bf16[8,7168]{1,0:T(8,128)(2,1)S(1)}, bf16[8,7168]{1,0:T(8,128)(2,1)S(1)}, u32[]{:S(2)}, u32[]{:S(2)}) %collective-permute-start.19) | collective-permute-done | bytes 114720 | tf_op jit(solution)/shard_map/ppermute | solution.py:86
  127.6 7.1 %collective-permute-done.20 = bf16[8,7168]{1,0:T(8,128)(2,1)S(1)} collective-permute-done((bf16[8,7168]{1,0:T(8,128)(2,1)S(1)}, bf16[8,7168]{1,0:T(8,128)(2,1)S(1)}, u32[]{:S(2)}, u32[]{:S(2)}) %collective-permute-start.20) | collective-permute-done | bytes 114720 | tf_op jit(solution)/shard_map/ppermute | solution.py:86
  (115 shorter events, 23.5 us)
Async XLA Ops:
  0.7 22.3 %collective-permute-start.4 = (bf16[8,7168]{1,0:T(8,128)(2,1)}, bf16[8,7168]{1,0:T(8,128)(2,1)}, u32[]{:S(2)}, u32[]{:S(2)}) collective-permute-start(bf16[8,7168]{1,0:T(8,128)(2,1)} %param.16), channel_id=1, source_target_pairs={{0,4},{4,8},{8,12},{12,16},{16,20},{20,24},{24,28},{28,0},{1,5},{5... | collective-permute-start | bytes 344072 | tf_op jit(solution)/shard_map/ppermute | solution.py:61
  3.7 20.7 %collective-permute-start.5 = (bf16[8,7168]{1,0:T(8,128)(2,1)}, bf16[8,7168]{1,0:T(8,128)(2,1)}, u32[]{:S(2)}, u32[]{:S(2)}) collective-permute-start(bf16[8,7168]{1,0:T(8,128)(2,1)} %param.16), channel_id=1, source_target_pairs={{0,8},{4,12},{8,16},{12,20},{16,24},{20,28},{24,0},{28,4},{1,9},{5... | collective-permute-start | bytes 344072 | tf_op jit(solution)/shard_map/ppermute | solution.py:61
  5.3 21.5 %collective-permute-start.12 = (bf16[8,7168]{1,0:T(8,128)(2,1)}, bf16[8,7168]{1,0:T(8,128)(2,1)}, u32[]{:S(2)}, u32[]{:S(2)}) collective-permute-start(bf16[8,7168]{1,0:T(8,128)(2,1)} %param.16), channel_id=1, source_target_pairs={{0,12},{4,16},{8,20},{12,24},{16,28},{20,0},{24,4},{28,8},{1,13},{... | collective-permute-start | bytes 344072 | tf_op jit(solution)/shard_map/ppermute | solution.py:61
  7.8 19.1 %collective-permute-start.13 = (bf16[8,7168]{1,0:T(8,128)(2,1)}, bf16[8,7168]{1,0:T(8,128)(2,1)}, u32[]{:S(2)}, u32[]{:S(2)}) collective-permute-start(bf16[8,7168]{1,0:T(8,128)(2,1)} %param.16), channel_id=1, source_target_pairs={{0,16},{4,20},{8,24},{12,28},{16,0},{20,4},{24,8},{28,12},{1,17},{... | collective-permute-start | bytes 344072 | tf_op jit(solution)/shard_map/ppermute | solution.py:61
  12.0 1.9 %collective-permute-start = (f32[2,128]{1,0:T(2,128)S(1)}, f32[2,128]{1,0:T(2,128)S(1)}, u32[]{:S(2)}, u32[]{:S(2)}) collective-permute-start(f32[2,128]{1,0:T(2,128)S(1)} %get-tuple-element.39), channel_id=1, source_target_pairs={{0,1},{1,0},{2,3},{3,2},{4,5},{5,4},{6,7},{7,6},{8,9},{9,8},{10,11... | collective-permute-start | bytes 3080 | tf_op jit(solution)/shard_map/ppermute | solution.py:130
  13.9 3.6 %collective-permute-start.1 = (f32[2,128]{1,0:T(2,128)S(1)}, f32[2,128]{1,0:T(2,128)S(1)}, u32[]{:S(2)}, u32[]{:S(2)}) collective-permute-start(f32[2,128]{1,0:T(2,128)S(1)} %max.6), channel_id=1, source_target_pairs={{0,2},{1,3},{2,0},{3,1},{4,6},{5,7},{6,4},{7,5},{8,10},{9,11},{10,... | collective-permute-start | bytes 3080 | tf_op jit(solution)/shard_map/ppermute | solution.py:130
  17.6 10.8 %collective-permute-start.14 = (bf16[8,7168]{1,0:T(8,128)(2,1)S(1)}, bf16[8,7168]{1,0:T(8,128)(2,1)S(1)}, u32[]{:S(2)}, u32[]{:S(2)}) collective-permute-start(bf16[8,7168]{1,0:T(8,128)(2,1)S(1)} %copy-done.10), channel_id=1, source_target_pairs={{0,20},{4,24},{8,28},{12,0},{16,4},{20,8},{24,12},{28,16},{1,21},{... | collective-permute-start | bytes 344072 | tf_op jit(solution)/shard_map/ppermute | solution.py:61
  22.9 7.1 %collective-permute-start.22 = (bf16[8,7168]{1,0:T(8,128)(2,1)S(1)}, bf16[8,7168]{1,0:T(8,128)(2,1)S(1)}, u32[]{:S(2)}, u32[]{:S(2)}) collective-permute-start(bf16[8,7168]{1,0:T(8,128)(2,1)S(1)} %copy-done.10), channel_id=1, source_target_pairs={{0,24},{4,28},{8,0},{12,4},{16,8},{20,12},{24,16},{28,20},{1,25},{... | collective-permute-start | bytes 344072 | tf_op jit(solution)/shard_map/ppermute | solution.py:61
  24.3 5.7 %collective-permute-start.23 = (bf16[8,7168]{1,0:T(8,128)(2,1)S(1)}, bf16[8,7168]{1,0:T(8,128)(2,1)S(1)}, u32[]{:S(2)}, u32[]{:S(2)}) collective-permute-start(bf16[8,7168]{1,0:T(8,128)(2,1)S(1)} %copy-done.10), channel_id=1, source_target_pairs={{0,28},{4,0},{8,4},{12,8},{16,12},{20,16},{24,20},{28,24},{1,29},{... | collective-permute-start | bytes 344072 | tf_op jit(solution)/shard_map/ppermute | solution.py:61
  26.8 4.9 %collective-permute-start.2 = (f32[2,2,32,513]{3,2,0,1:T(8,128)S(1)}, f32[2,2,32,513]{3,2,0,1:T(8,128)S(1)}, u32[]{:S(2)}, u32[]{:S(2)}) collective-permute-start(f32[2,2,32,513]{3,2,0,1:T(8,128)S(1)} %bitcast.166), channel_id=1, source_target_pairs={{0,1},{1,0},{2,3},{3,2},{4,5},{5,4},{6,7},{7,6},{8,9},{9,8},{10,11... | collective-permute-start | bytes 787976 | tf_op jit(solution)/shard_map/ppermute | solution.py:143
  26.9 27.1 %collective-permute-start.6 = (bf16[3,8,7168]{2,1,0:T(8,128)(2,1)S(1)}, bf16[3,8,7168]{2,1,0:T(8,128)(2,1)S(1)}, u32[]{:S(2)}, u32[]{:S(2)}) collective-permute-start(bf16[3,8,7168]{2,1,0:T(8,128)(2,1)S(1)} %get-tuple-element.21), channel_id=1, source_target_pairs={{0,2},{1,3},{2,0},{3,1},{4,6},{5,7},{6,4},{7,5},{8,10},{9,11},{10,... | collective-permute-start | bytes 1032200 | tf_op jit(solution)/shard_map/ppermute | solution.py:34
  29.4 25.7 %collective-permute-start.15 = (bf16[3,8,7168]{2,1,0:T(8,128)(2,1)S(1)}, bf16[3,8,7168]{2,1,0:T(8,128)(2,1)S(1)}, u32[]{:S(2)}, u32[]{:S(2)}) collective-permute-start(bf16[3,8,7168]{2,1,0:T(8,128)(2,1)S(1)} %get-tuple-element.26), channel_id=1, source_target_pairs={{0,2},{1,3},{2,0},{3,1},{4,6},{5,7},{6,4},{7,5},{8,10},{9,11},{10,... | collective-permute-start | bytes 1032200 | tf_op jit(solution)/shard_map/ppermute | solution.py:34
  30.1 20.0 %collective-permute-start.24 = (bf16[2,8,7168]{2,1,0:T(8,128)(2,1)S(1)}, bf16[2,8,7168]{2,1,0:T(8,128)(2,1)S(1)}, u32[]{:S(2)}, u32[]{:S(2)}) collective-permute-start(bf16[2,8,7168]{2,1,0:T(8,128)(2,1)S(1)} %get-tuple-element.30), channel_id=1, source_target_pairs={{0,2},{1,3},{2,0},{3,1},{4,6},{5,7},{6,4},{7,5},{8,10},{9,11},{10,... | collective-permute-start | bytes 688136 | tf_op jit(solution)/shard_map/ppermute | solution.py:34
  31.7 21.4 %collective-permute-start.3 = (f32[2,1,32,513]{3,2,0,1:T(8,128)S(1)}, f32[2,1,32,513]{3,2,0,1:T(8,128)S(1)}, u32[]{:S(2)}, u32[]{:S(2)}) collective-permute-start(f32[2,1,32,513]{3,2,0,1:T(8,128)S(1)} %constant_dynamic-slice_fusion), channel_id=1, source_target_pairs={{0,2},{1,3},{2,0},{3,1},{4,6},{5,7},{6,4},{7,5},{8,10},{9,11},{10,... | collective-permute-start | bytes 393992 | tf_op jit(solution)/shard_map/ppermute | solution.py:143
  50.1 6.7 %collective-permute-start.25 = (bf16[2,2,8,7168]{3,2,1,0:T(8,128)(2,1)S(1)}, bf16[2,2,8,7168]{3,2,1,0:T(8,128)(2,1)S(1)}, u32[]{:S(2)}, u32[]{:S(2)}) collective-permute-start(bf16[2,2,8,7168]{3,2,1,0:T(8,128)(2,1)S(1)} %get-tuple-element.17), channel_id=1, source_target_pairs={{0,1},{1,0},{2,3},{3,2},{4,5},{5,4},{6,7},{7,6},{8,9},{9,8},{10,11... | collective-permute-start | bytes 1376264 | tf_op jit(solution)/shard_map/ppermute | solution.py:34
  55.1 13.0 %collective-permute-start.7 = (bf16[2,3,8,7168]{3,2,1,0:T(8,128)(2,1)}, bf16[2,3,8,7168]{3,2,1,0:T(8,128)(2,1)}, u32[]{:S(2)}, u32[]{:S(2)}) collective-permute-start(bf16[2,3,8,7168]{3,2,1,0:T(8,128)(2,1)} %get-tuple-element.11), channel_id=1, source_target_pairs={{0,1},{1,0},{2,3},{3,2},{4,5},{5,4},{6,7},{7,6},{8,9},{9,8},{10,11... | collective-permute-start | bytes 2064392 | tf_op jit(solution)/shard_map/ppermute | solution.py:34
  56.3 25.6 %collective-permute-start.16 = (bf16[2,3,8,7168]{3,2,1,0:T(8,128)(2,1)}, bf16[2,3,8,7168]{3,2,1,0:T(8,128)(2,1)}, u32[]{:S(2)}, u32[]{:S(2)}) collective-permute-start(bf16[2,3,8,7168]{3,2,1,0:T(8,128)(2,1)} %get-tuple-element.13), channel_id=1, source_target_pairs={{0,1},{1,0},{2,3},{3,2},{4,5},{5,4},{6,7},{7,6},{8,9},{9,8},{10,11... | collective-permute-start | bytes 2064392 | tf_op jit(solution)/shard_map/ppermute | solution.py:34
  68.1 23.3 %collective-permute-start.26 = (f32[2,2,8,7168]{3,2,1,0:T(8,128)}, f32[2,2,8,7168]{3,2,1,0:T(8,128)}, u32[]{:S(2)}, u32[]{:S(2)}) collective-permute-start(f32[2,2,8,7168]{3,2,1,0:T(8,128)} %bitcast.54), channel_id=1, source_target_pairs={{0,1},{1,0},{2,3},{3,2},{4,5},{5,4},{6,7},{7,6},{8,9},{9,8},{10,11... | collective-permute-start | bytes 2752520 | tf_op jit(solution)/shard_map/ppermute | solution.py:40
  81.5 20.8 %collective-permute-start.8 = (f32[2,3,8,7168]{3,2,1,0:T(8,128)}, f32[2,3,8,7168]{3,2,1,0:T(8,128)}, u32[]{:S(2)}, u32[]{:S(2)}) collective-permute-start(f32[2,3,8,7168]{3,2,1,0:T(8,128)} %bitcast.19), channel_id=1, source_target_pairs={{0,1},{1,0},{2,3},{3,2},{4,5},{5,4},{6,7},{7,6},{8,9},{9,8},{10,11... | collective-permute-start | bytes 4128776 | tf_op jit(solution)/shard_map/ppermute | solution.py:40
  93.2 7.6 %collective-permute-start.27 = (bf16[2,8,7168]{2,1,0:T(8,128)(2,1)S(1)}, bf16[2,8,7168]{2,1,0:T(8,128)(2,1)S(1)}, u32[]{:S(2)}, u32[]{:S(2)}) collective-permute-start(bf16[2,8,7168]{2,1,0:T(8,128)(2,1)S(1)} %fusion.45), channel_id=1, source_target_pairs={{0,2},{1,3},{2,0},{3,1},{4,6},{5,7},{6,4},{7,5},{8,10},{9,11},{10,... | collective-permute-start | bytes 688136 | tf_op jit(solution)/shard_map/ppermute | solution.py:40
  95.0 10.4 %collective-permute-start.17 = (f32[2,3,8,7168]{3,2,1,0:T(8,128)S(1)}, f32[2,3,8,7168]{3,2,1,0:T(8,128)S(1)}, u32[]{:S(2)}, u32[]{:S(2)}) collective-permute-start(f32[2,3,8,7168]{3,2,1,0:T(8,128)S(1)} %bitcast.162), channel_id=1, source_target_pairs={{0,1},{1,0},{2,3},{3,2},{4,5},{5,4},{6,7},{7,6},{8,9},{9,8},{10,11... | collective-permute-start | bytes 4128776 | tf_op jit(solution)/shard_map/ppermute | solution.py:40
  100.9 23.1 %collective-permute-start.28 = (bf16[8,7168]{1,0:T(8,128)(2,1)S(1)}, bf16[8,7168]{1,0:T(8,128)(2,1)S(1)}, u32[]{:S(2)}, u32[]{:S(2)}) collective-permute-start(bf16[8,7168]{1,0:T(8,128)(2,1)S(1)} %get-tuple-element.27), channel_id=1, source_target_pairs={{0,8},{4,12},{8,16},{12,20},{16,24},{20,28},{24,0},{28,4},{1,9},{5... | collective-permute-start | bytes 344072 | tf_op jit(solution)/shard_map/ppermute | solution.py:86
  101.6 22.4 %collective-permute-start.29 = (bf16[8,7168]{1,0:T(8,128)(2,1)S(1)}, bf16[8,7168]{1,0:T(8,128)(2,1)S(1)}, u32[]{:S(2)}, u32[]{:S(2)}) collective-permute-start(bf16[8,7168]{1,0:T(8,128)(2,1)S(1)} %get-tuple-element.28), channel_id=1, source_target_pairs={{0,4},{4,8},{8,12},{12,16},{16,20},{20,24},{24,28},{28,0},{1,5},{5... | collective-permute-start | bytes 344072 | tf_op jit(solution)/shard_map/ppermute | solution.py:86
  103.8 11.1 %collective-permute-start.9 = (bf16[3,8,7168]{2,1,0:T(8,128)(2,1)S(1)}, bf16[3,8,7168]{2,1,0:T(8,128)(2,1)S(1)}, u32[]{:S(2)}, u32[]{:S(2)}) collective-permute-start(bf16[3,8,7168]{2,1,0:T(8,128)(2,1)S(1)} %fusion.41), channel_id=1, source_target_pairs={{0,2},{1,3},{2,0},{3,1},{4,6},{5,7},{6,4},{7,5},{8,10},{9,11},{10,... | collective-permute-start | bytes 1032200 | tf_op jit(solution)/shard_map/ppermute | solution.py:40
  105.6 30.0 %copy-start.12 = (f32[8]{0:T(128)S(1)}, f32[8]{0:T(128)}, u32[]{:S(2)}) copy-start(f32[8]{0:T(128)} %get-tuple-element.37) | copy-start | bytes 100
  105.6 30.0 %copy-start.13 = (f32[8]{0:T(128)S(1)}, f32[8]{0:T(128)}, u32[]{:S(2)}) copy-start(f32[8]{0:T(128)} %get-tuple-element.38) | copy-start | bytes 100
  105.6 14.8 %collective-permute-start.18 = (bf16[3,8,7168]{2,1,0:T(8,128)(2,1)S(1)}, bf16[3,8,7168]{2,1,0:T(8,128)(2,1)S(1)}, u32[]{:S(2)}, u32[]{:S(2)}) collective-permute-start(bf16[3,8,7168]{2,1,0:T(8,128)(2,1)S(1)} %fusion.42), channel_id=1, source_target_pairs={{0,2},{1,3},{2,0},{3,1},{4,6},{5,7},{6,4},{7,5},{8,10},{9,11},{10,... | collective-permute-start | bytes 1032200 | tf_op jit(solution)/shard_map/ppermute | solution.py:40
  115.0 10.5 %collective-permute-start.10 = (bf16[8,7168]{1,0:T(8,128)(2,1)S(1)}, bf16[8,7168]{1,0:T(8,128)(2,1)S(1)}, u32[]{:S(2)}, u32[]{:S(2)}) collective-permute-start(bf16[8,7168]{1,0:T(8,128)(2,1)S(1)} %get-tuple-element.18), channel_id=1, source_target_pairs={{0,28},{4,0},{8,4},{12,8},{16,12},{20,16},{24,20},{28,24},{1,29},{... | collective-permute-start | bytes 344072 | tf_op jit(solution)/shard_map/ppermute | solution.py:86
  119.1 6.3 %collective-permute-start.11 = (bf16[8,7168]{1,0:T(8,128)(2,1)S(1)}, bf16[8,7168]{1,0:T(8,128)(2,1)S(1)}, u32[]{:S(2)}, u32[]{:S(2)}) collective-permute-start(bf16[8,7168]{1,0:T(8,128)(2,1)S(1)} %get-tuple-element.19), channel_id=1, source_target_pairs={{0,24},{4,28},{8,0},{12,4},{16,8},{20,12},{24,16},{28,20},{1,25},{... | collective-permute-start | bytes 344072 | tf_op jit(solution)/shard_map/ppermute | solution.py:86
  120.6 7.0 %collective-permute-start.19 = (bf16[8,7168]{1,0:T(8,128)(2,1)S(1)}, bf16[8,7168]{1,0:T(8,128)(2,1)S(1)}, u32[]{:S(2)}, u32[]{:S(2)}) collective-permute-start(bf16[8,7168]{1,0:T(8,128)(2,1)S(1)} %get-tuple-element.22), channel_id=1, source_target_pairs={{0,20},{4,24},{8,28},{12,0},{16,4},{20,8},{24,12},{28,16},{1,21},{... | collective-permute-start | bytes 344072 | tf_op jit(solution)/shard_map/ppermute | solution.py:86
  124.0 10.7 %collective-permute-start.20 = (bf16[8,7168]{1,0:T(8,128)(2,1)S(1)}, bf16[8,7168]{1,0:T(8,128)(2,1)S(1)}, u32[]{:S(2)}, u32[]{:S(2)}) collective-permute-start(bf16[8,7168]{1,0:T(8,128)(2,1)S(1)} %get-tuple-element.24), channel_id=1, source_target_pairs={{0,16},{4,20},{8,24},{12,28},{16,0},{20,4},{24,8},{28,12},{1,17},{... | collective-permute-start | bytes 344072 | tf_op jit(solution)/shard_map/ppermute | solution.py:86
  124.0 11.6 %collective-permute-start.21 = (bf16[8,7168]{1,0:T(8,128)(2,1)S(1)}, bf16[8,7168]{1,0:T(8,128)(2,1)S(1)}, u32[]{:S(2)}, u32[]{:S(2)}) collective-permute-start(bf16[8,7168]{1,0:T(8,128)(2,1)S(1)} %get-tuple-element.23), channel_id=1, source_target_pairs={{0,12},{4,16},{8,20},{12,24},{16,28},{20,0},{24,4},{28,8},{1,13},{... | collective-permute-start | bytes 344072 | tf_op jit(solution)/shard_map/ppermute | solution.py:86
  (14 other events, 82.1 us)

commit v13 on v12

--- a/solution.py
+++ b/solution.py
@@ -53,9 +53,9 @@
         b //= 2
     hit = route_ids[:, :, None] == jnp.arange(n_experts, dtype=jnp.int32)[None, None, :]
     wmat = jnp.sum(jnp.where(hit, route_gates[:, :, None], 0.0), axis=1)
-    n_chunks = min(3, n_attn)
-    step = -(-n_attn // n_chunks)
-    bounds = [min(c * step, n_attn) for c in range(n_chunks)] + [n_attn]
+    split = max(1, (5 * n_attn) // 8)
+    bounds = [0, split, n_attn] if split < n_attn else [0, n_attn]
+    n_chunks = len(bounds) - 1
     pieces = [tokens]
     for k in range(1, n_attn):
         pieces.append(lax.ppermute(tokens, "attn", [(s, (s + k) % n_attn) for s in range(n_attn)]))

time: 137 us -> 132 us (0.964)
  local copies, waits for them, and re-layouts: 10 us -> 17.3 us
  matrix products: 27.5 us -> 21.9 us
  starting transfers between devices: 35.7 us -> 30.7 us
  other arithmetic: 14.9 us -> 10.5 us
  waiting for transfers between devices: 47.3 us -> 50.2 us
    unnamed x32 -> x34, local copies, waits for them, and re-layouts: 1.46 us -> 7.43 us
    dot_general x3 -> x2, matrix products: 20.4 us -> 15.5 us  [expert_part(): return jnp.dot(hidden, down_slice, preferred_element_type=jnp.float32)]
    ppermute x6 -> x4, waiting for transfers between devices: 14.4 us -> 18.4 us  [bit_reduce(): lax.ppermute(sent, axis, [(i, i ^ bit) for i in range(n)]).astype(x.dtype)]
    another operation x9 -> x5, other arithmetic: 7.25 us -> 3.5 us  [bit_gather(): return jnp.stack([x, other])]
    ppermute x7, starting transfers between devices: 11 us -> 7.42 us  [routed_experts(): lax.ppermute(expert_rows[kk], 'attn', [(s, (s - k) % n_attn) for s in ran...]
    ppermute x2, waiting for transfers between devices: 2.91 us -> 0.01 us  [per_device(): got = lax.ppermute(sent, 'exp', [(i, i ^ bit) for i in range(n_exp)])]
    ppermute x6 -> x4, starting transfers between devices: 4.3 us -> 2.63 us  [bit_gather(): other = lax.ppermute(x, axis, [(i, i ^ bit) for i in range(n)])]
    add x3 -> x2, other arithmetic: 3.44 us -> 1.88 us  [bit_reduce(): x[0]]
  transfers between devices with their start and end apart: 30 -> 26, of which waited for: 8 -> 8; matrix products, arithmetic and copies ran while one was open for 37% -> 35% of each run, Pallas kernels for 0% -> 0%
where the time goes in v13:
time: 132 us
  waiting for transfers between devices  50.2 us (38%)
  starting transfers between devices  30.7 us (23%)
  matrix products  21.9 us (17%)
  local copies, waits for them, and re-layouts  17.3 us (13%)
  other arithmetic  10.5 us (8%)
    ppermute x4, waiting for transfers between devices, bit_gather(): other = lax.ppermute(x, axis, [(i, i ^ bit) for i in range(n)])  18.9 us
    ppermute x4, waiting for transfers between devices, bit_reduce(): lax.ppermute(sent, axis, [(i, i ^ bit) for i in range(n)]).astype(x.dtype)  18.4 us
    dot_general x2, matrix products, expert_part(): return jnp.dot(hidden, down_slice, preferred_element_type=jnp.float32)  15.5 us
    ppermute x7, starting transfers between devices, routed_experts(): lax.ppermute(tokens, 'attn', [(s, (s + k) % n_attn) for s in range(n_attn)])  13.8 us
    ppermute x7, waiting for transfers between devices, routed_experts(): lax.ppermute(expert_rows[kk], 'attn', [(s, (s - k) % n_attn) for s in ran...  10.8 us
    unnamed x34, local copies, waits for them, and re-layouts  7.43 us
    ppermute x7, starting transfers between devices, routed_experts(): lax.ppermute(expert_rows[kk], 'attn', [(s, (s - k) % n_attn) for s in ran...  7.42 us
    slice x2, local copies, waits for them, and re-layouts, bit_reduce(): sent = x[1] if wire is None else x[1].astype(wire)  5.96 us
  transfers between devices with their start and end apart: 26, of which 8 were waited for; matrix products, arithmetic and copies ran while one was open for 35% of the time, Pallas kernels for 0%

profile of v13, /device:TPU:0, one launch (start us, length us, event | category | flops | bytes accessed | tf_op | source)
XLA Modules:
  0.0 131.6 jit_solution(14392068965141380909)
XLA Ops:
  0.7 3.0 %collective-permute-start.4 = (bf16[8,7168]{1,0:T(8,128)(2,1)}, bf16[8,7168]{1,0:T(8,128)(2,1)}, u32[]{:S(2)}, u32[]{:S(2)}) collective-permute-start(bf16[8,7168]{1,0:T(8,128)(2,1)} %param.16), channel_id=1, source_target_pairs={{0,4},{4,8},{8,12},{12,16},{16,20},{20,24},{24,28},{28,0},{1,5},{5... | collective-permute-start | bytes 344072 | tf_op jit(solution)/shard_map/ppermute | solution.py:61
  3.7 1.6 %collective-permute-start.5 = (bf16[8,7168]{1,0:T(8,128)(2,1)}, bf16[8,7168]{1,0:T(8,128)(2,1)}, u32[]{:S(2)}, u32[]{:S(2)}) collective-permute-start(bf16[8,7168]{1,0:T(8,128)(2,1)} %param.16), channel_id=1, source_target_pairs={{0,8},{4,12},{8,16},{12,20},{16,24},{20,28},{24,0},{28,4},{1,9},{5... | collective-permute-start | bytes 344072 | tf_op jit(solution)/shard_map/ppermute | solution.py:61
  5.3 2.5 %collective-permute-start.6 = (bf16[8,7168]{1,0:T(8,128)(2,1)}, bf16[8,7168]{1,0:T(8,128)(2,1)}, u32[]{:S(2)}, u32[]{:S(2)}) collective-permute-start(bf16[8,7168]{1,0:T(8,128)(2,1)} %param.16), channel_id=1, source_target_pairs={{0,12},{4,16},{8,20},{12,24},{16,28},{20,0},{24,4},{28,8},{1,13},{... | collective-permute-start | bytes 344072 | tf_op jit(solution)/shard_map/ppermute | solution.py:61
  9.8 1.8 %fusion.63 = f32[2,128,1024]{2,1,0:T(8,128)S(1)} fusion(bf16[2,128,512]{2,1,0:T(8,128)(2,1)} %param.11, bf16[2,1024,512]{2,1,0:T(8,128)(2,1)S(1)} %copy-done), kind=kOutput, calls=%fused_computation.115 | convolution fusion | flops 268435456 | bytes 3407872 | tf_op jit(solution)/shard_map/rhl,rpl->rhp/dot_general | solution.py:108
  14.6 1.6 %collective-permute-start.1 = (f32[2,128]{1,0:T(2,128)S(1)}, f32[2,128]{1,0:T(2,128)S(1)}, u32[]{:S(2)}, u32[]{:S(2)}) collective-permute-start(f32[2,128]{1,0:T(2,128)S(1)} %max.6), channel_id=1, source_target_pairs={{0,2},{1,3},{2,0},{3,1},{4,6},{5,7},{6,4},{7,5},{8,10},{9,11},{10,... | collective-permute-start | bytes 3080 | tf_op jit(solution)/shard_map/ppermute | solution.py:130
  16.1 2.1 %collective-permute-done.1 = f32[2,128]{1,0:T(2,128)S(1)} collective-permute-done((f32[2,128]{1,0:T(2,128)S(1)}, f32[2,128]{1,0:T(2,128)S(1)}, u32[]{:S(2)}, u32[]{:S(2)}) %collective-permute-start.1) | collective-permute-done | bytes 1056 | tf_op jit(solution)/shard_map/ppermute | solution.py:130
  18.2 2.6 %collective-permute-start.16 = (bf16[8,7168]{1,0:T(8,128)(2,1)S(1)}, bf16[8,7168]{1,0:T(8,128)(2,1)S(1)}, u32[]{:S(2)}, u32[]{:S(2)}) collective-permute-start(bf16[8,7168]{1,0:T(8,128)(2,1)S(1)} %copy-done.9), channel_id=1, source_target_pairs={{0,20},{4,24},{8,28},{12,0},{16,4},{20,8},{24,12},{28,16},{1,21},{... | collective-permute-start | bytes 344072 | tf_op jit(solution)/shard_map/ppermute | solution.py:61
  23.6 1.4 %collective-permute-start.17 = (bf16[8,7168]{1,0:T(8,128)(2,1)S(1)}, bf16[8,7168]{1,0:T(8,128)(2,1)S(1)}, u32[]{:S(2)}, u32[]{:S(2)}) collective-permute-start(bf16[8,7168]{1,0:T(8,128)(2,1)S(1)} %copy-done.9), channel_id=1, source_target_pairs={{0,24},{4,28},{8,0},{12,4},{16,8},{20,12},{24,16},{28,20},{1,25},{... | collective-permute-start | bytes 344072 | tf_op jit(solution)/shard_map/ppermute | solution.py:61
  25.0 1.5 %bitcast_dynamic-update-slice_fusion.3 = bf16[5,8,7168]{2,1,0:T(8,128)(2,1)} fusion(bf16[5,8,7168]{2,1,0:T(8,128)(2,1)} %bitcast_dynamic-update-slice_fusion.4, bf16[8,7168]{1,0:T(8,128)(2,1)} %collective-permute-done.4), kind=kLoop, calls=%fused_computation.71 | loop fusion | bytes 229376
  26.6 1.4 %collective-permute-start.18 = (bf16[8,7168]{1,0:T(8,128)(2,1)S(1)}, bf16[8,7168]{1,0:T(8,128)(2,1)S(1)}, u32[]{:S(2)}, u32[]{:S(2)}) collective-permute-start(bf16[8,7168]{1,0:T(8,128)(2,1)S(1)} %copy-done.9), channel_id=1, source_target_pairs={{0,28},{4,0},{8,4},{12,8},{16,12},{20,16},{24,20},{28,24},{1,29},{... | collective-permute-start | bytes 344072 | tf_op jit(solution)/shard_map/ppermute | solution.py:61
  28.0 1.6 %bitcast_dynamic-update-slice_fusion.2 = bf16[5,8,7168]{2,1,0:T(8,128)(2,1)} fusion(bf16[5,8,7168]{2,1,0:T(8,128)(2,1)} %bitcast_dynamic-update-slice_fusion.3, bf16[8,7168]{1,0:T(8,128)(2,1)} %collective-permute-done.5), kind=kLoop, calls=%fused_computation.70 | loop fusion | bytes 229376
  29.5 1.6 %bitcast_dynamic-update-slice_fusion.1 = bf16[5,8,7168]{2,1,0:T(8,128)(2,1)} fusion(bf16[5,8,7168]{2,1,0:T(8,128)(2,1)} %bitcast_dynamic-update-slice_fusion.2, bf16[8,7168]{1,0:T(8,128)(2,1)} %collective-permute-done.6), kind=kLoop, calls=%fused_computation.69 | loop fusion | bytes 229376
  31.1 1.5 %bitcast_dynamic-update-slice_fusion = bf16[5,8,7168]{2,1,0:T(8,128)(2,1)} fusion(bf16[5,8,7168]{2,1,0:T(8,128)(2,1)} %bitcast_dynamic-update-slice_fusion.1, bf16[8,7168]{1,0:T(8,128)(2,1)} %collective-permute-done.7), kind=kLoop, calls=%fused_computation.68 | loop fusion | bytes 229376 | tf_op jit(solution)/shard_map/stack | solution.py:64
  32.6 1.5 %collective-permute-start.8 = (bf16[5,8,7168]{2,1,0:T(8,128)(2,1)}, bf16[5,8,7168]{2,1,0:T(8,128)(2,1)S(1)}, u32[]{:S(2)}, u32[]{:S(2)}) collective-permute-start(bf16[5,8,7168]{2,1,0:T(8,128)(2,1)} %bitcast_dynamic-update-slice_fusion), channel_id=1, source_target_pairs={{0,2},{1,3},{2,0},{3,1},{4,6},{5,7},{6,4},{7,5},{8,10},{9,11},{10,... | collective-permute-start | bytes 1720328 | tf_op jit(solution)/shard_map/ppermute | solution.py:34
  35.6 1.5 %collective-permute-start.3 = (f32[2,1,32,513]{3,2,0,1:T(8,128)}, f32[2,1,32,513]{3,2,0,1:T(8,128)}, u32[]{:S(2)}, u32[]{:S(2)}) collective-permute-start(f32[2,1,32,513]{3,2,0,1:T(8,128)} %constant_dynamic-slice_fusion), channel_id=1, source_target_pairs={{0,2},{1,3},{2,0},{3,1},{4,6},{5,7},{6,4},{7,5},{8,10},{9,11},{10,... | collective-permute-start | bytes 393992 | tf_op jit(solution)/shard_map/ppermute | solution.py:143
  37.1 18.9 %collective-permute-done.19 = bf16[3,8,7168]{2,1,0:T(8,128)(2,1)S(1)} collective-permute-done((bf16[3,8,7168]{2,1,0:T(8,128)(2,1)S(1)}, bf16[3,8,7168]{2,1,0:T(8,128)(2,1)S(1)}, u32[]{:S(2)}, u32[]{:S(2)}) %collective-permute-start.19) | collective-permute-done | bytes 344096 | tf_op jit(solution)/shard_map/ppermute | solution.py:34
  56.2 1.6 %fusion.58 = (bf16[1,2,5,8,7168]{4,3,2,1,0:T(8,128)(2,1)}, bf16[2,5,8,7168]{3,2,1,0:T(8,128)(2,1)}) fusion(bf16[1,5,8,7168]{3,2,1,0:T(8,128)(2,1)S(1)} %bitcast.135, bf16[1,5,8,7168]{3,2,1,0:T(8,128)(2,1)S(1)} %bitcast.133), kind=kLoop, calls=%fused_computation.110 | loop fusion | flops 573440 | bytes 3440640 | tf_op jit(solution)/shard_map/stack | solution.py:35
  60.4 6.9 %fusion = f32[96,7168]{1,0:T(8,128)} fusion(bf16[1,256,7168]{2,1,0:T(8,128)(2,1)} %param.21, f32[96,256]{1,0:T(8,128)} %fusion.4, bf16[96,7168]{1,0:T(8,128)(2,1)S(1)} %bitcast.128, bf16[1,7168,256]{2,1,0:T(8,128)(2,1)} %param.19), kind=kOutput, calls=%fused_computation.1 | convolution fusion | flops 704790528 | bytes 11567104 | tf_op jit(solution)/shard_map/dot_general | solution.py:16
  67.3 3.2 %fusion.61 = (f32[48,7168]{1,0:T(8,128)}, f32[48,7168]{1,0:T(8,128)S(1)}) fusion(f32[96,7168]{1,0:T(8,128)} %fusion), kind=kLoop, calls=%fused_computation.113 | loop fusion | bytes 5505024 | tf_op jit(solution)/shard_map/slice | solution.py:39
  71.0 1.6 %pad_maximum_fusion = bf16[2,2,5,8,7168]{4,3,2,1,0:T(8,128)(2,1)S(1)} fusion(bf16[1,2,5,8,7168]{4,3,2,1,0:T(8,128)(2,1)} %bitcast.15, bf16[1,2,5,8,7168]{4,3,2,1,0:T(8,128)(2,1)S(1)} %copy-done.4), kind=kLoop, calls=%fused_computation.13 | loop fusion | flops 1146880 | bytes 4587520 | tf_op jit(solution)/shard_map/stack | solution.py:35
  72.6 1.4 %copy-done.1 = bf16[2,2,5,8,7168]{4,3,2,1,0:T(8,128)(2,1)} copy-done((bf16[2,2,5,8,7168]{4,3,2,1,0:T(8,128)(2,1)}, bf16[2,2,5,8,7168]{4,3,2,1,0:T(8,128)(2,1)S(1)}, u32[]{:S(2)}) %copy-start.1) | copy-done | bytes 2293784
  74.1 1.4 %fusion.6 = f32[160,256]{1,0:T(8,128)} fusion(bf16[160,7168]{1,0:T(8,128)(2,1)S(1)} %bitcast.125, bf16[1,7168,256]{2,1,0:T(8,128)(2,1)S(1)} %copy-done.3), kind=kOutput, calls=%fused_computation.7 | convolution fusion | flops 587202560 | bytes 6127616 | tf_op jit(solution)/shard_map/dot_general | solution.py:14
  75.5 8.6 %fusion.2 = f32[160,7168]{1,0:T(8,128)} fusion(bf16[1,256,7168]{2,1,0:T(8,128)(2,1)} %param.21, f32[160,256]{1,0:T(8,128)} %fusion.6, bf16[160,7168]{1,0:T(8,128)(2,1)} %bitcast.126, bf16[1,7168,256]{2,1,0:T(8,128)(2,1)} %param.19), kind=kOutput, calls=%fused_computation.3 | convolution fusion | flops 1174650880 | bytes 14385152 | tf_op jit(solution)/shard_map/dot_general | solution.py:16
  84.1 2.8 %fusion.60 = (f32[80,7168]{1,0:T(8,128)S(1)}, f32[80,7168]{1,0:T(8,128)S(1)}) fusion(f32[160,7168]{1,0:T(8,128)} %fusion.2), kind=kLoop, calls=%fused_computation.112 | loop fusion | bytes 9175040 | tf_op jit(solution)/shard_map/slice | solution.py:39
  87.0 1.5 %add.163 = f32[2,3,8,7168]{3,2,1,0:T(8,128)S(1)} add(f32[2,3,8,7168]{3,2,1,0:T(8,128)S(1)} %bitcast.130, f32[2,3,8,7168]{3,2,1,0:T(8,128)} %collective-permute-done.21) | non-fusion elementwise | flops 344064 | bytes 4128768 | tf_op jit(solution)/shard_map/add | solution.py:40
  88.5 1.6 %collective-permute-start.22 = (bf16[3,8,7168]{2,1,0:T(8,128)(2,1)S(1)}, bf16[3,8,7168]{2,1,0:T(8,128)(2,1)S(1)}, u32[]{:S(2)}, u32[]{:S(2)}) collective-permute-start(bf16[3,8,7168]{2,1,0:T(8,128)(2,1)S(1)} %fusion.26), channel_id=1, source_target_pairs={{0,2},{1,3},{2,0},{3,1},{4,6},{5,7},{6,4},{7,5},{8,10},{9,11},{10,... | collective-permute-start | bytes 1032200 | tf_op jit(solution)/shard_map/ppermute | solution.py:40
  91.1 7.9 %collective-permute-done.22 = bf16[3,8,7168]{2,1,0:T(8,128)(2,1)S(1)} collective-permute-done((bf16[3,8,7168]{2,1,0:T(8,128)(2,1)S(1)}, bf16[3,8,7168]{2,1,0:T(8,128)(2,1)S(1)}, u32[]{:S(2)}, u32[]{:S(2)}) %collective-permute-start.22) | collective-permute-done | bytes 344096 | tf_op jit(solution)/shard_map/ppermute | solution.py:40
  99.6 1.6 %collective-permute-start.11 = (bf16[5,8,7168]{2,1,0:T(8,128)(2,1)S(1)}, bf16[5,8,7168]{2,1,0:T(8,128)(2,1)S(1)}, u32[]{:S(2)}, u32[]{:S(2)}) collective-permute-start(bf16[5,8,7168]{2,1,0:T(8,128)(2,1)S(1)} %fusion.20), channel_id=1, source_target_pairs={{0,2},{1,3},{2,0},{3,1},{4,6},{5,7},{6,4},{7,5},{8,10},{9,11},{10,... | collective-permute-start | bytes 1720328 | tf_op jit(solution)/shard_map/ppermute | solution.py:40
  102.2 1.5 %collective-permute-start.25 = (bf16[8,7168]{1,0:T(8,128)(2,1)S(1)}, bf16[8,7168]{1,0:T(8,128)(2,1)S(1)}, u32[]{:S(2)}, u32[]{:S(2)}) collective-permute-start(bf16[8,7168]{1,0:T(8,128)(2,1)S(1)} %get-tuple-element.19), channel_id=1, source_target_pairs={{0,4},{4,8},{8,12},{12,16},{16,20},{20,24},{24,28},{28,0},{1,5},{5... | collective-permute-start | bytes 344072 | tf_op jit(solution)/shard_map/ppermute | solution.py:86
  103.7 10.5 %collective-permute-done.11 = bf16[5,8,7168]{2,1,0:T(8,128)(2,1)S(1)} collective-permute-done((bf16[5,8,7168]{2,1,0:T(8,128)(2,1)S(1)}, bf16[5,8,7168]{2,1,0:T(8,128)(2,1)S(1)}, u32[]{:S(2)}, u32[]{:S(2)}) %collective-permute-start.11) | collective-permute-done | bytes 573472 | tf_op jit(solution)/shard_map/ppermute | solution.py:40
  116.3 1.8 %collective-permute-start.14 = (bf16[8,7168]{1,0:T(8,128)(2,1)S(1)}, bf16[8,7168]{1,0:T(8,128)(2,1)S(1)}, u32[]{:S(2)}, u32[]{:S(2)}) collective-permute-start(bf16[8,7168]{1,0:T(8,128)(2,1)S(1)} %get-tuple-element.16), channel_id=1, source_target_pairs={{0,20},{4,24},{8,28},{12,0},{16,4},{20,8},{24,12},{28,16},{1,21},{... | collective-permute-start | bytes 344072 | tf_op jit(solution)/shard_map/ppermute | solution.py:86
  122.8 8.0 %collective-permute-done.15 = bf16[8,7168]{1,0:T(8,128)(2,1)S(1)} collective-permute-done((bf16[8,7168]{1,0:T(8,128)(2,1)S(1)}, bf16[8,7168]{1,0:T(8,128)(2,1)S(1)}, u32[]{:S(2)}, u32[]{:S(2)}) %collective-permute-start.15) | collective-permute-done | bytes 114720 | tf_op jit(solution)/shard_map/ppermute | solution.py:86
  (99 shorter events, 22.7 us)
Async XLA Ops:
  0.6 9.1 %copy-start = (bf16[2,1024,512]{2,1,0:T(8,128)(2,1)S(1)}, bf16[2,1024,512]{2,1,0:T(8,128)(2,1)}, u32[]{:S(2)}) copy-start(bf16[2,1024,512]{2,1,0:T(8,128)(2,1)} %param.13) | copy-start | bytes 6291460
  0.6 11.0 %copy-start.8 = (bf16[2,64,1024]{2,1,0:T(8,128)(2,1)S(1)}, bf16[2,64,1024]{2,1,0:T(8,128)(2,1)}, u32[]{:S(2)}) copy-start(bf16[2,64,1024]{2,1,0:T(8,128)(2,1)} %param.14) | copy-start | bytes 786436
  0.7 22.9 %collective-permute-start.4 = (bf16[8,7168]{1,0:T(8,128)(2,1)}, bf16[8,7168]{1,0:T(8,128)(2,1)}, u32[]{:S(2)}, u32[]{:S(2)}) collective-permute-start(bf16[8,7168]{1,0:T(8,128)(2,1)} %param.16), channel_id=1, source_target_pairs={{0,4},{4,8},{8,12},{12,16},{16,20},{20,24},{24,28},{28,0},{1,5},{5... | collective-permute-start | bytes 344072 | tf_op jit(solution)/shard_map/ppermute | solution.py:61
  3.7 22.9 %collective-permute-start.5 = (bf16[8,7168]{1,0:T(8,128)(2,1)}, bf16[8,7168]{1,0:T(8,128)(2,1)}, u32[]{:S(2)}, u32[]{:S(2)}) collective-permute-start(bf16[8,7168]{1,0:T(8,128)(2,1)} %param.16), channel_id=1, source_target_pairs={{0,8},{4,12},{8,16},{12,20},{16,24},{20,28},{24,0},{28,4},{1,9},{5... | collective-permute-start | bytes 344072 | tf_op jit(solution)/shard_map/ppermute | solution.py:61
  5.3 24.3 %collective-permute-start.6 = (bf16[8,7168]{1,0:T(8,128)(2,1)}, bf16[8,7168]{1,0:T(8,128)(2,1)}, u32[]{:S(2)}, u32[]{:S(2)}) collective-permute-start(bf16[8,7168]{1,0:T(8,128)(2,1)} %param.16), channel_id=1, source_target_pairs={{0,12},{4,16},{8,20},{12,24},{16,28},{20,0},{24,4},{28,8},{1,13},{... | collective-permute-start | bytes 344072 | tf_op jit(solution)/shard_map/ppermute | solution.py:61
  7.8 23.3 %collective-permute-start.7 = (bf16[8,7168]{1,0:T(8,128)(2,1)}, bf16[8,7168]{1,0:T(8,128)(2,1)}, u32[]{:S(2)}, u32[]{:S(2)}) collective-permute-start(bf16[8,7168]{1,0:T(8,128)(2,1)} %param.16), channel_id=1, source_target_pairs={{0,16},{4,20},{8,24},{12,28},{16,0},{20,4},{24,8},{28,12},{1,17},{... | collective-permute-start | bytes 344072 | tf_op jit(solution)/shard_map/ppermute | solution.py:61
  12.1 2.5 %collective-permute-start = (f32[2,128]{1,0:T(2,128)S(1)}, f32[2,128]{1,0:T(2,128)S(1)}, u32[]{:S(2)}, u32[]{:S(2)}) collective-permute-start(f32[2,128]{1,0:T(2,128)S(1)} %get-tuple-element.31), channel_id=1, source_target_pairs={{0,1},{1,0},{2,3},{3,2},{4,5},{5,4},{6,7},{7,6},{8,9},{9,8},{10,11... | collective-permute-start | bytes 3080 | tf_op jit(solution)/shard_map/ppermute | solution.py:130
  14.6 3.6 %collective-permute-start.1 = (f32[2,128]{1,0:T(2,128)S(1)}, f32[2,128]{1,0:T(2,128)S(1)}, u32[]{:S(2)}, u32[]{:S(2)}) collective-permute-start(f32[2,128]{1,0:T(2,128)S(1)} %max.6), channel_id=1, source_target_pairs={{0,2},{1,3},{2,0},{3,1},{4,6},{5,7},{6,4},{7,5},{8,10},{9,11},{10,... | collective-permute-start | bytes 3080 | tf_op jit(solution)/shard_map/ppermute | solution.py:130
  18.2 15.9 %collective-permute-start.16 = (bf16[8,7168]{1,0:T(8,128)(2,1)S(1)}, bf16[8,7168]{1,0:T(8,128)(2,1)S(1)}, u32[]{:S(2)}, u32[]{:S(2)}) collective-permute-start(bf16[8,7168]{1,0:T(8,128)(2,1)S(1)} %copy-done.9), channel_id=1, source_target_pairs={{0,20},{4,24},{8,28},{12,0},{16,4},{20,8},{24,12},{28,16},{1,21},{... | collective-permute-start | bytes 344072 | tf_op jit(solution)/shard_map/ppermute | solution.py:61
  23.6 10.5 %collective-permute-start.17 = (bf16[8,7168]{1,0:T(8,128)(2,1)S(1)}, bf16[8,7168]{1,0:T(8,128)(2,1)S(1)}, u32[]{:S(2)}, u32[]{:S(2)}) collective-permute-start(bf16[8,7168]{1,0:T(8,128)(2,1)S(1)} %copy-done.9), channel_id=1, source_target_pairs={{0,24},{4,28},{8,0},{12,4},{16,8},{20,12},{24,16},{28,20},{1,25},{... | collective-permute-start | bytes 344072 | tf_op jit(solution)/shard_map/ppermute | solution.py:61
  26.6 7.6 %collective-permute-start.18 = (bf16[8,7168]{1,0:T(8,128)(2,1)S(1)}, bf16[8,7168]{1,0:T(8,128)(2,1)S(1)}, u32[]{:S(2)}, u32[]{:S(2)}) collective-permute-start(bf16[8,7168]{1,0:T(8,128)(2,1)S(1)} %copy-done.9), channel_id=1, source_target_pairs={{0,28},{4,0},{8,4},{12,8},{16,12},{20,16},{24,20},{28,24},{1,29},{... | collective-permute-start | bytes 344072 | tf_op jit(solution)/shard_map/ppermute | solution.py:61
  29.5 5.3 %collective-permute-start.2 = (f32[2,2,32,513]{3,2,0,1:T(8,128)S(1)}, f32[2,2,32,513]{3,2,0,1:T(8,128)S(1)}, u32[]{:S(2)}, u32[]{:S(2)}) collective-permute-start(f32[2,2,32,513]{3,2,0,1:T(8,128)S(1)} %bitcast.137), channel_id=1, source_target_pairs={{0,1},{1,0},{2,3},{3,2},{4,5},{5,4},{6,7},{7,6},{8,9},{9,8},{10,11... | collective-permute-start | bytes 787976 | tf_op jit(solution)/shard_map/ppermute | solution.py:143
  32.6 23.5 %copy-start.7 = (bf16[5,8,7168]{2,1,0:T(8,128)(2,1)S(1)}, bf16[5,8,7168]{2,1,0:T(8,128)(2,1)}, u32[]{:S(2)}) copy-start(bf16[5,8,7168]{2,1,0:T(8,128)(2,1)} %bitcast_dynamic-update-slice_fusion) | copy-start | bytes 1720324
  32.6 23.5 %collective-permute-start.8 = (bf16[5,8,7168]{2,1,0:T(8,128)(2,1)}, bf16[5,8,7168]{2,1,0:T(8,128)(2,1)S(1)}, u32[]{:S(2)}, u32[]{:S(2)}) collective-permute-start(bf16[5,8,7168]{2,1,0:T(8,128)(2,1)} %bitcast_dynamic-update-slice_fusion), channel_id=1, source_target_pairs={{0,2},{1,3},{2,0},{3,1},{4,6},{5,7},{6,4},{7,5},{8,10},{9,11},{10,... | collective-permute-start | bytes 1720328 | tf_op jit(solution)/shard_map/ppermute | solution.py:34
  34.2 21.8 %collective-permute-start.19 = (bf16[3,8,7168]{2,1,0:T(8,128)(2,1)S(1)}, bf16[3,8,7168]{2,1,0:T(8,128)(2,1)S(1)}, u32[]{:S(2)}, u32[]{:S(2)}) collective-permute-start(bf16[3,8,7168]{2,1,0:T(8,128)(2,1)S(1)} %get-tuple-element.22), channel_id=1, source_target_pairs={{0,2},{1,3},{2,0},{3,1},{4,6},{5,7},{6,4},{7,5},{8,10},{9,11},{10,... | collective-permute-start | bytes 1032200 | tf_op jit(solution)/shard_map/ppermute | solution.py:34
  34.9 21.1 %copy-start.5 = (f32[2,2,32,513]{3,2,0,1:T(8,128)}, f32[2,2,32,513]{3,2,0,1:T(8,128)S(1)}, u32[]{:S(2)}) copy-start(f32[2,2,32,513]{3,2,0,1:T(8,128)S(1)} %bitcast_add_fusion) | copy-start | bytes 787972
  35.6 54.5 %collective-permute-start.3 = (f32[2,1,32,513]{3,2,0,1:T(8,128)}, f32[2,1,32,513]{3,2,0,1:T(8,128)}, u32[]{:S(2)}, u32[]{:S(2)}) collective-permute-start(f32[2,1,32,513]{3,2,0,1:T(8,128)} %constant_dynamic-slice_fusion), channel_id=1, source_target_pairs={{0,2},{1,3},{2,0},{3,1},{4,6},{5,7},{6,4},{7,5},{8,10},{9,11},{10,... | collective-permute-start | bytes 393992 | tf_op jit(solution)/shard_map/ppermute | solution.py:143
  56.1 2.2 %collective-permute-start.20 = (bf16[2,3,8,7168]{3,2,1,0:T(8,128)(2,1)S(1)}, bf16[2,3,8,7168]{3,2,1,0:T(8,128)(2,1)S(1)}, u32[]{:S(2)}, u32[]{:S(2)}) collective-permute-start(bf16[2,3,8,7168]{3,2,1,0:T(8,128)(2,1)S(1)} %get-tuple-element.11), channel_id=1, source_target_pairs={{0,1},{1,0},{2,3},{3,2},{4,5},{5,4},{6,7},{7,6},{8,9},{9,8},{10,11... | collective-permute-start | bytes 2064392 | tf_op jit(solution)/shard_map/ppermute | solution.py:34
  57.8 13.2 %collective-permute-start.9 = (bf16[2,5,8,7168]{3,2,1,0:T(8,128)(2,1)}, bf16[2,5,8,7168]{3,2,1,0:T(8,128)(2,1)}, u32[]{:S(2)}, u32[]{:S(2)}) collective-permute-start(bf16[2,5,8,7168]{3,2,1,0:T(8,128)(2,1)} %get-tuple-element.9), channel_id=1, source_target_pairs={{0,1},{1,0},{2,3},{3,2},{4,5},{5,4},{6,7},{7,6},{8,9},{9,8},{10,11... | collective-permute-start | bytes 3440648 | tf_op jit(solution)/shard_map/ppermute | solution.py:34
  70.5 16.4 %collective-permute-start.21 = (f32[2,3,8,7168]{3,2,1,0:T(8,128)}, f32[2,3,8,7168]{3,2,1,0:T(8,128)}, u32[]{:S(2)}, u32[]{:S(2)}) collective-permute-start(f32[2,3,8,7168]{3,2,1,0:T(8,128)} %bitcast.43), channel_id=1, source_target_pairs={{0,1},{1,0},{2,3},{3,2},{4,5},{5,4},{6,7},{7,6},{8,9},{9,8},{10,11... | collective-permute-start | bytes 4128776 | tf_op jit(solution)/shard_map/ppermute | solution.py:40
  86.9 12.3 %collective-permute-start.10 = (f32[2,5,8,7168]{3,2,1,0:T(8,128)S(1)}, f32[2,5,8,7168]{3,2,1,0:T(8,128)S(1)}, u32[]{:S(2)}, u32[]{:S(2)}) collective-permute-start(f32[2,5,8,7168]{3,2,1,0:T(8,128)S(1)} %bitcast.131), channel_id=1, source_target_pairs={{0,1},{1,0},{2,3},{3,2},{4,5},{5,4},{6,7},{7,6},{8,9},{9,8},{10,11... | collective-permute-start | bytes 6881288 | tf_op jit(solution)/shard_map/ppermute | solution.py:40
  88.5 10.5 %collective-permute-start.22 = (bf16[3,8,7168]{2,1,0:T(8,128)(2,1)S(1)}, bf16[3,8,7168]{2,1,0:T(8,128)(2,1)S(1)}, u32[]{:S(2)}, u32[]{:S(2)}) collective-permute-start(bf16[3,8,7168]{2,1,0:T(8,128)(2,1)S(1)} %fusion.26), channel_id=1, source_target_pairs={{0,2},{1,3},{2,0},{3,1},{4,6},{5,7},{6,4},{7,5},{8,10},{9,11},{10,... | collective-permute-start | bytes 1032200 | tf_op jit(solution)/shard_map/ppermute | solution.py:40
  99.6 31.2 %copy-start.11 = (f32[8]{0:T(128)S(1)}, f32[8]{0:T(128)}, u32[]{:S(2)}) copy-start(f32[8]{0:T(128)} %get-tuple-element.29) | copy-start | bytes 100
  99.6 31.2 %copy-start.12 = (f32[8]{0:T(128)S(1)}, f32[8]{0:T(128)}, u32[]{:S(2)}) copy-start(f32[8]{0:T(128)} %get-tuple-element.30) | copy-start | bytes 100
  99.6 14.6 %collective-permute-start.11 = (bf16[5,8,7168]{2,1,0:T(8,128)(2,1)S(1)}, bf16[5,8,7168]{2,1,0:T(8,128)(2,1)S(1)}, u32[]{:S(2)}, u32[]{:S(2)}) collective-permute-start(bf16[5,8,7168]{2,1,0:T(8,128)(2,1)S(1)} %fusion.20), channel_id=1, source_target_pairs={{0,2},{1,3},{2,0},{3,1},{4,6},{5,7},{6,4},{7,5},{8,10},{9,11},{10,... | collective-permute-start | bytes 1720328 | tf_op jit(solution)/shard_map/ppermute | solution.py:40
  101.2 15.1 %collective-permute-start.23 = (bf16[8,7168]{1,0:T(8,128)(2,1)S(1)}, bf16[8,7168]{1,0:T(8,128)(2,1)S(1)}, u32[]{:S(2)}, u32[]{:S(2)}) collective-permute-start(bf16[8,7168]{1,0:T(8,128)(2,1)S(1)} %get-tuple-element.18), channel_id=1, source_target_pairs={{0,12},{4,16},{8,20},{12,24},{16,28},{20,0},{24,4},{28,8},{1,13},{... | collective-permute-start | bytes 344072 | tf_op jit(solution)/shard_map/ppermute | solution.py:86
  102.0 16.1 %collective-permute-start.24 = (bf16[8,7168]{1,0:T(8,128)(2,1)S(1)}, bf16[8,7168]{1,0:T(8,128)(2,1)S(1)}, u32[]{:S(2)}, u32[]{:S(2)}) collective-permute-start(bf16[8,7168]{1,0:T(8,128)(2,1)S(1)} %get-tuple-element.20), channel_id=1, source_target_pairs={{0,8},{4,12},{8,16},{12,20},{16,24},{20,28},{24,0},{28,4},{1,9},{5... | collective-permute-start | bytes 344072 | tf_op jit(solution)/shard_map/ppermute | solution.py:86
  102.2 17.8 %collective-permute-start.25 = (bf16[8,7168]{1,0:T(8,128)(2,1)S(1)}, bf16[8,7168]{1,0:T(8,128)(2,1)S(1)}, u32[]{:S(2)}, u32[]{:S(2)}) collective-permute-start(bf16[8,7168]{1,0:T(8,128)(2,1)S(1)} %get-tuple-element.19), channel_id=1, source_target_pairs={{0,4},{4,8},{8,12},{12,16},{16,20},{20,24},{24,28},{28,0},{1,5},{5... | collective-permute-start | bytes 344072 | tf_op jit(solution)/shard_map/ppermute | solution.py:86
  114.4 6.1 %collective-permute-start.12 = (bf16[8,7168]{1,0:T(8,128)(2,1)S(1)}, bf16[8,7168]{1,0:T(8,128)(2,1)S(1)}, u32[]{:S(2)}, u32[]{:S(2)}) collective-permute-start(bf16[8,7168]{1,0:T(8,128)(2,1)S(1)} %get-tuple-element.14), channel_id=1, source_target_pairs={{0,28},{4,0},{8,4},{12,8},{16,12},{20,16},{24,20},{28,24},{1,29},{... | collective-permute-start | bytes 344072 | tf_op jit(solution)/shard_map/ppermute | solution.py:86
  114.9 6.7 %collective-permute-start.13 = (bf16[8,7168]{1,0:T(8,128)(2,1)S(1)}, bf16[8,7168]{1,0:T(8,128)(2,1)S(1)}, u32[]{:S(2)}, u32[]{:S(2)}) collective-permute-start(bf16[8,7168]{1,0:T(8,128)(2,1)S(1)} %get-tuple-element.17), channel_id=1, source_target_pairs={{0,24},{4,28},{8,0},{12,4},{16,8},{20,12},{24,16},{28,20},{1,25},{... | collective-permute-start | bytes 344072 | tf_op jit(solution)/shard_map/ppermute | solution.py:86
  116.3 6.5 %collective-permute-start.14 = (bf16[8,7168]{1,0:T(8,128)(2,1)S(1)}, bf16[8,7168]{1,0:T(8,128)(2,1)S(1)}, u32[]{:S(2)}, u32[]{:S(2)}) collective-permute-start(bf16[8,7168]{1,0:T(8,128)(2,1)S(1)} %get-tuple-element.16), channel_id=1, source_target_pairs={{0,20},{4,24},{8,28},{12,0},{16,4},{20,8},{24,12},{28,16},{1,21},{... | collective-permute-start | bytes 344072 | tf_op jit(solution)/shard_map/ppermute | solution.py:86
  118.0 12.7 %collective-permute-start.15 = (bf16[8,7168]{1,0:T(8,128)(2,1)S(1)}, bf16[8,7168]{1,0:T(8,128)(2,1)S(1)}, u32[]{:S(2)}, u32[]{:S(2)}) collective-permute-start(bf16[8,7168]{1,0:T(8,128)(2,1)S(1)} %get-tuple-element.15), channel_id=1, source_target_pairs={{0,16},{4,20},{8,24},{12,28},{16,0},{20,4},{24,8},{28,12},{1,17},{... | collective-permute-start | bytes 344072 | tf_op jit(solution)/shard_map/ppermute | solution.py:86
  (9 other events, 25.3 us)

commit v14 on v11

--- a/solution.py
+++ b/solution.py
@@ -69,9 +69,16 @@
     result = jnp.zeros((tok_count, model_width), jnp.float32)
     for i in range(n_local):
         chosen = jnp.take(wmat, owners * n_local + i, axis=1)
+        both = jnp.concatenate([block.reshape(-1, model_width) for block in blocks], axis=0)
+        gate_value = jnp.dot(both, w_gate[i], preferred_element_type=jnp.float32)
+        upward = jnp.dot(both, w_up[i], preferred_element_type=jnp.float32)
+        hidden = (jax.nn.silu(gate_value) * upward).astype(jnp.bfloat16)
+        offset = 0
         for c in range(n_chunks):
             block = blocks[c]
-            part = expert_part(block.reshape(-1, model_width), w_gate[i], w_up[i], w_down[i])
+            count = block.size // model_width
+            part = jnp.dot(hidden[offset : offset + count], w_down[i], preferred_element_type=jnp.float32)
+            offset += count
             part = part.reshape(block.shape[:-1] + (model_width,))
             for bit in reversed(bits):
                 wire = jnp.bfloat16 if bit == bits[0] else None

time: 119 us -> 98.2 us (0.83)
  matrix products: 20.1 us -> 7.13 us
  local copies, waits for them, and re-layouts: 12.8 us -> 4.81 us
  waiting for transfers between devices: 38 us -> 44.1 us
  other arithmetic: 10.5 us -> 5.73 us
    dot_general x4, matrix products: 16.5 us -> 3.58 us  [the longest x2 1.32 us: routed_experts(): jnp.dot(hidden[offset:offset + count], w_down[i], preferred_element_type=...]
    slice x2, local copies, waits for them, and re-layouts: 6.7 us -> 0.66 us  [bit_reduce(): sent = x[1] if wire is None else x[1].astype(wire)]
    ppermute x4, waiting for transfers between devices: 12.7 us -> 16.4 us  [bit_reduce(): lax.ppermute(sent, axis, [(i, i ^ bit) for i in range(n)]).astype(x.dtype)]
    ppermute x4, waiting for transfers between devices: 13.3 us -> 15.8 us  [bit_gather(): other = lax.ppermute(x, axis, [(i, i ^ bit) for i in range(n)])]
    another operation x6, other arithmetic: 4.07 us -> 1.8 us  [bit_gather(): return jnp.stack([x, other])]
    add x2, other arithmetic: 1.95 us -> 0.37 us  [bit_reduce(): x[0]]
    ppermute x4, starting transfers between devices: 3.04 us -> 1.84 us  [bit_reduce(): lax.ppermute(sent, axis, [(i, i ^ bit) for i in range(n)]).astype(x.dtype)]
    unnamed x28 -> x20, local copies, waits for them, and re-layouts: 3.8 us -> 3.02 us
  transfers between devices with their start and end apart: 26 -> 26, of which waited for: 9 -> 12; matrix products, arithmetic and copies ran while one was open for 33% -> 14% of each run, Pallas kernels for 0% -> 0%
where the time goes in v14:
time: 98.2 us; the launch traced here: 97.1 us
  waiting for transfers between devices  44.1 us (45%)
  starting transfers between devices  34.4 us (35%)
  matrix products  7.13 us (7%)
  other arithmetic  5.73 us (6%)
  local copies, waits for them, and re-layouts  4.81 us (5%)
    ppermute x4, waiting for transfers between devices, bit_reduce(): lax.ppermute(sent, axis, [(i, i ^ bit) for i in range(n)]).astype(x.dtype)  16.4 us
    ppermute x4, waiting for transfers between devices, bit_gather(): other = lax.ppermute(x, axis, [(i, i ^ bit) for i in range(n)])  15.8 us
    ppermute x7, starting transfers between devices, routed_experts(): lax.ppermute(expert_rows[kk], 'attn', [(s, (s - k) % n_attn) for s in ran...  13.6 us
    ppermute x7, starting transfers between devices, routed_experts(): lax.ppermute(tokens, 'attn', [(s, (s + k) % n_attn) for s in range(n_attn)])  12.5 us
    ppermute x7, waiting for transfers between devices, routed_experts(): lax.ppermute(expert_rows[kk], 'attn', [(s, (s - k) % n_attn) for s in ran...  5.54 us
    ppermute x7, waiting for transfers between devices, routed_experts(): lax.ppermute(tokens, 'attn', [(s, (s + k) % n_attn) for s in range(n_attn)])  4.31 us
    ppermute x4, starting transfers between devices, bit_gather(): other = lax.ppermute(x, axis, [(i, i ^ bit) for i in range(n)])  3.26 us
    unnamed x20, local copies, waits for them, and re-layouts  3.02 us
  transfers between devices with their start and end apart: 26, of which 12 were waited for; matrix products, arithmetic and copies ran while one was open for 14% of the time, Pallas kernels for 0%

profile of v14, /device:TPU:0, one launch (start us, length us, event | category | flops | bytes accessed | tf_op | source)
XLA Modules:
  0.0 97.1 jit_solution(7712080734423355156)
XLA Ops:
  0.7 6.1 %collective-permute-start.12 = (bf16[8,7168]{1,0:T(8,128)(2,1)}, bf16[8,7168]{1,0:T(8,128)(2,1)}, u32[]{:S(2)}, u32[]{:S(2)}) collective-permute-start(bf16[8,7168]{1,0:T(8,128)(2,1)} %param.16), channel_id=1, source_target_pairs={{0,28},{4,0},{8,4},{12,8},{16,12},{20,16},{24,20},{28,24},{1,29},{... | collective-permute-start | bytes 344072 | tf_op jit(solution)/shard_map/ppermute | solution.py:60
  7.2 3.0 %collective-permute-start.9 = (bf16[8,7168]{1,0:T(8,128)(2,1)}, bf16[8,7168]{1,0:T(8,128)(2,1)}, u32[]{:S(2)}, u32[]{:S(2)}) collective-permute-start(bf16[8,7168]{1,0:T(8,128)(2,1)} %param.16), channel_id=1, source_target_pairs={{0,16},{4,20},{8,24},{12,28},{16,0},{20,4},{24,8},{28,12},{1,17},{... | collective-permute-start | bytes 344072 | tf_op jit(solution)/shard_map/ppermute | solution.py:60
  10.2 1.8 %fusion.54 = f32[2,128,1024]{2,1,0:T(8,128)S(1)} fusion(bf16[2,128,512]{2,1,0:T(8,128)(2,1)} %param.11, bf16[2,1024,512]{2,1,0:T(8,128)(2,1)S(1)} %copy-done), kind=kOutput, calls=%fused_computation.108 | convolution fusion | flops 268435456 | bytes 3407872 | tf_op jit(solution)/shard_map/rhl,rpl->rhp/dot_general | solution.py:114
  13.8 1.6 %collective-permute-start.1 = (f32[2,128]{1,0:T(2,128)S(1)}, f32[2,128]{1,0:T(2,128)S(1)}, u32[]{:S(2)}, u32[]{:S(2)}) collective-permute-start(f32[2,128]{1,0:T(2,128)S(1)} %max.6), channel_id=1, source_target_pairs={{0,2},{1,3},{2,0},{3,1},{4,6},{5,7},{6,4},{7,5},{8,10},{9,11},{10,... | collective-permute-start | bytes 3080 | tf_op jit(solution)/shard_map/ppermute | solution.py:136
  15.3 2.1 %collective-permute-done.1 = f32[2,128]{1,0:T(2,128)S(1)} collective-permute-done((f32[2,128]{1,0:T(2,128)S(1)}, f32[2,128]{1,0:T(2,128)S(1)}, u32[]{:S(2)}, u32[]{:S(2)}) %collective-permute-start.1) | collective-permute-done | bytes 1056 | tf_op jit(solution)/shard_map/ppermute | solution.py:136
  17.4 1.4 %broadcast_multiply_fusion = f32[2,128,512]{2,1,0:T(8,128)} fusion(f32[2,128]{1,0:T(2,128)S(1)} %get-tuple-element.3, bf16[2,1024,512]{2,1,0:T(8,128)(2,1)S(1)} %copy-done, f32[2,128,1024]{2,1,0:T(8,128)S(1)} %get-tuple-element.34, f32[2,128]{1,0:T(2,128)S(1)} %get-tuple-element.33, pred[2,1024]{1,0:T(4,128)(4,1)S(1)} %broadcast_compare_fusion), kind=kOutput, calls=%fused_computation.45 | convolution fusion | flops 269352960 | bytes 3674112 | tf_op jit(solution)/shard_map/rhp,rpl->rhl/dot_general | solution.py:125
  19.0 1.1 %fusion.24 = (f32[2,2,1,32,513]{4,3,2,1,0:T(8,128)S(1)}, f32[2,2,1,32,513]{4,3,2,1,0:T(8,128)S(1)}) fusion(s32[]{:T(128)S(6)} %select_n.81, f32[2,2,2,32,512]{4,3,2,1,0:T(8,128)} %bitcast.109, f32[2,2,2,32,1]{4,3,2,1,0:T(8,128)S(1)} %concatenate.15, s32[]{:T(128)S(6)} %select_n.82), kind=kLoop, calls=%fused_computation.41 | loop fusion | flops 131328 | bytes 1050632 | tf_op jit(solution)/shard_map/concatenate | solution.py:140
  20.1 1.9 %collective-permute-start.5 = (bf16[8,7168]{1,0:T(8,128)(2,1)S(1)}, bf16[8,7168]{1,0:T(8,128)(2,1)S(1)}, u32[]{:S(2)}, u32[]{:S(2)}) collective-permute-start(bf16[8,7168]{1,0:T(8,128)(2,1)S(1)} %copy-done.3), channel_id=1, source_target_pairs={{0,8},{4,12},{8,16},{12,20},{16,24},{20,28},{24,0},{28,4},{1,9},{5... | collective-permute-start | bytes 344072 | tf_op jit(solution)/shard_map/ppermute | solution.py:60
  22.1 1.1 %collective-permute-start.4 = (bf16[8,7168]{1,0:T(8,128)(2,1)S(1)}, bf16[8,7168]{1,0:T(8,128)(2,1)S(1)}, u32[]{:S(2)}, u32[]{:S(2)}) collective-permute-start(bf16[8,7168]{1,0:T(8,128)(2,1)S(1)} %copy-done.3), channel_id=1, source_target_pairs={{0,4},{4,8},{8,12},{12,16},{16,20},{20,24},{24,28},{28,0},{1,5},{5... | collective-permute-start | bytes 344072 | tf_op jit(solution)/shard_map/ppermute | solution.py:60
  23.2 1.1 %fusion.48 = (bf16[1,4,8,7168]{3,2,1,0:T(8,128)(2,1)S(1)}, bf16[4,8,7168]{2,1,0:T(8,128)(2,1)S(1)}) fusion(bf16[1,8,7168]{2,1,0:T(8,128)(2,1)} %bitcast.19, bf16[1,8,7168]{2,1,0:T(8,128)(2,1)} %bitcast.18, bf16[1,8,7168]{2,1,0:T(8,128)(2,1)} %bitcast.17, bf16[1,8,7168]{2,1,0:T(8,128)(2,1)} %bitcast.16), kind=kLoop, calls=%fused_computation.102 | loop fusion | flops 688128 | bytes 1376256 | tf_op jit(solution)/shard_map/stack | solution.py:35
  24.3 1.6 %collective-permute-start.13 = (bf16[4,8,7168]{2,1,0:T(8,128)(2,1)S(1)}, bf16[4,8,7168]{2,1,0:T(8,128)(2,1)S(1)}, u32[]{:S(2)}, u32[]{:S(2)}) collective-permute-start(bf16[4,8,7168]{2,1,0:T(8,128)(2,1)S(1)} %get-tuple-element.24), channel_id=1, source_target_pairs={{0,2},{1,3},{2,0},{3,1},{4,6},{5,7},{6,4},{7,5},{8,10},{9,11},{10,... | collective-permute-start | bytes 1376264 | tf_op jit(solution)/shard_map/ppermute | solution.py:34
  25.9 1.8 %collective-permute-done.5 = bf16[8,7168]{1,0:T(8,128)(2,1)S(1)} collective-permute-done((bf16[8,7168]{1,0:T(8,128)(2,1)S(1)}, bf16[8,7168]{1,0:T(8,128)(2,1)S(1)}, u32[]{:S(2)}, u32[]{:S(2)}) %collective-permute-start.5) | collective-permute-done | bytes 114720 | tf_op jit(solution)/shard_map/ppermute | solution.py:60
  27.7 2.5 %collective-permute-done.4 = bf16[8,7168]{1,0:T(8,128)(2,1)S(1)} collective-permute-done((bf16[8,7168]{1,0:T(8,128)(2,1)S(1)}, bf16[8,7168]{1,0:T(8,128)(2,1)S(1)}, u32[]{:S(2)}, u32[]{:S(2)}) %collective-permute-start.4) | collective-permute-done | bytes 114720 | tf_op jit(solution)/shard_map/ppermute | solution.py:60
  30.3 1.6 %collective-permute-start.7 = (bf16[4,8,7168]{2,1,0:T(8,128)(2,1)S(1)}, bf16[4,8,7168]{2,1,0:T(8,128)(2,1)S(1)}, u32[]{:S(2)}, u32[]{:S(2)}) collective-permute-start(bf16[4,8,7168]{2,1,0:T(8,128)(2,1)S(1)} %get-tuple-element.22), channel_id=1, source_target_pairs={{0,2},{1,3},{2,0},{3,1},{4,6},{5,7},{6,4},{7,5},{8,10},{9,11},{10,... | collective-permute-start | bytes 1376264 | tf_op jit(solution)/shard_map/ppermute | solution.py:34
  31.9 5.8 %collective-permute-done.13 = bf16[4,8,7168]{2,1,0:T(8,128)(2,1)S(1)} collective-permute-done((bf16[4,8,7168]{2,1,0:T(8,128)(2,1)S(1)}, bf16[4,8,7168]{2,1,0:T(8,128)(2,1)S(1)}, u32[]{:S(2)}, u32[]{:S(2)}) %collective-permute-start.13) | collective-permute-done | bytes 458784 | tf_op jit(solution)/shard_map/ppermute | solution.py:34
  37.9 9.2 %collective-permute-done.7 = bf16[4,8,7168]{2,1,0:T(8,128)(2,1)S(1)} collective-permute-done((bf16[4,8,7168]{2,1,0:T(8,128)(2,1)S(1)}, bf16[4,8,7168]{2,1,0:T(8,128)(2,1)S(1)}, u32[]{:S(2)}, u32[]{:S(2)}) %collective-permute-start.7) | collective-permute-done | bytes 458784 | tf_op jit(solution)/shard_map/ppermute | solution.py:34
  47.4 1.6 %collective-permute-start.3 = (f32[2,1,32,513]{3,2,0,1:T(8,128)S(1)}, f32[2,1,32,513]{3,2,0,1:T(8,128)S(1)}, u32[]{:S(2)}, u32[]{:S(2)}) collective-permute-start(f32[2,1,32,513]{3,2,0,1:T(8,128)S(1)} %constant_dynamic-slice_fusion), channel_id=1, source_target_pairs={{0,2},{1,3},{2,0},{3,1},{4,6},{5,7},{6,4},{7,5},{8,10},{9,11},{10,... | collective-permute-start | bytes 393992 | tf_op jit(solution)/shard_map/ppermute | solution.py:149
  50.0 1.2 %copy-done.8 = bf16[1,7168,256]{2,1,0:T(8,128)(2,1)S(1)} copy-done((bf16[1,7168,256]{2,1,0:T(8,128)(2,1)S(1)}, bf16[1,7168,256]{2,1,0:T(8,128)(2,1)}, u32[]{:S(2)}) %copy-start.8) | copy-done | bytes 3670040
  51.2 1.1 %fusion.6 = f32[256,256]{1,0:T(8,128)S(1)} fusion(bf16[1,7168,256]{2,1,0:T(8,128)(2,1)S(1)} %copy-done.8, bf16[128,7168]{1,0:T(8,128)(2,1)S(1)} %bitcast.112, bf16[128,7168]{1,0:T(8,128)(2,1)S(1)} %bitcast.114), kind=kOutput, calls=%fused_computation.8 | convolution fusion | flops 946864128 | bytes 7602176 | tf_op jit(solution)/shard_map/dot_general | solution.py:73
  53.2 1.1 %multiply_convert_fusion = bf16[256,256]{1,0:T(8,128)(2,1)S(1)} fusion(f32[256,256]{1,0:T(8,128)S(1)} %fusion.6, bf16[1,7168,256]{2,1,0:T(8,128)(2,1)S(1)} %copy-done.9, bf16[128,7168]{1,0:T(8,128)(2,1)S(1)} %bitcast.113, bf16[128,7168]{1,0:T(8,128)(2,1)S(1)} %bitcast.115), kind=kOutput, calls=%fused_computation.44 | convolution fusion | flops 947257344 | bytes 7733248 | tf_op jit(solution)/shard_map/dot_general | solution.py:74
  54.3 0.9 copy-done.1
  58.0 2.8 %collective-permute-done.20 = f32[2,4,8,7168]{3,2,1,0:T(8,128)S(1)} collective-permute-done((f32[2,4,8,7168]{3,2,1,0:T(8,128)S(1)}, f32[2,4,8,7168]{3,2,1,0:T(8,128)S(1)}, u32[]{:S(2)}, u32[]{:S(2)}) %collective-permute-start.20) | collective-permute-done | bytes 1835040 | tf_op jit(solution)/shard_map/ppermute | solution.py:40
  61.6 1.8 %collective-permute-done.15 = f32[2,4,8,7168]{3,2,1,0:T(8,128)S(1)} collective-permute-done((f32[2,4,8,7168]{3,2,1,0:T(8,128)S(1)}, f32[2,4,8,7168]{3,2,1,0:T(8,128)S(1)}, u32[]{:S(2)}, u32[]{:S(2)}) %collective-permute-start.15) | collective-permute-done | bytes 1835040 | tf_op jit(solution)/shard_map/ppermute | solution.py:40
  64.2 10.2 %collective-permute-done.21 = bf16[4,8,7168]{2,1,0:T(8,128)(2,1)S(1)} collective-permute-done((bf16[4,8,7168]{2,1,0:T(8,128)(2,1)S(1)}, bf16[4,8,7168]{2,1,0:T(8,128)(2,1)S(1)}, u32[]{:S(2)}, u32[]{:S(2)}) %collective-permute-start.21) | collective-permute-done | bytes 458784 | tf_op jit(solution)/shard_map/ppermute | solution.py:40
  74.6 2.0 %collective-permute-start.25 = (bf16[8,7168]{1,0:T(8,128)(2,1)S(1)}, bf16[8,7168]{1,0:T(8,128)(2,1)S(1)}, u32[]{:S(2)}, u32[]{:S(2)}) collective-permute-start(bf16[8,7168]{1,0:T(8,128)(2,1)S(1)} %get-tuple-element.18), channel_id=1, source_target_pairs={{0,4},{4,8},{8,12},{12,16},{16,20},{20,24},{24,28},{28,0},{1,5},{5... | collective-permute-start | bytes 344072 | tf_op jit(solution)/shard_map/ppermute | solution.py:92
  76.5 2.5 %collective-permute-start.24 = (bf16[8,7168]{1,0:T(8,128)(2,1)S(1)}, bf16[8,7168]{1,0:T(8,128)(2,1)S(1)}, u32[]{:S(2)}, u32[]{:S(2)}) collective-permute-start(bf16[8,7168]{1,0:T(8,128)(2,1)S(1)} %get-tuple-element.19), channel_id=1, source_target_pairs={{0,8},{4,12},{8,16},{12,20},{16,24},{20,28},{24,0},{28,4},{1,9},{5... | collective-permute-start | bytes 344072 | tf_op jit(solution)/shard_map/ppermute | solution.py:92
  79.0 2.8 %collective-permute-start.22 = (bf16[8,7168]{1,0:T(8,128)(2,1)S(1)}, bf16[8,7168]{1,0:T(8,128)(2,1)S(1)}, u32[]{:S(2)}, u32[]{:S(2)}) collective-permute-start(bf16[8,7168]{1,0:T(8,128)(2,1)S(1)} %get-tuple-element.17), channel_id=1, source_target_pairs={{0,16},{4,20},{8,24},{12,28},{16,0},{20,4},{24,8},{28,12},{1,17},{... | collective-permute-start | bytes 344072 | tf_op jit(solution)/shard_map/ppermute | solution.py:92
  81.9 1.7 %collective-permute-done.16 = bf16[4,8,7168]{2,1,0:T(8,128)(2,1)S(1)} collective-permute-done((bf16[4,8,7168]{2,1,0:T(8,128)(2,1)S(1)}, bf16[4,8,7168]{2,1,0:T(8,128)(2,1)S(1)}, u32[]{:S(2)}, u32[]{:S(2)}) %collective-permute-start.16) | collective-permute-done | bytes 458784 | tf_op jit(solution)/shard_map/ppermute | solution.py:40
  83.7 3.4 %collective-permute-start.19 = (bf16[8,7168]{1,0:T(8,128)(2,1)S(1)}, bf16[8,7168]{1,0:T(8,128)(2,1)S(1)}, u32[]{:S(2)}, u32[]{:S(2)}) collective-permute-start(bf16[8,7168]{1,0:T(8,128)(2,1)S(1)} %get-tuple-element.15), channel_id=1, source_target_pairs={{0,20},{4,24},{8,28},{12,0},{16,4},{20,8},{24,12},{28,16},{1,21},{... | collective-permute-start | bytes 344072 | tf_op jit(solution)/shard_map/ppermute | solution.py:92
  87.1 2.9 %collective-permute-start.18 = (bf16[8,7168]{1,0:T(8,128)(2,1)S(1)}, bf16[8,7168]{1,0:T(8,128)(2,1)S(1)}, u32[]{:S(2)}, u32[]{:S(2)}) collective-permute-start(bf16[8,7168]{1,0:T(8,128)(2,1)S(1)} %get-tuple-element.16), channel_id=1, source_target_pairs={{0,24},{4,28},{8,0},{12,4},{16,8},{20,12},{24,16},{28,20},{1,25},{... | collective-permute-start | bytes 344072 | tf_op jit(solution)/shard_map/ppermute | solution.py:92
  91.5 4.7 %collective-permute-done.19 = bf16[8,7168]{1,0:T(8,128)(2,1)S(1)} collective-permute-done((bf16[8,7168]{1,0:T(8,128)(2,1)S(1)}, bf16[8,7168]{1,0:T(8,128)(2,1)S(1)}, u32[]{:S(2)}, u32[]{:S(2)}) %collective-permute-start.19) | collective-permute-done | bytes 114720 | tf_op jit(solution)/shard_map/ppermute | solution.py:92
  96.2 0.9 fusion.32
  (85 shorter events, 11.2 us)
Async XLA Ops:
  0.6 9.5 %copy-start = (bf16[2,1024,512]{2,1,0:T(8,128)(2,1)S(1)}, bf16[2,1024,512]{2,1,0:T(8,128)(2,1)}, u32[]{:S(2)}) copy-start(bf16[2,1024,512]{2,1,0:T(8,128)(2,1)} %param.13) | copy-start | bytes 6291460
  0.6 11.3 %copy-start.7 = (s32[2]{0:T(128)S(1)}, s32[2]{0:T(128)}, u32[]{:S(2)}) copy-start(s32[2]{0:T(128)} %param.15) | copy-start | bytes 28
  0.7 11.4 %copy-start.2 = (bf16[2,64,1024]{2,1,0:T(8,128)(2,1)S(1)}, bf16[2,64,1024]{2,1,0:T(8,128)(2,1)}, u32[]{:S(2)}) copy-start(bf16[2,64,1024]{2,1,0:T(8,128)(2,1)} %param.14) | copy-start | bytes 786436
  0.7 19.5 %collective-permute-start.12 = (bf16[8,7168]{1,0:T(8,128)(2,1)}, bf16[8,7168]{1,0:T(8,128)(2,1)}, u32[]{:S(2)}, u32[]{:S(2)}) collective-permute-start(bf16[8,7168]{1,0:T(8,128)(2,1)} %param.16), channel_id=1, source_target_pairs={{0,28},{4,0},{8,4},{12,8},{16,12},{20,16},{24,20},{28,24},{1,29},{... | collective-permute-start | bytes 344072 | tf_op jit(solution)/shard_map/ppermute | solution.py:60
  6.7 15.3 %collective-permute-start.11 = (bf16[8,7168]{1,0:T(8,128)(2,1)}, bf16[8,7168]{1,0:T(8,128)(2,1)}, u32[]{:S(2)}, u32[]{:S(2)}) collective-permute-start(bf16[8,7168]{1,0:T(8,128)(2,1)} %param.16), channel_id=1, source_target_pairs={{0,24},{4,28},{8,0},{12,4},{16,8},{20,12},{24,16},{28,20},{1,25},{... | collective-permute-start | bytes 344072 | tf_op jit(solution)/shard_map/ppermute | solution.py:60
  7.2 16.0 %collective-permute-start.10 = (bf16[8,7168]{1,0:T(8,128)(2,1)}, bf16[8,7168]{1,0:T(8,128)(2,1)}, u32[]{:S(2)}, u32[]{:S(2)}) collective-permute-start(bf16[8,7168]{1,0:T(8,128)(2,1)} %param.16), channel_id=1, source_target_pairs={{0,20},{4,24},{8,28},{12,0},{16,4},{20,8},{24,12},{28,16},{1,21},{... | collective-permute-start | bytes 344072 | tf_op jit(solution)/shard_map/ppermute | solution.py:60
  7.2 16.0 %collective-permute-start.9 = (bf16[8,7168]{1,0:T(8,128)(2,1)}, bf16[8,7168]{1,0:T(8,128)(2,1)}, u32[]{:S(2)}, u32[]{:S(2)}) collective-permute-start(bf16[8,7168]{1,0:T(8,128)(2,1)} %param.16), channel_id=1, source_target_pairs={{0,16},{4,20},{8,24},{12,28},{16,0},{20,4},{24,8},{28,12},{1,17},{... | collective-permute-start | bytes 344072 | tf_op jit(solution)/shard_map/ppermute | solution.py:60
  12.0 5.5 %copy-start.3 = (bf16[8,7168]{1,0:T(8,128)(2,1)S(1)}, bf16[8,7168]{1,0:T(8,128)(2,1)}, u32[]{:S(2)}) copy-start(bf16[8,7168]{1,0:T(8,128)(2,1)} %param.16) | copy-start | bytes 344068
  12.5 1.3 %collective-permute-start = (f32[2,128]{1,0:T(2,128)S(1)}, f32[2,128]{1,0:T(2,128)S(1)}, u32[]{:S(2)}, u32[]{:S(2)}) collective-permute-start(f32[2,128]{1,0:T(2,128)S(1)} %get-tuple-element.33), channel_id=1, source_target_pairs={{0,1},{1,0},{2,3},{3,2},{4,5},{5,4},{6,7},{7,6},{8,9},{9,8},{10,11... | collective-permute-start | bytes 3080 | tf_op jit(solution)/shard_map/ppermute | solution.py:136
  13.8 3.6 %collective-permute-start.1 = (f32[2,128]{1,0:T(2,128)S(1)}, f32[2,128]{1,0:T(2,128)S(1)}, u32[]{:S(2)}, u32[]{:S(2)}) collective-permute-start(f32[2,128]{1,0:T(2,128)S(1)} %max.6), channel_id=1, source_target_pairs={{0,2},{1,3},{2,0},{3,1},{4,6},{5,7},{6,4},{7,5},{8,10},{9,11},{10,... | collective-permute-start | bytes 3080 | tf_op jit(solution)/shard_map/ppermute | solution.py:136
  17.4 8.5 %collective-permute-start.6 = (bf16[8,7168]{1,0:T(8,128)(2,1)S(1)}, bf16[8,7168]{1,0:T(8,128)(2,1)S(1)}, u32[]{:S(2)}, u32[]{:S(2)}) collective-permute-start(bf16[8,7168]{1,0:T(8,128)(2,1)S(1)} %copy-done.3), channel_id=1, source_target_pairs={{0,12},{4,16},{8,20},{12,24},{16,28},{20,0},{24,4},{28,8},{1,13},{... | collective-permute-start | bytes 344072 | tf_op jit(solution)/shard_map/ppermute | solution.py:60
  20.1 7.6 %collective-permute-start.5 = (bf16[8,7168]{1,0:T(8,128)(2,1)S(1)}, bf16[8,7168]{1,0:T(8,128)(2,1)S(1)}, u32[]{:S(2)}, u32[]{:S(2)}) collective-permute-start(bf16[8,7168]{1,0:T(8,128)(2,1)S(1)} %copy-done.3), channel_id=1, source_target_pairs={{0,8},{4,12},{8,16},{12,20},{16,24},{20,28},{24,0},{28,4},{1,9},{5... | collective-permute-start | bytes 344072 | tf_op jit(solution)/shard_map/ppermute | solution.py:60
  22.1 8.1 %collective-permute-start.4 = (bf16[8,7168]{1,0:T(8,128)(2,1)S(1)}, bf16[8,7168]{1,0:T(8,128)(2,1)S(1)}, u32[]{:S(2)}, u32[]{:S(2)}) collective-permute-start(bf16[8,7168]{1,0:T(8,128)(2,1)S(1)} %copy-done.3), channel_id=1, source_target_pairs={{0,4},{4,8},{8,12},{12,16},{16,20},{20,24},{24,28},{28,0},{1,5},{5... | collective-permute-start | bytes 344072 | tf_op jit(solution)/shard_map/ppermute | solution.py:60
  23.2 8.7 %collective-permute-start.2 = (f32[2,2,32,513]{3,2,0,1:T(8,128)S(1)}, f32[2,2,32,513]{3,2,0,1:T(8,128)S(1)}, u32[]{:S(2)}, u32[]{:S(2)}) collective-permute-start(f32[2,2,32,513]{3,2,0,1:T(8,128)S(1)} %bitcast.120), channel_id=1, source_target_pairs={{0,1},{1,0},{2,3},{3,2},{4,5},{5,4},{6,7},{7,6},{8,9},{9,8},{10,11... | collective-permute-start | bytes 787976 | tf_op jit(solution)/shard_map/ppermute | solution.py:149
  24.3 13.4 %collective-permute-start.13 = (bf16[4,8,7168]{2,1,0:T(8,128)(2,1)S(1)}, bf16[4,8,7168]{2,1,0:T(8,128)(2,1)S(1)}, u32[]{:S(2)}, u32[]{:S(2)}) collective-permute-start(bf16[4,8,7168]{2,1,0:T(8,128)(2,1)S(1)} %get-tuple-element.24), channel_id=1, source_target_pairs={{0,2},{1,3},{2,0},{3,1},{4,6},{5,7},{6,4},{7,5},{8,10},{9,11},{10,... | collective-permute-start | bytes 1376264 | tf_op jit(solution)/shard_map/ppermute | solution.py:34
  30.3 16.9 %collective-permute-start.7 = (bf16[4,8,7168]{2,1,0:T(8,128)(2,1)S(1)}, bf16[4,8,7168]{2,1,0:T(8,128)(2,1)S(1)}, u32[]{:S(2)}, u32[]{:S(2)}) collective-permute-start(bf16[4,8,7168]{2,1,0:T(8,128)(2,1)S(1)} %get-tuple-element.22), channel_id=1, source_target_pairs={{0,2},{1,3},{2,0},{3,1},{4,6},{5,7},{6,4},{7,5},{8,10},{9,11},{10,... | collective-permute-start | bytes 1376264 | tf_op jit(solution)/shard_map/ppermute | solution.py:34
  37.8 11.1 %collective-permute-start.14 = (bf16[2,4,8,7168]{3,2,1,0:T(8,128)(2,1)S(1)}, bf16[2,4,8,7168]{3,2,1,0:T(8,128)(2,1)S(1)}, u32[]{:S(2)}, u32[]{:S(2)}) collective-permute-start(bf16[2,4,8,7168]{3,2,1,0:T(8,128)(2,1)S(1)} %get-tuple-element.11), channel_id=1, source_target_pairs={{0,1},{1,0},{2,3},{3,2},{4,5},{5,4},{6,7},{7,6},{8,9},{9,8},{10,11... | collective-permute-start | bytes 2752520 | tf_op jit(solution)/shard_map/ppermute | solution.py:34
  47.3 2.5 %collective-permute-start.8 = (bf16[2,4,8,7168]{3,2,1,0:T(8,128)(2,1)S(1)}, bf16[2,4,8,7168]{3,2,1,0:T(8,128)(2,1)S(1)}, u32[]{:S(2)}, u32[]{:S(2)}) collective-permute-start(bf16[2,4,8,7168]{3,2,1,0:T(8,128)(2,1)S(1)} %get-tuple-element.9), channel_id=1, source_target_pairs={{0,1},{1,0},{2,3},{3,2},{4,5},{5,4},{6,7},{7,6},{8,9},{9,8},{10,11... | collective-permute-start | bytes 2752520 | tf_op jit(solution)/shard_map/ppermute | solution.py:34
  47.4 10.5 %collective-permute-start.3 = (f32[2,1,32,513]{3,2,0,1:T(8,128)S(1)}, f32[2,1,32,513]{3,2,0,1:T(8,128)S(1)}, u32[]{:S(2)}, u32[]{:S(2)}) collective-permute-start(f32[2,1,32,513]{3,2,0,1:T(8,128)S(1)} %constant_dynamic-slice_fusion), channel_id=1, source_target_pairs={{0,2},{1,3},{2,0},{3,1},{4,6},{5,7},{6,4},{7,5},{8,10},{9,11},{10,... | collective-permute-start | bytes 393992 | tf_op jit(solution)/shard_map/ppermute | solution.py:149
  49.1 2.0 %copy-start.8 = (bf16[1,7168,256]{2,1,0:T(8,128)(2,1)S(1)}, bf16[1,7168,256]{2,1,0:T(8,128)(2,1)}, u32[]{:S(2)}) copy-start(bf16[1,7168,256]{2,1,0:T(8,128)(2,1)} %param.19) | copy-start | bytes 11010052
  51.2 2.0 %copy-start.9 = (bf16[1,7168,256]{2,1,0:T(8,128)(2,1)S(1)}, bf16[1,7168,256]{2,1,0:T(8,128)(2,1)}, u32[]{:S(2)}) copy-start(bf16[1,7168,256]{2,1,0:T(8,128)(2,1)} %param.20) | copy-start | bytes 11010052
  56.9 3.9 %collective-permute-start.20 = (f32[2,4,8,7168]{3,2,1,0:T(8,128)S(1)}, f32[2,4,8,7168]{3,2,1,0:T(8,128)S(1)}, u32[]{:S(2)}, u32[]{:S(2)}) collective-permute-start(f32[2,4,8,7168]{3,2,1,0:T(8,128)S(1)} %bitcast.111), channel_id=1, source_target_pairs={{0,1},{1,0},{2,3},{3,2},{4,5},{5,4},{6,7},{7,6},{8,9},{9,8},{10,11... | collective-permute-start | bytes 5505032 | tf_op jit(solution)/shard_map/ppermute | solution.py:40
  57.5 5.9 %collective-permute-start.15 = (f32[2,4,8,7168]{3,2,1,0:T(8,128)S(1)}, f32[2,4,8,7168]{3,2,1,0:T(8,128)S(1)}, u32[]{:S(2)}, u32[]{:S(2)}) collective-permute-start(f32[2,4,8,7168]{3,2,1,0:T(8,128)S(1)} %bitcast.110), channel_id=1, source_target_pairs={{0,1},{1,0},{2,3},{3,2},{4,5},{5,4},{6,7},{7,6},{8,9},{9,8},{10,11... | collective-permute-start | bytes 5505032 | tf_op jit(solution)/shard_map/ppermute | solution.py:40
  61.0 13.4 %collective-permute-start.21 = (bf16[4,8,7168]{2,1,0:T(8,128)(2,1)S(1)}, bf16[4,8,7168]{2,1,0:T(8,128)(2,1)S(1)}, u32[]{:S(2)}, u32[]{:S(2)}) collective-permute-start(bf16[4,8,7168]{2,1,0:T(8,128)(2,1)S(1)} %fusion.22), channel_id=1, source_target_pairs={{0,2},{1,3},{2,0},{3,1},{4,6},{5,7},{6,4},{7,5},{8,10},{9,11},{10,... | collective-permute-start | bytes 1376264 | tf_op jit(solution)/shard_map/ppermute | solution.py:40
  63.6 19.9 %collective-permute-start.16 = (bf16[4,8,7168]{2,1,0:T(8,128)(2,1)S(1)}, bf16[4,8,7168]{2,1,0:T(8,128)(2,1)S(1)}, u32[]{:S(2)}, u32[]{:S(2)}) collective-permute-start(bf16[4,8,7168]{2,1,0:T(8,128)(2,1)S(1)} %fusion.21), channel_id=1, source_target_pairs={{0,2},{1,3},{2,0},{3,1},{4,6},{5,7},{6,4},{7,5},{8,10},{9,11},{10,... | collective-permute-start | bytes 1376264 | tf_op jit(solution)/shard_map/ppermute | solution.py:40
  74.6 12.5 %collective-permute-start.25 = (bf16[8,7168]{1,0:T(8,128)(2,1)S(1)}, bf16[8,7168]{1,0:T(8,128)(2,1)S(1)}, u32[]{:S(2)}, u32[]{:S(2)}) collective-permute-start(bf16[8,7168]{1,0:T(8,128)(2,1)S(1)} %get-tuple-element.18), channel_id=1, source_target_pairs={{0,4},{4,8},{8,12},{12,16},{16,20},{20,24},{24,28},{28,0},{1,5},{5... | collective-permute-start | bytes 344072 | tf_op jit(solution)/shard_map/ppermute | solution.py:92
  76.5 13.4 %collective-permute-start.24 = (bf16[8,7168]{1,0:T(8,128)(2,1)S(1)}, bf16[8,7168]{1,0:T(8,128)(2,1)S(1)}, u32[]{:S(2)}, u32[]{:S(2)}) collective-permute-start(bf16[8,7168]{1,0:T(8,128)(2,1)S(1)} %get-tuple-element.19), channel_id=1, source_target_pairs={{0,8},{4,12},{8,16},{12,20},{16,24},{20,28},{24,0},{28,4},{1,9},{5... | collective-permute-start | bytes 344072 | tf_op jit(solution)/shard_map/ppermute | solution.py:92
  79.0 12.5 %collective-permute-start.23 = (bf16[8,7168]{1,0:T(8,128)(2,1)S(1)}, bf16[8,7168]{1,0:T(8,128)(2,1)S(1)}, u32[]{:S(2)}, u32[]{:S(2)}) collective-permute-start(bf16[8,7168]{1,0:T(8,128)(2,1)S(1)} %get-tuple-element.20), channel_id=1, source_target_pairs={{0,12},{4,16},{8,20},{12,24},{16,28},{20,0},{24,4},{28,8},{1,13},{... | collective-permute-start | bytes 344072 | tf_op jit(solution)/shard_map/ppermute | solution.py:92
  79.0 12.5 %collective-permute-start.22 = (bf16[8,7168]{1,0:T(8,128)(2,1)S(1)}, bf16[8,7168]{1,0:T(8,128)(2,1)S(1)}, u32[]{:S(2)}, u32[]{:S(2)}) collective-permute-start(bf16[8,7168]{1,0:T(8,128)(2,1)S(1)} %get-tuple-element.17), channel_id=1, source_target_pairs={{0,16},{4,20},{8,24},{12,28},{16,0},{20,4},{24,8},{28,12},{1,17},{... | collective-permute-start | bytes 344072 | tf_op jit(solution)/shard_map/ppermute | solution.py:92
  83.7 12.5 %collective-permute-start.19 = (bf16[8,7168]{1,0:T(8,128)(2,1)S(1)}, bf16[8,7168]{1,0:T(8,128)(2,1)S(1)}, u32[]{:S(2)}, u32[]{:S(2)}) collective-permute-start(bf16[8,7168]{1,0:T(8,128)(2,1)S(1)} %get-tuple-element.15), channel_id=1, source_target_pairs={{0,20},{4,24},{8,28},{12,0},{16,4},{20,8},{24,12},{28,16},{1,21},{... | collective-permute-start | bytes 344072 | tf_op jit(solution)/shard_map/ppermute | solution.py:92
  87.1 9.1 %collective-permute-start.18 = (bf16[8,7168]{1,0:T(8,128)(2,1)S(1)}, bf16[8,7168]{1,0:T(8,128)(2,1)S(1)}, u32[]{:S(2)}, u32[]{:S(2)}) collective-permute-start(bf16[8,7168]{1,0:T(8,128)(2,1)S(1)} %get-tuple-element.16), channel_id=1, source_target_pairs={{0,24},{4,28},{8,0},{12,4},{16,8},{20,12},{24,16},{28,20},{1,25},{... | collective-permute-start | bytes 344072 | tf_op jit(solution)/shard_map/ppermute | solution.py:92
  89.9 6.3 %collective-permute-start.17 = (bf16[8,7168]{1,0:T(8,128)(2,1)S(1)}, bf16[8,7168]{1,0:T(8,128)(2,1)S(1)}, u32[]{:S(2)}, u32[]{:S(2)}) collective-permute-start(bf16[8,7168]{1,0:T(8,128)(2,1)S(1)} %get-tuple-element.14), channel_id=1, source_target_pairs={{0,28},{4,0},{8,4},{12,8},{16,12},{20,16},{24,20},{28,24},{1,29},{... | collective-permute-start | bytes 344072 | tf_op jit(solution)/shard_map/ppermute | solution.py:92
  (4 other events, 6.0 us)

commit v15 on v14

--- a/solution.py
+++ b/solution.py
@@ -73,11 +73,12 @@
         gate_value = jnp.dot(both, w_gate[i], preferred_element_type=jnp.float32)
         upward = jnp.dot(both, w_up[i], preferred_element_type=jnp.float32)
         hidden = (jax.nn.silu(gate_value) * upward).astype(jnp.bfloat16)
+        down_all = jnp.dot(hidden, w_down[i], preferred_element_type=jnp.float32)
         offset = 0
         for c in range(n_chunks):
             block = blocks[c]
             count = block.size // model_width
-            part = jnp.dot(hidden[offset : offset + count], w_down[i], preferred_element_type=jnp.float32)
+            part = down_all[offset : offset + count]
             offset += count
             part = part.reshape(block.shape[:-1] + (model_width,))
             for bit in reversed(bits):

time: 98.2 us -> 128 us (1.30)
  waiting for transfers between devices: 44.1 us -> 52.7 us
  other arithmetic: 5.73 us -> 13.7 us
  matrix products: 7.13 us -> 15 us
  local copies, waits for them, and re-layouts: 4.81 us -> 8.64 us
  starting transfers between devices: 34.4 us -> 36.7 us
    dot_general x3 -> x1, matrix products: 2.47 us -> 11.1 us  [routed_experts(): down_all = jnp.dot(hidden, w_down[i], preferred_element_type=jnp.float32)]
    ppermute x2, waiting for transfers between devices: 0.01 us -> 7.06 us  [per_device(): got = lax.ppermute(sent, 'exp', [(i, i ^ bit) for i in range(n_exp)])]
    another operation x6, other arithmetic: 1.8 us -> 8.46 us  [bit_gather(): return jnp.stack([x, other])]
    ppermute x7, waiting for transfers between devices: 5.54 us -> 11.8 us  [routed_experts(): lax.ppermute(expert_rows[kk], 'attn', [(s, (s - k) % n_attn) for s in ran...]
    slice x2 -> x1, local copies, waits for them, and re-layouts: 0.66 us -> 6.26 us  [bit_reduce(): sent = x[1] if wire is None else x[1].astype(wire)]
    ppermute x4, waiting for transfers between devices: 16.4 us -> 12.1 us  [bit_reduce(): lax.ppermute(sent, axis, [(i, i ^ bit) for i in range(n)]).astype(x.dtype)]
    ppermute x7, waiting for transfers between devices: 4.31 us -> 6.85 us  [routed_experts(): lax.ppermute(tokens, 'attn', [(s, (s + k) % n_attn) for s in range(n_attn)])]
    ppermute x2, waiting for transfers between devices: 2.08 us -> 0.01 us  [per_device(): lax.ppermute(row_top, 'exp', [(i, i ^ bit) for i in range(n_exp)])]
  transfers between devices with their start and end apart: 26 -> 26, of which waited for: 12 -> 10; matrix products, arithmetic and copies ran while one was open for 14% -> 27% of each run, Pallas kernels for 0% -> 0%
where the time goes in v15:
time: 128 us
  waiting for transfers between devices  52.7 us (41%)
  starting transfers between devices  36.7 us (29%)
  matrix products  15 us (12%)
  other arithmetic  13.7 us (11%)
  local copies, waits for them, and re-layouts  8.64 us (7%)
    ppermute x7, starting transfers between devices, routed_experts(): lax.ppermute(expert_rows[kk], 'attn', [(s, (s - k) % n_attn) for s in ran...  15.4 us
    ppermute x4, waiting for transfers between devices, bit_gather(): other = lax.ppermute(x, axis, [(i, i ^ bit) for i in range(n)])  14.9 us
    ppermute x4, waiting for transfers between devices, bit_reduce(): lax.ppermute(sent, axis, [(i, i ^ bit) for i in range(n)]).astype(x.dtype)  12.1 us
    ppermute x7, starting transfers between devices, routed_experts(): lax.ppermute(tokens, 'attn', [(s, (s + k) % n_attn) for s in range(n_attn)])  12 us
    ppermute x7, waiting for transfers between devices, routed_experts(): lax.ppermute(expert_rows[kk], 'attn', [(s, (s - k) % n_attn) for s in ran...  11.8 us
    dot_general x1, matrix products, routed_experts(): down_all = jnp.dot(hidden, w_down[i], preferred_element_type=jnp.float32)  11.1 us
    another operation x6, other arithmetic, bit_gather(): return jnp.stack([x, other])  8.46 us
    ppermute x2, waiting for transfers between devices, per_device(): got = lax.ppermute(sent, 'exp', [(i, i ^ bit) for i in range(n_exp)])  7.06 us
  transfers between devices with their start and end apart: 26, of which 10 were waited for; matrix products, arithmetic and copies ran while one was open for 27% of the time, Pallas kernels for 0%

profile of v15, /device:TPU:0, one launch (start us, length us, event | category | flops | bytes accessed | tf_op | source)
XLA Modules:
  0.0 127.8 jit_solution(17043327285215790328)
XLA Ops:
  0.7 4.0 %collective-permute-start.6 = (bf16[8,7168]{1,0:T(8,128)(2,1)}, bf16[8,7168]{1,0:T(8,128)(2,1)}, u32[]{:S(2)}, u32[]{:S(2)}) collective-permute-start(bf16[8,7168]{1,0:T(8,128)(2,1)} %param.16), channel_id=1, source_target_pairs={{0,12},{4,16},{8,20},{12,24},{16,28},{20,0},{24,4},{28,8},{1,13},{... | collective-permute-start | bytes 344072 | tf_op jit(solution)/shard_map/ppermute | solution.py:60
  4.7 1.5 %collective-permute-start.4 = (bf16[8,7168]{1,0:T(8,128)(2,1)}, bf16[8,7168]{1,0:T(8,128)(2,1)}, u32[]{:S(2)}, u32[]{:S(2)}) collective-permute-start(bf16[8,7168]{1,0:T(8,128)(2,1)} %param.16), channel_id=1, source_target_pairs={{0,4},{4,8},{8,12},{12,16},{16,20},{20,24},{24,28},{28,0},{1,5},{5... | collective-permute-start | bytes 344072 | tf_op jit(solution)/shard_map/ppermute | solution.py:60
  6.2 1.6 %collective-permute-start.5 = (bf16[8,7168]{1,0:T(8,128)(2,1)}, bf16[8,7168]{1,0:T(8,128)(2,1)}, u32[]{:S(2)}, u32[]{:S(2)}) collective-permute-start(bf16[8,7168]{1,0:T(8,128)(2,1)} %param.16), channel_id=1, source_target_pairs={{0,8},{4,12},{8,16},{12,20},{16,24},{20,28},{24,0},{28,4},{1,9},{5... | collective-permute-start | bytes 344072 | tf_op jit(solution)/shard_map/ppermute | solution.py:60
  8.1 3.5 %collective-permute-start.10 = (bf16[8,7168]{1,0:T(8,128)(2,1)}, bf16[8,7168]{1,0:T(8,128)(2,1)}, u32[]{:S(2)}, u32[]{:S(2)}) collective-permute-start(bf16[8,7168]{1,0:T(8,128)(2,1)} %param.16), channel_id=1, source_target_pairs={{0,20},{4,24},{8,28},{12,0},{16,4},{20,8},{24,12},{28,16},{1,21},{... | collective-permute-start | bytes 344072 | tf_op jit(solution)/shard_map/ppermute | solution.py:60
  12.4 1.8 %fusion.54 = f32[2,128,1024]{2,1,0:T(8,128)S(1)} fusion(bf16[2,128,512]{2,1,0:T(8,128)(2,1)} %param.11, bf16[2,1024,512]{2,1,0:T(8,128)(2,1)S(1)} %copy-done), kind=kOutput, calls=%fused_computation.105 | convolution fusion | flops 268435456 | bytes 3407872 | tf_op jit(solution)/shard_map/rhl,rpl->rhp/dot_general | solution.py:115
  15.1 4.7 %collective-permute-done.6 = bf16[8,7168]{1,0:T(8,128)(2,1)} collective-permute-done((bf16[8,7168]{1,0:T(8,128)(2,1)}, bf16[8,7168]{1,0:T(8,128)(2,1)}, u32[]{:S(2)}, u32[]{:S(2)}) %collective-permute-start.6) | collective-permute-done | bytes 114720 | tf_op jit(solution)/shard_map/ppermute | solution.py:60
  20.9 1.1 fusion.50
  22.0 1.9 %collective-permute-start.7 = (bf16[4,8,7168]{2,1,0:T(8,128)(2,1)S(1)}, bf16[4,8,7168]{2,1,0:T(8,128)(2,1)S(1)}, u32[]{:S(2)}, u32[]{:S(2)}) collective-permute-start(bf16[4,8,7168]{2,1,0:T(8,128)(2,1)S(1)} %get-tuple-element.22), channel_id=1, source_target_pairs={{0,2},{1,3},{2,0},{3,1},{4,6},{5,7},{6,4},{7,5},{8,10},{9,11},{10,... | collective-permute-start | bytes 1376264 | tf_op jit(solution)/shard_map/ppermute | solution.py:34
  23.8 2.1 %collective-permute-done.11 = bf16[8,7168]{1,0:T(8,128)(2,1)S(1)} collective-permute-done((bf16[8,7168]{1,0:T(8,128)(2,1)S(1)}, bf16[8,7168]{1,0:T(8,128)(2,1)S(1)}, u32[]{:S(2)}, u32[]{:S(2)}) %collective-permute-start.11) | collective-permute-done | bytes 114720 | tf_op jit(solution)/shard_map/ppermute | solution.py:60
  26.9 1.7 %collective-permute-start.13 = (bf16[4,8,7168]{2,1,0:T(8,128)(2,1)S(1)}, bf16[4,8,7168]{2,1,0:T(8,128)(2,1)S(1)}, u32[]{:S(2)}, u32[]{:S(2)}) collective-permute-start(bf16[4,8,7168]{2,1,0:T(8,128)(2,1)S(1)} %get-tuple-element.24), channel_id=1, source_target_pairs={{0,2},{1,3},{2,0},{3,1},{4,6},{5,7},{6,4},{7,5},{8,10},{9,11},{10,... | collective-permute-start | bytes 1376264 | tf_op jit(solution)/shard_map/ppermute | solution.py:34
  28.6 6.8 %collective-permute-done.7 = bf16[4,8,7168]{2,1,0:T(8,128)(2,1)S(1)} collective-permute-done((bf16[4,8,7168]{2,1,0:T(8,128)(2,1)S(1)}, bf16[4,8,7168]{2,1,0:T(8,128)(2,1)S(1)}, u32[]{:S(2)}, u32[]{:S(2)}) %collective-permute-start.7) | collective-permute-done | bytes 458784 | tf_op jit(solution)/shard_map/ppermute | solution.py:34
  35.4 1.4 %fusion.48 = (bf16[1,2,4,8,7168]{4,3,2,1,0:T(8,128)(2,1)}, bf16[2,4,8,7168]{3,2,1,0:T(8,128)(2,1)}) fusion(bf16[1,4,8,7168]{3,2,1,0:T(8,128)(2,1)S(1)} %bitcast.115, bf16[1,4,8,7168]{3,2,1,0:T(8,128)(2,1)S(1)} %get-tuple-element.21), kind=kLoop, calls=%fused_computation.99 | loop fusion | flops 458752 | bytes 2752512 | tf_op jit(solution)/shard_map/stack | solution.py:35
  36.8 8.1 %collective-permute-done.13 = bf16[4,8,7168]{2,1,0:T(8,128)(2,1)S(1)} collective-permute-done((bf16[4,8,7168]{2,1,0:T(8,128)(2,1)S(1)}, bf16[4,8,7168]{2,1,0:T(8,128)(2,1)S(1)}, u32[]{:S(2)}, u32[]{:S(2)}) %collective-permute-start.13) | collective-permute-done | bytes 458784 | tf_op jit(solution)/shard_map/ppermute | solution.py:34
  44.9 1.4 %fusion.47 = (bf16[1,2,4,8,7168]{4,3,2,1,0:T(8,128)(2,1)}, bf16[2,4,8,7168]{3,2,1,0:T(8,128)(2,1)}) fusion(bf16[1,4,8,7168]{3,2,1,0:T(8,128)(2,1)S(1)} %bitcast.116, bf16[1,4,8,7168]{3,2,1,0:T(8,128)(2,1)S(1)} %get-tuple-element.23), kind=kLoop, calls=%fused_computation.98 | loop fusion | flops 458752 | bytes 2752512 | tf_op jit(solution)/shard_map/stack | solution.py:35
  46.3 1.8 %collective-permute-start.1 = (f32[2,128]{1,0:T(2,128)S(1)}, f32[2,128]{1,0:T(2,128)S(1)}, u32[]{:S(2)}, u32[]{:S(2)}) collective-permute-start(f32[2,128]{1,0:T(2,128)S(1)} %max.6), channel_id=1, source_target_pairs={{0,2},{1,3},{2,0},{3,1},{4,6},{5,7},{6,4},{7,5},{8,10},{9,11},{10,... | collective-permute-start | bytes 3080 | tf_op jit(solution)/shard_map/ppermute | solution.py:137
  48.1 1.6 %pad_maximum_fusion.3 = bf16[2,2,4,8,7168]{4,3,2,1,0:T(8,128)(2,1)S(1)} fusion(bf16[1,2,4,8,7168]{4,3,2,1,0:T(8,128)(2,1)} %bitcast.14, bf16[1,2,4,8,7168]{4,3,2,1,0:T(8,128)(2,1)} %get-tuple-element.8), kind=kLoop, calls=%fused_computation.8 | loop fusion | flops 917504 | bytes 3670016 | tf_op jit(solution)/shard_map/stack | solution.py:35
  49.8 2.0 %pad_maximum_fusion.4 = bf16[2,2,4,8,7168]{4,3,2,1,0:T(8,128)(2,1)S(1)} fusion(bf16[1,2,4,8,7168]{4,3,2,1,0:T(8,128)(2,1)} %bitcast.23, bf16[1,2,4,8,7168]{4,3,2,1,0:T(8,128)(2,1)S(1)} %copy-done.5), kind=kLoop, calls=%fused_computation.9 | loop fusion | flops 917504 | bytes 3670016 | tf_op jit(solution)/shard_map/stack | solution.py:35
  51.8 1.2 copy-done.2
  53.0 1.1 fusion.2
  54.1 11.1 %fusion = f32[256,7168]{1,0:T(8,128)} fusion(bf16[1,256,7168]{2,1,0:T(8,128)(2,1)} %param.21, f32[256,256]{1,0:T(8,128)S(1)} %fusion.2, bf16[1,7168,256]{2,1,0:T(8,128)(2,1)} %param.19, bf16[128,7168]{1,0:T(8,128)(2,1)} %bitcast.110, bf16[128,7168]{1,0:T(8,128)(2,1)} %bitcast.108), kind=kOutput, calls=%fused_computation.2 | convolution fusion | flops 1886781440 | bytes 18612224 | tf_op jit(solution)/shard_map/dot_general | solution.py:76
  65.3 6.3 %fusion.52 = (f32[64,7168]{1,0:T(8,128)}, f32[64,7168]{1,0:T(8,128)}, f32[64,7168]{1,0:T(8,128)}, f32[64,7168]{1,0:T(8,128)}) fusion(f32[256,7168]{1,0:T(8,128)} %fusion), kind=kLoop, calls=%fused_computation.103 | loop fusion | bytes 14680064 | tf_op jit(solution)/shard_map/slice | solution.py:39
  73.8 2.0 %collective-permute-done.2 = f32[2,2,32,513]{3,2,0,1:T(8,128)S(1)} collective-permute-done((f32[2,2,32,513]{3,2,0,1:T(8,128)S(1)}, f32[2,2,32,513]{3,2,0,1:T(8,128)S(1)}, u32[]{:S(2)}, u32[]{:S(2)}) %collective-permute-start.2) | collective-permute-done | bytes 262688 | tf_op jit(solution)/shard_map/ppermute | solution.py:150
  75.9 1.3 %collective-permute-start.3 = (f32[2,1,32,513]{3,2,0,1:T(8,128)S(1)}, f32[2,1,32,513]{3,2,0,1:T(8,128)S(1)}, u32[]{:S(2)}, u32[]{:S(2)}) collective-permute-start(f32[2,1,32,513]{3,2,0,1:T(8,128)S(1)} %constant_dynamic-slice_fusion), channel_id=1, source_target_pairs={{0,2},{1,3},{2,0},{3,1},{4,6},{5,7},{6,4},{7,5},{8,10},{9,11},{10,... | collective-permute-start | bytes 393992 | tf_op jit(solution)/shard_map/ppermute | solution.py:150
  77.2 5.0 %collective-permute-done.3 = f32[2,1,32,513]{3,2,0,1:T(8,128)S(1)} collective-permute-done((f32[2,1,32,513]{3,2,0,1:T(8,128)S(1)}, f32[2,1,32,513]{3,2,0,1:T(8,128)S(1)}, u32[]{:S(2)}, u32[]{:S(2)}) %collective-permute-start.3) | collective-permute-done | bytes 131360 | tf_op jit(solution)/shard_map/ppermute | solution.py:150
  82.3 1.9 %add.152 = f32[2,4,8,7168]{3,2,1,0:T(8,128)S(1)} add(f32[2,4,8,7168]{3,2,1,0:T(8,128)S(1)} %bitcast.112, f32[2,4,8,7168]{3,2,1,0:T(8,128)} %collective-permute-done.15) | non-fusion elementwise | flops 458752 | bytes 5505024 | tf_op jit(solution)/shard_map/add | solution.py:40
  84.3 1.3 %collective-permute-start.16 = (bf16[4,8,7168]{2,1,0:T(8,128)(2,1)S(1)}, bf16[4,8,7168]{2,1,0:T(8,128)(2,1)S(1)}, u32[]{:S(2)}, u32[]{:S(2)}) collective-permute-start(bf16[4,8,7168]{2,1,0:T(8,128)(2,1)S(1)} %fusion.19), channel_id=1, source_target_pairs={{0,2},{1,3},{2,0},{3,1},{4,6},{5,7},{6,4},{7,5},{8,10},{9,11},{10,... | collective-permute-start | bytes 1376264 | tf_op jit(solution)/shard_map/ppermute | solution.py:40
  86.7 11.1 %collective-permute-done.16 = bf16[4,8,7168]{2,1,0:T(8,128)(2,1)S(1)} collective-permute-done((bf16[4,8,7168]{2,1,0:T(8,128)(2,1)S(1)}, bf16[4,8,7168]{2,1,0:T(8,128)(2,1)S(1)}, u32[]{:S(2)}, u32[]{:S(2)}) %collective-permute-start.16) | collective-permute-done | bytes 458784 | tf_op jit(solution)/shard_map/ppermute | solution.py:40
  97.9 7.1 %collective-permute-start.17 = (bf16[8,7168]{1,0:T(8,128)(2,1)S(1)}, bf16[8,7168]{1,0:T(8,128)(2,1)S(1)}, u32[]{:S(2)}, u32[]{:S(2)}) collective-permute-start(bf16[8,7168]{1,0:T(8,128)(2,1)S(1)} %get-tuple-element.14), channel_id=1, source_target_pairs={{0,28},{4,0},{8,4},{12,8},{16,12},{20,16},{24,20},{28,24},{1,29},{... | collective-permute-start | bytes 344072 | tf_op jit(solution)/shard_map/ppermute | solution.py:93
  106.1 3.1 %collective-permute-start.22 = (bf16[8,7168]{1,0:T(8,128)(2,1)S(1)}, bf16[8,7168]{1,0:T(8,128)(2,1)S(1)}, u32[]{:S(2)}, u32[]{:S(2)}) collective-permute-start(bf16[8,7168]{1,0:T(8,128)(2,1)S(1)} %get-tuple-element.17), channel_id=1, source_target_pairs={{0,16},{4,20},{8,24},{12,28},{16,0},{20,4},{24,8},{28,12},{1,17},{... | collective-permute-start | bytes 344072 | tf_op jit(solution)/shard_map/ppermute | solution.py:93
  109.1 4.6 %collective-permute-start.23 = (bf16[8,7168]{1,0:T(8,128)(2,1)S(1)}, bf16[8,7168]{1,0:T(8,128)(2,1)S(1)}, u32[]{:S(2)}, u32[]{:S(2)}) collective-permute-start(bf16[8,7168]{1,0:T(8,128)(2,1)S(1)} %get-tuple-element.20), channel_id=1, source_target_pairs={{0,12},{4,16},{8,20},{12,24},{16,28},{20,0},{24,4},{28,8},{1,13},{... | collective-permute-start | bytes 344072 | tf_op jit(solution)/shard_map/ppermute | solution.py:93
  115.1 6.8 %collective-permute-done.22 = bf16[8,7168]{1,0:T(8,128)(2,1)S(1)} collective-permute-done((bf16[8,7168]{1,0:T(8,128)(2,1)S(1)}, bf16[8,7168]{1,0:T(8,128)(2,1)S(1)}, u32[]{:S(2)}, u32[]{:S(2)}) %collective-permute-start.22) | collective-permute-done | bytes 114720 | tf_op jit(solution)/shard_map/ppermute | solution.py:93
  121.9 5.0 %collective-permute-done.23 = bf16[8,7168]{1,0:T(8,128)(2,1)S(1)} collective-permute-done((bf16[8,7168]{1,0:T(8,128)(2,1)S(1)}, bf16[8,7168]{1,0:T(8,128)(2,1)S(1)}, u32[]{:S(2)}, u32[]{:S(2)}) %collective-permute-start.23) | collective-permute-done | bytes 114720 | tf_op jit(solution)/shard_map/ppermute | solution.py:93
  (86 shorter events, 10.8 us)
Async XLA Ops:
  0.6 11.8 %copy-start = (bf16[2,1024,512]{2,1,0:T(8,128)(2,1)S(1)}, bf16[2,1024,512]{2,1,0:T(8,128)(2,1)}, u32[]{:S(2)}) copy-start(bf16[2,1024,512]{2,1,0:T(8,128)(2,1)} %param.13) | copy-start | bytes 6291460
  0.6 13.6 %copy-start.6 = (bf16[2,64,1024]{2,1,0:T(8,128)(2,1)S(1)}, bf16[2,64,1024]{2,1,0:T(8,128)(2,1)}, u32[]{:S(2)}) copy-start(bf16[2,64,1024]{2,1,0:T(8,128)(2,1)} %param.14) | copy-start | bytes 786436
  0.7 19.2 %collective-permute-start.6 = (bf16[8,7168]{1,0:T(8,128)(2,1)}, bf16[8,7168]{1,0:T(8,128)(2,1)}, u32[]{:S(2)}, u32[]{:S(2)}) collective-permute-start(bf16[8,7168]{1,0:T(8,128)(2,1)} %param.16), channel_id=1, source_target_pairs={{0,12},{4,16},{8,20},{12,24},{16,28},{20,0},{24,4},{28,8},{1,13},{... | collective-permute-start | bytes 344072 | tf_op jit(solution)/shard_map/ppermute | solution.py:60
  4.7 15.2 %collective-permute-start.4 = (bf16[8,7168]{1,0:T(8,128)(2,1)}, bf16[8,7168]{1,0:T(8,128)(2,1)}, u32[]{:S(2)}, u32[]{:S(2)}) collective-permute-start(bf16[8,7168]{1,0:T(8,128)(2,1)} %param.16), channel_id=1, source_target_pairs={{0,4},{4,8},{8,12},{12,16},{16,20},{20,24},{24,28},{28,0},{1,5},{5... | collective-permute-start | bytes 344072 | tf_op jit(solution)/shard_map/ppermute | solution.py:60
  6.2 14.7 %collective-permute-start.5 = (bf16[8,7168]{1,0:T(8,128)(2,1)}, bf16[8,7168]{1,0:T(8,128)(2,1)}, u32[]{:S(2)}, u32[]{:S(2)}) collective-permute-start(bf16[8,7168]{1,0:T(8,128)(2,1)} %param.16), channel_id=1, source_target_pairs={{0,8},{4,12},{8,16},{12,20},{16,24},{20,28},{24,0},{28,4},{1,9},{5... | collective-permute-start | bytes 344072 | tf_op jit(solution)/shard_map/ppermute | solution.py:60
  7.8 14.2 %collective-permute-start.9 = (bf16[8,7168]{1,0:T(8,128)(2,1)}, bf16[8,7168]{1,0:T(8,128)(2,1)S(1)}, u32[]{:S(2)}, u32[]{:S(2)}) collective-permute-start(bf16[8,7168]{1,0:T(8,128)(2,1)} %param.16), channel_id=1, source_target_pairs={{0,16},{4,20},{8,24},{12,28},{16,0},{20,4},{24,8},{28,12},{1,17},{... | collective-permute-start | bytes 344072 | tf_op jit(solution)/shard_map/ppermute | solution.py:60
  8.1 15.7 %collective-permute-start.10 = (bf16[8,7168]{1,0:T(8,128)(2,1)}, bf16[8,7168]{1,0:T(8,128)(2,1)}, u32[]{:S(2)}, u32[]{:S(2)}) collective-permute-start(bf16[8,7168]{1,0:T(8,128)(2,1)} %param.16), channel_id=1, source_target_pairs={{0,20},{4,24},{8,28},{12,0},{16,4},{20,8},{24,12},{28,16},{1,21},{... | collective-permute-start | bytes 344072 | tf_op jit(solution)/shard_map/ppermute | solution.py:60
  14.2 5.6 %copy-start.7 = (bf16[8,7168]{1,0:T(8,128)(2,1)S(1)}, bf16[8,7168]{1,0:T(8,128)(2,1)}, u32[]{:S(2)}) copy-start(bf16[8,7168]{1,0:T(8,128)(2,1)} %param.16) | copy-start | bytes 344068
  19.9 6.1 %collective-permute-start.11 = (bf16[8,7168]{1,0:T(8,128)(2,1)S(1)}, bf16[8,7168]{1,0:T(8,128)(2,1)S(1)}, u32[]{:S(2)}, u32[]{:S(2)}) collective-permute-start(bf16[8,7168]{1,0:T(8,128)(2,1)S(1)} %copy-done.7), channel_id=1, source_target_pairs={{0,24},{4,28},{8,0},{12,4},{16,8},{20,12},{24,16},{28,20},{1,25},{... | collective-permute-start | bytes 344072 | tf_op jit(solution)/shard_map/ppermute | solution.py:60
  19.9 6.1 %collective-permute-start.12 = (bf16[8,7168]{1,0:T(8,128)(2,1)S(1)}, bf16[8,7168]{1,0:T(8,128)(2,1)S(1)}, u32[]{:S(2)}, u32[]{:S(2)}) collective-permute-start(bf16[8,7168]{1,0:T(8,128)(2,1)S(1)} %copy-done.7), channel_id=1, source_target_pairs={{0,28},{4,0},{8,4},{12,8},{16,12},{20,16},{24,20},{28,24},{1,29},{... | collective-permute-start | bytes 344072 | tf_op jit(solution)/shard_map/ppermute | solution.py:60
  20.9 25.4 %collective-permute-start = (f32[2,128]{1,0:T(2,128)S(1)}, f32[2,128]{1,0:T(2,128)S(1)}, u32[]{:S(2)}, u32[]{:S(2)}) collective-permute-start(f32[2,128]{1,0:T(2,128)S(1)} %get-tuple-element.33), channel_id=1, source_target_pairs={{0,1},{1,0},{2,3},{3,2},{4,5},{5,4},{6,7},{7,6},{8,9},{9,8},{10,11... | collective-permute-start | bytes 3080 | tf_op jit(solution)/shard_map/ppermute | solution.py:137
  22.0 13.4 %collective-permute-start.7 = (bf16[4,8,7168]{2,1,0:T(8,128)(2,1)S(1)}, bf16[4,8,7168]{2,1,0:T(8,128)(2,1)S(1)}, u32[]{:S(2)}, u32[]{:S(2)}) collective-permute-start(bf16[4,8,7168]{2,1,0:T(8,128)(2,1)S(1)} %get-tuple-element.22), channel_id=1, source_target_pairs={{0,2},{1,3},{2,0},{3,1},{4,6},{5,7},{6,4},{7,5},{8,10},{9,11},{10,... | collective-permute-start | bytes 1376264 | tf_op jit(solution)/shard_map/ppermute | solution.py:34
  26.9 17.9 %collective-permute-start.13 = (bf16[4,8,7168]{2,1,0:T(8,128)(2,1)S(1)}, bf16[4,8,7168]{2,1,0:T(8,128)(2,1)S(1)}, u32[]{:S(2)}, u32[]{:S(2)}) collective-permute-start(bf16[4,8,7168]{2,1,0:T(8,128)(2,1)S(1)} %get-tuple-element.24), channel_id=1, source_target_pairs={{0,2},{1,3},{2,0},{3,1},{4,6},{5,7},{6,4},{7,5},{8,10},{9,11},{10,... | collective-permute-start | bytes 1376264 | tf_op jit(solution)/shard_map/ppermute | solution.py:34
  36.7 11.3 %collective-permute-start.8 = (bf16[2,4,8,7168]{3,2,1,0:T(8,128)(2,1)}, bf16[2,4,8,7168]{3,2,1,0:T(8,128)(2,1)}, u32[]{:S(2)}, u32[]{:S(2)}) collective-permute-start(bf16[2,4,8,7168]{3,2,1,0:T(8,128)(2,1)} %get-tuple-element.9), channel_id=1, source_target_pairs={{0,1},{1,0},{2,3},{3,2},{4,5},{5,4},{6,7},{7,6},{8,9},{9,8},{10,11... | collective-permute-start | bytes 2752520 | tf_op jit(solution)/shard_map/ppermute | solution.py:34
  46.2 3.5 %collective-permute-start.14 = (bf16[2,4,8,7168]{3,2,1,0:T(8,128)(2,1)}, bf16[2,4,8,7168]{3,2,1,0:T(8,128)(2,1)}, u32[]{:S(2)}, u32[]{:S(2)}) collective-permute-start(bf16[2,4,8,7168]{3,2,1,0:T(8,128)(2,1)} %get-tuple-element.11), channel_id=1, source_target_pairs={{0,1},{1,0},{2,3},{3,2},{4,5},{5,4},{6,7},{7,6},{8,9},{9,8},{10,11... | collective-permute-start | bytes 2752520 | tf_op jit(solution)/shard_map/ppermute | solution.py:34
  46.2 3.5 %copy-start.5 = (bf16[1,2,4,8,7168]{4,3,2,1,0:T(8,128)(2,1)S(1)}, bf16[1,2,4,8,7168]{4,3,2,1,0:T(8,128)(2,1)}, u32[]{:S(2)}) copy-start(bf16[1,2,4,8,7168]{4,3,2,1,0:T(8,128)(2,1)} %get-tuple-element.10) | copy-start | bytes 2752516
  46.3 25.4 %collective-permute-start.1 = (f32[2,128]{1,0:T(2,128)S(1)}, f32[2,128]{1,0:T(2,128)S(1)}, u32[]{:S(2)}, u32[]{:S(2)}) collective-permute-start(f32[2,128]{1,0:T(2,128)S(1)} %max.6), channel_id=1, source_target_pairs={{0,2},{1,3},{2,0},{3,1},{4,6},{5,7},{6,4},{7,5},{8,10},{9,11},{10,... | collective-permute-start | bytes 3080 | tf_op jit(solution)/shard_map/ppermute | solution.py:137
  49.7 3.3 %copy-start.11 = (bf16[1,7168,256]{2,1,0:T(8,128)(2,1)S(1)}, bf16[1,7168,256]{2,1,0:T(8,128)(2,1)}, u32[]{:S(2)}) copy-start(bf16[1,7168,256]{2,1,0:T(8,128)(2,1)} %param.20) | copy-start | bytes 11010052
  71.5 10.8 %collective-permute-start.15 = (f32[2,4,8,7168]{3,2,1,0:T(8,128)}, f32[2,4,8,7168]{3,2,1,0:T(8,128)}, u32[]{:S(2)}, u32[]{:S(2)}) collective-permute-start(f32[2,4,8,7168]{3,2,1,0:T(8,128)} %bitcast.29), channel_id=1, source_target_pairs={{0,1},{1,0},{2,3},{3,2},{4,5},{5,4},{6,7},{7,6},{8,9},{9,8},{10,11... | collective-permute-start | bytes 5505032 | tf_op jit(solution)/shard_map/ppermute | solution.py:40
  72.6 3.2 %collective-permute-start.2 = (f32[2,2,32,513]{3,2,0,1:T(8,128)S(1)}, f32[2,2,32,513]{3,2,0,1:T(8,128)S(1)}, u32[]{:S(2)}, u32[]{:S(2)}) collective-permute-start(f32[2,2,32,513]{3,2,0,1:T(8,128)S(1)} %bitcast.117), channel_id=1, source_target_pairs={{0,1},{1,0},{2,3},{3,2},{4,5},{5,4},{6,7},{7,6},{8,9},{9,8},{10,11... | collective-permute-start | bytes 787976 | tf_op jit(solution)/shard_map/ppermute | solution.py:150
  73.7 8.7 %copy-start.4 = (f32[64,7168]{1,0:T(8,128)S(1)}, f32[64,7168]{1,0:T(8,128)}, u32[]{:S(2)}) copy-start(f32[64,7168]{1,0:T(8,128)} %get-tuple-element.7) | copy-start | bytes 5505028
  75.9 6.4 %collective-permute-start.3 = (f32[2,1,32,513]{3,2,0,1:T(8,128)S(1)}, f32[2,1,32,513]{3,2,0,1:T(8,128)S(1)}, u32[]{:S(2)}, u32[]{:S(2)}) collective-permute-start(f32[2,1,32,513]{3,2,0,1:T(8,128)S(1)} %constant_dynamic-slice_fusion), channel_id=1, source_target_pairs={{0,2},{1,3},{2,0},{3,1},{4,6},{5,7},{6,4},{7,5},{8,10},{9,11},{10,... | collective-permute-start | bytes 393992 | tf_op jit(solution)/shard_map/ppermute | solution.py:150
  77.2 8.4 %collective-permute-start.20 = (f32[2,4,8,7168]{3,2,1,0:T(8,128)}, f32[2,4,8,7168]{3,2,1,0:T(8,128)S(1)}, u32[]{:S(2)}, u32[]{:S(2)}) collective-permute-start(f32[2,4,8,7168]{3,2,1,0:T(8,128)} %bitcast.114), channel_id=1, source_target_pairs={{0,1},{1,0},{2,3},{3,2},{4,5},{5,4},{6,7},{7,6},{8,9},{9,8},{10,11... | collective-permute-start | bytes 5505032 | tf_op jit(solution)/shard_map/ppermute | solution.py:40
  84.3 13.5 %collective-permute-start.16 = (bf16[4,8,7168]{2,1,0:T(8,128)(2,1)S(1)}, bf16[4,8,7168]{2,1,0:T(8,128)(2,1)S(1)}, u32[]{:S(2)}, u32[]{:S(2)}) collective-permute-start(bf16[4,8,7168]{2,1,0:T(8,128)(2,1)S(1)} %fusion.19), channel_id=1, source_target_pairs={{0,2},{1,3},{2,0},{3,1},{4,6},{5,7},{6,4},{7,5},{8,10},{9,11},{10,... | collective-permute-start | bytes 1376264 | tf_op jit(solution)/shard_map/ppermute | solution.py:40
  85.8 20.1 %collective-permute-start.21 = (bf16[4,8,7168]{2,1,0:T(8,128)(2,1)S(1)}, bf16[4,8,7168]{2,1,0:T(8,128)(2,1)S(1)}, u32[]{:S(2)}, u32[]{:S(2)}) collective-permute-start(bf16[4,8,7168]{2,1,0:T(8,128)(2,1)S(1)} %fusion.20), channel_id=1, source_target_pairs={{0,2},{1,3},{2,0},{3,1},{4,6},{5,7},{6,4},{7,5},{8,10},{9,11},{10,... | collective-permute-start | bytes 1376264 | tf_op jit(solution)/shard_map/ppermute | solution.py:40
  97.9 15.9 %collective-permute-start.17 = (bf16[8,7168]{1,0:T(8,128)(2,1)S(1)}, bf16[8,7168]{1,0:T(8,128)(2,1)S(1)}, u32[]{:S(2)}, u32[]{:S(2)}) collective-permute-start(bf16[8,7168]{1,0:T(8,128)(2,1)S(1)} %get-tuple-element.14), channel_id=1, source_target_pairs={{0,28},{4,0},{8,4},{12,8},{16,12},{20,16},{24,20},{28,24},{1,29},{... | collective-permute-start | bytes 344072 | tf_op jit(solution)/shard_map/ppermute | solution.py:93
  105.0 8.8 %collective-permute-start.18 = (bf16[8,7168]{1,0:T(8,128)(2,1)S(1)}, bf16[8,7168]{1,0:T(8,128)(2,1)S(1)}, u32[]{:S(2)}, u32[]{:S(2)}) collective-permute-start(bf16[8,7168]{1,0:T(8,128)(2,1)S(1)} %get-tuple-element.16), channel_id=1, source_target_pairs={{0,24},{4,28},{8,0},{12,4},{16,8},{20,12},{24,16},{28,20},{1,25},{... | collective-permute-start | bytes 344072 | tf_op jit(solution)/shard_map/ppermute | solution.py:93
  105.0 10.0 %collective-permute-start.19 = (bf16[8,7168]{1,0:T(8,128)(2,1)S(1)}, bf16[8,7168]{1,0:T(8,128)(2,1)S(1)}, u32[]{:S(2)}, u32[]{:S(2)}) collective-permute-start(bf16[8,7168]{1,0:T(8,128)(2,1)S(1)} %get-tuple-element.15), channel_id=1, source_target_pairs={{0,20},{4,24},{8,28},{12,0},{16,4},{20,8},{24,12},{28,16},{1,21},{... | collective-permute-start | bytes 344072 | tf_op jit(solution)/shard_map/ppermute | solution.py:93
  106.1 15.8 %collective-permute-start.22 = (bf16[8,7168]{1,0:T(8,128)(2,1)S(1)}, bf16[8,7168]{1,0:T(8,128)(2,1)S(1)}, u32[]{:S(2)}, u32[]{:S(2)}) collective-permute-start(bf16[8,7168]{1,0:T(8,128)(2,1)S(1)} %get-tuple-element.17), channel_id=1, source_target_pairs={{0,16},{4,20},{8,24},{12,28},{16,0},{20,4},{24,8},{28,12},{1,17},{... | collective-permute-start | bytes 344072 | tf_op jit(solution)/shard_map/ppermute | solution.py:93
  109.1 17.7 %collective-permute-start.23 = (bf16[8,7168]{1,0:T(8,128)(2,1)S(1)}, bf16[8,7168]{1,0:T(8,128)(2,1)S(1)}, u32[]{:S(2)}, u32[]{:S(2)}) collective-permute-start(bf16[8,7168]{1,0:T(8,128)(2,1)S(1)} %get-tuple-element.20), channel_id=1, source_target_pairs={{0,12},{4,16},{8,20},{12,24},{16,28},{20,0},{24,4},{28,8},{1,13},{... | collective-permute-start | bytes 344072 | tf_op jit(solution)/shard_map/ppermute | solution.py:93
  113.8 13.1 %collective-permute-start.24 = (bf16[8,7168]{1,0:T(8,128)(2,1)S(1)}, bf16[8,7168]{1,0:T(8,128)(2,1)S(1)}, u32[]{:S(2)}, u32[]{:S(2)}) collective-permute-start(bf16[8,7168]{1,0:T(8,128)(2,1)S(1)} %get-tuple-element.19), channel_id=1, source_target_pairs={{0,8},{4,12},{8,16},{12,20},{16,24},{20,28},{24,0},{28,4},{1,9},{5... | collective-permute-start | bytes 344072 | tf_op jit(solution)/shard_map/ppermute | solution.py:93
  113.8 13.1 %collective-permute-start.25 = (bf16[8,7168]{1,0:T(8,128)(2,1)S(1)}, bf16[8,7168]{1,0:T(8,128)(2,1)S(1)}, u32[]{:S(2)}, u32[]{:S(2)}) collective-permute-start(bf16[8,7168]{1,0:T(8,128)(2,1)S(1)} %get-tuple-element.18), channel_id=1, source_target_pairs={{0,4},{4,8},{8,12},{12,16},{16,20},{20,24},{24,28},{28,0},{1,5},{5... | collective-permute-start | bytes 344072 | tf_op jit(solution)/shard_map/ppermute | solution.py:93
  (6 other events, 10.7 us)

commit v16 on v14

--- a/solution.py
+++ b/solution.py
@@ -53,7 +53,7 @@
         b //= 2
     hit = route_ids[:, :, None] == jnp.arange(n_experts, dtype=jnp.int32)[None, None, :]
     wmat = jnp.sum(jnp.where(hit, route_gates[:, :, None], 0.0), axis=1)
-    n_chunks = 2 if n_attn % 2 == 0 else 1
+    n_chunks = 4 if n_attn % 4 == 0 else 1
     per_chunk = n_attn // n_chunks
     pieces = [tokens]
     for k in range(1, n_attn):

time: 98.2 us -> 102 us (1.039)
  starting transfers between devices: 34.4 us -> 40.8 us
  waiting for transfers between devices: 44.1 us -> 37.9 us
  matrix products: 7.13 us -> 9.78 us
  other arithmetic: 5.73 us -> 7.11 us
    ppermute x4 -> x8, waiting for transfers between devices: 16.4 us -> 7.17 us  [bit_reduce(): lax.ppermute(sent, axis, [(i, i ^ bit) for i in range(n)]).astype(x.dtype)]
    ppermute x4 -> x8, starting transfers between devices: 1.84 us -> 6.36 us  [bit_reduce(): lax.ppermute(sent, axis, [(i, i ^ bit) for i in range(n)]).astype(x.dtype)]
    ppermute x7, waiting for transfers between devices: 5.54 us -> 9.89 us  [routed_experts(): lax.ppermute(expert_rows[kk], 'attn', [(s, (s - k) % n_attn) for s in ran...]
    ppermute x7, waiting for transfers between devices: 4.31 us -> 1.1 us  [routed_experts(): lax.ppermute(tokens, 'attn', [(s, (s + k) % n_attn) for s in range(n_attn)])]
    ppermute x2, waiting for transfers between devices: 0.01 us -> 2.91 us  [per_device(): got = lax.ppermute(sent, 'exp', [(i, i ^ bit) for i in range(n_exp)])]
    ppermute x4 -> x8, starting transfers between devices: 3.26 us -> 5.55 us  [bit_gather(): other = lax.ppermute(x, axis, [(i, i ^ bit) for i in range(n)])]
    dot_general x2 -> x4, matrix products: 1.32 us -> 3.01 us  [routed_experts(): jnp.dot(hidden[offset:offset + count], w_down[i], preferred_element_type=...]
    ppermute x4 -> x8, waiting for transfers between devices: 15.8 us -> 14.8 us  [bit_gather(): other = lax.ppermute(x, axis, [(i, i ^ bit) for i in range(n)])]
  transfers between devices with their start and end apart: 26 -> 34, of which waited for: 12 -> 14; matrix products, arithmetic and copies ran while one was open for 14% -> 12% of each run, Pallas kernels for 0% -> 0%
where the time goes in v16:
time: 102 us
  starting transfers between devices  40.8 us (40%)
  waiting for transfers between devices  37.9 us (37%)
  matrix products  9.78 us (10%)
  other arithmetic  7.11 us (7%)
  local copies, waits for them, and re-layouts  5.07 us (5%)
  between operations  1.17 us (1%)
    ppermute x8, waiting for transfers between devices, bit_gather(): other = lax.ppermute(x, axis, [(i, i ^ bit) for i in range(n)])  14.8 us
    ppermute x7, starting transfers between devices, routed_experts(): lax.ppermute(expert_rows[kk], 'attn', [(s, (s - k) % n_attn) for s in ran...  13.6 us
    ppermute x7, starting transfers between devices, routed_experts(): lax.ppermute(tokens, 'attn', [(s, (s + k) % n_attn) for s in range(n_attn)])  12.9 us
    ppermute x7, waiting for transfers between devices, routed_experts(): lax.ppermute(expert_rows[kk], 'attn', [(s, (s - k) % n_attn) for s in ran...  9.89 us
    ppermute x8, waiting for transfers between devices, bit_reduce(): lax.ppermute(sent, axis, [(i, i ^ bit) for i in range(n)]).astype(x.dtype)  7.17 us
    ppermute x8, starting transfers between devices, bit_reduce(): lax.ppermute(sent, axis, [(i, i ^ bit) for i in range(n)]).astype(x.dtype)  6.36 us
    ppermute x8, starting transfers between devices, bit_gather(): other = lax.ppermute(x, axis, [(i, i ^ bit) for i in range(n)])  5.55 us
    unnamed x14, local copies, waits for them, and re-layouts  3.46 us
  transfers between devices with their start and end apart: 34, of which 14 were waited for; matrix products, arithmetic and copies ran while one was open for 12% of the time, Pallas kernels for 0%

profile of v16, /device:TPU:0, one launch (start us, length us, event | category | flops | bytes accessed | tf_op | source)
XLA Modules:
  0.0 101.8 jit_solution(11670563012602845752)
XLA Ops:
  0.7 3.1 %collective-permute-start.7 = (bf16[8,7168]{1,0:T(8,128)(2,1)}, bf16[8,7168]{1,0:T(8,128)(2,1)}, u32[]{:S(2)}, u32[]{:S(2)}) collective-permute-start(bf16[8,7168]{1,0:T(8,128)(2,1)} %param.16), channel_id=1, source_target_pairs={{0,8},{4,12},{8,16},{12,20},{16,24},{20,28},{24,0},{28,4},{1,9},{5... | collective-permute-start | bytes 344072 | tf_op jit(solution)/shard_map/ppermute | solution.py:60
  3.8 2.5 %collective-permute-start.8 = (bf16[8,7168]{1,0:T(8,128)(2,1)}, bf16[8,7168]{1,0:T(8,128)(2,1)}, u32[]{:S(2)}, u32[]{:S(2)}) collective-permute-start(bf16[8,7168]{1,0:T(8,128)(2,1)} %param.16), channel_id=1, source_target_pairs={{0,12},{4,16},{8,20},{12,24},{16,28},{20,0},{24,4},{28,8},{1,13},{... | collective-permute-start | bytes 344072 | tf_op jit(solution)/shard_map/ppermute | solution.py:60
  6.3 1.2 %collective-permute-start.11 = (bf16[8,7168]{1,0:T(8,128)(2,1)}, bf16[8,7168]{1,0:T(8,128)(2,1)S(1)}, u32[]{:S(2)}, u32[]{:S(2)}) collective-permute-start(bf16[8,7168]{1,0:T(8,128)(2,1)} %param.16), channel_id=1, source_target_pairs={{0,16},{4,20},{8,24},{12,28},{16,0},{20,4},{24,8},{28,12},{1,17},{... | collective-permute-start | bytes 344072 | tf_op jit(solution)/shard_map/ppermute | solution.py:60
  7.5 2.6 %collective-permute-start.12 = (bf16[8,7168]{1,0:T(8,128)(2,1)}, bf16[8,7168]{1,0:T(8,128)(2,1)S(1)}, u32[]{:S(2)}, u32[]{:S(2)}) collective-permute-start(bf16[8,7168]{1,0:T(8,128)(2,1)} %param.16), channel_id=1, source_target_pairs={{0,20},{4,24},{8,28},{12,0},{16,4},{20,8},{24,12},{28,16},{1,21},{... | collective-permute-start | bytes 344072 | tf_op jit(solution)/shard_map/ppermute | solution.py:60
  10.9 1.8 %fusion.76 = f32[2,128,1024]{2,1,0:T(8,128)S(1)} fusion(bf16[2,128,512]{2,1,0:T(8,128)(2,1)} %param.11, bf16[2,1024,512]{2,1,0:T(8,128)(2,1)S(1)} %copy-done), kind=kOutput, calls=%fused_computation.137 | convolution fusion | flops 268435456 | bytes 3407872 | tf_op jit(solution)/shard_map/rhl,rpl->rhp/dot_general | solution.py:114
  12.7 1.4 %fusion.75 = (f32[2,128]{1,0:T(2,128)S(1)}, f32[2,128,1024]{2,1,0:T(8,128)S(1)}) fusion(f32[2,128,1024]{2,1,0:T(8,128)S(1)} %fusion.76, bf16[2,64,128]{2,1,0:T(8,128)(2,1)} %param.12, bf16[2,64,1024]{2,1,0:T(8,128)(2,1)} %param.14, pred[2,1024]{1,0:T(4,128)(4,1)S(1)} %broadcast_compare_fusion), kind=kOutput, calls=%fused_computation.136 | convolution fusion | flops 34602752 | bytes 2395136 | tf_op jit(solution)/shard_map/rdh,rdp->rhp/dot_general | solution.py:115
  15.4 1.6 %collective-permute-start.1 = (f32[2,128]{1,0:T(2,128)S(1)}, f32[2,128]{1,0:T(2,128)S(1)}, u32[]{:S(2)}, u32[]{:S(2)}) collective-permute-start(f32[2,128]{1,0:T(2,128)S(1)} %max.6), channel_id=1, source_target_pairs={{0,2},{1,3},{2,0},{3,1},{4,6},{5,7},{6,4},{7,5},{8,10},{9,11},{10,... | collective-permute-start | bytes 3080 | tf_op jit(solution)/shard_map/ppermute | solution.py:136
  17.0 2.1 %collective-permute-done.1 = f32[2,128]{1,0:T(2,128)S(1)} collective-permute-done((f32[2,128]{1,0:T(2,128)S(1)}, f32[2,128]{1,0:T(2,128)S(1)}, u32[]{:S(2)}, u32[]{:S(2)}) %collective-permute-start.1) | collective-permute-done | bytes 1056 | tf_op jit(solution)/shard_map/ppermute | solution.py:136
  19.0 1.4 %collective-permute-start.15 = (bf16[8,7168]{1,0:T(8,128)(2,1)S(1)}, bf16[8,7168]{1,0:T(8,128)(2,1)}, u32[]{:S(2)}, u32[]{:S(2)}) collective-permute-start(bf16[8,7168]{1,0:T(8,128)(2,1)S(1)} %copy-done.2), channel_id=1, source_target_pairs={{0,24},{4,28},{8,0},{12,4},{16,8},{20,12},{24,16},{28,20},{1,25},{... | collective-permute-start | bytes 344072 | tf_op jit(solution)/shard_map/ppermute | solution.py:60
  20.4 1.3 %broadcast_multiply_fusion = f32[2,128,512]{2,1,0:T(8,128)} fusion(f32[2,128]{1,0:T(2,128)S(1)} %get-tuple-element.3, bf16[2,1024,512]{2,1,0:T(8,128)(2,1)S(1)} %copy-done, f32[2,128,1024]{2,1,0:T(8,128)S(1)} %get-tuple-element.45, f32[2,128]{1,0:T(2,128)S(1)} %get-tuple-element.44, pred[2,1024]{1,0:T(4,128)(4,1)S(1)} %broadcast_compare_fusion), kind=kOutput, calls=%fused_computation.58 | convolution fusion | flops 269352960 | bytes 3674112 | tf_op jit(solution)/shard_map/rhp,rpl->rhl/dot_general | solution.py:125
  23.1 1.5 %collective-permute-start.16 = (bf16[8,7168]{1,0:T(8,128)(2,1)S(1)}, bf16[8,7168]{1,0:T(8,128)(2,1)S(1)}, u32[]{:S(2)}, u32[]{:S(2)}) collective-permute-start(bf16[8,7168]{1,0:T(8,128)(2,1)S(1)} %copy-done.2), channel_id=1, source_target_pairs={{0,28},{4,0},{8,4},{12,8},{16,12},{20,16},{24,20},{28,24},{1,29},{... | collective-permute-start | bytes 344072 | tf_op jit(solution)/shard_map/ppermute | solution.py:60
  26.3 1.6 %collective-permute-start.9 = (bf16[2,8,7168]{2,1,0:T(8,128)(2,1)S(1)}, bf16[2,8,7168]{2,1,0:T(8,128)(2,1)S(1)}, u32[]{:S(2)}, u32[]{:S(2)}) collective-permute-start(bf16[2,8,7168]{2,1,0:T(8,128)(2,1)S(1)} %get-tuple-element.31), channel_id=1, source_target_pairs={{0,2},{1,3},{2,0},{3,1},{4,6},{5,7},{6,4},{7,5},{8,10},{9,11},{10,... | collective-permute-start | bytes 688136 | tf_op jit(solution)/shard_map/ppermute | solution.py:34
  29.4 1.6 %collective-permute-start.17 = (bf16[2,8,7168]{2,1,0:T(8,128)(2,1)S(1)}, bf16[2,8,7168]{2,1,0:T(8,128)(2,1)S(1)}, u32[]{:S(2)}, u32[]{:S(2)}) collective-permute-start(bf16[2,8,7168]{2,1,0:T(8,128)(2,1)S(1)} %get-tuple-element.35), channel_id=1, source_target_pairs={{0,2},{1,3},{2,0},{3,1},{4,6},{5,7},{6,4},{7,5},{8,10},{9,11},{10,... | collective-permute-start | bytes 688136 | tf_op jit(solution)/shard_map/ppermute | solution.py:34
  32.1 1.6 %collective-permute-start.5 = (bf16[2,8,7168]{2,1,0:T(8,128)(2,1)S(1)}, bf16[2,8,7168]{2,1,0:T(8,128)(2,1)S(1)}, u32[]{:S(2)}, u32[]{:S(2)}) collective-permute-start(bf16[2,8,7168]{2,1,0:T(8,128)(2,1)S(1)} %get-tuple-element.29), channel_id=1, source_target_pairs={{0,2},{1,3},{2,0},{3,1},{4,6},{5,7},{6,4},{7,5},{8,10},{9,11},{10,... | collective-permute-start | bytes 688136 | tf_op jit(solution)/shard_map/ppermute | solution.py:34
  34.9 4.8 %collective-permute-done.13 = bf16[2,8,7168]{2,1,0:T(8,128)(2,1)S(1)} collective-permute-done((bf16[2,8,7168]{2,1,0:T(8,128)(2,1)S(1)}, bf16[2,8,7168]{2,1,0:T(8,128)(2,1)S(1)}, u32[]{:S(2)}, u32[]{:S(2)}) %collective-permute-start.13) | collective-permute-done | bytes 229408 | tf_op jit(solution)/shard_map/ppermute | solution.py:34
  39.8 4.8 %collective-permute-done.17 = bf16[2,8,7168]{2,1,0:T(8,128)(2,1)S(1)} collective-permute-done((bf16[2,8,7168]{2,1,0:T(8,128)(2,1)S(1)}, bf16[2,8,7168]{2,1,0:T(8,128)(2,1)S(1)}, u32[]{:S(2)}, u32[]{:S(2)}) %collective-permute-start.17) | collective-permute-done | bytes 229408 | tf_op jit(solution)/shard_map/ppermute | solution.py:34
  44.7 4.8 %collective-permute-done.5 = bf16[2,8,7168]{2,1,0:T(8,128)(2,1)S(1)} collective-permute-done((bf16[2,8,7168]{2,1,0:T(8,128)(2,1)S(1)}, bf16[2,8,7168]{2,1,0:T(8,128)(2,1)S(1)}, u32[]{:S(2)}, u32[]{:S(2)}) %collective-permute-start.5) | collective-permute-done | bytes 229408 | tf_op jit(solution)/shard_map/ppermute | solution.py:34
  49.6 2.9 %collective-permute-done.3 = f32[2,1,32,513]{3,2,0,1:T(8,128)S(1)} collective-permute-done((f32[2,1,32,513]{3,2,0,1:T(8,128)S(1)}, f32[2,1,32,513]{3,2,0,1:T(8,128)S(1)}, u32[]{:S(2)}, u32[]{:S(2)}) %collective-permute-start.3) | collective-permute-done | bytes 131360 | tf_op jit(solution)/shard_map/ppermute | solution.py:149
  53.1 1.6 %copy-done.5 = bf16[1,7168,256]{2,1,0:T(8,128)(2,1)S(1)} copy-done((bf16[1,7168,256]{2,1,0:T(8,128)(2,1)S(1)}, bf16[1,7168,256]{2,1,0:T(8,128)(2,1)}, u32[]{:S(2)}) %copy-start.5) | copy-done | bytes 3670040
  56.7 1.2 %fusion.17 = bf16[256,256]{1,0:T(8,128)(2,1)S(1)} fusion(bf16[1,7168,256]{2,1,0:T(8,128)(2,1)S(1)} %copy-done.6, bf16[64,7168]{1,0:T(8,128)(2,1)S(1)} %bitcast.161, bf16[64,7168]{1,0:T(8,128)(2,1)S(1)} %bitcast.159, bf16[64,7168]{1,0:T(8,128)(2,1)S(1)} %bitcast.157, bf16[64,7168]{1,0:T(8,128)(2,1)S(1)} %bitcast.163, f32[256,256]{1,0:T(8,128)S(1)} %fusion.10), kind=kOutput, calls=%fused_computation.18 | convolution fusion | flops 954597376 | bytes 7733248 | tf_op jit(solution)/shard_map/dot_general | solution.py:74
  64.6 1.6 %collective-permute-start.20 = (bf16[2,8,7168]{2,1,0:T(8,128)(2,1)S(1)}, bf16[2,8,7168]{2,1,0:T(8,128)(2,1)S(1)}, u32[]{:S(2)}, u32[]{:S(2)}) collective-permute-start(bf16[2,8,7168]{2,1,0:T(8,128)(2,1)S(1)} %fusion.37), channel_id=1, source_target_pairs={{0,2},{1,3},{2,0},{3,1},{4,6},{5,7},{6,4},{7,5},{8,10},{9,11},{10,... | collective-permute-start | bytes 688136 | tf_op jit(solution)/shard_map/ppermute | solution.py:40
  66.3 1.2 %collective-permute-start.23 = (bf16[2,8,7168]{2,1,0:T(8,128)(2,1)S(1)}, bf16[2,8,7168]{2,1,0:T(8,128)(2,1)S(1)}, u32[]{:S(2)}, u32[]{:S(2)}) collective-permute-start(bf16[2,8,7168]{2,1,0:T(8,128)(2,1)S(1)} %fusion.38), channel_id=1, source_target_pairs={{0,2},{1,3},{2,0},{3,1},{4,6},{5,7},{6,4},{7,5},{8,10},{9,11},{10,... | collective-permute-start | bytes 688136 | tf_op jit(solution)/shard_map/ppermute | solution.py:40
  67.6 1.2 %collective-permute-start.27 = (bf16[2,8,7168]{2,1,0:T(8,128)(2,1)S(1)}, bf16[2,8,7168]{2,1,0:T(8,128)(2,1)S(1)}, u32[]{:S(2)}, u32[]{:S(2)}) collective-permute-start(bf16[2,8,7168]{2,1,0:T(8,128)(2,1)S(1)} %fusion.39), channel_id=1, source_target_pairs={{0,2},{1,3},{2,0},{3,1},{4,6},{5,7},{6,4},{7,5},{8,10},{9,11},{10,... | collective-permute-start | bytes 688136 | tf_op jit(solution)/shard_map/ppermute | solution.py:40
  68.9 1.2 %collective-permute-start.31 = (bf16[2,8,7168]{2,1,0:T(8,128)(2,1)S(1)}, bf16[2,8,7168]{2,1,0:T(8,128)(2,1)S(1)}, u32[]{:S(2)}, u32[]{:S(2)}) collective-permute-start(bf16[2,8,7168]{2,1,0:T(8,128)(2,1)S(1)} %fusion.40), channel_id=1, source_target_pairs={{0,2},{1,3},{2,0},{3,1},{4,6},{5,7},{6,4},{7,5},{8,10},{9,11},{10,... | collective-permute-start | bytes 688136 | tf_op jit(solution)/shard_map/ppermute | solution.py:40
  70.1 3.0 %collective-permute-done.20 = bf16[2,8,7168]{2,1,0:T(8,128)(2,1)S(1)} collective-permute-done((bf16[2,8,7168]{2,1,0:T(8,128)(2,1)S(1)}, bf16[2,8,7168]{2,1,0:T(8,128)(2,1)S(1)}, u32[]{:S(2)}, u32[]{:S(2)}) %collective-permute-start.20) | collective-permute-done | bytes 229408 | tf_op jit(solution)/shard_map/ppermute | solution.py:40
  73.2 4.2 %collective-permute-start.21 = (bf16[8,7168]{1,0:T(8,128)(2,1)S(1)}, bf16[8,7168]{1,0:T(8,128)(2,1)S(1)}, u32[]{:S(2)}, u32[]{:S(2)}) collective-permute-start(bf16[8,7168]{1,0:T(8,128)(2,1)S(1)} %slice_bitcast_fusion.10), channel_id=1, source_target_pairs={{0,28},{4,0},{8,4},{12,8},{16,12},{20,16},{24,20},{28,24},{1,29},{... | collective-permute-start | bytes 344072 | tf_op jit(solution)/shard_map/ppermute | solution.py:92
  78.6 3.5 %collective-permute-start.25 = (bf16[8,7168]{1,0:T(8,128)(2,1)S(1)}, bf16[8,7168]{1,0:T(8,128)(2,1)S(1)}, u32[]{:S(2)}, u32[]{:S(2)}) collective-permute-start(bf16[8,7168]{1,0:T(8,128)(2,1)S(1)} %get-tuple-element.23), channel_id=1, source_target_pairs={{0,20},{4,24},{8,28},{12,0},{16,4},{20,8},{24,12},{28,16},{1,21},{... | collective-permute-start | bytes 344072 | tf_op jit(solution)/shard_map/ppermute | solution.py:92
  83.0 2.3 %collective-permute-start.28 = (bf16[8,7168]{1,0:T(8,128)(2,1)S(1)}, bf16[8,7168]{1,0:T(8,128)(2,1)S(1)}, u32[]{:S(2)}, u32[]{:S(2)}) collective-permute-start(bf16[8,7168]{1,0:T(8,128)(2,1)S(1)} %get-tuple-element.24), channel_id=1, source_target_pairs={{0,16},{4,20},{8,24},{12,28},{16,0},{20,4},{24,8},{28,12},{1,17},{... | collective-permute-start | bytes 344072 | tf_op jit(solution)/shard_map/ppermute | solution.py:92
  85.3 1.7 %collective-permute-done.31 = bf16[2,8,7168]{2,1,0:T(8,128)(2,1)S(1)} collective-permute-done((bf16[2,8,7168]{2,1,0:T(8,128)(2,1)S(1)}, bf16[2,8,7168]{2,1,0:T(8,128)(2,1)S(1)}, u32[]{:S(2)}, u32[]{:S(2)}) %collective-permute-start.31) | collective-permute-done | bytes 229408 | tf_op jit(solution)/shard_map/ppermute | solution.py:40
  87.1 2.5 %collective-permute-start.29 = (bf16[8,7168]{1,0:T(8,128)(2,1)S(1)}, bf16[8,7168]{1,0:T(8,128)(2,1)S(1)}, u32[]{:S(2)}, u32[]{:S(2)}) collective-permute-start(bf16[8,7168]{1,0:T(8,128)(2,1)S(1)} %get-tuple-element.25), channel_id=1, source_target_pairs={{0,12},{4,16},{8,20},{12,24},{16,28},{20,0},{24,4},{28,8},{1,13},{... | collective-permute-start | bytes 344072 | tf_op jit(solution)/shard_map/ppermute | solution.py:92
  91.0 6.9 %collective-permute-done.28 = bf16[8,7168]{1,0:T(8,128)(2,1)S(1)} collective-permute-done((bf16[8,7168]{1,0:T(8,128)(2,1)S(1)}, bf16[8,7168]{1,0:T(8,128)(2,1)S(1)}, u32[]{:S(2)}, u32[]{:S(2)}) %collective-permute-start.28) | collective-permute-done | bytes 114720 | tf_op jit(solution)/shard_map/ppermute | solution.py:92
  97.9 3.0 %collective-permute-done.29 = bf16[8,7168]{1,0:T(8,128)(2,1)S(1)} collective-permute-done((bf16[8,7168]{1,0:T(8,128)(2,1)S(1)}, bf16[8,7168]{1,0:T(8,128)(2,1)S(1)}, u32[]{:S(2)}, u32[]{:S(2)}) %collective-permute-start.29) | collective-permute-done | bytes 114720 | tf_op jit(solution)/shard_map/ppermute | solution.py:92
  (113 shorter events, 23.2 us)
Async XLA Ops:
  0.7 22.4 %collective-permute-start.7 = (bf16[8,7168]{1,0:T(8,128)(2,1)}, bf16[8,7168]{1,0:T(8,128)(2,1)}, u32[]{:S(2)}, u32[]{:S(2)}) collective-permute-start(bf16[8,7168]{1,0:T(8,128)(2,1)} %param.16), channel_id=1, source_target_pairs={{0,8},{4,12},{8,16},{12,20},{16,24},{20,28},{24,0},{28,4},{1,9},{5... | collective-permute-start | bytes 344072 | tf_op jit(solution)/shard_map/ppermute | solution.py:60
  3.8 20.8 %collective-permute-start.8 = (bf16[8,7168]{1,0:T(8,128)(2,1)}, bf16[8,7168]{1,0:T(8,128)(2,1)}, u32[]{:S(2)}, u32[]{:S(2)}) collective-permute-start(bf16[8,7168]{1,0:T(8,128)(2,1)} %param.16), channel_id=1, source_target_pairs={{0,12},{4,16},{8,20},{12,24},{16,28},{20,0},{24,4},{28,8},{1,13},{... | collective-permute-start | bytes 344072 | tf_op jit(solution)/shard_map/ppermute | solution.py:60
  6.3 19.9 %collective-permute-start.11 = (bf16[8,7168]{1,0:T(8,128)(2,1)}, bf16[8,7168]{1,0:T(8,128)(2,1)S(1)}, u32[]{:S(2)}, u32[]{:S(2)}) collective-permute-start(bf16[8,7168]{1,0:T(8,128)(2,1)} %param.16), channel_id=1, source_target_pairs={{0,16},{4,20},{8,24},{12,28},{16,0},{20,4},{24,8},{28,12},{1,17},{... | collective-permute-start | bytes 344072 | tf_op jit(solution)/shard_map/ppermute | solution.py:60
  7.5 18.7 %collective-permute-start.12 = (bf16[8,7168]{1,0:T(8,128)(2,1)}, bf16[8,7168]{1,0:T(8,128)(2,1)S(1)}, u32[]{:S(2)}, u32[]{:S(2)}) collective-permute-start(bf16[8,7168]{1,0:T(8,128)(2,1)} %param.16), channel_id=1, source_target_pairs={{0,20},{4,24},{8,28},{12,0},{16,4},{20,8},{24,12},{28,16},{1,21},{... | collective-permute-start | bytes 344072 | tf_op jit(solution)/shard_map/ppermute | solution.py:60
  15.4 3.6 %collective-permute-start.1 = (f32[2,128]{1,0:T(2,128)S(1)}, f32[2,128]{1,0:T(2,128)S(1)}, u32[]{:S(2)}, u32[]{:S(2)}) collective-permute-start(f32[2,128]{1,0:T(2,128)S(1)} %max.6), channel_id=1, source_target_pairs={{0,2},{1,3},{2,0},{3,1},{4,6},{5,7},{6,4},{7,5},{8,10},{9,11},{10,... | collective-permute-start | bytes 3080 | tf_op jit(solution)/shard_map/ppermute | solution.py:136
  19.0 8.8 %collective-permute-start.15 = (bf16[8,7168]{1,0:T(8,128)(2,1)S(1)}, bf16[8,7168]{1,0:T(8,128)(2,1)}, u32[]{:S(2)}, u32[]{:S(2)}) collective-permute-start(bf16[8,7168]{1,0:T(8,128)(2,1)S(1)} %copy-done.2), channel_id=1, source_target_pairs={{0,24},{4,28},{8,0},{12,4},{16,8},{20,12},{24,16},{28,20},{1,25},{... | collective-permute-start | bytes 344072 | tf_op jit(solution)/shard_map/ppermute | solution.py:60
  23.1 5.4 %collective-permute-start.16 = (bf16[8,7168]{1,0:T(8,128)(2,1)S(1)}, bf16[8,7168]{1,0:T(8,128)(2,1)S(1)}, u32[]{:S(2)}, u32[]{:S(2)}) collective-permute-start(bf16[8,7168]{1,0:T(8,128)(2,1)S(1)} %copy-done.2), channel_id=1, source_target_pairs={{0,28},{4,0},{8,4},{12,8},{16,12},{20,16},{24,20},{28,24},{1,29},{... | collective-permute-start | bytes 344072 | tf_op jit(solution)/shard_map/ppermute | solution.py:60
  24.6 7.5 %collective-permute-start.4 = (bf16[8,7168]{1,0:T(8,128)(2,1)S(1)}, bf16[8,7168]{1,0:T(8,128)(2,1)S(1)}, u32[]{:S(2)}, u32[]{:S(2)}) collective-permute-start(bf16[8,7168]{1,0:T(8,128)(2,1)S(1)} %copy-done.2), channel_id=1, source_target_pairs={{0,4},{4,8},{8,12},{12,16},{16,20},{20,24},{24,28},{28,0},{1,5},{5... | collective-permute-start | bytes 344072 | tf_op jit(solution)/shard_map/ppermute | solution.py:60
  26.2 7.5 %collective-permute-start.2 = (f32[2,2,32,513]{3,2,0,1:T(8,128)S(1)}, f32[2,2,32,513]{3,2,0,1:T(8,128)S(1)}, u32[]{:S(2)}, u32[]{:S(2)}) collective-permute-start(f32[2,2,32,513]{3,2,0,1:T(8,128)S(1)} %bitcast.168), channel_id=1, source_target_pairs={{0,1},{1,0},{2,3},{3,2},{4,5},{5,4},{6,7},{7,6},{8,9},{9,8},{10,11... | collective-permute-start | bytes 787976 | tf_op jit(solution)/shard_map/ppermute | solution.py:149
  26.3 8.5 %collective-permute-start.9 = (bf16[2,8,7168]{2,1,0:T(8,128)(2,1)S(1)}, bf16[2,8,7168]{2,1,0:T(8,128)(2,1)S(1)}, u32[]{:S(2)}, u32[]{:S(2)}) collective-permute-start(bf16[2,8,7168]{2,1,0:T(8,128)(2,1)S(1)} %get-tuple-element.31), channel_id=1, source_target_pairs={{0,2},{1,3},{2,0},{3,1},{4,6},{5,7},{6,4},{7,5},{8,10},{9,11},{10,... | collective-permute-start | bytes 688136 | tf_op jit(solution)/shard_map/ppermute | solution.py:34
  27.9 11.8 %collective-permute-start.13 = (bf16[2,8,7168]{2,1,0:T(8,128)(2,1)S(1)}, bf16[2,8,7168]{2,1,0:T(8,128)(2,1)S(1)}, u32[]{:S(2)}, u32[]{:S(2)}) collective-permute-start(bf16[2,8,7168]{2,1,0:T(8,128)(2,1)S(1)} %get-tuple-element.33), channel_id=1, source_target_pairs={{0,2},{1,3},{2,0},{3,1},{4,6},{5,7},{6,4},{7,5},{8,10},{9,11},{10,... | collective-permute-start | bytes 688136 | tf_op jit(solution)/shard_map/ppermute | solution.py:34
  29.4 15.2 %collective-permute-start.17 = (bf16[2,8,7168]{2,1,0:T(8,128)(2,1)S(1)}, bf16[2,8,7168]{2,1,0:T(8,128)(2,1)S(1)}, u32[]{:S(2)}, u32[]{:S(2)}) collective-permute-start(bf16[2,8,7168]{2,1,0:T(8,128)(2,1)S(1)} %get-tuple-element.35), channel_id=1, source_target_pairs={{0,2},{1,3},{2,0},{3,1},{4,6},{5,7},{6,4},{7,5},{8,10},{9,11},{10,... | collective-permute-start | bytes 688136 | tf_op jit(solution)/shard_map/ppermute | solution.py:34
  32.1 17.4 %collective-permute-start.5 = (bf16[2,8,7168]{2,1,0:T(8,128)(2,1)S(1)}, bf16[2,8,7168]{2,1,0:T(8,128)(2,1)S(1)}, u32[]{:S(2)}, u32[]{:S(2)}) collective-permute-start(bf16[2,8,7168]{2,1,0:T(8,128)(2,1)S(1)} %get-tuple-element.29), channel_id=1, source_target_pairs={{0,2},{1,3},{2,0},{3,1},{4,6},{5,7},{6,4},{7,5},{8,10},{9,11},{10,... | collective-permute-start | bytes 688136 | tf_op jit(solution)/shard_map/ppermute | solution.py:34
  33.7 18.8 %collective-permute-start.3 = (f32[2,1,32,513]{3,2,0,1:T(8,128)S(1)}, f32[2,1,32,513]{3,2,0,1:T(8,128)S(1)}, u32[]{:S(2)}, u32[]{:S(2)}) collective-permute-start(f32[2,1,32,513]{3,2,0,1:T(8,128)S(1)} %constant_dynamic-slice_fusion), channel_id=1, source_target_pairs={{0,2},{1,3},{2,0},{3,1},{4,6},{5,7},{6,4},{7,5},{8,10},{9,11},{10,... | collective-permute-start | bytes 393992 | tf_op jit(solution)/shard_map/ppermute | solution.py:149
  34.8 17.8 %collective-permute-start.10 = (bf16[2,2,8,7168]{3,2,1,0:T(8,128)(2,1)S(1)}, bf16[2,2,8,7168]{3,2,1,0:T(8,128)(2,1)S(1)}, u32[]{:S(2)}, u32[]{:S(2)}) collective-permute-start(bf16[2,2,8,7168]{3,2,1,0:T(8,128)(2,1)S(1)} %get-tuple-element.17), channel_id=1, source_target_pairs={{0,1},{1,0},{2,3},{3,2},{4,5},{5,4},{6,7},{7,6},{8,9},{9,8},{10,11... | collective-permute-start | bytes 1376264 | tf_op jit(solution)/shard_map/ppermute | solution.py:34
  39.7 13.0 %collective-permute-start.14 = (bf16[2,2,8,7168]{3,2,1,0:T(8,128)(2,1)S(1)}, bf16[2,2,8,7168]{3,2,1,0:T(8,128)(2,1)S(1)}, u32[]{:S(2)}, u32[]{:S(2)}) collective-permute-start(bf16[2,2,8,7168]{3,2,1,0:T(8,128)(2,1)S(1)} %get-tuple-element.19), channel_id=1, source_target_pairs={{0,1},{1,0},{2,3},{3,2},{4,5},{5,4},{6,7},{7,6},{8,9},{9,8},{10,11... | collective-permute-start | bytes 1376264 | tf_op jit(solution)/shard_map/ppermute | solution.py:34
  44.6 8.2 %collective-permute-start.18 = (bf16[2,2,8,7168]{3,2,1,0:T(8,128)(2,1)S(1)}, bf16[2,2,8,7168]{3,2,1,0:T(8,128)(2,1)S(1)}, u32[]{:S(2)}, u32[]{:S(2)}) collective-permute-start(bf16[2,2,8,7168]{3,2,1,0:T(8,128)(2,1)S(1)} %get-tuple-element.21), channel_id=1, source_target_pairs={{0,1},{1,0},{2,3},{3,2},{4,5},{5,4},{6,7},{7,6},{8,9},{9,8},{10,11... | collective-permute-start | bytes 1376264 | tf_op jit(solution)/shard_map/ppermute | solution.py:34
  49.6 3.4 %collective-permute-start.6 = (bf16[2,2,8,7168]{3,2,1,0:T(8,128)(2,1)S(1)}, bf16[2,2,8,7168]{3,2,1,0:T(8,128)(2,1)S(1)}, u32[]{:S(2)}, u32[]{:S(2)}) collective-permute-start(bf16[2,2,8,7168]{3,2,1,0:T(8,128)(2,1)S(1)} %get-tuple-element.15), channel_id=1, source_target_pairs={{0,1},{1,0},{2,3},{3,2},{4,5},{5,4},{6,7},{7,6},{8,9},{9,8},{10,11... | collective-permute-start | bytes 1376264 | tf_op jit(solution)/shard_map/ppermute | solution.py:34
  62.1 4.0 %collective-permute-start.22 = (f32[2,2,8,7168]{3,2,1,0:T(8,128)S(1)}, f32[2,2,8,7168]{3,2,1,0:T(8,128)S(1)}, u32[]{:S(2)}, u32[]{:S(2)}) collective-permute-start(f32[2,2,8,7168]{3,2,1,0:T(8,128)S(1)} %bitcast.154), channel_id=1, source_target_pairs={{0,1},{1,0},{2,3},{3,2},{4,5},{5,4},{6,7},{7,6},{8,9},{9,8},{10,11... | collective-permute-start | bytes 2752520 | tf_op jit(solution)/shard_map/ppermute | solution.py:40
  62.8 4.7 %collective-permute-start.26 = (f32[2,2,8,7168]{3,2,1,0:T(8,128)S(1)}, f32[2,2,8,7168]{3,2,1,0:T(8,128)S(1)}, u32[]{:S(2)}, u32[]{:S(2)}) collective-permute-start(f32[2,2,8,7168]{3,2,1,0:T(8,128)S(1)} %bitcast.153), channel_id=1, source_target_pairs={{0,1},{1,0},{2,3},{3,2},{4,5},{5,4},{6,7},{7,6},{8,9},{9,8},{10,11... | collective-permute-start | bytes 2752520 | tf_op jit(solution)/shard_map/ppermute | solution.py:40
  63.0 5.8 %collective-permute-start.30 = (f32[2,2,8,7168]{3,2,1,0:T(8,128)S(1)}, f32[2,2,8,7168]{3,2,1,0:T(8,128)S(1)}, u32[]{:S(2)}, u32[]{:S(2)}) collective-permute-start(f32[2,2,8,7168]{3,2,1,0:T(8,128)S(1)} %bitcast.152), channel_id=1, source_target_pairs={{0,1},{1,0},{2,3},{3,2},{4,5},{5,4},{6,7},{7,6},{8,9},{9,8},{10,11... | collective-permute-start | bytes 2752520 | tf_op jit(solution)/shard_map/ppermute | solution.py:40
  64.6 8.5 %collective-permute-start.20 = (bf16[2,8,7168]{2,1,0:T(8,128)(2,1)S(1)}, bf16[2,8,7168]{2,1,0:T(8,128)(2,1)S(1)}, u32[]{:S(2)}, u32[]{:S(2)}) collective-permute-start(bf16[2,8,7168]{2,1,0:T(8,128)(2,1)S(1)} %fusion.37), channel_id=1, source_target_pairs={{0,2},{1,3},{2,0},{3,1},{4,6},{5,7},{6,4},{7,5},{8,10},{9,11},{10,... | collective-permute-start | bytes 688136 | tf_op jit(solution)/shard_map/ppermute | solution.py:40
  66.3 11.7 %collective-permute-start.23 = (bf16[2,8,7168]{2,1,0:T(8,128)(2,1)S(1)}, bf16[2,8,7168]{2,1,0:T(8,128)(2,1)S(1)}, u32[]{:S(2)}, u32[]{:S(2)}) collective-permute-start(bf16[2,8,7168]{2,1,0:T(8,128)(2,1)S(1)} %fusion.38), channel_id=1, source_target_pairs={{0,2},{1,3},{2,0},{3,1},{4,6},{5,7},{6,4},{7,5},{8,10},{9,11},{10,... | collective-permute-start | bytes 688136 | tf_op jit(solution)/shard_map/ppermute | solution.py:40
  67.6 15.3 %collective-permute-start.27 = (bf16[2,8,7168]{2,1,0:T(8,128)(2,1)S(1)}, bf16[2,8,7168]{2,1,0:T(8,128)(2,1)S(1)}, u32[]{:S(2)}, u32[]{:S(2)}) collective-permute-start(bf16[2,8,7168]{2,1,0:T(8,128)(2,1)S(1)} %fusion.39), channel_id=1, source_target_pairs={{0,2},{1,3},{2,0},{3,1},{4,6},{5,7},{6,4},{7,5},{8,10},{9,11},{10,... | collective-permute-start | bytes 688136 | tf_op jit(solution)/shard_map/ppermute | solution.py:40
  68.9 18.1 %collective-permute-start.31 = (bf16[2,8,7168]{2,1,0:T(8,128)(2,1)S(1)}, bf16[2,8,7168]{2,1,0:T(8,128)(2,1)S(1)}, u32[]{:S(2)}, u32[]{:S(2)}) collective-permute-start(bf16[2,8,7168]{2,1,0:T(8,128)(2,1)S(1)} %fusion.40), channel_id=1, source_target_pairs={{0,2},{1,3},{2,0},{3,1},{4,6},{5,7},{6,4},{7,5},{8,10},{9,11},{10,... | collective-permute-start | bytes 688136 | tf_op jit(solution)/shard_map/ppermute | solution.py:40
  73.2 16.5 %collective-permute-start.21 = (bf16[8,7168]{1,0:T(8,128)(2,1)S(1)}, bf16[8,7168]{1,0:T(8,128)(2,1)S(1)}, u32[]{:S(2)}, u32[]{:S(2)}) collective-permute-start(bf16[8,7168]{1,0:T(8,128)(2,1)S(1)} %slice_bitcast_fusion.10), channel_id=1, source_target_pairs={{0,28},{4,0},{8,4},{12,8},{16,12},{20,16},{24,20},{28,24},{1,29},{... | collective-permute-start | bytes 344072 | tf_op jit(solution)/shard_map/ppermute | solution.py:92
  78.1 11.6 %collective-permute-start.24 = (bf16[8,7168]{1,0:T(8,128)(2,1)S(1)}, bf16[8,7168]{1,0:T(8,128)(2,1)S(1)}, u32[]{:S(2)}, u32[]{:S(2)}) collective-permute-start(bf16[8,7168]{1,0:T(8,128)(2,1)S(1)} %get-tuple-element.22), channel_id=1, source_target_pairs={{0,24},{4,28},{8,0},{12,4},{16,8},{20,12},{24,16},{28,20},{1,25},{... | collective-permute-start | bytes 344072 | tf_op jit(solution)/shard_map/ppermute | solution.py:92
  78.6 12.4 %collective-permute-start.25 = (bf16[8,7168]{1,0:T(8,128)(2,1)S(1)}, bf16[8,7168]{1,0:T(8,128)(2,1)S(1)}, u32[]{:S(2)}, u32[]{:S(2)}) collective-permute-start(bf16[8,7168]{1,0:T(8,128)(2,1)S(1)} %get-tuple-element.23), channel_id=1, source_target_pairs={{0,20},{4,24},{8,28},{12,0},{16,4},{20,8},{24,12},{28,16},{1,21},{... | collective-permute-start | bytes 344072 | tf_op jit(solution)/shard_map/ppermute | solution.py:92
  83.0 14.9 %collective-permute-start.28 = (bf16[8,7168]{1,0:T(8,128)(2,1)S(1)}, bf16[8,7168]{1,0:T(8,128)(2,1)S(1)}, u32[]{:S(2)}, u32[]{:S(2)}) collective-permute-start(bf16[8,7168]{1,0:T(8,128)(2,1)S(1)} %get-tuple-element.24), channel_id=1, source_target_pairs={{0,16},{4,20},{8,24},{12,28},{16,0},{20,4},{24,8},{28,12},{1,17},{... | collective-permute-start | bytes 344072 | tf_op jit(solution)/shard_map/ppermute | solution.py:92
  87.1 13.8 %collective-permute-start.29 = (bf16[8,7168]{1,0:T(8,128)(2,1)S(1)}, bf16[8,7168]{1,0:T(8,128)(2,1)S(1)}, u32[]{:S(2)}, u32[]{:S(2)}) collective-permute-start(bf16[8,7168]{1,0:T(8,128)(2,1)S(1)} %get-tuple-element.25), channel_id=1, source_target_pairs={{0,12},{4,16},{8,20},{12,24},{16,28},{20,0},{24,4},{28,8},{1,13},{... | collective-permute-start | bytes 344072 | tf_op jit(solution)/shard_map/ppermute | solution.py:92
  89.7 11.2 %collective-permute-start.32 = (bf16[8,7168]{1,0:T(8,128)(2,1)S(1)}, bf16[8,7168]{1,0:T(8,128)(2,1)S(1)}, u32[]{:S(2)}, u32[]{:S(2)}) collective-permute-start(bf16[8,7168]{1,0:T(8,128)(2,1)S(1)} %get-tuple-element.26), channel_id=1, source_target_pairs={{0,8},{4,12},{8,16},{12,20},{16,24},{20,28},{24,0},{28,4},{1,9},{5... | collective-permute-start | bytes 344072 | tf_op jit(solution)/shard_map/ppermute | solution.py:92
  89.7 11.1 %collective-permute-start.33 = (bf16[8,7168]{1,0:T(8,128)(2,1)S(1)}, bf16[8,7168]{1,0:T(8,128)(2,1)S(1)}, u32[]{:S(2)}, u32[]{:S(2)}) collective-permute-start(bf16[8,7168]{1,0:T(8,128)(2,1)S(1)} %get-tuple-element.27), channel_id=1, source_target_pairs={{0,4},{4,8},{8,12},{12,16},{16,20},{20,24},{24,28},{28,0},{1,5},{5... | collective-permute-start | bytes 344072 | tf_op jit(solution)/shard_map/ppermute | solution.py:92
  (9 other events, 65.7 us)

commit v17 on v14

--- a/solution.py
+++ b/solution.py
@@ -81,7 +81,7 @@
             offset += count
             part = part.reshape(block.shape[:-1] + (model_width,))
             for bit in reversed(bits):
-                wire = jnp.bfloat16 if bit == bits[0] else None
+                wire = jnp.bfloat16
                 part = bit_reduce(part, "exp", bit, n_exp, wire)
             expert_rows = part.astype(jnp.bfloat16)
             for kk in range(per_chunk):

time: 98.2 us -> 98.7 us (level)
  local copies, waits for them, and re-layouts: 4.81 us -> 8.12 us
  waiting for transfers between devices: 44.1 us -> 41.1 us
    ppermute x4, waiting for transfers between devices: 16.4 us -> 13.4 us  [bit_reduce(): lax.ppermute(sent, axis, [(i, i ^ bit) for i in range(n)]).astype(x.dtype)]
    unnamed x20 -> x24, local copies, waits for them, and re-layouts: 3.02 us -> 6.05 us
  transfers between devices with their start and end apart: 26 -> 26, of which waited for: 12 -> 11; matrix products, arithmetic and copies ran while one was open for 14% -> 14% of each run, Pallas kernels for 0% -> 0%
where the time goes in v17:
time: 98.7 us; the launch traced here: 97.5 us
  waiting for transfers between devices  41.1 us (42%)
  starting transfers between devices  34.5 us (35%)
  local copies, waits for them, and re-layouts  8.12 us (8%)
  matrix products  7.13 us (7%)
  other arithmetic  5.68 us (6%)
  between operations  0.99 us (1%)
    ppermute x4, waiting for transfers between devices, bit_gather(): other = lax.ppermute(x, axis, [(i, i ^ bit) for i in range(n)])  15.7 us
    ppermute x7, starting transfers between devices, routed_experts(): lax.ppermute(expert_rows[kk], 'attn', [(s, (s - k) % n_attn) for s in ran...  13.5 us
    ppermute x4, waiting for transfers between devices, bit_reduce(): lax.ppermute(sent, axis, [(i, i ^ bit) for i in range(n)]).astype(x.dtype)  13.4 us
    ppermute x7, starting transfers between devices, routed_experts(): lax.ppermute(tokens, 'attn', [(s, (s + k) % n_attn) for s in range(n_attn)])  12.5 us
    unnamed x24, local copies, waits for them, and re-layouts  6.05 us
    ppermute x7, waiting for transfers between devices, routed_experts(): lax.ppermute(expert_rows[kk], 'attn', [(s, (s - k) % n_attn) for s in ran...  5.54 us
    ppermute x7, waiting for transfers between devices, routed_experts(): lax.ppermute(tokens, 'attn', [(s, (s + k) % n_attn) for s in range(n_attn)])  4.32 us
    ppermute x4, starting transfers between devices, bit_gather(): other = lax.ppermute(x, axis, [(i, i ^ bit) for i in range(n)])  3.27 us
  transfers between devices with their start and end apart: 26, of which 11 were waited for; matrix products, arithmetic and copies ran while one was open for 14% of the time, Pallas kernels for 0%

profile of v17, /device:TPU:0, one launch (start us, length us, event | category | flops | bytes accessed | tf_op | source)
XLA Modules:
  0.0 97.5 jit_solution(11275786675350692181)
XLA Ops:
  0.7 6.1 %collective-permute-start.12 = (bf16[8,7168]{1,0:T(8,128)(2,1)}, bf16[8,7168]{1,0:T(8,128)(2,1)}, u32[]{:S(2)}, u32[]{:S(2)}) collective-permute-start(bf16[8,7168]{1,0:T(8,128)(2,1)} %param.16), channel_id=1, source_target_pairs={{0,28},{4,0},{8,4},{12,8},{16,12},{20,16},{24,20},{28,24},{1,29},{... | collective-permute-start | bytes 344072 | tf_op jit(solution)/shard_map/ppermute | solution.py:60
  7.2 3.0 %collective-permute-start.9 = (bf16[8,7168]{1,0:T(8,128)(2,1)}, bf16[8,7168]{1,0:T(8,128)(2,1)}, u32[]{:S(2)}, u32[]{:S(2)}) collective-permute-start(bf16[8,7168]{1,0:T(8,128)(2,1)} %param.16), channel_id=1, source_target_pairs={{0,16},{4,20},{8,24},{12,28},{16,0},{20,4},{24,8},{28,12},{1,17},{... | collective-permute-start | bytes 344072 | tf_op jit(solution)/shard_map/ppermute | solution.py:60
  10.2 1.8 %fusion.52 = f32[2,128,1024]{2,1,0:T(8,128)S(1)} fusion(bf16[2,128,512]{2,1,0:T(8,128)(2,1)} %param.11, bf16[2,1024,512]{2,1,0:T(8,128)(2,1)S(1)} %copy-done), kind=kOutput, calls=%fused_computation.110 | convolution fusion | flops 268435456 | bytes 3407872 | tf_op jit(solution)/shard_map/rhl,rpl->rhp/dot_general | solution.py:114
  13.8 1.5 %collective-permute-start.1 = (f32[2,128]{1,0:T(2,128)S(1)}, f32[2,128]{1,0:T(2,128)S(1)}, u32[]{:S(2)}, u32[]{:S(2)}) collective-permute-start(f32[2,128]{1,0:T(2,128)S(1)} %max.6), channel_id=1, source_target_pairs={{0,2},{1,3},{2,0},{3,1},{4,6},{5,7},{6,4},{7,5},{8,10},{9,11},{10,... | collective-permute-start | bytes 3080 | tf_op jit(solution)/shard_map/ppermute | solution.py:136
  15.3 2.1 %collective-permute-done.1 = f32[2,128]{1,0:T(2,128)S(1)} collective-permute-done((f32[2,128]{1,0:T(2,128)S(1)}, f32[2,128]{1,0:T(2,128)S(1)}, u32[]{:S(2)}, u32[]{:S(2)}) %collective-permute-start.1) | collective-permute-done | bytes 1056 | tf_op jit(solution)/shard_map/ppermute | solution.py:136
  17.4 1.4 %broadcast_multiply_fusion = f32[2,128,512]{2,1,0:T(8,128)} fusion(f32[2,128]{1,0:T(2,128)S(1)} %get-tuple-element.3, bf16[2,1024,512]{2,1,0:T(8,128)(2,1)S(1)} %copy-done, f32[2,128,1024]{2,1,0:T(8,128)S(1)} %get-tuple-element.30, f32[2,128]{1,0:T(2,128)S(1)} %get-tuple-element.29, pred[2,1024]{1,0:T(4,128)(4,1)S(1)} %broadcast_compare_fusion), kind=kOutput, calls=%fused_computation.49 | convolution fusion | flops 269352960 | bytes 3674112 | tf_op jit(solution)/shard_map/rhp,rpl->rhl/dot_general | solution.py:125
  19.0 1.1 %fusion.24 = (f32[2,2,1,32,513]{4,3,2,1,0:T(8,128)S(1)}, f32[2,2,1,32,513]{4,3,2,1,0:T(8,128)S(1)}) fusion(s32[]{:T(128)S(6)} %select_n.81, f32[2,2,2,32,512]{4,3,2,1,0:T(8,128)} %bitcast.109, f32[2,2,2,32,1]{4,3,2,1,0:T(8,128)S(1)} %concatenate.15, s32[]{:T(128)S(6)} %select_n.82), kind=kLoop, calls=%fused_computation.45 | loop fusion | flops 131328 | bytes 1050632 | tf_op jit(solution)/shard_map/concatenate | solution.py:140
  20.1 1.9 %collective-permute-start.5 = (bf16[8,7168]{1,0:T(8,128)(2,1)S(1)}, bf16[8,7168]{1,0:T(8,128)(2,1)S(1)}, u32[]{:S(2)}, u32[]{:S(2)}) collective-permute-start(bf16[8,7168]{1,0:T(8,128)(2,1)S(1)} %copy-done.5), channel_id=1, source_target_pairs={{0,8},{4,12},{8,16},{12,20},{16,24},{20,28},{24,0},{28,4},{1,9},{5... | collective-permute-start | bytes 344072 | tf_op jit(solution)/shard_map/ppermute | solution.py:60
  22.0 1.1 %collective-permute-start.4 = (bf16[8,7168]{1,0:T(8,128)(2,1)S(1)}, bf16[8,7168]{1,0:T(8,128)(2,1)S(1)}, u32[]{:S(2)}, u32[]{:S(2)}) collective-permute-start(bf16[8,7168]{1,0:T(8,128)(2,1)S(1)} %copy-done.5), channel_id=1, source_target_pairs={{0,4},{4,8},{8,12},{12,16},{16,20},{20,24},{24,28},{28,0},{1,5},{5... | collective-permute-start | bytes 344072 | tf_op jit(solution)/shard_map/ppermute | solution.py:60
  23.2 1.1 %fusion.48 = (bf16[1,4,8,7168]{3,2,1,0:T(8,128)(2,1)S(1)}, bf16[4,8,7168]{2,1,0:T(8,128)(2,1)S(1)}) fusion(bf16[1,8,7168]{2,1,0:T(8,128)(2,1)} %bitcast.19, bf16[1,8,7168]{2,1,0:T(8,128)(2,1)} %bitcast.18, bf16[1,8,7168]{2,1,0:T(8,128)(2,1)} %bitcast.17, bf16[1,8,7168]{2,1,0:T(8,128)(2,1)} %bitcast.16), kind=kLoop, calls=%fused_computation.106 | loop fusion | flops 688128 | bytes 1376256 | tf_op jit(solution)/shard_map/stack | solution.py:35
  24.3 1.6 %collective-permute-start.13 = (bf16[4,8,7168]{2,1,0:T(8,128)(2,1)S(1)}, bf16[4,8,7168]{2,1,0:T(8,128)(2,1)S(1)}, u32[]{:S(2)}, u32[]{:S(2)}) collective-permute-start(bf16[4,8,7168]{2,1,0:T(8,128)(2,1)S(1)} %get-tuple-element.20), channel_id=1, source_target_pairs={{0,2},{1,3},{2,0},{3,1},{4,6},{5,7},{6,4},{7,5},{8,10},{9,11},{10,... | collective-permute-start | bytes 1376264 | tf_op jit(solution)/shard_map/ppermute | solution.py:34
  25.9 1.8 %collective-permute-done.5 = bf16[8,7168]{1,0:T(8,128)(2,1)S(1)} collective-permute-done((bf16[8,7168]{1,0:T(8,128)(2,1)S(1)}, bf16[8,7168]{1,0:T(8,128)(2,1)S(1)}, u32[]{:S(2)}, u32[]{:S(2)}) %collective-permute-start.5) | collective-permute-done | bytes 114720 | tf_op jit(solution)/shard_map/ppermute | solution.py:60
  27.7 2.5 %collective-permute-done.4 = bf16[8,7168]{1,0:T(8,128)(2,1)S(1)} collective-permute-done((bf16[8,7168]{1,0:T(8,128)(2,1)S(1)}, bf16[8,7168]{1,0:T(8,128)(2,1)S(1)}, u32[]{:S(2)}, u32[]{:S(2)}) %collective-permute-start.4) | collective-permute-done | bytes 114720 | tf_op jit(solution)/shard_map/ppermute | solution.py:60
  30.3 1.6 %collective-permute-start.7 = (bf16[4,8,7168]{2,1,0:T(8,128)(2,1)S(1)}, bf16[4,8,7168]{2,1,0:T(8,128)(2,1)S(1)}, u32[]{:S(2)}, u32[]{:S(2)}) collective-permute-start(bf16[4,8,7168]{2,1,0:T(8,128)(2,1)S(1)} %get-tuple-element.18), channel_id=1, source_target_pairs={{0,2},{1,3},{2,0},{3,1},{4,6},{5,7},{6,4},{7,5},{8,10},{9,11},{10,... | collective-permute-start | bytes 1376264 | tf_op jit(solution)/shard_map/ppermute | solution.py:34
  31.9 5.8 %collective-permute-done.13 = bf16[4,8,7168]{2,1,0:T(8,128)(2,1)S(1)} collective-permute-done((bf16[4,8,7168]{2,1,0:T(8,128)(2,1)S(1)}, bf16[4,8,7168]{2,1,0:T(8,128)(2,1)S(1)}, u32[]{:S(2)}, u32[]{:S(2)}) %collective-permute-start.13) | collective-permute-done | bytes 458784 | tf_op jit(solution)/shard_map/ppermute | solution.py:34
  37.9 9.2 %collective-permute-done.7 = bf16[4,8,7168]{2,1,0:T(8,128)(2,1)S(1)} collective-permute-done((bf16[4,8,7168]{2,1,0:T(8,128)(2,1)S(1)}, bf16[4,8,7168]{2,1,0:T(8,128)(2,1)S(1)}, u32[]{:S(2)}, u32[]{:S(2)}) %collective-permute-start.7) | collective-permute-done | bytes 458784 | tf_op jit(solution)/shard_map/ppermute | solution.py:34
  47.4 1.6 %collective-permute-start.3 = (f32[2,1,32,513]{3,2,0,1:T(8,128)S(1)}, f32[2,1,32,513]{3,2,0,1:T(8,128)S(1)}, u32[]{:S(2)}, u32[]{:S(2)}) collective-permute-start(f32[2,1,32,513]{3,2,0,1:T(8,128)S(1)} %constant_dynamic-slice_fusion), channel_id=1, source_target_pairs={{0,2},{1,3},{2,0},{3,1},{4,6},{5,7},{6,4},{7,5},{8,10},{9,11},{10,... | collective-permute-start | bytes 393992 | tf_op jit(solution)/shard_map/ppermute | solution.py:149
  50.0 1.2 %copy-done.10 = bf16[1,7168,256]{2,1,0:T(8,128)(2,1)S(1)} copy-done((bf16[1,7168,256]{2,1,0:T(8,128)(2,1)S(1)}, bf16[1,7168,256]{2,1,0:T(8,128)(2,1)}, u32[]{:S(2)}) %copy-start.10) | copy-done | bytes 3670040
  51.1 1.1 %fusion.6 = f32[256,256]{1,0:T(8,128)S(1)} fusion(bf16[1,7168,256]{2,1,0:T(8,128)(2,1)S(1)} %copy-done.10, bf16[128,7168]{1,0:T(8,128)(2,1)S(1)} %bitcast.110, bf16[128,7168]{1,0:T(8,128)(2,1)S(1)} %bitcast.112), kind=kOutput, calls=%fused_computation.8 | convolution fusion | flops 946864128 | bytes 7602176 | tf_op jit(solution)/shard_map/dot_general | solution.py:73
  53.2 1.1 %multiply_convert_fusion = bf16[256,256]{1,0:T(8,128)(2,1)S(1)} fusion(f32[256,256]{1,0:T(8,128)S(1)} %fusion.6, bf16[1,7168,256]{2,1,0:T(8,128)(2,1)S(1)} %copy-done.11, bf16[128,7168]{1,0:T(8,128)(2,1)S(1)} %bitcast.111, bf16[128,7168]{1,0:T(8,128)(2,1)S(1)} %bitcast.113), kind=kOutput, calls=%fused_computation.48 | convolution fusion | flops 947257344 | bytes 7733248 | tf_op jit(solution)/shard_map/dot_general | solution.py:74
  54.3 0.9 copy-done.1
  56.4 1.3 %copy-done.2 = f32[128,7168]{1,0:T(8,128)} copy-done((f32[128,7168]{1,0:T(8,128)}, f32[128,7168]{1,0:T(8,128)S(1)}, u32[]{:S(2)}) %copy-start.2) | copy-done | bytes 3670040
  58.4 1.8 %copy-done.3 = f32[128,7168]{1,0:T(8,128)} copy-done((f32[128,7168]{1,0:T(8,128)}, f32[128,7168]{1,0:T(8,128)S(1)}, u32[]{:S(2)}) %copy-start.3) | copy-done | bytes 3670040
  62.9 0.9 collective-permute-start.16
  63.8 11.0 %collective-permute-done.21 = bf16[4,8,7168]{2,1,0:T(8,128)(2,1)S(1)} collective-permute-done((bf16[4,8,7168]{2,1,0:T(8,128)(2,1)S(1)}, bf16[4,8,7168]{2,1,0:T(8,128)(2,1)S(1)}, u32[]{:S(2)}, u32[]{:S(2)}) %collective-permute-start.21) | collective-permute-done | bytes 458784 | tf_op jit(solution)/shard_map/ppermute | solution.py:40
  75.0 2.0 %collective-permute-start.25 = (bf16[8,7168]{1,0:T(8,128)(2,1)S(1)}, bf16[8,7168]{1,0:T(8,128)(2,1)S(1)}, u32[]{:S(2)}, u32[]{:S(2)}) collective-permute-start(bf16[8,7168]{1,0:T(8,128)(2,1)S(1)} %get-tuple-element.14), channel_id=1, source_target_pairs={{0,4},{4,8},{8,12},{12,16},{16,20},{20,24},{24,28},{28,0},{1,5},{5... | collective-permute-start | bytes 344072 | tf_op jit(solution)/shard_map/ppermute | solution.py:92
  76.9 2.5 %collective-permute-start.24 = (bf16[8,7168]{1,0:T(8,128)(2,1)S(1)}, bf16[8,7168]{1,0:T(8,128)(2,1)S(1)}, u32[]{:S(2)}, u32[]{:S(2)}) collective-permute-start(bf16[8,7168]{1,0:T(8,128)(2,1)S(1)} %get-tuple-element.15), channel_id=1, source_target_pairs={{0,8},{4,12},{8,16},{12,20},{16,24},{20,28},{24,0},{28,4},{1,9},{5... | collective-permute-start | bytes 344072 | tf_op jit(solution)/shard_map/ppermute | solution.py:92
  79.5 2.8 %collective-permute-start.22 = (bf16[8,7168]{1,0:T(8,128)(2,1)S(1)}, bf16[8,7168]{1,0:T(8,128)(2,1)S(1)}, u32[]{:S(2)}, u32[]{:S(2)}) collective-permute-start(bf16[8,7168]{1,0:T(8,128)(2,1)S(1)} %get-tuple-element.13), channel_id=1, source_target_pairs={{0,16},{4,20},{8,24},{12,28},{16,0},{20,4},{24,8},{28,12},{1,17},{... | collective-permute-start | bytes 344072 | tf_op jit(solution)/shard_map/ppermute | solution.py:92
  82.3 1.7 %collective-permute-done.16 = bf16[4,8,7168]{2,1,0:T(8,128)(2,1)S(1)} collective-permute-done((bf16[4,8,7168]{2,1,0:T(8,128)(2,1)S(1)}, bf16[4,8,7168]{2,1,0:T(8,128)(2,1)S(1)}, u32[]{:S(2)}, u32[]{:S(2)}) %collective-permute-start.16) | collective-permute-done | bytes 458784 | tf_op jit(solution)/shard_map/ppermute | solution.py:40
  84.1 3.4 %collective-permute-start.19 = (bf16[8,7168]{1,0:T(8,128)(2,1)S(1)}, bf16[8,7168]{1,0:T(8,128)(2,1)S(1)}, u32[]{:S(2)}, u32[]{:S(2)}) collective-permute-start(bf16[8,7168]{1,0:T(8,128)(2,1)S(1)} %get-tuple-element.11), channel_id=1, source_target_pairs={{0,20},{4,24},{8,28},{12,0},{16,4},{20,8},{24,12},{28,16},{1,21},{... | collective-permute-start | bytes 344072 | tf_op jit(solution)/shard_map/ppermute | solution.py:92
  87.5 2.9 %collective-permute-start.18 = (bf16[8,7168]{1,0:T(8,128)(2,1)S(1)}, bf16[8,7168]{1,0:T(8,128)(2,1)S(1)}, u32[]{:S(2)}, u32[]{:S(2)}) collective-permute-start(bf16[8,7168]{1,0:T(8,128)(2,1)S(1)} %get-tuple-element.12), channel_id=1, source_target_pairs={{0,24},{4,28},{8,0},{12,4},{16,8},{20,12},{24,16},{28,20},{1,25},{... | collective-permute-start | bytes 344072 | tf_op jit(solution)/shard_map/ppermute | solution.py:92
  91.9 4.7 %collective-permute-done.19 = bf16[8,7168]{1,0:T(8,128)(2,1)S(1)} collective-permute-done((bf16[8,7168]{1,0:T(8,128)(2,1)S(1)}, bf16[8,7168]{1,0:T(8,128)(2,1)S(1)}, u32[]{:S(2)}, u32[]{:S(2)}) %collective-permute-start.19) | collective-permute-done | bytes 114720 | tf_op jit(solution)/shard_map/ppermute | solution.py:92
  (93 shorter events, 12.2 us)
Async XLA Ops:
  0.6 9.5 %copy-start = (bf16[2,1024,512]{2,1,0:T(8,128)(2,1)S(1)}, bf16[2,1024,512]{2,1,0:T(8,128)(2,1)}, u32[]{:S(2)}) copy-start(bf16[2,1024,512]{2,1,0:T(8,128)(2,1)} %param.13) | copy-start | bytes 6291460
  0.6 11.3 %copy-start.9 = (s32[2]{0:T(128)S(1)}, s32[2]{0:T(128)}, u32[]{:S(2)}) copy-start(s32[2]{0:T(128)} %param.15) | copy-start | bytes 28
  0.7 11.4 %copy-start.4 = (bf16[2,64,1024]{2,1,0:T(8,128)(2,1)S(1)}, bf16[2,64,1024]{2,1,0:T(8,128)(2,1)}, u32[]{:S(2)}) copy-start(bf16[2,64,1024]{2,1,0:T(8,128)(2,1)} %param.14) | copy-start | bytes 786436
  0.7 19.4 %collective-permute-start.12 = (bf16[8,7168]{1,0:T(8,128)(2,1)}, bf16[8,7168]{1,0:T(8,128)(2,1)}, u32[]{:S(2)}, u32[]{:S(2)}) collective-permute-start(bf16[8,7168]{1,0:T(8,128)(2,1)} %param.16), channel_id=1, source_target_pairs={{0,28},{4,0},{8,4},{12,8},{16,12},{20,16},{24,20},{28,24},{1,29},{... | collective-permute-start | bytes 344072 | tf_op jit(solution)/shard_map/ppermute | solution.py:60
  6.7 15.3 %collective-permute-start.11 = (bf16[8,7168]{1,0:T(8,128)(2,1)}, bf16[8,7168]{1,0:T(8,128)(2,1)}, u32[]{:S(2)}, u32[]{:S(2)}) collective-permute-start(bf16[8,7168]{1,0:T(8,128)(2,1)} %param.16), channel_id=1, source_target_pairs={{0,24},{4,28},{8,0},{12,4},{16,8},{20,12},{24,16},{28,20},{1,25},{... | collective-permute-start | bytes 344072 | tf_op jit(solution)/shard_map/ppermute | solution.py:60
  7.2 16.0 %collective-permute-start.10 = (bf16[8,7168]{1,0:T(8,128)(2,1)}, bf16[8,7168]{1,0:T(8,128)(2,1)}, u32[]{:S(2)}, u32[]{:S(2)}) collective-permute-start(bf16[8,7168]{1,0:T(8,128)(2,1)} %param.16), channel_id=1, source_target_pairs={{0,20},{4,24},{8,28},{12,0},{16,4},{20,8},{24,12},{28,16},{1,21},{... | collective-permute-start | bytes 344072 | tf_op jit(solution)/shard_map/ppermute | solution.py:60
  7.2 16.0 %collective-permute-start.9 = (bf16[8,7168]{1,0:T(8,128)(2,1)}, bf16[8,7168]{1,0:T(8,128)(2,1)}, u32[]{:S(2)}, u32[]{:S(2)}) collective-permute-start(bf16[8,7168]{1,0:T(8,128)(2,1)} %param.16), channel_id=1, source_target_pairs={{0,16},{4,20},{8,24},{12,28},{16,0},{20,4},{24,8},{28,12},{1,17},{... | collective-permute-start | bytes 344072 | tf_op jit(solution)/shard_map/ppermute | solution.py:60
  12.0 5.4 %copy-start.5 = (bf16[8,7168]{1,0:T(8,128)(2,1)S(1)}, bf16[8,7168]{1,0:T(8,128)(2,1)}, u32[]{:S(2)}) copy-start(bf16[8,7168]{1,0:T(8,128)(2,1)} %param.16) | copy-start | bytes 344068
  12.5 1.3 %collective-permute-start = (f32[2,128]{1,0:T(2,128)S(1)}, f32[2,128]{1,0:T(2,128)S(1)}, u32[]{:S(2)}, u32[]{:S(2)}) collective-permute-start(f32[2,128]{1,0:T(2,128)S(1)} %get-tuple-element.29), channel_id=1, source_target_pairs={{0,1},{1,0},{2,3},{3,2},{4,5},{5,4},{6,7},{7,6},{8,9},{9,8},{10,11... | collective-permute-start | bytes 3080 | tf_op jit(solution)/shard_map/ppermute | solution.py:136
  13.8 3.6 %collective-permute-start.1 = (f32[2,128]{1,0:T(2,128)S(1)}, f32[2,128]{1,0:T(2,128)S(1)}, u32[]{:S(2)}, u32[]{:S(2)}) collective-permute-start(f32[2,128]{1,0:T(2,128)S(1)} %max.6), channel_id=1, source_target_pairs={{0,2},{1,3},{2,0},{3,1},{4,6},{5,7},{6,4},{7,5},{8,10},{9,11},{10,... | collective-permute-start | bytes 3080 | tf_op jit(solution)/shard_map/ppermute | solution.py:136
  17.4 8.5 %collective-permute-start.6 = (bf16[8,7168]{1,0:T(8,128)(2,1)S(1)}, bf16[8,7168]{1,0:T(8,128)(2,1)S(1)}, u32[]{:S(2)}, u32[]{:S(2)}) collective-permute-start(bf16[8,7168]{1,0:T(8,128)(2,1)S(1)} %copy-done.5), channel_id=1, source_target_pairs={{0,12},{4,16},{8,20},{12,24},{16,28},{20,0},{24,4},{28,8},{1,13},{... | collective-permute-start | bytes 344072 | tf_op jit(solution)/shard_map/ppermute | solution.py:60
  20.1 7.6 %collective-permute-start.5 = (bf16[8,7168]{1,0:T(8,128)(2,1)S(1)}, bf16[8,7168]{1,0:T(8,128)(2,1)S(1)}, u32[]{:S(2)}, u32[]{:S(2)}) collective-permute-start(bf16[8,7168]{1,0:T(8,128)(2,1)S(1)} %copy-done.5), channel_id=1, source_target_pairs={{0,8},{4,12},{8,16},{12,20},{16,24},{20,28},{24,0},{28,4},{1,9},{5... | collective-permute-start | bytes 344072 | tf_op jit(solution)/shard_map/ppermute | solution.py:60
  22.0 8.2 %collective-permute-start.4 = (bf16[8,7168]{1,0:T(8,128)(2,1)S(1)}, bf16[8,7168]{1,0:T(8,128)(2,1)S(1)}, u32[]{:S(2)}, u32[]{:S(2)}) collective-permute-start(bf16[8,7168]{1,0:T(8,128)(2,1)S(1)} %copy-done.5), channel_id=1, source_target_pairs={{0,4},{4,8},{8,12},{12,16},{16,20},{20,24},{24,28},{28,0},{1,5},{5... | collective-permute-start | bytes 344072 | tf_op jit(solution)/shard_map/ppermute | solution.py:60
  23.2 8.7 %collective-permute-start.2 = (f32[2,2,32,513]{3,2,0,1:T(8,128)S(1)}, f32[2,2,32,513]{3,2,0,1:T(8,128)S(1)}, u32[]{:S(2)}, u32[]{:S(2)}) collective-permute-start(f32[2,2,32,513]{3,2,0,1:T(8,128)S(1)} %bitcast.120), channel_id=1, source_target_pairs={{0,1},{1,0},{2,3},{3,2},{4,5},{5,4},{6,7},{7,6},{8,9},{9,8},{10,11... | collective-permute-start | bytes 787976 | tf_op jit(solution)/shard_map/ppermute | solution.py:149
  24.3 13.4 %collective-permute-start.13 = (bf16[4,8,7168]{2,1,0:T(8,128)(2,1)S(1)}, bf16[4,8,7168]{2,1,0:T(8,128)(2,1)S(1)}, u32[]{:S(2)}, u32[]{:S(2)}) collective-permute-start(bf16[4,8,7168]{2,1,0:T(8,128)(2,1)S(1)} %get-tuple-element.20), channel_id=1, source_target_pairs={{0,2},{1,3},{2,0},{3,1},{4,6},{5,7},{6,4},{7,5},{8,10},{9,11},{10,... | collective-permute-start | bytes 1376264 | tf_op jit(solution)/shard_map/ppermute | solution.py:34
  30.3 16.9 %collective-permute-start.7 = (bf16[4,8,7168]{2,1,0:T(8,128)(2,1)S(1)}, bf16[4,8,7168]{2,1,0:T(8,128)(2,1)S(1)}, u32[]{:S(2)}, u32[]{:S(2)}) collective-permute-start(bf16[4,8,7168]{2,1,0:T(8,128)(2,1)S(1)} %get-tuple-element.18), channel_id=1, source_target_pairs={{0,2},{1,3},{2,0},{3,1},{4,6},{5,7},{6,4},{7,5},{8,10},{9,11},{10,... | collective-permute-start | bytes 1376264 | tf_op jit(solution)/shard_map/ppermute | solution.py:34
  37.8 11.1 %collective-permute-start.14 = (bf16[2,4,8,7168]{3,2,1,0:T(8,128)(2,1)S(1)}, bf16[2,4,8,7168]{3,2,1,0:T(8,128)(2,1)S(1)}, u32[]{:S(2)}, u32[]{:S(2)}) collective-permute-start(bf16[2,4,8,7168]{3,2,1,0:T(8,128)(2,1)S(1)} %get-tuple-element.7), channel_id=1, source_target_pairs={{0,1},{1,0},{2,3},{3,2},{4,5},{5,4},{6,7},{7,6},{8,9},{9,8},{10,11... | collective-permute-start | bytes 2752520 | tf_op jit(solution)/shard_map/ppermute | solution.py:34
  47.3 2.5 %collective-permute-start.8 = (bf16[2,4,8,7168]{3,2,1,0:T(8,128)(2,1)S(1)}, bf16[2,4,8,7168]{3,2,1,0:T(8,128)(2,1)S(1)}, u32[]{:S(2)}, u32[]{:S(2)}) collective-permute-start(bf16[2,4,8,7168]{3,2,1,0:T(8,128)(2,1)S(1)} %get-tuple-element.5), channel_id=1, source_target_pairs={{0,1},{1,0},{2,3},{3,2},{4,5},{5,4},{6,7},{7,6},{8,9},{9,8},{10,11... | collective-permute-start | bytes 2752520 | tf_op jit(solution)/shard_map/ppermute | solution.py:34
  47.4 8.9 %collective-permute-start.3 = (f32[2,1,32,513]{3,2,0,1:T(8,128)S(1)}, f32[2,1,32,513]{3,2,0,1:T(8,128)S(1)}, u32[]{:S(2)}, u32[]{:S(2)}) collective-permute-start(f32[2,1,32,513]{3,2,0,1:T(8,128)S(1)} %constant_dynamic-slice_fusion), channel_id=1, source_target_pairs={{0,2},{1,3},{2,0},{3,1},{4,6},{5,7},{6,4},{7,5},{8,10},{9,11},{10,... | collective-permute-start | bytes 393992 | tf_op jit(solution)/shard_map/ppermute | solution.py:149
  49.1 2.0 %copy-start.10 = (bf16[1,7168,256]{2,1,0:T(8,128)(2,1)S(1)}, bf16[1,7168,256]{2,1,0:T(8,128)(2,1)}, u32[]{:S(2)}) copy-start(bf16[1,7168,256]{2,1,0:T(8,128)(2,1)} %param.19) | copy-start | bytes 11010052
  56.0 4.4 %collective-permute-start.20 = (bf16[2,4,8,7168]{3,2,1,0:T(8,128)(2,1)S(1)}, bf16[2,4,8,7168]{3,2,1,0:T(8,128)(2,1)S(1)}, u32[]{:S(2)}, u32[]{:S(2)}) collective-permute-start(bf16[2,4,8,7168]{3,2,1,0:T(8,128)(2,1)S(1)} %bitcast.116), channel_id=1, source_target_pairs={{0,1},{1,0},{2,3},{3,2},{4,5},{5,4},{6,7},{7,6},{8,9},{9,8},{10,11... | collective-permute-start | bytes 2752520 | tf_op jit(solution)/shard_map/ppermute | solution.py:40
  58.3 2.8 %slice-start = ((f32[128,7168]{1,0:T(8,128)}), f32[64,7168]{1,0:T(8,128)S(1)}, s32[]{:S(2)}) async-start(f32[128,7168]{1,0:T(8,128)} %copy-done.2), calls=%async_computation | async-start | bytes 3670016 | tf_op jit(solution)/shard_map/slice | solution.py:40
  60.2 2.5 %collective-permute-start.15 = (bf16[2,4,8,7168]{3,2,1,0:T(8,128)(2,1)S(1)}, bf16[2,4,8,7168]{3,2,1,0:T(8,128)(2,1)S(1)}, u32[]{:S(2)}, u32[]{:S(2)}) collective-permute-start(bf16[2,4,8,7168]{3,2,1,0:T(8,128)(2,1)S(1)} %bitcast.117), channel_id=1, source_target_pairs={{0,1},{1,0},{2,3},{3,2},{4,5},{5,4},{6,7},{7,6},{8,9},{9,8},{10,11... | collective-permute-start | bytes 2752520 | tf_op jit(solution)/shard_map/ppermute | solution.py:40
  61.4 13.4 %collective-permute-start.21 = (bf16[4,8,7168]{2,1,0:T(8,128)(2,1)S(1)}, bf16[4,8,7168]{2,1,0:T(8,128)(2,1)S(1)}, u32[]{:S(2)}, u32[]{:S(2)}) collective-permute-start(bf16[4,8,7168]{2,1,0:T(8,128)(2,1)S(1)} %fusion.22), channel_id=1, source_target_pairs={{0,2},{1,3},{2,0},{3,1},{4,6},{5,7},{6,4},{7,5},{8,10},{9,11},{10,... | collective-permute-start | bytes 1376264 | tf_op jit(solution)/shard_map/ppermute | solution.py:40
  62.9 21.1 %collective-permute-start.16 = (bf16[4,8,7168]{2,1,0:T(8,128)(2,1)S(1)}, bf16[4,8,7168]{2,1,0:T(8,128)(2,1)S(1)}, u32[]{:S(2)}, u32[]{:S(2)}) collective-permute-start(bf16[4,8,7168]{2,1,0:T(8,128)(2,1)S(1)} %fusion.21), channel_id=1, source_target_pairs={{0,2},{1,3},{2,0},{3,1},{4,6},{5,7},{6,4},{7,5},{8,10},{9,11},{10,... | collective-permute-start | bytes 1376264 | tf_op jit(solution)/shard_map/ppermute | solution.py:40
  75.0 12.5 %collective-permute-start.25 = (bf16[8,7168]{1,0:T(8,128)(2,1)S(1)}, bf16[8,7168]{1,0:T(8,128)(2,1)S(1)}, u32[]{:S(2)}, u32[]{:S(2)}) collective-permute-start(bf16[8,7168]{1,0:T(8,128)(2,1)S(1)} %get-tuple-element.14), channel_id=1, source_target_pairs={{0,4},{4,8},{8,12},{12,16},{16,20},{20,24},{24,28},{28,0},{1,5},{5... | collective-permute-start | bytes 344072 | tf_op jit(solution)/shard_map/ppermute | solution.py:92
  76.9 13.4 %collective-permute-start.24 = (bf16[8,7168]{1,0:T(8,128)(2,1)S(1)}, bf16[8,7168]{1,0:T(8,128)(2,1)S(1)}, u32[]{:S(2)}, u32[]{:S(2)}) collective-permute-start(bf16[8,7168]{1,0:T(8,128)(2,1)S(1)} %get-tuple-element.15), channel_id=1, source_target_pairs={{0,8},{4,12},{8,16},{12,20},{16,24},{20,28},{24,0},{28,4},{1,9},{5... | collective-permute-start | bytes 344072 | tf_op jit(solution)/shard_map/ppermute | solution.py:92
  79.4 12.5 %collective-permute-start.23 = (bf16[8,7168]{1,0:T(8,128)(2,1)S(1)}, bf16[8,7168]{1,0:T(8,128)(2,1)S(1)}, u32[]{:S(2)}, u32[]{:S(2)}) collective-permute-start(bf16[8,7168]{1,0:T(8,128)(2,1)S(1)} %get-tuple-element.16), channel_id=1, source_target_pairs={{0,12},{4,16},{8,20},{12,24},{16,28},{20,0},{24,4},{28,8},{1,13},{... | collective-permute-start | bytes 344072 | tf_op jit(solution)/shard_map/ppermute | solution.py:92
  79.5 12.5 %collective-permute-start.22 = (bf16[8,7168]{1,0:T(8,128)(2,1)S(1)}, bf16[8,7168]{1,0:T(8,128)(2,1)S(1)}, u32[]{:S(2)}, u32[]{:S(2)}) collective-permute-start(bf16[8,7168]{1,0:T(8,128)(2,1)S(1)} %get-tuple-element.13), channel_id=1, source_target_pairs={{0,16},{4,20},{8,24},{12,28},{16,0},{20,4},{24,8},{28,12},{1,17},{... | collective-permute-start | bytes 344072 | tf_op jit(solution)/shard_map/ppermute | solution.py:92
  84.1 12.5 %collective-permute-start.19 = (bf16[8,7168]{1,0:T(8,128)(2,1)S(1)}, bf16[8,7168]{1,0:T(8,128)(2,1)S(1)}, u32[]{:S(2)}, u32[]{:S(2)}) collective-permute-start(bf16[8,7168]{1,0:T(8,128)(2,1)S(1)} %get-tuple-element.11), channel_id=1, source_target_pairs={{0,20},{4,24},{8,28},{12,0},{16,4},{20,8},{24,12},{28,16},{1,21},{... | collective-permute-start | bytes 344072 | tf_op jit(solution)/shard_map/ppermute | solution.py:92
  87.5 9.1 %collective-permute-start.18 = (bf16[8,7168]{1,0:T(8,128)(2,1)S(1)}, bf16[8,7168]{1,0:T(8,128)(2,1)S(1)}, u32[]{:S(2)}, u32[]{:S(2)}) collective-permute-start(bf16[8,7168]{1,0:T(8,128)(2,1)S(1)} %get-tuple-element.12), channel_id=1, source_target_pairs={{0,24},{4,28},{8,0},{12,4},{16,8},{20,12},{24,16},{28,20},{1,25},{... | collective-permute-start | bytes 344072 | tf_op jit(solution)/shard_map/ppermute | solution.py:92
  90.3 6.3 %collective-permute-start.17 = (bf16[8,7168]{1,0:T(8,128)(2,1)S(1)}, bf16[8,7168]{1,0:T(8,128)(2,1)S(1)}, u32[]{:S(2)}, u32[]{:S(2)}) collective-permute-start(bf16[8,7168]{1,0:T(8,128)(2,1)S(1)} %get-tuple-element.10), channel_id=1, source_target_pairs={{0,28},{4,0},{8,4},{12,8},{16,12},{20,16},{24,20},{28,24},{1,29},{... | collective-permute-start | bytes 344072 | tf_op jit(solution)/shard_map/ppermute | solution.py:92
  (8 other events, 13.2 us)

commit v18 on v14

--- a/solution.py
+++ b/solution.py
@@ -73,12 +73,15 @@
         gate_value = jnp.dot(both, w_gate[i], preferred_element_type=jnp.float32)
         upward = jnp.dot(both, w_up[i], preferred_element_type=jnp.float32)
         hidden = (jax.nn.silu(gate_value) * upward).astype(jnp.bfloat16)
-        offset = 0
-        for c in range(n_chunks):
+        count = blocks[0].size // model_width
+        previous = None
+        for c in reversed(range(n_chunks)):
             block = blocks[c]
-            count = block.size // model_width
-            part = jnp.dot(hidden[offset : offset + count], w_down[i], preferred_element_type=jnp.float32)
-            offset += count
+            rows_in = hidden[c * count : (c + 1) * count]
+            if previous is not None:
+                rows_in, _ = lax.optimization_barrier((rows_in, previous))
+            part = jnp.dot(rows_in, w_down[i], preferred_element_type=jnp.float32)
+            previous = part
             part = part.reshape(block.shape[:-1] + (model_width,))
             for bit in reversed(bits):
                 wire = jnp.bfloat16 if bit == bits[0] else None

time: 98.2 us -> 105 us (1.069)
  waiting for transfers between devices: 44.1 us -> 53.4 us
  starting transfers between devices: 34.4 us -> 30.9 us
  other arithmetic: 5.73 us -> 7.23 us
    ppermute x7, waiting for transfers between devices: 5.54 us -> 12 us  [routed_experts(): lax.ppermute(expert_rows[kk], 'attn', [(s, (s - k) % n_attn) for s in ran...]
    ppermute x7, starting transfers between devices: 13.6 us -> 8.74 us  [routed_experts(): lax.ppermute(expert_rows[kk], 'attn', [(s, (s - k) % n_attn) for s in ran...]
    ppermute x4, waiting for transfers between devices: 16.4 us -> 20.1 us  [bit_reduce(): lax.ppermute(sent, axis, [(i, i ^ bit) for i in range(n)]).astype(x.dtype)]
    ppermute x7, waiting for transfers between devices: 4.31 us -> 1.62 us  [routed_experts(): lax.ppermute(tokens, 'attn', [(s, (s + k) % n_attn) for s in range(n_attn)])]
    ppermute x4, waiting for transfers between devices: 15.8 us -> 17.6 us  [bit_gather(): other = lax.ppermute(x, axis, [(i, i ^ bit) for i in range(n)])]
    ppermute x7, starting transfers between devices: 12.5 us -> 13.8 us  [routed_experts(): lax.ppermute(tokens, 'attn', [(s, (s + k) % n_attn) for s in range(n_attn)])]
    unnamed x20 -> x18, local copies, waits for them, and re-layouts: 3.02 us -> 3 us
  transfers between devices with their start and end apart: 26 -> 26, of which waited for: 12 -> 12; matrix products, arithmetic and copies ran while one was open for 14% -> 15% of each run, Pallas kernels for 0% -> 0%
where the time goes in v18:
time: 105 us; the launch traced here: 104 us
  waiting for transfers between devices  53.4 us (51%)
  starting transfers between devices  30.9 us (29%)
  other arithmetic  7.23 us (7%)
  matrix products  7.11 us (7%)
  local copies, waits for them, and re-layouts  4.79 us (5%)
    ppermute x4, waiting for transfers between devices, bit_reduce(): lax.ppermute(sent, axis, [(i, i ^ bit) for i in range(n)]).astype(x.dtype)  20.1 us
    ppermute x4, waiting for transfers between devices, bit_gather(): other = lax.ppermute(x, axis, [(i, i ^ bit) for i in range(n)])  17.6 us
    ppermute x7, starting transfers between devices, routed_experts(): lax.ppermute(tokens, 'attn', [(s, (s + k) % n_attn) for s in range(n_attn)])  13.8 us
    ppermute x7, waiting for transfers between devices, routed_experts(): lax.ppermute(expert_rows[kk], 'attn', [(s, (s - k) % n_attn) for s in ran...  12 us
    ppermute x7, starting transfers between devices, routed_experts(): lax.ppermute(expert_rows[kk], 'attn', [(s, (s - k) % n_attn) for s in ran...  8.74 us
    ppermute x4, starting transfers between devices, bit_gather(): other = lax.ppermute(x, axis, [(i, i ^ bit) for i in range(n)])  3.24 us
    unnamed x18, local copies, waits for them, and re-layouts  3 us
    another operation x6, other arithmetic, bit_gather(): return jnp.stack([x, other])  2.64 us
  transfers between devices with their start and end apart: 26, of which 12 were waited for; matrix products, arithmetic and copies ran while one was open for 15% of the time, Pallas kernels for 0%

profile of v18, /device:TPU:0, one launch (start us, length us, event | category | flops | bytes accessed | tf_op | source)
XLA Modules:
  0.0 104.4 jit_solution(12632920486980040413)
XLA Ops:
  0.7 4.0 %collective-permute-start.6 = (bf16[8,7168]{1,0:T(8,128)(2,1)}, bf16[8,7168]{1,0:T(8,128)(2,1)}, u32[]{:S(2)}, u32[]{:S(2)}) collective-permute-start(bf16[8,7168]{1,0:T(8,128)(2,1)} %param.16), channel_id=1, source_target_pairs={{0,12},{4,16},{8,20},{12,24},{16,28},{20,0},{24,4},{28,8},{1,13},{... | collective-permute-start | bytes 344072 | tf_op jit(solution)/shard_map/ppermute | solution.py:60
  4.7 1.5 %collective-permute-start.4 = (bf16[8,7168]{1,0:T(8,128)(2,1)}, bf16[8,7168]{1,0:T(8,128)(2,1)}, u32[]{:S(2)}, u32[]{:S(2)}) collective-permute-start(bf16[8,7168]{1,0:T(8,128)(2,1)} %param.16), channel_id=1, source_target_pairs={{0,4},{4,8},{8,12},{12,16},{16,20},{20,24},{24,28},{28,0},{1,5},{5... | collective-permute-start | bytes 344072 | tf_op jit(solution)/shard_map/ppermute | solution.py:60
  6.2 1.6 %collective-permute-start.5 = (bf16[8,7168]{1,0:T(8,128)(2,1)}, bf16[8,7168]{1,0:T(8,128)(2,1)}, u32[]{:S(2)}, u32[]{:S(2)}) collective-permute-start(bf16[8,7168]{1,0:T(8,128)(2,1)} %param.16), channel_id=1, source_target_pairs={{0,8},{4,12},{8,16},{12,20},{16,24},{20,28},{24,0},{28,4},{1,9},{5... | collective-permute-start | bytes 344072 | tf_op jit(solution)/shard_map/ppermute | solution.py:60
  8.9 1.7 %fusion.50 = f32[2,128,1024]{2,1,0:T(8,128)S(1)} fusion(bf16[2,128,512]{2,1,0:T(8,128)(2,1)} %param.11, bf16[2,1024,512]{2,1,0:T(8,128)(2,1)S(1)} %copy-done), kind=kOutput, calls=%fused_computation.104 | convolution fusion | flops 268435456 | bytes 3407872 | tf_op jit(solution)/shard_map/rhl,rpl->rhp/dot_general | solution.py:117
  12.5 1.6 %collective-permute-start.1 = (f32[2,128]{1,0:T(2,128)S(1)}, f32[2,128]{1,0:T(2,128)S(1)}, u32[]{:S(2)}, u32[]{:S(2)}) collective-permute-start(f32[2,128]{1,0:T(2,128)S(1)} %max.6), channel_id=1, source_target_pairs={{0,2},{1,3},{2,0},{3,1},{4,6},{5,7},{6,4},{7,5},{8,10},{9,11},{10,... | collective-permute-start | bytes 3080 | tf_op jit(solution)/shard_map/ppermute | solution.py:139
  14.0 2.1 %collective-permute-done.1 = f32[2,128]{1,0:T(2,128)S(1)} collective-permute-done((f32[2,128]{1,0:T(2,128)S(1)}, f32[2,128]{1,0:T(2,128)S(1)}, u32[]{:S(2)}, u32[]{:S(2)}) %collective-permute-start.1) | collective-permute-done | bytes 1056 | tf_op jit(solution)/shard_map/ppermute | solution.py:139
  16.1 3.6 %collective-permute-start.10 = (bf16[8,7168]{1,0:T(8,128)(2,1)S(1)}, bf16[8,7168]{1,0:T(8,128)(2,1)S(1)}, u32[]{:S(2)}, u32[]{:S(2)}) collective-permute-start(bf16[8,7168]{1,0:T(8,128)(2,1)S(1)} %copy-done.3), channel_id=1, source_target_pairs={{0,20},{4,24},{8,28},{12,0},{16,4},{20,8},{24,12},{28,16},{1,21},{... | collective-permute-start | bytes 344072 | tf_op jit(solution)/shard_map/ppermute | solution.py:60
  19.7 1.3 %broadcast_multiply_fusion = f32[2,128,512]{2,1,0:T(8,128)} fusion(f32[2,128]{1,0:T(2,128)S(1)} %get-tuple-element.5, bf16[2,1024,512]{2,1,0:T(8,128)(2,1)S(1)} %copy-done, f32[2,128,1024]{2,1,0:T(8,128)S(1)} %get-tuple-element.36, f32[2,128]{1,0:T(2,128)S(1)} %get-tuple-element.35, pred[2,1024]{1,0:T(4,128)(4,1)S(1)} %broadcast_compare_fusion), kind=kOutput, calls=%fused_computation.45 | convolution fusion | flops 269352960 | bytes 3674112 | tf_op jit(solution)/shard_map/rhp,rpl->rhl/dot_general | solution.py:128
  21.2 1.1 %fusion.24 = (f32[2,2,1,32,513]{4,3,2,1,0:T(8,128)S(1)}, f32[2,2,1,32,513]{4,3,2,1,0:T(8,128)S(1)}) fusion(s32[]{:T(128)S(6)} %select_n.81, f32[2,2,2,32,512]{4,3,2,1,0:T(8,128)} %bitcast.110, f32[2,2,2,32,1]{4,3,2,1,0:T(8,128)S(1)} %concatenate.15, s32[]{:T(128)S(6)} %select_n.82), kind=kLoop, calls=%fused_computation.41 | loop fusion | flops 131328 | bytes 1050632 | tf_op jit(solution)/shard_map/concatenate | solution.py:143
  22.3 2.3 %collective-permute-start.11 = (bf16[8,7168]{1,0:T(8,128)(2,1)S(1)}, bf16[8,7168]{1,0:T(8,128)(2,1)S(1)}, u32[]{:S(2)}, u32[]{:S(2)}) collective-permute-start(bf16[8,7168]{1,0:T(8,128)(2,1)S(1)} %copy-done.3), channel_id=1, source_target_pairs={{0,24},{4,28},{8,0},{12,4},{16,8},{20,12},{24,16},{28,20},{1,25},{... | collective-permute-start | bytes 344072 | tf_op jit(solution)/shard_map/ppermute | solution.py:60
  25.2 1.1 %fusion.45 = (bf16[1,4,8,7168]{3,2,1,0:T(8,128)(2,1)S(1)}, bf16[4,8,7168]{2,1,0:T(8,128)(2,1)S(1)}) fusion(bf16[1,8,7168]{2,1,0:T(8,128)(2,1)} %bitcast.10, bf16[1,8,7168]{2,1,0:T(8,128)(2,1)} %bitcast.9, bf16[1,8,7168]{2,1,0:T(8,128)(2,1)} %bitcast.8, bf16[1,8,7168]{2,1,0:T(8,128)(2,1)S(1)} %bitcast.122), kind=kLoop, calls=%fused_computation.99 | loop fusion | flops 688128 | bytes 1376256 | tf_op jit(solution)/shard_map/stack | solution.py:35
  26.3 1.6 %collective-permute-start.7 = (bf16[4,8,7168]{2,1,0:T(8,128)(2,1)S(1)}, bf16[4,8,7168]{2,1,0:T(8,128)(2,1)S(1)}, u32[]{:S(2)}, u32[]{:S(2)}) collective-permute-start(bf16[4,8,7168]{2,1,0:T(8,128)(2,1)S(1)} %get-tuple-element.24), channel_id=1, source_target_pairs={{0,2},{1,3},{2,0},{3,1},{4,6},{5,7},{6,4},{7,5},{8,10},{9,11},{10,... | collective-permute-start | bytes 1376264 | tf_op jit(solution)/shard_map/ppermute | solution.py:34
  27.8 1.1 %collective-permute-done.11 = bf16[8,7168]{1,0:T(8,128)(2,1)S(1)} collective-permute-done((bf16[8,7168]{1,0:T(8,128)(2,1)S(1)}, bf16[8,7168]{1,0:T(8,128)(2,1)S(1)}, u32[]{:S(2)}, u32[]{:S(2)}) %collective-permute-start.11) | collective-permute-done | bytes 114720 | tf_op jit(solution)/shard_map/ppermute | solution.py:60
  29.4 1.0 fusion.44
  30.4 1.5 %collective-permute-start.13 = (bf16[4,8,7168]{2,1,0:T(8,128)(2,1)S(1)}, bf16[4,8,7168]{2,1,0:T(8,128)(2,1)S(1)}, u32[]{:S(2)}, u32[]{:S(2)}) collective-permute-start(bf16[4,8,7168]{2,1,0:T(8,128)(2,1)S(1)} %get-tuple-element.26), channel_id=1, source_target_pairs={{0,2},{1,3},{2,0},{3,1},{4,6},{5,7},{6,4},{7,5},{8,10},{9,11},{10,... | collective-permute-start | bytes 1376264 | tf_op jit(solution)/shard_map/ppermute | solution.py:34
  32.0 7.6 %collective-permute-done.7 = bf16[4,8,7168]{2,1,0:T(8,128)(2,1)S(1)} collective-permute-done((bf16[4,8,7168]{2,1,0:T(8,128)(2,1)S(1)}, bf16[4,8,7168]{2,1,0:T(8,128)(2,1)S(1)}, u32[]{:S(2)}, u32[]{:S(2)}) %collective-permute-start.7) | collective-permute-done | bytes 458784 | tf_op jit(solution)/shard_map/ppermute | solution.py:34
  39.9 9.2 %collective-permute-done.13 = bf16[4,8,7168]{2,1,0:T(8,128)(2,1)S(1)} collective-permute-done((bf16[4,8,7168]{2,1,0:T(8,128)(2,1)S(1)}, bf16[4,8,7168]{2,1,0:T(8,128)(2,1)S(1)}, u32[]{:S(2)}, u32[]{:S(2)}) %collective-permute-start.13) | collective-permute-done | bytes 458784 | tf_op jit(solution)/shard_map/ppermute | solution.py:34
  49.3 1.6 %collective-permute-start.3 = (f32[2,1,32,513]{3,2,0,1:T(8,128)S(1)}, f32[2,1,32,513]{3,2,0,1:T(8,128)S(1)}, u32[]{:S(2)}, u32[]{:S(2)}) collective-permute-start(f32[2,1,32,513]{3,2,0,1:T(8,128)S(1)} %constant_dynamic-slice_fusion), channel_id=1, source_target_pairs={{0,2},{1,3},{2,0},{3,1},{4,6},{5,7},{6,4},{7,5},{8,10},{9,11},{10,... | collective-permute-start | bytes 393992 | tf_op jit(solution)/shard_map/ppermute | solution.py:152
  51.9 1.2 %copy-done.7 = bf16[1,7168,256]{2,1,0:T(8,128)(2,1)S(1)} copy-done((bf16[1,7168,256]{2,1,0:T(8,128)(2,1)S(1)}, bf16[1,7168,256]{2,1,0:T(8,128)(2,1)}, u32[]{:S(2)}) %copy-start.7) | copy-done | bytes 3670040
  53.1 1.1 %fusion.6 = f32[256,256]{1,0:T(8,128)S(1)} fusion(bf16[1,7168,256]{2,1,0:T(8,128)(2,1)S(1)} %copy-done.7, bf16[128,7168]{1,0:T(8,128)(2,1)S(1)} %bitcast.115, bf16[128,7168]{1,0:T(8,128)(2,1)S(1)} %bitcast.113), kind=kOutput, calls=%fused_computation.8 | convolution fusion | flops 946864128 | bytes 7602176 | tf_op jit(solution)/shard_map/dot_general | solution.py:73
  55.1 1.1 %multiply_convert_fusion = bf16[256,256]{1,0:T(8,128)(2,1)S(1)} fusion(f32[256,256]{1,0:T(8,128)S(1)} %fusion.6, bf16[1,7168,256]{2,1,0:T(8,128)(2,1)S(1)} %copy-done.8, bf16[128,7168]{1,0:T(8,128)(2,1)S(1)} %bitcast.116, bf16[128,7168]{1,0:T(8,128)(2,1)S(1)} %bitcast.114), kind=kOutput, calls=%fused_computation.44 | convolution fusion | flops 947257344 | bytes 7733248 | tf_op jit(solution)/shard_map/dot_general | solution.py:74
  56.3 0.9 copy-done.1
  59.9 2.8 %collective-permute-done.21 = f32[2,4,8,7168]{3,2,1,0:T(8,128)S(1)} collective-permute-done((f32[2,4,8,7168]{3,2,1,0:T(8,128)S(1)}, f32[2,4,8,7168]{3,2,1,0:T(8,128)S(1)}, u32[]{:S(2)}, u32[]{:S(2)}) %collective-permute-start.21) | collective-permute-done | bytes 1835040 | tf_op jit(solution)/shard_map/ppermute | solution.py:40
  63.5 1.8 %collective-permute-done.15 = f32[2,4,8,7168]{3,2,1,0:T(8,128)S(1)} collective-permute-done((f32[2,4,8,7168]{3,2,1,0:T(8,128)S(1)}, f32[2,4,8,7168]{3,2,1,0:T(8,128)S(1)}, u32[]{:S(2)}, u32[]{:S(2)}) %collective-permute-start.15) | collective-permute-done | bytes 1835040 | tf_op jit(solution)/shard_map/ppermute | solution.py:40
  66.2 10.2 %collective-permute-done.22 = bf16[4,8,7168]{2,1,0:T(8,128)(2,1)S(1)} collective-permute-done((bf16[4,8,7168]{2,1,0:T(8,128)(2,1)S(1)}, bf16[4,8,7168]{2,1,0:T(8,128)(2,1)S(1)}, u32[]{:S(2)}, u32[]{:S(2)}) %collective-permute-start.22) | collective-permute-done | bytes 458784 | tf_op jit(solution)/shard_map/ppermute | solution.py:40
  76.5 1.5 %collective-permute-start.23 = (bf16[8,7168]{1,0:T(8,128)(2,1)S(1)}, bf16[8,7168]{1,0:T(8,128)(2,1)S(1)}, u32[]{:S(2)}, u32[]{:S(2)}) collective-permute-start(bf16[8,7168]{1,0:T(8,128)(2,1)S(1)} %get-tuple-element.20), channel_id=1, source_target_pairs={{0,28},{4,0},{8,4},{12,8},{16,12},{20,16},{24,20},{28,24},{1,29},{... | collective-permute-start | bytes 344072 | tf_op jit(solution)/shard_map/ppermute | solution.py:95
  78.4 1.7 %collective-permute-start.25 = (bf16[8,7168]{1,0:T(8,128)(2,1)S(1)}, bf16[8,7168]{1,0:T(8,128)(2,1)S(1)}, u32[]{:S(2)}, u32[]{:S(2)}) collective-permute-start(bf16[8,7168]{1,0:T(8,128)(2,1)S(1)} %get-tuple-element.21), channel_id=1, source_target_pairs={{0,20},{4,24},{8,28},{12,0},{16,4},{20,8},{24,12},{28,16},{1,21},{... | collective-permute-start | bytes 344072 | tf_op jit(solution)/shard_map/ppermute | solution.py:95
  80.1 5.4 %collective-permute-done.16 = bf16[4,8,7168]{2,1,0:T(8,128)(2,1)S(1)} collective-permute-done((bf16[4,8,7168]{2,1,0:T(8,128)(2,1)S(1)}, bf16[4,8,7168]{2,1,0:T(8,128)(2,1)S(1)}, u32[]{:S(2)}, u32[]{:S(2)}) %collective-permute-start.16) | collective-permute-done | bytes 458784 | tf_op jit(solution)/shard_map/ppermute | solution.py:40
  85.8 1.8 %collective-permute-start.18 = (bf16[8,7168]{1,0:T(8,128)(2,1)S(1)}, bf16[8,7168]{1,0:T(8,128)(2,1)S(1)}, u32[]{:S(2)}, u32[]{:S(2)}) collective-permute-start(bf16[8,7168]{1,0:T(8,128)(2,1)S(1)} %get-tuple-element.19), channel_id=1, source_target_pairs={{0,12},{4,16},{8,20},{12,24},{16,28},{20,0},{24,4},{28,8},{1,13},{... | collective-permute-start | bytes 344072 | tf_op jit(solution)/shard_map/ppermute | solution.py:95
  87.6 2.5 %collective-permute-start.19 = (bf16[8,7168]{1,0:T(8,128)(2,1)S(1)}, bf16[8,7168]{1,0:T(8,128)(2,1)S(1)}, u32[]{:S(2)}, u32[]{:S(2)}) collective-permute-start(bf16[8,7168]{1,0:T(8,128)(2,1)S(1)} %get-tuple-element.18), channel_id=1, source_target_pairs={{0,8},{4,12},{8,16},{12,20},{16,24},{20,28},{24,0},{28,4},{1,9},{5... | collective-permute-start | bytes 344072 | tf_op jit(solution)/shard_map/ppermute | solution.py:95
  91.4 6.9 %collective-permute-done.17 = bf16[8,7168]{1,0:T(8,128)(2,1)S(1)} collective-permute-done((bf16[8,7168]{1,0:T(8,128)(2,1)S(1)}, bf16[8,7168]{1,0:T(8,128)(2,1)S(1)}, u32[]{:S(2)}, u32[]{:S(2)}) %collective-permute-start.17) | collective-permute-done | bytes 114720 | tf_op jit(solution)/shard_map/ppermute | solution.py:95
  98.4 5.1 %collective-permute-done.18 = bf16[8,7168]{1,0:T(8,128)(2,1)S(1)} collective-permute-done((bf16[8,7168]{1,0:T(8,128)(2,1)S(1)}, bf16[8,7168]{1,0:T(8,128)(2,1)S(1)}, u32[]{:S(2)}, u32[]{:S(2)}) %collective-permute-start.18) | collective-permute-done | bytes 114720 | tf_op jit(solution)/shard_map/ppermute | solution.py:95
  (84 shorter events, 14.0 us)
Async XLA Ops:
  0.6 8.2 %copy-start = (bf16[2,1024,512]{2,1,0:T(8,128)(2,1)S(1)}, bf16[2,1024,512]{2,1,0:T(8,128)(2,1)}, u32[]{:S(2)}) copy-start(bf16[2,1024,512]{2,1,0:T(8,128)(2,1)} %param.13) | copy-start | bytes 6291460
  0.6 10.0 %copy-start.2 = (bf16[2,64,1024]{2,1,0:T(8,128)(2,1)S(1)}, bf16[2,64,1024]{2,1,0:T(8,128)(2,1)}, u32[]{:S(2)}) copy-start(bf16[2,64,1024]{2,1,0:T(8,128)(2,1)} %param.14) | copy-start | bytes 786436
  0.7 21.7 %collective-permute-start.6 = (bf16[8,7168]{1,0:T(8,128)(2,1)}, bf16[8,7168]{1,0:T(8,128)(2,1)}, u32[]{:S(2)}, u32[]{:S(2)}) collective-permute-start(bf16[8,7168]{1,0:T(8,128)(2,1)} %param.16), channel_id=1, source_target_pairs={{0,12},{4,16},{8,20},{12,24},{16,28},{20,0},{24,4},{28,8},{1,13},{... | collective-permute-start | bytes 344072 | tf_op jit(solution)/shard_map/ppermute | solution.py:60
  4.7 20.0 %collective-permute-start.4 = (bf16[8,7168]{1,0:T(8,128)(2,1)}, bf16[8,7168]{1,0:T(8,128)(2,1)}, u32[]{:S(2)}, u32[]{:S(2)}) collective-permute-start(bf16[8,7168]{1,0:T(8,128)(2,1)} %param.16), channel_id=1, source_target_pairs={{0,4},{4,8},{8,12},{12,16},{16,20},{20,24},{24,28},{28,0},{1,5},{5... | collective-permute-start | bytes 344072 | tf_op jit(solution)/shard_map/ppermute | solution.py:60
  6.2 19.0 %collective-permute-start.5 = (bf16[8,7168]{1,0:T(8,128)(2,1)}, bf16[8,7168]{1,0:T(8,128)(2,1)}, u32[]{:S(2)}, u32[]{:S(2)}) collective-permute-start(bf16[8,7168]{1,0:T(8,128)(2,1)} %param.16), channel_id=1, source_target_pairs={{0,8},{4,12},{8,16},{12,20},{16,24},{20,28},{24,0},{28,4},{1,9},{5... | collective-permute-start | bytes 344072 | tf_op jit(solution)/shard_map/ppermute | solution.py:60
  7.8 18.5 %collective-permute-start.9 = (bf16[8,7168]{1,0:T(8,128)(2,1)}, bf16[8,7168]{1,0:T(8,128)(2,1)}, u32[]{:S(2)}, u32[]{:S(2)}) collective-permute-start(bf16[8,7168]{1,0:T(8,128)(2,1)} %param.16), channel_id=1, source_target_pairs={{0,16},{4,20},{8,24},{12,28},{16,0},{20,4},{24,8},{28,12},{1,17},{... | collective-permute-start | bytes 344072 | tf_op jit(solution)/shard_map/ppermute | solution.py:60
  8.1 2.5 %copy-start.4 = (bf16[2,64,128]{2,1,0:T(8,128)(2,1)S(1)}, bf16[2,64,128]{2,1,0:T(8,128)(2,1)}, u32[]{:S(2)}) copy-start(bf16[2,64,128]{2,1,0:T(8,128)(2,1)} %param.12) | copy-start | bytes 98308
  8.9 2.4 %copy-start.5 = (f32[8,4]{0,1:T(4,128)S(1)}, f32[8,4]{0,1:T(4,128)}, u32[]{:S(2)}) copy-start(f32[8,4]{0,1:T(4,128)} %param.18) | copy-start | bytes 388
  8.9 2.4 %copy-start.6 = (s32[8,4]{0,1:T(4,128)S(1)}, s32[8,4]{0,1:T(4,128)}, u32[]{:S(2)}) copy-start(s32[8,4]{0,1:T(4,128)} %param.17) | copy-start | bytes 388
  10.7 5.4 %copy-start.3 = (bf16[8,7168]{1,0:T(8,128)(2,1)S(1)}, bf16[8,7168]{1,0:T(8,128)(2,1)}, u32[]{:S(2)}) copy-start(bf16[8,7168]{1,0:T(8,128)(2,1)} %param.16) | copy-start | bytes 344068
  11.1 1.3 %collective-permute-start = (f32[2,128]{1,0:T(2,128)S(1)}, f32[2,128]{1,0:T(2,128)S(1)}, u32[]{:S(2)}, u32[]{:S(2)}) collective-permute-start(f32[2,128]{1,0:T(2,128)S(1)} %get-tuple-element.35), channel_id=1, source_target_pairs={{0,1},{1,0},{2,3},{3,2},{4,5},{5,4},{6,7},{7,6},{8,9},{9,8},{10,11... | collective-permute-start | bytes 3080 | tf_op jit(solution)/shard_map/ppermute | solution.py:139
  12.5 3.6 %collective-permute-start.1 = (f32[2,128]{1,0:T(2,128)S(1)}, f32[2,128]{1,0:T(2,128)S(1)}, u32[]{:S(2)}, u32[]{:S(2)}) collective-permute-start(f32[2,128]{1,0:T(2,128)S(1)} %max.6), channel_id=1, source_target_pairs={{0,2},{1,3},{2,0},{3,1},{4,6},{5,7},{6,4},{7,5},{8,10},{9,11},{10,... | collective-permute-start | bytes 3080 | tf_op jit(solution)/shard_map/ppermute | solution.py:139
  16.1 11.7 %collective-permute-start.10 = (bf16[8,7168]{1,0:T(8,128)(2,1)S(1)}, bf16[8,7168]{1,0:T(8,128)(2,1)S(1)}, u32[]{:S(2)}, u32[]{:S(2)}) collective-permute-start(bf16[8,7168]{1,0:T(8,128)(2,1)S(1)} %copy-done.3), channel_id=1, source_target_pairs={{0,20},{4,24},{8,28},{12,0},{16,4},{20,8},{24,12},{28,16},{1,21},{... | collective-permute-start | bytes 344072 | tf_op jit(solution)/shard_map/ppermute | solution.py:60
  22.3 6.5 %collective-permute-start.11 = (bf16[8,7168]{1,0:T(8,128)(2,1)S(1)}, bf16[8,7168]{1,0:T(8,128)(2,1)S(1)}, u32[]{:S(2)}, u32[]{:S(2)}) collective-permute-start(bf16[8,7168]{1,0:T(8,128)(2,1)S(1)} %copy-done.3), channel_id=1, source_target_pairs={{0,24},{4,28},{8,0},{12,4},{16,8},{20,12},{24,16},{28,20},{1,25},{... | collective-permute-start | bytes 344072 | tf_op jit(solution)/shard_map/ppermute | solution.py:60
  24.6 4.8 %collective-permute-start.12 = (bf16[8,7168]{1,0:T(8,128)(2,1)S(1)}, bf16[8,7168]{1,0:T(8,128)(2,1)S(1)}, u32[]{:S(2)}, u32[]{:S(2)}) collective-permute-start(bf16[8,7168]{1,0:T(8,128)(2,1)S(1)} %copy-done.3), channel_id=1, source_target_pairs={{0,28},{4,0},{8,4},{12,8},{16,12},{20,16},{24,20},{28,24},{1,29},{... | collective-permute-start | bytes 344072 | tf_op jit(solution)/shard_map/ppermute | solution.py:60
  25.2 6.8 %collective-permute-start.2 = (f32[2,2,32,513]{3,2,0,1:T(8,128)S(1)}, f32[2,2,32,513]{3,2,0,1:T(8,128)S(1)}, u32[]{:S(2)}, u32[]{:S(2)}) collective-permute-start(f32[2,2,32,513]{3,2,0,1:T(8,128)S(1)} %bitcast.121), channel_id=1, source_target_pairs={{0,1},{1,0},{2,3},{3,2},{4,5},{5,4},{6,7},{7,6},{8,9},{9,8},{10,11... | collective-permute-start | bytes 787976 | tf_op jit(solution)/shard_map/ppermute | solution.py:152
  26.3 13.4 %collective-permute-start.7 = (bf16[4,8,7168]{2,1,0:T(8,128)(2,1)S(1)}, bf16[4,8,7168]{2,1,0:T(8,128)(2,1)S(1)}, u32[]{:S(2)}, u32[]{:S(2)}) collective-permute-start(bf16[4,8,7168]{2,1,0:T(8,128)(2,1)S(1)} %get-tuple-element.24), channel_id=1, source_target_pairs={{0,2},{1,3},{2,0},{3,1},{4,6},{5,7},{6,4},{7,5},{8,10},{9,11},{10,... | collective-permute-start | bytes 1376264 | tf_op jit(solution)/shard_map/ppermute | solution.py:34
  30.4 18.7 %collective-permute-start.13 = (bf16[4,8,7168]{2,1,0:T(8,128)(2,1)S(1)}, bf16[4,8,7168]{2,1,0:T(8,128)(2,1)S(1)}, u32[]{:S(2)}, u32[]{:S(2)}) collective-permute-start(bf16[4,8,7168]{2,1,0:T(8,128)(2,1)S(1)} %get-tuple-element.26), channel_id=1, source_target_pairs={{0,2},{1,3},{2,0},{3,1},{4,6},{5,7},{6,4},{7,5},{8,10},{9,11},{10,... | collective-permute-start | bytes 1376264 | tf_op jit(solution)/shard_map/ppermute | solution.py:34
  39.8 11.1 %collective-permute-start.8 = (bf16[2,4,8,7168]{3,2,1,0:T(8,128)(2,1)S(1)}, bf16[2,4,8,7168]{3,2,1,0:T(8,128)(2,1)S(1)}, u32[]{:S(2)}, u32[]{:S(2)}) collective-permute-start(bf16[2,4,8,7168]{3,2,1,0:T(8,128)(2,1)S(1)} %get-tuple-element.11), channel_id=1, source_target_pairs={{0,1},{1,0},{2,3},{3,2},{4,5},{5,4},{6,7},{7,6},{8,9},{9,8},{10,11... | collective-permute-start | bytes 2752520 | tf_op jit(solution)/shard_map/ppermute | solution.py:34
  49.2 2.5 %collective-permute-start.14 = (bf16[2,4,8,7168]{3,2,1,0:T(8,128)(2,1)S(1)}, bf16[2,4,8,7168]{3,2,1,0:T(8,128)(2,1)S(1)}, u32[]{:S(2)}, u32[]{:S(2)}) collective-permute-start(bf16[2,4,8,7168]{3,2,1,0:T(8,128)(2,1)S(1)} %get-tuple-element.13), channel_id=1, source_target_pairs={{0,1},{1,0},{2,3},{3,2},{4,5},{5,4},{6,7},{7,6},{8,9},{9,8},{10,11... | collective-permute-start | bytes 2752520 | tf_op jit(solution)/shard_map/ppermute | solution.py:34
  49.3 10.5 %collective-permute-start.3 = (f32[2,1,32,513]{3,2,0,1:T(8,128)S(1)}, f32[2,1,32,513]{3,2,0,1:T(8,128)S(1)}, u32[]{:S(2)}, u32[]{:S(2)}) collective-permute-start(f32[2,1,32,513]{3,2,0,1:T(8,128)S(1)} %constant_dynamic-slice_fusion), channel_id=1, source_target_pairs={{0,2},{1,3},{2,0},{3,1},{4,6},{5,7},{6,4},{7,5},{8,10},{9,11},{10,... | collective-permute-start | bytes 393992 | tf_op jit(solution)/shard_map/ppermute | solution.py:152
  58.8 3.9 %collective-permute-start.21 = (f32[2,4,8,7168]{3,2,1,0:T(8,128)S(1)}, f32[2,4,8,7168]{3,2,1,0:T(8,128)S(1)}, u32[]{:S(2)}, u32[]{:S(2)}) collective-permute-start(f32[2,4,8,7168]{3,2,1,0:T(8,128)S(1)} %bitcast.112), channel_id=1, source_target_pairs={{0,1},{1,0},{2,3},{3,2},{4,5},{5,4},{6,7},{7,6},{8,9},{9,8},{10,11... | collective-permute-start | bytes 5505032 | tf_op jit(solution)/shard_map/ppermute | solution.py:40
  59.5 5.9 %collective-permute-start.15 = (f32[2,4,8,7168]{3,2,1,0:T(8,128)S(1)}, f32[2,4,8,7168]{3,2,1,0:T(8,128)S(1)}, u32[]{:S(2)}, u32[]{:S(2)}) collective-permute-start(f32[2,4,8,7168]{3,2,1,0:T(8,128)S(1)} %bitcast.111), channel_id=1, source_target_pairs={{0,1},{1,0},{2,3},{3,2},{4,5},{5,4},{6,7},{7,6},{8,9},{9,8},{10,11... | collective-permute-start | bytes 5505032 | tf_op jit(solution)/shard_map/ppermute | solution.py:40
  62.9 13.4 %collective-permute-start.22 = (bf16[4,8,7168]{2,1,0:T(8,128)(2,1)S(1)}, bf16[4,8,7168]{2,1,0:T(8,128)(2,1)S(1)}, u32[]{:S(2)}, u32[]{:S(2)}) collective-permute-start(bf16[4,8,7168]{2,1,0:T(8,128)(2,1)S(1)} %fusion.22), channel_id=1, source_target_pairs={{0,2},{1,3},{2,0},{3,1},{4,6},{5,7},{6,4},{7,5},{8,10},{9,11},{10,... | collective-permute-start | bytes 1376264 | tf_op jit(solution)/shard_map/ppermute | solution.py:40
  65.6 19.9 %collective-permute-start.16 = (bf16[4,8,7168]{2,1,0:T(8,128)(2,1)S(1)}, bf16[4,8,7168]{2,1,0:T(8,128)(2,1)S(1)}, u32[]{:S(2)}, u32[]{:S(2)}) collective-permute-start(bf16[4,8,7168]{2,1,0:T(8,128)(2,1)S(1)} %fusion.21), channel_id=1, source_target_pairs={{0,2},{1,3},{2,0},{3,1},{4,6},{5,7},{6,4},{7,5},{8,10},{9,11},{10,... | collective-permute-start | bytes 1376264 | tf_op jit(solution)/shard_map/ppermute | solution.py:40
  76.5 11.2 %collective-permute-start.23 = (bf16[8,7168]{1,0:T(8,128)(2,1)S(1)}, bf16[8,7168]{1,0:T(8,128)(2,1)S(1)}, u32[]{:S(2)}, u32[]{:S(2)}) collective-permute-start(bf16[8,7168]{1,0:T(8,128)(2,1)S(1)} %get-tuple-element.20), channel_id=1, source_target_pairs={{0,28},{4,0},{8,4},{12,8},{16,12},{20,16},{24,20},{28,24},{1,29},{... | collective-permute-start | bytes 344072 | tf_op jit(solution)/shard_map/ppermute | solution.py:95
  77.9 12.2 %collective-permute-start.24 = (bf16[8,7168]{1,0:T(8,128)(2,1)S(1)}, bf16[8,7168]{1,0:T(8,128)(2,1)S(1)}, u32[]{:S(2)}, u32[]{:S(2)}) collective-permute-start(bf16[8,7168]{1,0:T(8,128)(2,1)S(1)} %get-tuple-element.22), channel_id=1, source_target_pairs={{0,24},{4,28},{8,0},{12,4},{16,8},{20,12},{24,16},{28,20},{1,25},{... | collective-permute-start | bytes 344072 | tf_op jit(solution)/shard_map/ppermute | solution.py:95
  78.4 13.1 %collective-permute-start.25 = (bf16[8,7168]{1,0:T(8,128)(2,1)S(1)}, bf16[8,7168]{1,0:T(8,128)(2,1)S(1)}, u32[]{:S(2)}, u32[]{:S(2)}) collective-permute-start(bf16[8,7168]{1,0:T(8,128)(2,1)S(1)} %get-tuple-element.21), channel_id=1, source_target_pairs={{0,20},{4,24},{8,28},{12,0},{16,4},{20,8},{24,12},{28,16},{1,21},{... | collective-permute-start | bytes 344072 | tf_op jit(solution)/shard_map/ppermute | solution.py:95
  85.6 12.8 %collective-permute-start.17 = (bf16[8,7168]{1,0:T(8,128)(2,1)S(1)}, bf16[8,7168]{1,0:T(8,128)(2,1)S(1)}, u32[]{:S(2)}, u32[]{:S(2)}) collective-permute-start(bf16[8,7168]{1,0:T(8,128)(2,1)S(1)} %get-tuple-element.16), channel_id=1, source_target_pairs={{0,16},{4,20},{8,24},{12,28},{16,0},{20,4},{24,8},{28,12},{1,17},{... | collective-permute-start | bytes 344072 | tf_op jit(solution)/shard_map/ppermute | solution.py:95
  85.8 17.6 %collective-permute-start.18 = (bf16[8,7168]{1,0:T(8,128)(2,1)S(1)}, bf16[8,7168]{1,0:T(8,128)(2,1)S(1)}, u32[]{:S(2)}, u32[]{:S(2)}) collective-permute-start(bf16[8,7168]{1,0:T(8,128)(2,1)S(1)} %get-tuple-element.19), channel_id=1, source_target_pairs={{0,12},{4,16},{8,20},{12,24},{16,28},{20,0},{24,4},{28,8},{1,13},{... | collective-permute-start | bytes 344072 | tf_op jit(solution)/shard_map/ppermute | solution.py:95
  87.6 15.8 %collective-permute-start.19 = (bf16[8,7168]{1,0:T(8,128)(2,1)S(1)}, bf16[8,7168]{1,0:T(8,128)(2,1)S(1)}, u32[]{:S(2)}, u32[]{:S(2)}) collective-permute-start(bf16[8,7168]{1,0:T(8,128)(2,1)S(1)} %get-tuple-element.18), channel_id=1, source_target_pairs={{0,8},{4,12},{8,16},{12,20},{16,24},{20,28},{24,0},{28,4},{1,9},{5... | collective-permute-start | bytes 344072 | tf_op jit(solution)/shard_map/ppermute | solution.py:95
  90.1 13.3 %collective-permute-start.20 = (bf16[8,7168]{1,0:T(8,128)(2,1)S(1)}, bf16[8,7168]{1,0:T(8,128)(2,1)S(1)}, u32[]{:S(2)}, u32[]{:S(2)}) collective-permute-start(bf16[8,7168]{1,0:T(8,128)(2,1)S(1)} %get-tuple-element.17), channel_id=1, source_target_pairs={{0,4},{4,8},{8,12},{12,16},{16,20},{20,24},{24,28},{28,0},{1,5},{5... | collective-permute-start | bytes 344072 | tf_op jit(solution)/shard_map/ppermute | solution.py:95
  (3 other events, 6.1 us)

commit v19 on v16

--- a/solution.py
+++ b/solution.py
@@ -53,14 +53,15 @@
         b //= 2
     hit = route_ids[:, :, None] == jnp.arange(n_experts, dtype=jnp.int32)[None, None, :]
     wmat = jnp.sum(jnp.where(hit, route_gates[:, :, None], 0.0), axis=1)
-    n_chunks = 4 if n_attn % 4 == 0 else 1
-    per_chunk = n_attn // n_chunks
+    split = max(1, (3 * n_attn) // 8)
+    bounds = [0, split, n_attn] if split < n_attn else [0, n_attn]
+    n_chunks = len(bounds) - 1
     pieces = [tokens]
     for k in range(1, n_attn):
         pieces.append(lax.ppermute(tokens, "attn", [(s, (s + k) % n_attn) for s in range(n_attn)]))
     blocks = []
     for c in range(n_chunks):
-        block = jnp.stack(pieces[c * per_chunk : (c + 1) * per_chunk])
+        block = jnp.stack(pieces[bounds[c] : bounds[c + 1]])
         for bit in bits:
             block = bit_gather(block, "exp", bit, n_exp)
         blocks.append(block)
@@ -84,8 +85,8 @@
                 wire = jnp.bfloat16 if bit == bits[0] else None
                 part = bit_reduce(part, "exp", bit, n_exp, wire)
             expert_rows = part.astype(jnp.bfloat16)
-            for kk in range(per_chunk):
-                k = c * per_chunk + kk
+            for kk in range(bounds[c + 1] - bounds[c]):
+                k = bounds[c] + kk
                 if k == 0:
                     back = expert_rows[kk]
                 else:

time: 102 us -> 110 us (1.078)
  waiting for transfers between devices: 37.9 us -> 56.4 us
  starting transfers between devices: 40.8 us -> 31.9 us
  local copies, waits for them, and re-layouts: 5.07 us -> 8.09 us
  matrix products: 9.78 us -> 7.35 us
  other arithmetic: 7.11 us -> 5.3 us
    ppermute x8 -> x4, waiting for transfers between devices: 7.17 us -> 20.9 us  [bit_reduce(): lax.ppermute(sent, axis, [(i, i ^ bit) for i in range(n)]).astype(x.dtype)]
    ppermute x8 -> x4, waiting for transfers between devices: 14.8 us -> 19.6 us  [bit_gather(): other = lax.ppermute(x, axis, [(i, i ^ bit) for i in range(n)])]
    ppermute x7, starting transfers between devices: 13.6 us -> 9.67 us  [routed_experts(): lax.ppermute(expert_rows[kk], 'attn', [(s, (s - k) % n_attn) for s in ran...]
    ppermute x8 -> x4, starting transfers between devices: 5.55 us -> 2.3 us  [bit_gather(): other = lax.ppermute(x, axis, [(i, i ^ bit) for i in range(n)])]
    ppermute x2, waiting for transfers between devices: 2.91 us -> 0.01 us  [per_device(): got = lax.ppermute(sent, 'exp', [(i, i ^ bit) for i in range(n_exp)])]
    unnamed x14 -> x22, local copies, waits for them, and re-layouts: 3.46 us -> 6.34 us
    ppermute x8 -> x4, starting transfers between devices: 6.36 us -> 3.74 us  [bit_reduce(): lax.ppermute(sent, axis, [(i, i ^ bit) for i in range(n)]).astype(x.dtype)]
    another operation x12 -> x5, other arithmetic: 2.57 us -> 0.63 us  [bit_gather(): return jnp.stack([x, other])]
  transfers between devices with their start and end apart: 34 -> 26, of which waited for: 14 -> 11; matrix products, arithmetic and copies ran while one was open for 12% -> 14% of each run, Pallas kernels for 0% -> 0%
where the time goes in v19:
time: 110 us
  waiting for transfers between devices  56.4 us (51%)
  starting transfers between devices  31.9 us (29%)
  local copies, waits for them, and re-layouts  8.09 us (7%)
  matrix products  7.35 us (7%)
  other arithmetic  5.3 us (5%)
    ppermute x4, waiting for transfers between devices, bit_reduce(): lax.ppermute(sent, axis, [(i, i ^ bit) for i in range(n)]).astype(x.dtype)  20.9 us
    ppermute x4, waiting for transfers between devices, bit_gather(): other = lax.ppermute(x, axis, [(i, i ^ bit) for i in range(n)])  19.6 us
    ppermute x7, starting transfers between devices, routed_experts(): lax.ppermute(tokens, 'attn', [(s, (s + k) % n_attn) for s in range(n_attn)])  13 us
    ppermute x7, waiting for transfers between devices, routed_experts(): lax.ppermute(expert_rows[kk], 'attn', [(s, (s - k) % n_attn) for s in ran...  11 us
    ppermute x7, starting transfers between devices, routed_experts(): lax.ppermute(expert_rows[kk], 'attn', [(s, (s - k) % n_attn) for s in ran...  9.67 us
    unnamed x22, local copies, waits for them, and re-layouts  6.34 us
    ppermute x4, starting transfers between devices, bit_reduce(): lax.ppermute(sent, axis, [(i, i ^ bit) for i in range(n)]).astype(x.dtype)  3.74 us
    ppermute x7, waiting for transfers between devices, routed_experts(): lax.ppermute(tokens, 'attn', [(s, (s + k) % n_attn) for s in range(n_attn)])  2.76 us
  transfers between devices with their start and end apart: 26, of which 11 were waited for; matrix products, arithmetic and copies ran while one was open for 14% of the time, Pallas kernels for 0%

profile of v19, /device:TPU:0, one launch (start us, length us, event | category | flops | bytes accessed | tf_op | source)
XLA Modules:
  0.0 110.0 jit_solution(926608525733113262)
XLA Ops:
  0.7 4.0 %collective-permute-start.8 = (bf16[8,7168]{1,0:T(8,128)(2,1)}, bf16[8,7168]{1,0:T(8,128)(2,1)}, u32[]{:S(2)}, u32[]{:S(2)}) collective-permute-start(bf16[8,7168]{1,0:T(8,128)(2,1)} %param.16), channel_id=1, source_target_pairs={{0,12},{4,16},{8,20},{12,24},{16,28},{20,0},{24,4},{28,8},{1,13},{... | collective-permute-start | bytes 344072 | tf_op jit(solution)/shard_map/ppermute | solution.py:61
  4.7 2.6 %collective-permute-start.9 = (bf16[8,7168]{1,0:T(8,128)(2,1)}, bf16[8,7168]{1,0:T(8,128)(2,1)}, u32[]{:S(2)}, u32[]{:S(2)}) collective-permute-start(bf16[8,7168]{1,0:T(8,128)(2,1)} %param.16), channel_id=1, source_target_pairs={{0,16},{4,20},{8,24},{12,28},{16,0},{20,4},{24,8},{28,12},{1,17},{... | collective-permute-start | bytes 344072 | tf_op jit(solution)/shard_map/ppermute | solution.py:61
  7.3 1.3 %collective-permute-start.10 = (bf16[8,7168]{1,0:T(8,128)(2,1)}, bf16[8,7168]{1,0:T(8,128)(2,1)}, u32[]{:S(2)}, u32[]{:S(2)}) collective-permute-start(bf16[8,7168]{1,0:T(8,128)(2,1)} %param.16), channel_id=1, source_target_pairs={{0,20},{4,24},{8,28},{12,0},{16,4},{20,8},{24,12},{28,16},{1,21},{... | collective-permute-start | bytes 344072 | tf_op jit(solution)/shard_map/ppermute | solution.py:61
  8.6 1.3 %collective-permute-start.11 = (bf16[8,7168]{1,0:T(8,128)(2,1)}, bf16[8,7168]{1,0:T(8,128)(2,1)S(1)}, u32[]{:S(2)}, u32[]{:S(2)}) collective-permute-start(bf16[8,7168]{1,0:T(8,128)(2,1)} %param.16), channel_id=1, source_target_pairs={{0,24},{4,28},{8,0},{12,4},{16,8},{20,12},{24,16},{28,20},{1,25},{... | collective-permute-start | bytes 344072 | tf_op jit(solution)/shard_map/ppermute | solution.py:61
  10.7 1.8 %fusion.53 = f32[2,128,1024]{2,1,0:T(8,128)S(1)} fusion(bf16[2,128,512]{2,1,0:T(8,128)(2,1)} %param.11, bf16[2,1024,512]{2,1,0:T(8,128)(2,1)S(1)} %copy-done), kind=kOutput, calls=%fused_computation.111 | convolution fusion | flops 268435456 | bytes 3407872 | tf_op jit(solution)/shard_map/rhl,rpl->rhp/dot_general | solution.py:115
  14.2 1.6 %collective-permute-start.1 = (f32[2,128]{1,0:T(2,128)S(1)}, f32[2,128]{1,0:T(2,128)S(1)}, u32[]{:S(2)}, u32[]{:S(2)}) collective-permute-start(f32[2,128]{1,0:T(2,128)S(1)} %max.6), channel_id=1, source_target_pairs={{0,2},{1,3},{2,0},{3,1},{4,6},{5,7},{6,4},{7,5},{8,10},{9,11},{10,... | collective-permute-start | bytes 3080 | tf_op jit(solution)/shard_map/ppermute | solution.py:137
  15.8 2.1 %collective-permute-done.1 = f32[2,128]{1,0:T(2,128)S(1)} collective-permute-done((f32[2,128]{1,0:T(2,128)S(1)}, f32[2,128]{1,0:T(2,128)S(1)}, u32[]{:S(2)}, u32[]{:S(2)}) %collective-permute-start.1) | collective-permute-done | bytes 1056 | tf_op jit(solution)/shard_map/ppermute | solution.py:137
  18.5 1.3 %broadcast_multiply_fusion = f32[2,128,512]{2,1,0:T(8,128)} fusion(f32[2,128]{1,0:T(2,128)S(1)} %get-tuple-element.3, bf16[2,1024,512]{2,1,0:T(8,128)(2,1)S(1)} %copy-done, f32[2,128,1024]{2,1,0:T(8,128)S(1)} %get-tuple-element.32, f32[2,128]{1,0:T(2,128)S(1)} %get-tuple-element.31, pred[2,1024]{1,0:T(4,128)(4,1)S(1)} %broadcast_compare_fusion), kind=kOutput, calls=%fused_computation.44 | convolution fusion | flops 269352960 | bytes 3674112 | tf_op jit(solution)/shard_map/rhp,rpl->rhl/dot_general | solution.py:126
  20.1 1.1 fusion.24
  21.2 1.6 %collective-permute-start.5 = (bf16[8,7168]{1,0:T(8,128)(2,1)S(1)}, bf16[8,7168]{1,0:T(8,128)(2,1)S(1)}, u32[]{:S(2)}, u32[]{:S(2)}) collective-permute-start(bf16[8,7168]{1,0:T(8,128)(2,1)S(1)} %copy-done.3), channel_id=1, source_target_pairs={{0,8},{4,12},{8,16},{12,20},{16,24},{20,28},{24,0},{28,4},{1,9},{5... | collective-permute-start | bytes 344072 | tf_op jit(solution)/shard_map/ppermute | solution.py:61
  23.8 1.8 %collective-permute-done.4 = bf16[8,7168]{1,0:T(8,128)(2,1)S(1)} collective-permute-done((bf16[8,7168]{1,0:T(8,128)(2,1)}, bf16[8,7168]{1,0:T(8,128)(2,1)S(1)}, u32[]{:S(2)}, u32[]{:S(2)}) %collective-permute-start.4) | collective-permute-done | bytes 114720 | tf_op jit(solution)/shard_map/ppermute | solution.py:61
  25.6 1.4 %collective-permute-start.12 = (bf16[8,7168]{1,0:T(8,128)(2,1)S(1)}, bf16[8,7168]{1,0:T(8,128)(2,1)S(1)}, u32[]{:S(2)}, u32[]{:S(2)}) collective-permute-start(bf16[8,7168]{1,0:T(8,128)(2,1)S(1)} %copy-done.3), channel_id=1, source_target_pairs={{0,28},{4,0},{8,4},{12,8},{16,12},{20,16},{24,20},{28,24},{1,29},{... | collective-permute-start | bytes 344072 | tf_op jit(solution)/shard_map/ppermute | solution.py:61
  28.0 1.5 %collective-permute-start.6 = (bf16[3,8,7168]{2,1,0:T(8,128)(2,1)S(1)}, bf16[3,8,7168]{2,1,0:T(8,128)(2,1)S(1)}, u32[]{:S(2)}, u32[]{:S(2)}) collective-permute-start(bf16[3,8,7168]{2,1,0:T(8,128)(2,1)S(1)} %get-tuple-element.22), channel_id=1, source_target_pairs={{0,2},{1,3},{2,0},{3,1},{4,6},{5,7},{6,4},{7,5},{8,10},{9,11},{10,... | collective-permute-start | bytes 1032200 | tf_op jit(solution)/shard_map/ppermute | solution.py:34
  32.1 6.9 %collective-permute-done.6 = bf16[3,8,7168]{2,1,0:T(8,128)(2,1)S(1)} collective-permute-done((bf16[3,8,7168]{2,1,0:T(8,128)(2,1)S(1)}, bf16[3,8,7168]{2,1,0:T(8,128)(2,1)S(1)}, u32[]{:S(2)}, u32[]{:S(2)}) %collective-permute-start.6) | collective-permute-done | bytes 344096 | tf_op jit(solution)/shard_map/ppermute | solution.py:34
  39.1 11.7 %collective-permute-done.13 = bf16[5,8,7168]{2,1,0:T(8,128)(2,1)S(1)} collective-permute-done((bf16[5,8,7168]{2,1,0:T(8,128)(2,1)S(1)}, bf16[5,8,7168]{2,1,0:T(8,128)(2,1)S(1)}, u32[]{:S(2)}, u32[]{:S(2)}) %collective-permute-start.13) | collective-permute-done | bytes 573472 | tf_op jit(solution)/shard_map/ppermute | solution.py:34
  51.2 1.5 %collective-permute-start.3 = (f32[2,1,32,513]{3,2,0,1:T(8,128)S(1)}, f32[2,1,32,513]{3,2,0,1:T(8,128)S(1)}, u32[]{:S(2)}, u32[]{:S(2)}) collective-permute-start(f32[2,1,32,513]{3,2,0,1:T(8,128)S(1)} %constant_dynamic-slice_fusion), channel_id=1, source_target_pairs={{0,2},{1,3},{2,0},{3,1},{4,6},{5,7},{6,4},{7,5},{8,10},{9,11},{10,... | collective-permute-start | bytes 393992 | tf_op jit(solution)/shard_map/ppermute | solution.py:150
  52.9 1.0 collective-permute-done.14
  54.1 1.8 %copy-done.7 = bf16[1,7168,256]{2,1,0:T(8,128)(2,1)S(1)} copy-done((bf16[1,7168,256]{2,1,0:T(8,128)(2,1)S(1)}, bf16[1,7168,256]{2,1,0:T(8,128)(2,1)}, u32[]{:S(2)}) %copy-start.7) | copy-done | bytes 3670040
  55.9 1.1 %fusion.6 = f32[256,256]{1,0:T(8,128)S(1)} fusion(bf16[1,7168,256]{2,1,0:T(8,128)(2,1)S(1)} %copy-done.7, bf16[160,7168]{1,0:T(8,128)(2,1)S(1)} %bitcast.114, bf16[96,7168]{1,0:T(8,128)(2,1)S(1)} %bitcast.118), kind=kOutput, calls=%fused_computation.8 | convolution fusion | flops 946864128 | bytes 7602176 | tf_op jit(solution)/shard_map/dot_general | solution.py:74
  58.0 1.2 %multiply_convert_fusion = bf16[256,256]{1,0:T(8,128)(2,1)S(1)} fusion(f32[256,256]{1,0:T(8,128)S(1)} %fusion.6, bf16[1,7168,256]{2,1,0:T(8,128)(2,1)S(1)} %copy-done.8, bf16[160,7168]{1,0:T(8,128)(2,1)S(1)} %bitcast.115, bf16[96,7168]{1,0:T(8,128)(2,1)S(1)} %bitcast.119), kind=kOutput, calls=%fused_computation.43 | convolution fusion | flops 947257344 | bytes 7733248 | tf_op jit(solution)/shard_map/dot_general | solution.py:75
  62.8 2.1 %collective-permute-done.15 = f32[2,3,8,7168]{3,2,1,0:T(8,128)S(1)} collective-permute-done((f32[2,3,8,7168]{3,2,1,0:T(8,128)S(1)}, f32[2,3,8,7168]{3,2,1,0:T(8,128)S(1)}, u32[]{:S(2)}, u32[]{:S(2)}) %collective-permute-start.15) | collective-permute-done | bytes 1376288 | tf_op jit(solution)/shard_map/ppermute | solution.py:40
  65.1 1.6 %collective-permute-start.16 = (bf16[3,8,7168]{2,1,0:T(8,128)(2,1)S(1)}, bf16[3,8,7168]{2,1,0:T(8,128)(2,1)S(1)}, u32[]{:S(2)}, u32[]{:S(2)}) collective-permute-start(bf16[3,8,7168]{2,1,0:T(8,128)(2,1)S(1)} %fusion.22), channel_id=1, source_target_pairs={{0,2},{1,3},{2,0},{3,1},{4,6},{5,7},{6,4},{7,5},{8,10},{9,11},{10,... | collective-permute-start | bytes 1032200 | tf_op jit(solution)/shard_map/ppermute | solution.py:40
  66.7 8.5 %collective-permute-done.16 = bf16[3,8,7168]{2,1,0:T(8,128)(2,1)S(1)} collective-permute-done((bf16[3,8,7168]{2,1,0:T(8,128)(2,1)S(1)}, bf16[3,8,7168]{2,1,0:T(8,128)(2,1)S(1)}, u32[]{:S(2)}, u32[]{:S(2)}) %collective-permute-start.16) | collective-permute-done | bytes 344096 | tf_op jit(solution)/shard_map/ppermute | solution.py:40
  75.7 1.6 %collective-permute-start.20 = (bf16[5,8,7168]{2,1,0:T(8,128)(2,1)S(1)}, bf16[5,8,7168]{2,1,0:T(8,128)(2,1)S(1)}, u32[]{:S(2)}, u32[]{:S(2)}) collective-permute-start(bf16[5,8,7168]{2,1,0:T(8,128)(2,1)S(1)} %fusion.16), channel_id=1, source_target_pairs={{0,2},{1,3},{2,0},{3,1},{4,6},{5,7},{6,4},{7,5},{8,10},{9,11},{10,... | collective-permute-start | bytes 1720328 | tf_op jit(solution)/shard_map/ppermute | solution.py:40
  77.3 2.3 %collective-permute-start.17 = (bf16[8,7168]{1,0:T(8,128)(2,1)S(1)}, bf16[8,7168]{1,0:T(8,128)(2,1)S(1)}, u32[]{:S(2)}, u32[]{:S(2)}) collective-permute-start(bf16[8,7168]{1,0:T(8,128)(2,1)S(1)} %get-tuple-element.19), channel_id=1, source_target_pairs={{0,28},{4,0},{8,4},{12,8},{16,12},{20,16},{24,20},{28,24},{1,29},{... | collective-permute-start | bytes 344072 | tf_op jit(solution)/shard_map/ppermute | solution.py:93
  79.8 10.2 %collective-permute-done.20 = bf16[5,8,7168]{2,1,0:T(8,128)(2,1)S(1)} collective-permute-done((bf16[5,8,7168]{2,1,0:T(8,128)(2,1)S(1)}, bf16[5,8,7168]{2,1,0:T(8,128)(2,1)S(1)}, u32[]{:S(2)}, u32[]{:S(2)}) %collective-permute-start.20) | collective-permute-done | bytes 573472 | tf_op jit(solution)/shard_map/ppermute | solution.py:40
  90.2 1.0 collective-permute-start.21
  91.1 2.9 %collective-permute-start.22 = (bf16[8,7168]{1,0:T(8,128)(2,1)S(1)}, bf16[8,7168]{1,0:T(8,128)(2,1)S(1)}, u32[]{:S(2)}, u32[]{:S(2)}) collective-permute-start(bf16[8,7168]{1,0:T(8,128)(2,1)S(1)} %get-tuple-element.18), channel_id=1, source_target_pairs={{0,16},{4,20},{8,24},{12,28},{16,0},{20,4},{24,8},{28,12},{1,17},{... | collective-permute-start | bytes 344072 | tf_op jit(solution)/shard_map/ppermute | solution.py:93
  94.0 1.0 collective-permute-start.24
  95.0 2.4 %collective-permute-start.25 = (bf16[8,7168]{1,0:T(8,128)(2,1)S(1)}, bf16[8,7168]{1,0:T(8,128)(2,1)S(1)}, u32[]{:S(2)}, u32[]{:S(2)}) collective-permute-start(bf16[8,7168]{1,0:T(8,128)(2,1)S(1)} %get-tuple-element.15), channel_id=1, source_target_pairs={{0,4},{4,8},{8,12},{12,16},{16,20},{20,24},{24,28},{28,0},{1,5},{5... | collective-permute-start | bytes 344072 | tf_op jit(solution)/shard_map/ppermute | solution.py:93
  98.1 8.8 %collective-permute-done.22 = bf16[8,7168]{1,0:T(8,128)(2,1)S(1)} collective-permute-done((bf16[8,7168]{1,0:T(8,128)(2,1)S(1)}, bf16[8,7168]{1,0:T(8,128)(2,1)S(1)}, u32[]{:S(2)}, u32[]{:S(2)}) %collective-permute-start.22) | collective-permute-done | bytes 114720 | tf_op jit(solution)/shard_map/ppermute | solution.py:93
  106.9 2.2 %collective-permute-done.23 = bf16[8,7168]{1,0:T(8,128)(2,1)S(1)} collective-permute-done((bf16[8,7168]{1,0:T(8,128)(2,1)S(1)}, bf16[8,7168]{1,0:T(8,128)(2,1)S(1)}, u32[]{:S(2)}, u32[]{:S(2)}) %collective-permute-start.23) | collective-permute-done | bytes 114720 | tf_op jit(solution)/shard_map/ppermute | solution.py:93
  (87 shorter events, 15.6 us)
Async XLA Ops:
  0.6 10.0 %copy-start = (bf16[2,1024,512]{2,1,0:T(8,128)(2,1)S(1)}, bf16[2,1024,512]{2,1,0:T(8,128)(2,1)}, u32[]{:S(2)}) copy-start(bf16[2,1024,512]{2,1,0:T(8,128)(2,1)} %param.13) | copy-start | bytes 6291460
  0.6 11.8 %copy-start.2 = (bf16[2,64,1024]{2,1,0:T(8,128)(2,1)S(1)}, bf16[2,64,1024]{2,1,0:T(8,128)(2,1)}, u32[]{:S(2)}) copy-start(bf16[2,64,1024]{2,1,0:T(8,128)(2,1)} %param.14) | copy-start | bytes 786436
  0.7 20.6 %collective-permute-start.8 = (bf16[8,7168]{1,0:T(8,128)(2,1)}, bf16[8,7168]{1,0:T(8,128)(2,1)}, u32[]{:S(2)}, u32[]{:S(2)}) collective-permute-start(bf16[8,7168]{1,0:T(8,128)(2,1)} %param.16), channel_id=1, source_target_pairs={{0,12},{4,16},{8,20},{12,24},{16,28},{20,0},{24,4},{28,8},{1,13},{... | collective-permute-start | bytes 344072 | tf_op jit(solution)/shard_map/ppermute | solution.py:61
  4.7 23.3 %collective-permute-start.9 = (bf16[8,7168]{1,0:T(8,128)(2,1)}, bf16[8,7168]{1,0:T(8,128)(2,1)}, u32[]{:S(2)}, u32[]{:S(2)}) collective-permute-start(bf16[8,7168]{1,0:T(8,128)(2,1)} %param.16), channel_id=1, source_target_pairs={{0,16},{4,20},{8,24},{12,28},{16,0},{20,4},{24,8},{28,12},{1,17},{... | collective-permute-start | bytes 344072 | tf_op jit(solution)/shard_map/ppermute | solution.py:61
  7.3 23.2 %collective-permute-start.10 = (bf16[8,7168]{1,0:T(8,128)(2,1)}, bf16[8,7168]{1,0:T(8,128)(2,1)}, u32[]{:S(2)}, u32[]{:S(2)}) collective-permute-start(bf16[8,7168]{1,0:T(8,128)(2,1)} %param.16), channel_id=1, source_target_pairs={{0,20},{4,24},{8,28},{12,0},{16,4},{20,8},{24,12},{28,16},{1,21},{... | collective-permute-start | bytes 344072 | tf_op jit(solution)/shard_map/ppermute | solution.py:61
  8.6 22.8 %collective-permute-start.11 = (bf16[8,7168]{1,0:T(8,128)(2,1)}, bf16[8,7168]{1,0:T(8,128)(2,1)S(1)}, u32[]{:S(2)}, u32[]{:S(2)}) collective-permute-start(bf16[8,7168]{1,0:T(8,128)(2,1)} %param.16), channel_id=1, source_target_pairs={{0,24},{4,28},{8,0},{12,4},{16,8},{20,12},{24,16},{28,20},{1,25},{... | collective-permute-start | bytes 344072 | tf_op jit(solution)/shard_map/ppermute | solution.py:61
  9.9 2.6 %copy-start.4 = (bf16[2,64,128]{2,1,0:T(8,128)(2,1)S(1)}, bf16[2,64,128]{2,1,0:T(8,128)(2,1)}, u32[]{:S(2)}) copy-start(bf16[2,64,128]{2,1,0:T(8,128)(2,1)} %param.12) | copy-start | bytes 98308
  10.7 2.4 %copy-start.5 = (f32[8,4]{0,1:T(4,128)S(1)}, f32[8,4]{0,1:T(4,128)}, u32[]{:S(2)}) copy-start(f32[8,4]{0,1:T(4,128)} %param.18) | copy-start | bytes 388
  10.7 2.4 %copy-start.6 = (s32[8,4]{0,1:T(4,128)S(1)}, s32[8,4]{0,1:T(4,128)}, u32[]{:S(2)}) copy-start(s32[8,4]{0,1:T(4,128)} %param.17) | copy-start | bytes 388
  12.9 1.3 %collective-permute-start = (f32[2,128]{1,0:T(2,128)S(1)}, f32[2,128]{1,0:T(2,128)S(1)}, u32[]{:S(2)}, u32[]{:S(2)}) collective-permute-start(f32[2,128]{1,0:T(2,128)S(1)} %get-tuple-element.31), channel_id=1, source_target_pairs={{0,1},{1,0},{2,3},{3,2},{4,5},{5,4},{6,7},{7,6},{8,9},{9,8},{10,11... | collective-permute-start | bytes 3080 | tf_op jit(solution)/shard_map/ppermute | solution.py:137
  14.2 3.6 %collective-permute-start.1 = (f32[2,128]{1,0:T(2,128)S(1)}, f32[2,128]{1,0:T(2,128)S(1)}, u32[]{:S(2)}, u32[]{:S(2)}) collective-permute-start(f32[2,128]{1,0:T(2,128)S(1)} %max.6), channel_id=1, source_target_pairs={{0,2},{1,3},{2,0},{3,1},{4,6},{5,7},{6,4},{7,5},{8,10},{9,11},{10,... | collective-permute-start | bytes 3080 | tf_op jit(solution)/shard_map/ppermute | solution.py:137
  17.9 7.7 %collective-permute-start.4 = (bf16[8,7168]{1,0:T(8,128)(2,1)}, bf16[8,7168]{1,0:T(8,128)(2,1)S(1)}, u32[]{:S(2)}, u32[]{:S(2)}) collective-permute-start(bf16[8,7168]{1,0:T(8,128)(2,1)} %param.16), channel_id=1, source_target_pairs={{0,4},{4,8},{8,12},{12,16},{16,20},{20,24},{24,28},{28,0},{1,5},{5... | collective-permute-start | bytes 344072 | tf_op jit(solution)/shard_map/ppermute | solution.py:61
  18.5 2.7 %copy-start.3 = (bf16[8,7168]{1,0:T(8,128)(2,1)S(1)}, bf16[8,7168]{1,0:T(8,128)(2,1)}, u32[]{:S(2)}) copy-start(bf16[8,7168]{1,0:T(8,128)(2,1)} %param.16) | copy-start | bytes 344068
  21.2 6.7 %collective-permute-start.5 = (bf16[8,7168]{1,0:T(8,128)(2,1)S(1)}, bf16[8,7168]{1,0:T(8,128)(2,1)S(1)}, u32[]{:S(2)}, u32[]{:S(2)}) collective-permute-start(bf16[8,7168]{1,0:T(8,128)(2,1)S(1)} %copy-done.3), channel_id=1, source_target_pairs={{0,8},{4,12},{8,16},{12,20},{16,24},{20,28},{24,0},{28,4},{1,9},{5... | collective-permute-start | bytes 344072 | tf_op jit(solution)/shard_map/ppermute | solution.py:61
  25.6 5.8 %collective-permute-start.12 = (bf16[8,7168]{1,0:T(8,128)(2,1)S(1)}, bf16[8,7168]{1,0:T(8,128)(2,1)S(1)}, u32[]{:S(2)}, u32[]{:S(2)}) collective-permute-start(bf16[8,7168]{1,0:T(8,128)(2,1)S(1)} %copy-done.3), channel_id=1, source_target_pairs={{0,28},{4,0},{8,4},{12,8},{16,12},{20,16},{24,20},{28,24},{1,29},{... | collective-permute-start | bytes 344072 | tf_op jit(solution)/shard_map/ppermute | solution.py:61
  28.0 23.1 %collective-permute-start.2 = (f32[2,2,32,513]{3,2,0,1:T(8,128)S(1)}, f32[2,2,32,513]{3,2,0,1:T(8,128)S(1)}, u32[]{:S(2)}, u32[]{:S(2)}) collective-permute-start(f32[2,2,32,513]{3,2,0,1:T(8,128)S(1)} %bitcast.125), channel_id=1, source_target_pairs={{0,1},{1,0},{2,3},{3,2},{4,5},{5,4},{6,7},{7,6},{8,9},{9,8},{10,11... | collective-permute-start | bytes 787976 | tf_op jit(solution)/shard_map/ppermute | solution.py:150
  28.0 10.9 %collective-permute-start.6 = (bf16[3,8,7168]{2,1,0:T(8,128)(2,1)S(1)}, bf16[3,8,7168]{2,1,0:T(8,128)(2,1)S(1)}, u32[]{:S(2)}, u32[]{:S(2)}) collective-permute-start(bf16[3,8,7168]{2,1,0:T(8,128)(2,1)S(1)} %get-tuple-element.22), channel_id=1, source_target_pairs={{0,2},{1,3},{2,0},{3,1},{4,6},{5,7},{6,4},{7,5},{8,10},{9,11},{10,... | collective-permute-start | bytes 1032200 | tf_op jit(solution)/shard_map/ppermute | solution.py:34
  31.4 19.4 %collective-permute-start.13 = (bf16[5,8,7168]{2,1,0:T(8,128)(2,1)S(1)}, bf16[5,8,7168]{2,1,0:T(8,128)(2,1)S(1)}, u32[]{:S(2)}, u32[]{:S(2)}) collective-permute-start(bf16[5,8,7168]{2,1,0:T(8,128)(2,1)S(1)} %bitcast_dynamic-update-slice_fusion), channel_id=1, source_target_pairs={{0,2},{1,3},{2,0},{3,1},{4,6},{5,7},{6,4},{7,5},{8,10},{9,11},{10,... | collective-permute-start | bytes 1720328 | tf_op jit(solution)/shard_map/ppermute | solution.py:34
  39.0 13.7 %collective-permute-start.7 = (bf16[2,3,8,7168]{3,2,1,0:T(8,128)(2,1)S(1)}, bf16[2,3,8,7168]{3,2,1,0:T(8,128)(2,1)S(1)}, u32[]{:S(2)}, u32[]{:S(2)}) collective-permute-start(bf16[2,3,8,7168]{3,2,1,0:T(8,128)(2,1)S(1)} %get-tuple-element.11), channel_id=1, source_target_pairs={{0,1},{1,0},{2,3},{3,2},{4,5},{5,4},{6,7},{7,6},{8,9},{9,8},{10,11... | collective-permute-start | bytes 2064392 | tf_op jit(solution)/shard_map/ppermute | solution.py:34
  51.0 2.9 %collective-permute-start.14 = (bf16[2,5,8,7168]{3,2,1,0:T(8,128)(2,1)S(1)}, bf16[2,5,8,7168]{3,2,1,0:T(8,128)(2,1)S(1)}, u32[]{:S(2)}, u32[]{:S(2)}) collective-permute-start(bf16[2,5,8,7168]{3,2,1,0:T(8,128)(2,1)S(1)} %get-tuple-element.9), channel_id=1, source_target_pairs={{0,1},{1,0},{2,3},{3,2},{4,5},{5,4},{6,7},{7,6},{8,9},{9,8},{10,11... | collective-permute-start | bytes 3440648 | tf_op jit(solution)/shard_map/ppermute | solution.py:34
  51.2 15.5 %collective-permute-start.3 = (f32[2,1,32,513]{3,2,0,1:T(8,128)S(1)}, f32[2,1,32,513]{3,2,0,1:T(8,128)S(1)}, u32[]{:S(2)}, u32[]{:S(2)}) collective-permute-start(f32[2,1,32,513]{3,2,0,1:T(8,128)S(1)} %constant_dynamic-slice_fusion), channel_id=1, source_target_pairs={{0,2},{1,3},{2,0},{3,1},{4,6},{5,7},{6,4},{7,5},{8,10},{9,11},{10,... | collective-permute-start | bytes 393992 | tf_op jit(solution)/shard_map/ppermute | solution.py:150
  61.7 3.2 %collective-permute-start.15 = (f32[2,3,8,7168]{3,2,1,0:T(8,128)S(1)}, f32[2,3,8,7168]{3,2,1,0:T(8,128)S(1)}, u32[]{:S(2)}, u32[]{:S(2)}) collective-permute-start(f32[2,3,8,7168]{3,2,1,0:T(8,128)S(1)} %bitcast.117), channel_id=1, source_target_pairs={{0,1},{1,0},{2,3},{3,2},{4,5},{5,4},{6,7},{7,6},{8,9},{9,8},{10,11... | collective-permute-start | bytes 4128776 | tf_op jit(solution)/shard_map/ppermute | solution.py:40
  62.3 13.0 %collective-permute-start.19 = (f32[2,5,8,7168]{3,2,1,0:T(8,128)S(1)}, f32[2,5,8,7168]{3,2,1,0:T(8,128)S(1)}, u32[]{:S(2)}, u32[]{:S(2)}) collective-permute-start(f32[2,5,8,7168]{3,2,1,0:T(8,128)S(1)} %bitcast.113), channel_id=1, source_target_pairs={{0,1},{1,0},{2,3},{3,2},{4,5},{5,4},{6,7},{7,6},{8,9},{9,8},{10,11... | collective-permute-start | bytes 6881288 | tf_op jit(solution)/shard_map/ppermute | solution.py:40
  65.1 10.2 %collective-permute-start.16 = (bf16[3,8,7168]{2,1,0:T(8,128)(2,1)S(1)}, bf16[3,8,7168]{2,1,0:T(8,128)(2,1)S(1)}, u32[]{:S(2)}, u32[]{:S(2)}) collective-permute-start(bf16[3,8,7168]{2,1,0:T(8,128)(2,1)S(1)} %fusion.22), channel_id=1, source_target_pairs={{0,2},{1,3},{2,0},{3,1},{4,6},{5,7},{6,4},{7,5},{8,10},{9,11},{10,... | collective-permute-start | bytes 1032200 | tf_op jit(solution)/shard_map/ppermute | solution.py:40
  75.7 14.3 %collective-permute-start.20 = (bf16[5,8,7168]{2,1,0:T(8,128)(2,1)S(1)}, bf16[5,8,7168]{2,1,0:T(8,128)(2,1)S(1)}, u32[]{:S(2)}, u32[]{:S(2)}) collective-permute-start(bf16[5,8,7168]{2,1,0:T(8,128)(2,1)S(1)} %fusion.16), channel_id=1, source_target_pairs={{0,2},{1,3},{2,0},{3,1},{4,6},{5,7},{6,4},{7,5},{8,10},{9,11},{10,... | collective-permute-start | bytes 1720328 | tf_op jit(solution)/shard_map/ppermute | solution.py:40
  77.3 16.7 %collective-permute-start.17 = (bf16[8,7168]{1,0:T(8,128)(2,1)S(1)}, bf16[8,7168]{1,0:T(8,128)(2,1)S(1)}, u32[]{:S(2)}, u32[]{:S(2)}) collective-permute-start(bf16[8,7168]{1,0:T(8,128)(2,1)S(1)} %get-tuple-element.19), channel_id=1, source_target_pairs={{0,28},{4,0},{8,4},{12,8},{16,12},{20,16},{24,20},{28,24},{1,29},{... | collective-permute-start | bytes 344072 | tf_op jit(solution)/shard_map/ppermute | solution.py:93
  79.6 15.4 %collective-permute-start.18 = (bf16[8,7168]{1,0:T(8,128)(2,1)S(1)}, bf16[8,7168]{1,0:T(8,128)(2,1)S(1)}, u32[]{:S(2)}, u32[]{:S(2)}) collective-permute-start(bf16[8,7168]{1,0:T(8,128)(2,1)S(1)} %get-tuple-element.20), channel_id=1, source_target_pairs={{0,24},{4,28},{8,0},{12,4},{16,8},{20,12},{24,16},{28,20},{1,25},{... | collective-permute-start | bytes 344072 | tf_op jit(solution)/shard_map/ppermute | solution.py:93
  90.2 7.9 %collective-permute-start.21 = (bf16[8,7168]{1,0:T(8,128)(2,1)S(1)}, bf16[8,7168]{1,0:T(8,128)(2,1)S(1)}, u32[]{:S(2)}, u32[]{:S(2)}) collective-permute-start(bf16[8,7168]{1,0:T(8,128)(2,1)S(1)} %get-tuple-element.14), channel_id=1, source_target_pairs={{0,20},{4,24},{8,28},{12,0},{16,4},{20,8},{24,12},{28,16},{1,21},{... | collective-permute-start | bytes 344072 | tf_op jit(solution)/shard_map/ppermute | solution.py:93
  91.1 15.8 %collective-permute-start.22 = (bf16[8,7168]{1,0:T(8,128)(2,1)S(1)}, bf16[8,7168]{1,0:T(8,128)(2,1)S(1)}, u32[]{:S(2)}, u32[]{:S(2)}) collective-permute-start(bf16[8,7168]{1,0:T(8,128)(2,1)S(1)} %get-tuple-element.18), channel_id=1, source_target_pairs={{0,16},{4,20},{8,24},{12,28},{16,0},{20,4},{24,8},{28,12},{1,17},{... | collective-permute-start | bytes 344072 | tf_op jit(solution)/shard_map/ppermute | solution.py:93
  94.0 15.1 %collective-permute-start.23 = (bf16[8,7168]{1,0:T(8,128)(2,1)S(1)}, bf16[8,7168]{1,0:T(8,128)(2,1)S(1)}, u32[]{:S(2)}, u32[]{:S(2)}) collective-permute-start(bf16[8,7168]{1,0:T(8,128)(2,1)S(1)} %get-tuple-element.17), channel_id=1, source_target_pairs={{0,12},{4,16},{8,20},{12,24},{16,28},{20,0},{24,4},{28,8},{1,13},{... | collective-permute-start | bytes 344072 | tf_op jit(solution)/shard_map/ppermute | solution.py:93
  94.0 15.1 %collective-permute-start.24 = (bf16[8,7168]{1,0:T(8,128)(2,1)S(1)}, bf16[8,7168]{1,0:T(8,128)(2,1)S(1)}, u32[]{:S(2)}, u32[]{:S(2)}) collective-permute-start(bf16[8,7168]{1,0:T(8,128)(2,1)S(1)} %get-tuple-element.16), channel_id=1, source_target_pairs={{0,8},{4,12},{8,16},{12,20},{16,24},{20,28},{24,0},{28,4},{1,9},{5... | collective-permute-start | bytes 344072 | tf_op jit(solution)/shard_map/ppermute | solution.py:93
  95.0 14.1 %collective-permute-start.25 = (bf16[8,7168]{1,0:T(8,128)(2,1)S(1)}, bf16[8,7168]{1,0:T(8,128)(2,1)S(1)}, u32[]{:S(2)}, u32[]{:S(2)}) collective-permute-start(bf16[8,7168]{1,0:T(8,128)(2,1)S(1)} %get-tuple-element.15), channel_id=1, source_target_pairs={{0,4},{4,8},{8,12},{12,16},{16,20},{20,24},{24,28},{28,0},{1,5},{5... | collective-permute-start | bytes 344072 | tf_op jit(solution)/shard_map/ppermute | solution.py:93
  (3 other events, 6.1 us)

commit v20 on v14

--- a/solution.py
+++ b/solution.py
@@ -74,18 +74,24 @@
         upward = jnp.dot(both, w_up[i], preferred_element_type=jnp.float32)
         hidden = (jax.nn.silu(gate_value) * upward).astype(jnp.bfloat16)
         offset = 0
-        for c in range(n_chunks):
+        sub = 2 if per_chunk % 2 == 0 else 1
+        width_k = per_chunk // sub
+        for piece in range(n_chunks * sub):
+            c, s = divmod(piece, sub)
             block = blocks[c]
             count = block.size // model_width
-            part = jnp.dot(hidden[offset : offset + count], w_down[i], preferred_element_type=jnp.float32)
-            offset += count
-            part = part.reshape(block.shape[:-1] + (model_width,))
+            lead = block.shape[:-1]
+            chunk_hidden = hidden[c * count : (c + 1) * count].reshape(lead + (-1,))
+            chunk_hidden = lax.slice_in_dim(chunk_hidden, s * width_k, (s + 1) * width_k, axis=len(bits))
+            sub_lead = chunk_hidden.shape[:-1]
+            part = jnp.dot(chunk_hidden.reshape(-1, chunk_hidden.shape[-1]), w_down[i], preferred_element_type=jnp.float32)
+            part = part.reshape(sub_lead + (model_width,))
             for bit in reversed(bits):
                 wire = jnp.bfloat16 if bit == bits[0] else None
                 part = bit_reduce(part, "exp", bit, n_exp, wire)
             expert_rows = part.astype(jnp.bfloat16)
-            for kk in range(per_chunk):
-                k = c * per_chunk + kk
+            for kk in range(width_k):
+                k = c * per_chunk + s * width_k + kk
                 if k == 0:
                     back = expert_rows[kk]
                 else:

time: 98.2 us -> 103 us (1.049)
  waiting for transfers between devices: 44.1 us -> 49.9 us
  starting transfers between devices: 34.4 us -> 30.9 us
  matrix products: 7.13 us -> 9.8 us
  other arithmetic: 5.73 us -> 7.26 us
  local copies, waits for them, and re-layouts: 4.81 us -> 3.39 us
    ppermute x2, waiting for transfers between devices: 0.01 us -> 12.3 us  [per_device(): got = lax.ppermute(sent, 'exp', [(i, i ^ bit) for i in range(n_exp)])]
    ppermute x7, starting transfers between devices: 13.6 us -> 6.07 us  [routed_experts(): lax.ppermute(expert_rows[kk], 'attn', [(s, (s - k) % n_attn) for s in ran...]
    ppermute x7, waiting for transfers between devices: 5.54 us -> 10.6 us  [routed_experts(): lax.ppermute(expert_rows[kk], 'attn', [(s, (s - k) % n_attn) for s in ran...]
    ppermute x4, waiting for transfers between devices: 15.8 us -> 11 us  [bit_gather(): other = lax.ppermute(x, axis, [(i, i ^ bit) for i in range(n)])]
    ppermute x7, waiting for transfers between devices: 4.31 us -> 0.48 us  [routed_experts(): lax.ppermute(tokens, 'attn', [(s, (s + k) % n_attn) for s in range(n_attn)])]
    ppermute x4 -> x8, starting transfers between devices: 1.84 us -> 5.59 us  [bit_reduce(): lax.ppermute(sent, axis, [(i, i ^ bit) for i in range(n)]).astype(x.dtype)]
    ppermute x4 -> x8, waiting for transfers between devices: 16.4 us -> 13.6 us  [bit_reduce(): lax.ppermute(sent, axis, [(i, i ^ bit) for i in range(n)]).astype(x.dtype)]
    dot_general x2 -> x4, matrix products: 1.32 us -> 3.01 us  [routed_experts(): jnp.dot(chunk_hidden.reshape(-1, chunk_hidden.shape[-1]), w_down[i], pref...]
  transfers between devices with their start and end apart: 26 -> 30, of which waited for: 12 -> 12; matrix products, arithmetic and copies ran while one was open for 14% -> 14% of each run, Pallas kernels for 0% -> 0%
where the time goes in v20:
time: 103 us; the launch traced here: 102 us
  waiting for transfers between devices  49.9 us (48%)
  starting transfers between devices  30.9 us (30%)
  matrix products  9.8 us (10%)
  other arithmetic  7.26 us (7%)
  local copies, waits for them, and re-layouts  3.39 us (3%)
  between operations  1.1 us (1%)
    ppermute x7, starting transfers between devices, routed_experts(): lax.ppermute(tokens, 'attn', [(s, (s + k) % n_attn) for s in range(n_attn)])  13.8 us
    ppermute x8, waiting for transfers between devices, bit_reduce(): lax.ppermute(sent, axis, [(i, i ^ bit) for i in range(n)]).astype(x.dtype)  13.6 us
    ppermute x2, waiting for transfers between devices, per_device(): got = lax.ppermute(sent, 'exp', [(i, i ^ bit) for i in range(n_exp)])  12.3 us
    ppermute x4, waiting for transfers between devices, bit_gather(): other = lax.ppermute(x, axis, [(i, i ^ bit) for i in range(n)])  11 us
    ppermute x7, waiting for transfers between devices, routed_experts(): lax.ppermute(expert_rows[kk], 'attn', [(s, (s - k) % n_attn) for s in ran...  10.6 us
    ppermute x7, starting transfers between devices, routed_experts(): lax.ppermute(expert_rows[kk], 'attn', [(s, (s - k) % n_attn) for s in ran...  6.07 us
    ppermute x8, starting transfers between devices, bit_reduce(): lax.ppermute(sent, axis, [(i, i ^ bit) for i in range(n)]).astype(x.dtype)  5.59 us
    ppermute x4, starting transfers between devices, bit_gather(): other = lax.ppermute(x, axis, [(i, i ^ bit) for i in range(n)])  3.19 us
  transfers between devices with their start and end apart: 30, of which 12 were waited for; matrix products, arithmetic and copies ran while one was open for 14% of the time, Pallas kernels for 0%

profile of v20, /device:TPU:0, one launch (start us, length us, event | category | flops | bytes accessed | tf_op | source)
XLA Modules:
  0.0 102.4 jit_solution(6433999575240634141)
XLA Ops:
  0.7 4.0 %collective-permute-start.6 = (bf16[8,7168]{1,0:T(8,128)(2,1)}, bf16[8,7168]{1,0:T(8,128)(2,1)S(1)}, u32[]{:S(2)}, u32[]{:S(2)}) collective-permute-start(bf16[8,7168]{1,0:T(8,128)(2,1)} %param.16), channel_id=1, source_target_pairs={{0,12},{4,16},{8,20},{12,24},{16,28},{20,0},{24,4},{28,8},{1,13},{... | collective-permute-start | bytes 344072 | tf_op jit(solution)/shard_map/ppermute | solution.py:60
  4.7 1.5 %collective-permute-start.4 = (bf16[8,7168]{1,0:T(8,128)(2,1)}, bf16[8,7168]{1,0:T(8,128)(2,1)}, u32[]{:S(2)}, u32[]{:S(2)}) collective-permute-start(bf16[8,7168]{1,0:T(8,128)(2,1)} %param.16), channel_id=1, source_target_pairs={{0,4},{4,8},{8,12},{12,16},{16,20},{20,24},{24,28},{28,0},{1,5},{5... | collective-permute-start | bytes 344072 | tf_op jit(solution)/shard_map/ppermute | solution.py:60
  6.2 1.6 %collective-permute-start.5 = (bf16[8,7168]{1,0:T(8,128)(2,1)}, bf16[8,7168]{1,0:T(8,128)(2,1)}, u32[]{:S(2)}, u32[]{:S(2)}) collective-permute-start(bf16[8,7168]{1,0:T(8,128)(2,1)} %param.16), channel_id=1, source_target_pairs={{0,8},{4,12},{8,16},{12,20},{16,24},{20,28},{24,0},{28,4},{1,9},{5... | collective-permute-start | bytes 344072 | tf_op jit(solution)/shard_map/ppermute | solution.py:60
  8.9 1.8 %fusion.67 = f32[2,128,1024]{2,1,0:T(8,128)S(1)} fusion(bf16[2,128,512]{2,1,0:T(8,128)(2,1)} %param.11, bf16[2,1024,512]{2,1,0:T(8,128)(2,1)S(1)} %copy-done), kind=kOutput, calls=%fused_computation.125 | convolution fusion | flops 268435456 | bytes 3407872 | tf_op jit(solution)/shard_map/rhl,rpl->rhp/dot_general | solution.py:120
  10.6 1.4 %fusion.66 = (f32[2,128]{1,0:T(2,128)S(1)}, f32[2,128,1024]{2,1,0:T(8,128)S(1)}) fusion(f32[2,128,1024]{2,1,0:T(8,128)S(1)} %fusion.67, bf16[2,64,128]{2,1,0:T(8,128)(2,1)} %param.12, bf16[2,64,1024]{2,1,0:T(8,128)(2,1)} %param.14, pred[2,1024]{1,0:T(4,128)(4,1)S(1)} %broadcast_compare_fusion), kind=kOutput, calls=%fused_computation.124 | convolution fusion | flops 34602752 | bytes 2395136 | tf_op jit(solution)/shard_map/rdh,rdp->rhp/dot_general | solution.py:121
  13.4 1.6 %collective-permute-start.1 = (f32[2,128]{1,0:T(2,128)S(1)}, f32[2,128]{1,0:T(2,128)S(1)}, u32[]{:S(2)}, u32[]{:S(2)}) collective-permute-start(f32[2,128]{1,0:T(2,128)S(1)} %max.6), channel_id=1, source_target_pairs={{0,2},{1,3},{2,0},{3,1},{4,6},{5,7},{6,4},{7,5},{8,10},{9,11},{10,... | collective-permute-start | bytes 3080 | tf_op jit(solution)/shard_map/ppermute | solution.py:142
  14.9 2.1 %collective-permute-done.1 = f32[2,128]{1,0:T(2,128)S(1)} collective-permute-done((f32[2,128]{1,0:T(2,128)S(1)}, f32[2,128]{1,0:T(2,128)S(1)}, u32[]{:S(2)}, u32[]{:S(2)}) %collective-permute-start.1) | collective-permute-done | bytes 1056 | tf_op jit(solution)/shard_map/ppermute | solution.py:142
  17.0 3.5 %collective-permute-start.10 = (bf16[8,7168]{1,0:T(8,128)(2,1)S(1)}, bf16[8,7168]{1,0:T(8,128)(2,1)}, u32[]{:S(2)}, u32[]{:S(2)}) collective-permute-start(bf16[8,7168]{1,0:T(8,128)(2,1)S(1)} %copy-done.2), channel_id=1, source_target_pairs={{0,20},{4,24},{8,28},{12,0},{16,4},{20,8},{24,12},{28,16},{1,21},{... | collective-permute-start | bytes 344072 | tf_op jit(solution)/shard_map/ppermute | solution.py:60
  20.6 1.3 %broadcast_multiply_fusion = f32[2,128,512]{2,1,0:T(8,128)} fusion(f32[2,128]{1,0:T(2,128)S(1)} %get-tuple-element.3, bf16[2,1024,512]{2,1,0:T(8,128)(2,1)S(1)} %copy-done, f32[2,128,1024]{2,1,0:T(8,128)S(1)} %get-tuple-element.43, f32[2,128]{1,0:T(2,128)S(1)} %get-tuple-element.42, pred[2,1024]{1,0:T(4,128)(4,1)S(1)} %broadcast_compare_fusion), kind=kOutput, calls=%fused_computation.55 | convolution fusion | flops 269352960 | bytes 3674112 | tf_op jit(solution)/shard_map/rhp,rpl->rhl/dot_general | solution.py:131
  22.1 1.1 %fusion.30 = (f32[2,2,1,32,513]{4,3,2,1,0:T(8,128)S(1)}, f32[2,2,1,32,513]{4,3,2,1,0:T(8,128)S(1)}) fusion(s32[]{:T(128)S(6)} %select_n.81, f32[2,2,2,32,512]{4,3,2,1,0:T(8,128)} %bitcast.145, f32[2,2,2,32,1]{4,3,2,1,0:T(8,128)S(1)} %concatenate.15, s32[]{:T(128)S(6)} %select_n.82), kind=kLoop, calls=%fused_computation.51 | loop fusion | flops 131328 | bytes 1050632 | tf_op jit(solution)/shard_map/concatenate | solution.py:146
  23.2 2.3 %collective-permute-start.11 = (bf16[8,7168]{1,0:T(8,128)(2,1)S(1)}, bf16[8,7168]{1,0:T(8,128)(2,1)S(1)}, u32[]{:S(2)}, u32[]{:S(2)}) collective-permute-start(bf16[8,7168]{1,0:T(8,128)(2,1)S(1)} %copy-done.2), channel_id=1, source_target_pairs={{0,24},{4,28},{8,0},{12,4},{16,8},{20,12},{24,16},{28,20},{1,25},{... | collective-permute-start | bytes 344072 | tf_op jit(solution)/shard_map/ppermute | solution.py:60
  26.1 1.0 %fusion.57 = (bf16[1,4,8,7168]{3,2,1,0:T(8,128)(2,1)S(1)}, bf16[4,8,7168]{2,1,0:T(8,128)(2,1)S(1)}) fusion(bf16[1,8,7168]{2,1,0:T(8,128)(2,1)S(1)} %bitcast.167, bf16[1,8,7168]{2,1,0:T(8,128)(2,1)} %bitcast.9, bf16[1,8,7168]{2,1,0:T(8,128)(2,1)} %bitcast.8, bf16[1,8,7168]{2,1,0:T(8,128)(2,1)S(1)} %bitcast.165), kind=kLoop, calls=%fused_computation.115 | loop fusion | flops 688128 | bytes 1376256 | tf_op jit(solution)/shard_map/stack | solution.py:35
  27.7 1.5 %collective-permute-start.7 = (bf16[4,8,7168]{2,1,0:T(8,128)(2,1)S(1)}, bf16[4,8,7168]{2,1,0:T(8,128)(2,1)S(1)}, u32[]{:S(2)}, u32[]{:S(2)}) collective-permute-start(bf16[4,8,7168]{2,1,0:T(8,128)(2,1)S(1)} %get-tuple-element.19), channel_id=1, source_target_pairs={{0,2},{1,3},{2,0},{3,1},{4,6},{5,7},{6,4},{7,5},{8,10},{9,11},{10,... | collective-permute-start | bytes 1376264 | tf_op jit(solution)/shard_map/ppermute | solution.py:34
  30.3 1.0 fusion.56
  31.3 1.6 %collective-permute-start.13 = (bf16[4,8,7168]{2,1,0:T(8,128)(2,1)S(1)}, bf16[4,8,7168]{2,1,0:T(8,128)(2,1)S(1)}, u32[]{:S(2)}, u32[]{:S(2)}) collective-permute-start(bf16[4,8,7168]{2,1,0:T(8,128)(2,1)S(1)} %get-tuple-element.21), channel_id=1, source_target_pairs={{0,2},{1,3},{2,0},{3,1},{4,6},{5,7},{6,4},{7,5},{8,10},{9,11},{10,... | collective-permute-start | bytes 1376264 | tf_op jit(solution)/shard_map/ppermute | solution.py:34
  32.9 11.7 %collective-permute-done.3 = f32[2,1,32,513]{3,2,0,1:T(8,128)S(1)} collective-permute-done((f32[2,1,32,513]{3,2,0,1:T(8,128)S(1)}, f32[2,1,32,513]{3,2,0,1:T(8,128)S(1)}, u32[]{:S(2)}, u32[]{:S(2)}) %collective-permute-start.3) | collective-permute-done | bytes 131360 | tf_op jit(solution)/shard_map/ppermute | solution.py:155
  44.8 8.8 %collective-permute-done.13 = bf16[4,8,7168]{2,1,0:T(8,128)(2,1)S(1)} collective-permute-done((bf16[4,8,7168]{2,1,0:T(8,128)(2,1)S(1)}, bf16[4,8,7168]{2,1,0:T(8,128)(2,1)S(1)}, u32[]{:S(2)}, u32[]{:S(2)}) %collective-permute-start.13) | collective-permute-done | bytes 458784 | tf_op jit(solution)/shard_map/ppermute | solution.py:34
  54.1 2.2 %collective-permute-done.14 = bf16[2,4,8,7168]{3,2,1,0:T(8,128)(2,1)S(1)} collective-permute-done((bf16[2,4,8,7168]{3,2,1,0:T(8,128)(2,1)S(1)}, bf16[2,4,8,7168]{3,2,1,0:T(8,128)(2,1)S(1)}, u32[]{:S(2)}, u32[]{:S(2)}) %collective-permute-start.14) | collective-permute-done | bytes 917536 | tf_op jit(solution)/shard_map/ppermute | solution.py:34
  56.5 1.1 %fusion.10 = f32[256,256]{1,0:T(8,128)S(1)} fusion(bf16[1,7168,256]{2,1,0:T(8,128)(2,1)S(1)} %copy-done.5, bf16[128,7168]{1,0:T(8,128)(2,1)S(1)} %bitcast.148, bf16[128,7168]{1,0:T(8,128)(2,1)S(1)} %bitcast.146), kind=kOutput, calls=%fused_computation.12 | convolution fusion | flops 946864128 | bytes 7602176 | tf_op jit(solution)/shard_map/dot_general | solution.py:73
  58.5 1.2 %multiply_convert_fusion = bf16[256,256]{1,0:T(8,128)(2,1)S(1)} fusion(f32[256,256]{1,0:T(8,128)S(1)} %fusion.10, bf16[1,7168,256]{2,1,0:T(8,128)(2,1)S(1)} %copy-done.6, bf16[128,7168]{1,0:T(8,128)(2,1)S(1)} %bitcast.149, bf16[128,7168]{1,0:T(8,128)(2,1)S(1)} %bitcast.147), kind=kOutput, calls=%fused_computation.54 | convolution fusion | flops 947257344 | bytes 7733248 | tf_op jit(solution)/shard_map/dot_general | solution.py:74
  65.5 1.6 %collective-permute-start.16 = (bf16[2,8,7168]{2,1,0:T(8,128)(2,1)S(1)}, bf16[2,8,7168]{2,1,0:T(8,128)(2,1)S(1)}, u32[]{:S(2)}, u32[]{:S(2)}) collective-permute-start(bf16[2,8,7168]{2,1,0:T(8,128)(2,1)S(1)} %fusion.31), channel_id=1, source_target_pairs={{0,2},{1,3},{2,0},{3,1},{4,6},{5,7},{6,4},{7,5},{8,10},{9,11},{10,... | collective-permute-start | bytes 688136 | tf_op jit(solution)/shard_map/ppermute | solution.py:40
  68.0 1.6 %collective-permute-start.23 = (bf16[2,8,7168]{2,1,0:T(8,128)(2,1)S(1)}, bf16[2,8,7168]{2,1,0:T(8,128)(2,1)S(1)}, u32[]{:S(2)}, u32[]{:S(2)}) collective-permute-start(bf16[2,8,7168]{2,1,0:T(8,128)(2,1)S(1)} %fusion.33), channel_id=1, source_target_pairs={{0,2},{1,3},{2,0},{3,1},{4,6},{5,7},{6,4},{7,5},{8,10},{9,11},{10,... | collective-permute-start | bytes 688136 | tf_op jit(solution)/shard_map/ppermute | solution.py:40
  70.3 3.8 %collective-permute-done.16 = bf16[2,8,7168]{2,1,0:T(8,128)(2,1)S(1)} collective-permute-done((bf16[2,8,7168]{2,1,0:T(8,128)(2,1)S(1)}, bf16[2,8,7168]{2,1,0:T(8,128)(2,1)S(1)}, u32[]{:S(2)}, u32[]{:S(2)}) %collective-permute-start.16) | collective-permute-done | bytes 229408 | tf_op jit(solution)/shard_map/ppermute | solution.py:40
  74.1 1.4 %collective-permute-start.17 = (bf16[8,7168]{1,0:T(8,128)(2,1)S(1)}, bf16[8,7168]{1,0:T(8,128)(2,1)S(1)}, u32[]{:S(2)}, u32[]{:S(2)}) collective-permute-start(bf16[8,7168]{1,0:T(8,128)(2,1)S(1)} %slice_bitcast_fusion.10), channel_id=1, source_target_pairs={{0,28},{4,0},{8,4},{12,8},{16,12},{20,16},{24,20},{28,24},{1,29},{... | collective-permute-start | bytes 344072 | tf_op jit(solution)/shard_map/ppermute | solution.py:98
  75.5 3.4 %collective-permute-done.19 = bf16[2,8,7168]{2,1,0:T(8,128)(2,1)S(1)} collective-permute-done((bf16[2,8,7168]{2,1,0:T(8,128)(2,1)S(1)}, bf16[2,8,7168]{2,1,0:T(8,128)(2,1)S(1)}, u32[]{:S(2)}, u32[]{:S(2)}) %collective-permute-start.19) | collective-permute-done | bytes 229408 | tf_op jit(solution)/shard_map/ppermute | solution.py:40
  79.1 2.1 %collective-permute-start.21 = (bf16[8,7168]{1,0:T(8,128)(2,1)S(1)}, bf16[8,7168]{1,0:T(8,128)(2,1)S(1)}, u32[]{:S(2)}, u32[]{:S(2)}) collective-permute-start(bf16[8,7168]{1,0:T(8,128)(2,1)S(1)} %get-tuple-element.23), channel_id=1, source_target_pairs={{0,20},{4,24},{8,28},{12,0},{16,4},{20,8},{24,12},{28,16},{1,21},{... | collective-permute-start | bytes 344072 | tf_op jit(solution)/shard_map/ppermute | solution.py:98
  81.3 2.6 %collective-permute-done.23 = bf16[2,8,7168]{2,1,0:T(8,128)(2,1)S(1)} collective-permute-done((bf16[2,8,7168]{2,1,0:T(8,128)(2,1)S(1)}, bf16[2,8,7168]{2,1,0:T(8,128)(2,1)S(1)}, u32[]{:S(2)}, u32[]{:S(2)}) %collective-permute-start.23) | collective-permute-done | bytes 229408 | tf_op jit(solution)/shard_map/ppermute | solution.py:40
  84.2 3.8 %collective-permute-done.27 = bf16[2,8,7168]{2,1,0:T(8,128)(2,1)S(1)} collective-permute-done((bf16[2,8,7168]{2,1,0:T(8,128)(2,1)S(1)}, bf16[2,8,7168]{2,1,0:T(8,128)(2,1)S(1)}, u32[]{:S(2)}, u32[]{:S(2)}) %collective-permute-start.27) | collective-permute-done | bytes 229408 | tf_op jit(solution)/shard_map/ppermute | solution.py:40
  89.1 1.1 %collective-permute-start.29 = (bf16[8,7168]{1,0:T(8,128)(2,1)S(1)}, bf16[8,7168]{1,0:T(8,128)(2,1)S(1)}, u32[]{:S(2)}, u32[]{:S(2)}) collective-permute-start(bf16[8,7168]{1,0:T(8,128)(2,1)S(1)} %get-tuple-element.27), channel_id=1, source_target_pairs={{0,4},{4,8},{8,12},{12,16},{16,20},{20,24},{24,28},{28,0},{1,5},{5... | collective-permute-start | bytes 344072 | tf_op jit(solution)/shard_map/ppermute | solution.py:98
  90.9 7.2 %collective-permute-done.24 = bf16[8,7168]{1,0:T(8,128)(2,1)S(1)} collective-permute-done((bf16[8,7168]{1,0:T(8,128)(2,1)S(1)}, bf16[8,7168]{1,0:T(8,128)(2,1)S(1)}, u32[]{:S(2)}, u32[]{:S(2)}) %collective-permute-start.24) | collective-permute-done | bytes 114720 | tf_op jit(solution)/shard_map/ppermute | solution.py:98
  98.2 3.3 %collective-permute-done.25 = bf16[8,7168]{1,0:T(8,128)(2,1)S(1)} collective-permute-done((bf16[8,7168]{1,0:T(8,128)(2,1)S(1)}, bf16[8,7168]{1,0:T(8,128)(2,1)S(1)}, u32[]{:S(2)}, u32[]{:S(2)}) %collective-permute-start.25) | collective-permute-done | bytes 114720 | tf_op jit(solution)/shard_map/ppermute | solution.py:98
  101.5 0.9 fusion.42
  (102 shorter events, 16.2 us)
Async XLA Ops:
  0.6 16.4 %copy-start.2 = (bf16[8,7168]{1,0:T(8,128)(2,1)S(1)}, bf16[8,7168]{1,0:T(8,128)(2,1)}, u32[]{:S(2)}) copy-start(bf16[8,7168]{1,0:T(8,128)(2,1)} %param.16) | copy-start | bytes 344068
  0.7 11.5 %copy-start.4 = (s32[8,4]{0,1:T(4,128)S(1)}, s32[8,4]{0,1:T(4,128)}, u32[]{:S(2)}) copy-start(s32[8,4]{0,1:T(4,128)} %param.17) | copy-start | bytes 388
  0.7 22.6 %collective-permute-start.6 = (bf16[8,7168]{1,0:T(8,128)(2,1)}, bf16[8,7168]{1,0:T(8,128)(2,1)S(1)}, u32[]{:S(2)}, u32[]{:S(2)}) collective-permute-start(bf16[8,7168]{1,0:T(8,128)(2,1)} %param.16), channel_id=1, source_target_pairs={{0,12},{4,16},{8,20},{12,24},{16,28},{20,0},{24,4},{28,8},{1,13},{... | collective-permute-start | bytes 344072 | tf_op jit(solution)/shard_map/ppermute | solution.py:60
  4.7 20.8 %collective-permute-start.4 = (bf16[8,7168]{1,0:T(8,128)(2,1)}, bf16[8,7168]{1,0:T(8,128)(2,1)}, u32[]{:S(2)}, u32[]{:S(2)}) collective-permute-start(bf16[8,7168]{1,0:T(8,128)(2,1)} %param.16), channel_id=1, source_target_pairs={{0,4},{4,8},{8,12},{12,16},{16,20},{20,24},{24,28},{28,0},{1,5},{5... | collective-permute-start | bytes 344072 | tf_op jit(solution)/shard_map/ppermute | solution.py:60
  6.2 19.8 %collective-permute-start.5 = (bf16[8,7168]{1,0:T(8,128)(2,1)}, bf16[8,7168]{1,0:T(8,128)(2,1)}, u32[]{:S(2)}, u32[]{:S(2)}) collective-permute-start(bf16[8,7168]{1,0:T(8,128)(2,1)} %param.16), channel_id=1, source_target_pairs={{0,8},{4,12},{8,16},{12,20},{16,24},{20,28},{24,0},{28,4},{1,9},{5... | collective-permute-start | bytes 344072 | tf_op jit(solution)/shard_map/ppermute | solution.py:60
  7.8 21.5 %collective-permute-start.9 = (bf16[8,7168]{1,0:T(8,128)(2,1)}, bf16[8,7168]{1,0:T(8,128)(2,1)S(1)}, u32[]{:S(2)}, u32[]{:S(2)}) collective-permute-start(bf16[8,7168]{1,0:T(8,128)(2,1)} %param.16), channel_id=1, source_target_pairs={{0,16},{4,20},{8,24},{12,28},{16,0},{20,4},{24,8},{28,12},{1,17},{... | collective-permute-start | bytes 344072 | tf_op jit(solution)/shard_map/ppermute | solution.py:60
  12.1 1.3 %collective-permute-start = (f32[2,128]{1,0:T(2,128)S(1)}, f32[2,128]{1,0:T(2,128)S(1)}, u32[]{:S(2)}, u32[]{:S(2)}) collective-permute-start(f32[2,128]{1,0:T(2,128)S(1)} %get-tuple-element.42), channel_id=1, source_target_pairs={{0,1},{1,0},{2,3},{3,2},{4,5},{5,4},{6,7},{7,6},{8,9},{9,8},{10,11... | collective-permute-start | bytes 3080 | tf_op jit(solution)/shard_map/ppermute | solution.py:142
  13.4 3.6 %collective-permute-start.1 = (f32[2,128]{1,0:T(2,128)S(1)}, f32[2,128]{1,0:T(2,128)S(1)}, u32[]{:S(2)}, u32[]{:S(2)}) collective-permute-start(f32[2,128]{1,0:T(2,128)S(1)} %max.6), channel_id=1, source_target_pairs={{0,2},{1,3},{2,0},{3,1},{4,6},{5,7},{6,4},{7,5},{8,10},{9,11},{10,... | collective-permute-start | bytes 3080 | tf_op jit(solution)/shard_map/ppermute | solution.py:142
  17.0 12.9 %collective-permute-start.10 = (bf16[8,7168]{1,0:T(8,128)(2,1)S(1)}, bf16[8,7168]{1,0:T(8,128)(2,1)}, u32[]{:S(2)}, u32[]{:S(2)}) collective-permute-start(bf16[8,7168]{1,0:T(8,128)(2,1)S(1)} %copy-done.2), channel_id=1, source_target_pairs={{0,20},{4,24},{8,28},{12,0},{16,4},{20,8},{24,12},{28,16},{1,21},{... | collective-permute-start | bytes 344072 | tf_op jit(solution)/shard_map/ppermute | solution.py:60
  23.2 6.6 %collective-permute-start.11 = (bf16[8,7168]{1,0:T(8,128)(2,1)S(1)}, bf16[8,7168]{1,0:T(8,128)(2,1)S(1)}, u32[]{:S(2)}, u32[]{:S(2)}) collective-permute-start(bf16[8,7168]{1,0:T(8,128)(2,1)S(1)} %copy-done.2), channel_id=1, source_target_pairs={{0,24},{4,28},{8,0},{12,4},{16,8},{20,12},{24,16},{28,20},{1,25},{... | collective-permute-start | bytes 344072 | tf_op jit(solution)/shard_map/ppermute | solution.py:60
  25.5 4.8 %collective-permute-start.12 = (bf16[8,7168]{1,0:T(8,128)(2,1)S(1)}, bf16[8,7168]{1,0:T(8,128)(2,1)S(1)}, u32[]{:S(2)}, u32[]{:S(2)}) collective-permute-start(bf16[8,7168]{1,0:T(8,128)(2,1)S(1)} %copy-done.2), channel_id=1, source_target_pairs={{0,28},{4,0},{8,4},{12,8},{16,12},{20,16},{24,20},{28,24},{1,29},{... | collective-permute-start | bytes 344072 | tf_op jit(solution)/shard_map/ppermute | solution.py:60
  26.1 1.6 %collective-permute-start.2 = (f32[2,2,32,513]{3,2,0,1:T(8,128)S(1)}, f32[2,2,32,513]{3,2,0,1:T(8,128)S(1)}, u32[]{:S(2)}, u32[]{:S(2)}) collective-permute-start(f32[2,2,32,513]{3,2,0,1:T(8,128)S(1)} %bitcast.158), channel_id=1, source_target_pairs={{0,1},{1,0},{2,3},{3,2},{4,5},{5,4},{6,7},{7,6},{8,9},{9,8},{10,11... | collective-permute-start | bytes 787976 | tf_op jit(solution)/shard_map/ppermute | solution.py:155
  27.7 16.9 %collective-permute-start.7 = (bf16[4,8,7168]{2,1,0:T(8,128)(2,1)S(1)}, bf16[4,8,7168]{2,1,0:T(8,128)(2,1)S(1)}, u32[]{:S(2)}, u32[]{:S(2)}) collective-permute-start(bf16[4,8,7168]{2,1,0:T(8,128)(2,1)S(1)} %get-tuple-element.19), channel_id=1, source_target_pairs={{0,2},{1,3},{2,0},{3,1},{4,6},{5,7},{6,4},{7,5},{8,10},{9,11},{10,... | collective-permute-start | bytes 1376264 | tf_op jit(solution)/shard_map/ppermute | solution.py:34
  29.3 15.3 %collective-permute-start.3 = (f32[2,1,32,513]{3,2,0,1:T(8,128)S(1)}, f32[2,1,32,513]{3,2,0,1:T(8,128)S(1)}, u32[]{:S(2)}, u32[]{:S(2)}) collective-permute-start(f32[2,1,32,513]{3,2,0,1:T(8,128)S(1)} %constant_dynamic-slice_fusion), channel_id=1, source_target_pairs={{0,2},{1,3},{2,0},{3,1},{4,6},{5,7},{6,4},{7,5},{8,10},{9,11},{10,... | collective-permute-start | bytes 393992 | tf_op jit(solution)/shard_map/ppermute | solution.py:155
  31.3 22.3 %collective-permute-start.13 = (bf16[4,8,7168]{2,1,0:T(8,128)(2,1)S(1)}, bf16[4,8,7168]{2,1,0:T(8,128)(2,1)S(1)}, u32[]{:S(2)}, u32[]{:S(2)}) collective-permute-start(bf16[4,8,7168]{2,1,0:T(8,128)(2,1)S(1)} %get-tuple-element.21), channel_id=1, source_target_pairs={{0,2},{1,3},{2,0},{3,1},{4,6},{5,7},{6,4},{7,5},{8,10},{9,11},{10,... | collective-permute-start | bytes 1376264 | tf_op jit(solution)/shard_map/ppermute | solution.py:34
  44.7 9.2 %collective-permute-start.8 = (bf16[2,4,8,7168]{3,2,1,0:T(8,128)(2,1)S(1)}, bf16[2,4,8,7168]{3,2,1,0:T(8,128)(2,1)S(1)}, u32[]{:S(2)}, u32[]{:S(2)}) collective-permute-start(bf16[2,4,8,7168]{3,2,1,0:T(8,128)(2,1)S(1)} %get-tuple-element.13), channel_id=1, source_target_pairs={{0,1},{1,0},{2,3},{3,2},{4,5},{5,4},{6,7},{7,6},{8,9},{9,8},{10,11... | collective-permute-start | bytes 2752520 | tf_op jit(solution)/shard_map/ppermute | solution.py:34
  53.7 2.5 %collective-permute-start.14 = (bf16[2,4,8,7168]{3,2,1,0:T(8,128)(2,1)S(1)}, bf16[2,4,8,7168]{3,2,1,0:T(8,128)(2,1)S(1)}, u32[]{:S(2)}, u32[]{:S(2)}) collective-permute-start(bf16[2,4,8,7168]{3,2,1,0:T(8,128)(2,1)S(1)} %get-tuple-element.15), channel_id=1, source_target_pairs={{0,1},{1,0},{2,3},{3,2},{4,5},{5,4},{6,7},{7,6},{8,9},{9,8},{10,11... | collective-permute-start | bytes 2752520 | tf_op jit(solution)/shard_map/ppermute | solution.py:34
  61.4 3.9 %collective-permute-start.15 = (f32[2,2,8,7168]{3,2,1,0:T(8,128)S(1)}, f32[2,2,8,7168]{3,2,1,0:T(8,128)S(1)}, u32[]{:S(2)}, u32[]{:S(2)}) collective-permute-start(f32[2,2,8,7168]{3,2,1,0:T(8,128)S(1)} %bitcast.152), channel_id=1, source_target_pairs={{0,1},{1,0},{2,3},{3,2},{4,5},{5,4},{6,7},{7,6},{8,9},{9,8},{10,11... | collective-permute-start | bytes 2752520 | tf_op jit(solution)/shard_map/ppermute | solution.py:40
  62.5 4.6 %collective-permute-start.18 = (f32[2,2,8,7168]{3,2,1,0:T(8,128)S(1)}, f32[2,2,8,7168]{3,2,1,0:T(8,128)S(1)}, u32[]{:S(2)}, u32[]{:S(2)}) collective-permute-start(f32[2,2,8,7168]{3,2,1,0:T(8,128)S(1)} %bitcast.150), channel_id=1, source_target_pairs={{0,1},{1,0},{2,3},{3,2},{4,5},{5,4},{6,7},{7,6},{8,9},{9,8},{10,11... | collective-permute-start | bytes 2752520 | tf_op jit(solution)/shard_map/ppermute | solution.py:40
  63.8 4.0 %collective-permute-start.22 = (f32[2,2,8,7168]{3,2,1,0:T(8,128)S(1)}, f32[2,2,8,7168]{3,2,1,0:T(8,128)S(1)}, u32[]{:S(2)}, u32[]{:S(2)}) collective-permute-start(f32[2,2,8,7168]{3,2,1,0:T(8,128)S(1)} %bitcast.153), channel_id=1, source_target_pairs={{0,1},{1,0},{2,3},{3,2},{4,5},{5,4},{6,7},{7,6},{8,9},{9,8},{10,11... | collective-permute-start | bytes 2752520 | tf_op jit(solution)/shard_map/ppermute | solution.py:40
  64.9 4.6 %collective-permute-start.26 = (f32[2,2,8,7168]{3,2,1,0:T(8,128)S(1)}, f32[2,2,8,7168]{3,2,1,0:T(8,128)S(1)}, u32[]{:S(2)}, u32[]{:S(2)}) collective-permute-start(f32[2,2,8,7168]{3,2,1,0:T(8,128)S(1)} %bitcast.151), channel_id=1, source_target_pairs={{0,1},{1,0},{2,3},{3,2},{4,5},{5,4},{6,7},{7,6},{8,9},{9,8},{10,11... | collective-permute-start | bytes 2752520 | tf_op jit(solution)/shard_map/ppermute | solution.py:40
  65.5 8.5 %collective-permute-start.16 = (bf16[2,8,7168]{2,1,0:T(8,128)(2,1)S(1)}, bf16[2,8,7168]{2,1,0:T(8,128)(2,1)S(1)}, u32[]{:S(2)}, u32[]{:S(2)}) collective-permute-start(bf16[2,8,7168]{2,1,0:T(8,128)(2,1)S(1)} %fusion.31), channel_id=1, source_target_pairs={{0,2},{1,3},{2,0},{3,1},{4,6},{5,7},{6,4},{7,5},{8,10},{9,11},{10,... | collective-permute-start | bytes 688136 | tf_op jit(solution)/shard_map/ppermute | solution.py:40
  67.2 11.7 %collective-permute-start.19 = (bf16[2,8,7168]{2,1,0:T(8,128)(2,1)S(1)}, bf16[2,8,7168]{2,1,0:T(8,128)(2,1)S(1)}, u32[]{:S(2)}, u32[]{:S(2)}) collective-permute-start(bf16[2,8,7168]{2,1,0:T(8,128)(2,1)S(1)} %fusion.32), channel_id=1, source_target_pairs={{0,2},{1,3},{2,0},{3,1},{4,6},{5,7},{6,4},{7,5},{8,10},{9,11},{10,... | collective-permute-start | bytes 688136 | tf_op jit(solution)/shard_map/ppermute | solution.py:40
  68.0 15.9 %collective-permute-start.23 = (bf16[2,8,7168]{2,1,0:T(8,128)(2,1)S(1)}, bf16[2,8,7168]{2,1,0:T(8,128)(2,1)S(1)}, u32[]{:S(2)}, u32[]{:S(2)}) collective-permute-start(bf16[2,8,7168]{2,1,0:T(8,128)(2,1)S(1)} %fusion.33), channel_id=1, source_target_pairs={{0,2},{1,3},{2,0},{3,1},{4,6},{5,7},{6,4},{7,5},{8,10},{9,11},{10,... | collective-permute-start | bytes 688136 | tf_op jit(solution)/shard_map/ppermute | solution.py:40
  69.7 18.3 %collective-permute-start.27 = (bf16[2,8,7168]{2,1,0:T(8,128)(2,1)S(1)}, bf16[2,8,7168]{2,1,0:T(8,128)(2,1)S(1)}, u32[]{:S(2)}, u32[]{:S(2)}) collective-permute-start(bf16[2,8,7168]{2,1,0:T(8,128)(2,1)S(1)} %fusion.34), channel_id=1, source_target_pairs={{0,2},{1,3},{2,0},{3,1},{4,6},{5,7},{6,4},{7,5},{8,10},{9,11},{10,... | collective-permute-start | bytes 688136 | tf_op jit(solution)/shard_map/ppermute | solution.py:40
  74.1 14.7 %collective-permute-start.17 = (bf16[8,7168]{1,0:T(8,128)(2,1)S(1)}, bf16[8,7168]{1,0:T(8,128)(2,1)S(1)}, u32[]{:S(2)}, u32[]{:S(2)}) collective-permute-start(bf16[8,7168]{1,0:T(8,128)(2,1)S(1)} %slice_bitcast_fusion.10), channel_id=1, source_target_pairs={{0,28},{4,0},{8,4},{12,8},{16,12},{20,16},{24,20},{28,24},{1,29},{... | collective-permute-start | bytes 344072 | tf_op jit(solution)/shard_map/ppermute | solution.py:98
  79.0 10.1 %collective-permute-start.20 = (bf16[8,7168]{1,0:T(8,128)(2,1)S(1)}, bf16[8,7168]{1,0:T(8,128)(2,1)S(1)}, u32[]{:S(2)}, u32[]{:S(2)}) collective-permute-start(bf16[8,7168]{1,0:T(8,128)(2,1)S(1)} %get-tuple-element.22), channel_id=1, source_target_pairs={{0,24},{4,28},{8,0},{12,4},{16,8},{20,12},{24,16},{28,20},{1,25},{... | collective-permute-start | bytes 344072 | tf_op jit(solution)/shard_map/ppermute | solution.py:98
  79.1 11.8 %collective-permute-start.21 = (bf16[8,7168]{1,0:T(8,128)(2,1)S(1)}, bf16[8,7168]{1,0:T(8,128)(2,1)S(1)}, u32[]{:S(2)}, u32[]{:S(2)}) collective-permute-start(bf16[8,7168]{1,0:T(8,128)(2,1)S(1)} %get-tuple-element.23), channel_id=1, source_target_pairs={{0,20},{4,24},{8,28},{12,0},{16,4},{20,8},{24,12},{28,16},{1,21},{... | collective-permute-start | bytes 344072 | tf_op jit(solution)/shard_map/ppermute | solution.py:98
  83.9 14.2 %collective-permute-start.24 = (bf16[8,7168]{1,0:T(8,128)(2,1)S(1)}, bf16[8,7168]{1,0:T(8,128)(2,1)S(1)}, u32[]{:S(2)}, u32[]{:S(2)}) collective-permute-start(bf16[8,7168]{1,0:T(8,128)(2,1)S(1)} %get-tuple-element.24), channel_id=1, source_target_pairs={{0,16},{4,20},{8,24},{12,28},{16,0},{20,4},{24,8},{28,12},{1,17},{... | collective-permute-start | bytes 344072 | tf_op jit(solution)/shard_map/ppermute | solution.py:98
  88.0 13.5 %collective-permute-start.25 = (bf16[8,7168]{1,0:T(8,128)(2,1)S(1)}, bf16[8,7168]{1,0:T(8,128)(2,1)S(1)}, u32[]{:S(2)}, u32[]{:S(2)}) collective-permute-start(bf16[8,7168]{1,0:T(8,128)(2,1)S(1)} %get-tuple-element.25), channel_id=1, source_target_pairs={{0,12},{4,16},{8,20},{12,24},{16,28},{20,0},{24,4},{28,8},{1,13},{... | collective-permute-start | bytes 344072 | tf_op jit(solution)/shard_map/ppermute | solution.py:98
  88.8 12.7 %collective-permute-start.28 = (bf16[8,7168]{1,0:T(8,128)(2,1)S(1)}, bf16[8,7168]{1,0:T(8,128)(2,1)S(1)}, u32[]{:S(2)}, u32[]{:S(2)}) collective-permute-start(bf16[8,7168]{1,0:T(8,128)(2,1)S(1)} %get-tuple-element.26), channel_id=1, source_target_pairs={{0,8},{4,12},{8,16},{12,20},{16,24},{20,28},{24,0},{28,4},{1,9},{5... | collective-permute-start | bytes 344072 | tf_op jit(solution)/shard_map/ppermute | solution.py:98
  89.1 12.4 %collective-permute-start.29 = (bf16[8,7168]{1,0:T(8,128)(2,1)S(1)}, bf16[8,7168]{1,0:T(8,128)(2,1)S(1)}, u32[]{:S(2)}, u32[]{:S(2)}) collective-permute-start(bf16[8,7168]{1,0:T(8,128)(2,1)S(1)} %get-tuple-element.27), channel_id=1, source_target_pairs={{0,4},{4,8},{8,12},{12,16},{16,20},{20,24},{24,28},{28,0},{1,5},{5... | collective-permute-start | bytes 344072 | tf_op jit(solution)/shard_map/ppermute | solution.py:98
  (5 other events, 26.4 us)

commit v21 on v14

--- a/solution.py
+++ b/solution.py
@@ -55,12 +55,13 @@
     wmat = jnp.sum(jnp.where(hit, route_gates[:, :, None], 0.0), axis=1)
     n_chunks = 2 if n_attn % 2 == 0 else 1
     per_chunk = n_attn // n_chunks
+    order = sorted(range(n_attn), key=lambda k: (min(k, n_attn - k), -k))
     pieces = [tokens]
     for k in range(1, n_attn):
         pieces.append(lax.ppermute(tokens, "attn", [(s, (s + k) % n_attn) for s in range(n_attn)]))
     blocks = []
     for c in range(n_chunks):
-        block = jnp.stack(pieces[c * per_chunk : (c + 1) * per_chunk])
+        block = jnp.stack([pieces[k] for k in order[c * per_chunk : (c + 1) * per_chunk]])
         for bit in bits:
             block = bit_gather(block, "exp", bit, n_exp)
         blocks.append(block)
@@ -85,7 +86,7 @@
                 part = bit_reduce(part, "exp", bit, n_exp, wire)
             expert_rows = part.astype(jnp.bfloat16)
             for kk in range(per_chunk):
-                k = c * per_chunk + kk
+                k = order[c * per_chunk + kk]
                 if k == 0:
                     back = expert_rows[kk]
                 else:

time: 98.2 us -> 103 us (1.049)
  waiting for transfers between devices: 44.1 us -> 47.8 us
  starting transfers between devices: 34.4 us -> 36.3 us
    ppermute x7, starting transfers between devices: 12.5 us -> 16.5 us  [routed_experts(): lax.ppermute(tokens, 'attn', [(s, (s + k) % n_attn) for s in range(n_attn)])]
    ppermute x7, waiting for transfers between devices: 5.54 us -> 8.32 us  [routed_experts(): lax.ppermute(expert_rows[kk], 'attn', [(s, (s - k) % n_attn) for s in ran...]
    ppermute x4, waiting for transfers between devices: 15.8 us -> 18.4 us  [bit_gather(): other = lax.ppermute(x, axis, [(i, i ^ bit) for i in range(n)])]
    ppermute x7, waiting for transfers between devices: 4.31 us -> 1.68 us  [routed_experts(): lax.ppermute(tokens, 'attn', [(s, (s + k) % n_attn) for s in range(n_attn)])]
    ppermute x7, starting transfers between devices: 13.6 us -> 11.5 us  [routed_experts(): lax.ppermute(expert_rows[kk], 'attn', [(s, (s - k) % n_attn) for s in ran...]
  transfers between devices with their start and end apart: 26 -> 26, of which waited for: 12 -> 14; matrix products, arithmetic and copies ran while one was open for 14% -> 13% of each run, Pallas kernels for 0% -> 0%
where the time goes in v21:
time: 103 us
  waiting for transfers between devices  47.8 us (46%)
  starting transfers between devices  36.3 us (35%)
  matrix products  7.13 us (7%)
  other arithmetic  5.72 us (6%)
  local copies, waits for them, and re-layouts  4.8 us (5%)
    ppermute x4, waiting for transfers between devices, bit_gather(): other = lax.ppermute(x, axis, [(i, i ^ bit) for i in range(n)])  18.4 us
    ppermute x4, waiting for transfers between devices, bit_reduce(): lax.ppermute(sent, axis, [(i, i ^ bit) for i in range(n)]).astype(x.dtype)  17.3 us
    ppermute x7, starting transfers between devices, routed_experts(): lax.ppermute(tokens, 'attn', [(s, (s + k) % n_attn) for s in range(n_attn)])  16.5 us
    ppermute x7, starting transfers between devices, routed_experts(): lax.ppermute(expert_rows[kk], 'attn', [(s, (s - k) % n_attn) for s in ran...  11.5 us
    ppermute x7, waiting for transfers between devices, routed_experts(): lax.ppermute(expert_rows[kk], 'attn', [(s, (s - k) % n_attn) for s in ran...  8.32 us
    ppermute x4, starting transfers between devices, bit_gather(): other = lax.ppermute(x, axis, [(i, i ^ bit) for i in range(n)])  3.24 us
    unnamed x20, local copies, waits for them, and re-layouts  3.01 us
    ppermute x2, waiting for transfers between devices, per_device(): lax.ppermute(row_top, 'exp', [(i, i ^ bit) for i in range(n_exp)])  2.08 us
  transfers between devices with their start and end apart: 26, of which 14 were waited for; matrix products, arithmetic and copies ran while one was open for 13% of the time, Pallas kernels for 0%

profile of v21, /device:TPU:0, one launch (start us, length us, event | category | flops | bytes accessed | tf_op | source)
XLA Modules:
  0.0 102.8 jit_solution(3752213257413055753)
XLA Ops:
  0.7 4.1 %collective-permute-start.12 = (bf16[8,7168]{1,0:T(8,128)(2,1)}, bf16[8,7168]{1,0:T(8,128)(2,1)}, u32[]{:S(2)}, u32[]{:S(2)}) collective-permute-start(bf16[8,7168]{1,0:T(8,128)(2,1)} %param.16), channel_id=1, source_target_pairs={{0,16},{4,20},{8,24},{12,28},{16,0},{20,4},{24,8},{28,12},{1,17},{... | collective-permute-start | bytes 344072 | tf_op jit(solution)/shard_map/ppermute | solution.py:61
  4.8 2.5 %collective-permute-start.11 = (bf16[8,7168]{1,0:T(8,128)(2,1)}, bf16[8,7168]{1,0:T(8,128)(2,1)}, u32[]{:S(2)}, u32[]{:S(2)}) collective-permute-start(bf16[8,7168]{1,0:T(8,128)(2,1)} %param.16), channel_id=1, source_target_pairs={{0,12},{4,16},{8,20},{12,24},{16,28},{20,0},{24,4},{28,8},{1,13},{... | collective-permute-start | bytes 344072 | tf_op jit(solution)/shard_map/ppermute | solution.py:61
  7.3 1.3 %collective-permute-start.10 = (bf16[8,7168]{1,0:T(8,128)(2,1)}, bf16[8,7168]{1,0:T(8,128)(2,1)}, u32[]{:S(2)}, u32[]{:S(2)}) collective-permute-start(bf16[8,7168]{1,0:T(8,128)(2,1)} %param.16), channel_id=1, source_target_pairs={{0,20},{4,24},{8,28},{12,0},{16,4},{20,8},{24,12},{28,16},{1,21},{... | collective-permute-start | bytes 344072 | tf_op jit(solution)/shard_map/ppermute | solution.py:61
  8.6 1.6 %collective-permute-start.9 = (bf16[8,7168]{1,0:T(8,128)(2,1)}, bf16[8,7168]{1,0:T(8,128)(2,1)}, u32[]{:S(2)}, u32[]{:S(2)}) collective-permute-start(bf16[8,7168]{1,0:T(8,128)(2,1)} %param.16), channel_id=1, source_target_pairs={{0,8},{4,12},{8,16},{12,20},{16,24},{20,28},{24,0},{28,4},{1,9},{5... | collective-permute-start | bytes 344072 | tf_op jit(solution)/shard_map/ppermute | solution.py:61
  10.2 1.8 %fusion.54 = f32[2,128,1024]{2,1,0:T(8,128)S(1)} fusion(bf16[2,128,512]{2,1,0:T(8,128)(2,1)} %param.11, bf16[2,1024,512]{2,1,0:T(8,128)(2,1)S(1)} %copy-done), kind=kOutput, calls=%fused_computation.108 | convolution fusion | flops 268435456 | bytes 3407872 | tf_op jit(solution)/shard_map/rhl,rpl->rhp/dot_general | solution.py:115
  13.8 1.6 %collective-permute-start.1 = (f32[2,128]{1,0:T(2,128)S(1)}, f32[2,128]{1,0:T(2,128)S(1)}, u32[]{:S(2)}, u32[]{:S(2)}) collective-permute-start(f32[2,128]{1,0:T(2,128)S(1)} %max.6), channel_id=1, source_target_pairs={{0,2},{1,3},{2,0},{3,1},{4,6},{5,7},{6,4},{7,5},{8,10},{9,11},{10,... | collective-permute-start | bytes 3080 | tf_op jit(solution)/shard_map/ppermute | solution.py:137
  15.4 2.1 %collective-permute-done.1 = f32[2,128]{1,0:T(2,128)S(1)} collective-permute-done((f32[2,128]{1,0:T(2,128)S(1)}, f32[2,128]{1,0:T(2,128)S(1)}, u32[]{:S(2)}, u32[]{:S(2)}) %collective-permute-start.1) | collective-permute-done | bytes 1056 | tf_op jit(solution)/shard_map/ppermute | solution.py:137
  17.4 2.2 %collective-permute-start.6 = (bf16[8,7168]{1,0:T(8,128)(2,1)S(1)}, bf16[8,7168]{1,0:T(8,128)(2,1)S(1)}, u32[]{:S(2)}, u32[]{:S(2)}) collective-permute-start(bf16[8,7168]{1,0:T(8,128)(2,1)S(1)} %copy-done.3), channel_id=1, source_target_pairs={{0,24},{4,28},{8,0},{12,4},{16,8},{20,12},{24,16},{28,20},{1,25},{... | collective-permute-start | bytes 344072 | tf_op jit(solution)/shard_map/ppermute | solution.py:61
  19.7 1.4 %broadcast_multiply_fusion = f32[2,128,512]{2,1,0:T(8,128)} fusion(f32[2,128]{1,0:T(2,128)S(1)} %get-tuple-element.3, bf16[2,1024,512]{2,1,0:T(8,128)(2,1)S(1)} %copy-done, f32[2,128,1024]{2,1,0:T(8,128)S(1)} %get-tuple-element.34, f32[2,128]{1,0:T(2,128)S(1)} %get-tuple-element.33, pred[2,1024]{1,0:T(4,128)(4,1)S(1)} %broadcast_compare_fusion), kind=kOutput, calls=%fused_computation.45 | convolution fusion | flops 269352960 | bytes 3674112 | tf_op jit(solution)/shard_map/rhp,rpl->rhl/dot_general | solution.py:126
  21.3 1.1 %fusion.24 = (f32[2,2,1,32,513]{4,3,2,1,0:T(8,128)S(1)}, f32[2,2,1,32,513]{4,3,2,1,0:T(8,128)S(1)}) fusion(s32[]{:T(128)S(6)} %select_n.81, f32[2,2,2,32,512]{4,3,2,1,0:T(8,128)} %bitcast.109, f32[2,2,2,32,1]{4,3,2,1,0:T(8,128)S(1)} %concatenate.15, s32[]{:T(128)S(6)} %select_n.82), kind=kLoop, calls=%fused_computation.41 | loop fusion | flops 131328 | bytes 1050632 | tf_op jit(solution)/shard_map/concatenate | solution.py:141
  22.4 2.5 %collective-permute-start.5 = (bf16[8,7168]{1,0:T(8,128)(2,1)S(1)}, bf16[8,7168]{1,0:T(8,128)(2,1)S(1)}, u32[]{:S(2)}, u32[]{:S(2)}) collective-permute-start(bf16[8,7168]{1,0:T(8,128)(2,1)S(1)} %copy-done.3), channel_id=1, source_target_pairs={{0,4},{4,8},{8,12},{12,16},{16,20},{20,24},{24,28},{28,0},{1,5},{5... | collective-permute-start | bytes 344072 | tf_op jit(solution)/shard_map/ppermute | solution.py:61
  24.9 2.3 %collective-permute-start.4 = (bf16[8,7168]{1,0:T(8,128)(2,1)S(1)}, bf16[8,7168]{1,0:T(8,128)(2,1)S(1)}, u32[]{:S(2)}, u32[]{:S(2)}) collective-permute-start(bf16[8,7168]{1,0:T(8,128)(2,1)S(1)} %copy-done.3), channel_id=1, source_target_pairs={{0,28},{4,0},{8,4},{12,8},{16,12},{20,16},{24,20},{28,24},{1,29},{... | collective-permute-start | bytes 344072 | tf_op jit(solution)/shard_map/ppermute | solution.py:61
  27.2 1.1 %fusion.48 = (bf16[1,4,8,7168]{3,2,1,0:T(8,128)(2,1)S(1)}, bf16[4,8,7168]{2,1,0:T(8,128)(2,1)S(1)}) fusion(bf16[1,8,7168]{2,1,0:T(8,128)(2,1)} %bitcast.19, bf16[1,8,7168]{2,1,0:T(8,128)(2,1)} %bitcast.18, bf16[1,8,7168]{2,1,0:T(8,128)(2,1)} %bitcast.17, bf16[1,8,7168]{2,1,0:T(8,128)(2,1)} %bitcast.16), kind=kLoop, calls=%fused_computation.102 | loop fusion | flops 688128 | bytes 1376256 | tf_op jit(solution)/shard_map/stack | solution.py:35
  28.3 1.5 %collective-permute-start.13 = (bf16[4,8,7168]{2,1,0:T(8,128)(2,1)S(1)}, bf16[4,8,7168]{2,1,0:T(8,128)(2,1)S(1)}, u32[]{:S(2)}, u32[]{:S(2)}) collective-permute-start(bf16[4,8,7168]{2,1,0:T(8,128)(2,1)S(1)} %get-tuple-element.24), channel_id=1, source_target_pairs={{0,2},{1,3},{2,0},{3,1},{4,6},{5,7},{6,4},{7,5},{8,10},{9,11},{10,... | collective-permute-start | bytes 1376264 | tf_op jit(solution)/shard_map/ppermute | solution.py:34
  30.1 1.5 %collective-permute-done.4 = bf16[8,7168]{1,0:T(8,128)(2,1)S(1)} collective-permute-done((bf16[8,7168]{1,0:T(8,128)(2,1)S(1)}, bf16[8,7168]{1,0:T(8,128)(2,1)S(1)}, u32[]{:S(2)}, u32[]{:S(2)}) %collective-permute-start.4) | collective-permute-done | bytes 114720 | tf_op jit(solution)/shard_map/ppermute | solution.py:61
  31.6 1.6 %collective-permute-start.7 = (bf16[4,8,7168]{2,1,0:T(8,128)(2,1)S(1)}, bf16[4,8,7168]{2,1,0:T(8,128)(2,1)S(1)}, u32[]{:S(2)}, u32[]{:S(2)}) collective-permute-start(bf16[4,8,7168]{2,1,0:T(8,128)(2,1)S(1)} %get-tuple-element.22), channel_id=1, source_target_pairs={{0,2},{1,3},{2,0},{3,1},{4,6},{5,7},{6,4},{7,5},{8,10},{9,11},{10,... | collective-permute-start | bytes 1376264 | tf_op jit(solution)/shard_map/ppermute | solution.py:34
  33.3 8.5 %collective-permute-done.13 = bf16[4,8,7168]{2,1,0:T(8,128)(2,1)S(1)} collective-permute-done((bf16[4,8,7168]{2,1,0:T(8,128)(2,1)S(1)}, bf16[4,8,7168]{2,1,0:T(8,128)(2,1)S(1)}, u32[]{:S(2)}, u32[]{:S(2)}) %collective-permute-start.13) | collective-permute-done | bytes 458784 | tf_op jit(solution)/shard_map/ppermute | solution.py:34
  41.9 9.2 %collective-permute-done.7 = bf16[4,8,7168]{2,1,0:T(8,128)(2,1)S(1)} collective-permute-done((bf16[4,8,7168]{2,1,0:T(8,128)(2,1)S(1)}, bf16[4,8,7168]{2,1,0:T(8,128)(2,1)S(1)}, u32[]{:S(2)}, u32[]{:S(2)}) %collective-permute-start.7) | collective-permute-done | bytes 458784 | tf_op jit(solution)/shard_map/ppermute | solution.py:34
  51.4 1.5 %collective-permute-start.3 = (f32[2,1,32,513]{3,2,0,1:T(8,128)S(1)}, f32[2,1,32,513]{3,2,0,1:T(8,128)S(1)}, u32[]{:S(2)}, u32[]{:S(2)}) collective-permute-start(f32[2,1,32,513]{3,2,0,1:T(8,128)S(1)} %constant_dynamic-slice_fusion), channel_id=1, source_target_pairs={{0,2},{1,3},{2,0},{3,1},{4,6},{5,7},{6,4},{7,5},{8,10},{9,11},{10,... | collective-permute-start | bytes 393992 | tf_op jit(solution)/shard_map/ppermute | solution.py:150
  54.0 1.2 %copy-done.8 = bf16[1,7168,256]{2,1,0:T(8,128)(2,1)S(1)} copy-done((bf16[1,7168,256]{2,1,0:T(8,128)(2,1)S(1)}, bf16[1,7168,256]{2,1,0:T(8,128)(2,1)}, u32[]{:S(2)}) %copy-start.8) | copy-done | bytes 3670040
  55.2 1.1 %fusion.6 = f32[256,256]{1,0:T(8,128)S(1)} fusion(bf16[1,7168,256]{2,1,0:T(8,128)(2,1)S(1)} %copy-done.8, bf16[128,7168]{1,0:T(8,128)(2,1)S(1)} %bitcast.112, bf16[128,7168]{1,0:T(8,128)(2,1)S(1)} %bitcast.114), kind=kOutput, calls=%fused_computation.8 | convolution fusion | flops 946864128 | bytes 7602176 | tf_op jit(solution)/shard_map/dot_general | solution.py:74
  57.2 1.1 %multiply_convert_fusion = bf16[256,256]{1,0:T(8,128)(2,1)S(1)} fusion(f32[256,256]{1,0:T(8,128)S(1)} %fusion.6, bf16[1,7168,256]{2,1,0:T(8,128)(2,1)S(1)} %copy-done.9, bf16[128,7168]{1,0:T(8,128)(2,1)S(1)} %bitcast.113, bf16[128,7168]{1,0:T(8,128)(2,1)S(1)} %bitcast.115), kind=kOutput, calls=%fused_computation.44 | convolution fusion | flops 947257344 | bytes 7733248 | tf_op jit(solution)/shard_map/dot_general | solution.py:75
  62.0 2.8 %collective-permute-done.20 = f32[2,4,8,7168]{3,2,1,0:T(8,128)S(1)} collective-permute-done((f32[2,4,8,7168]{3,2,1,0:T(8,128)S(1)}, f32[2,4,8,7168]{3,2,1,0:T(8,128)S(1)}, u32[]{:S(2)}, u32[]{:S(2)}) %collective-permute-start.20) | collective-permute-done | bytes 1835040 | tf_op jit(solution)/shard_map/ppermute | solution.py:40
  65.6 1.8 %collective-permute-done.15 = f32[2,4,8,7168]{3,2,1,0:T(8,128)S(1)} collective-permute-done((f32[2,4,8,7168]{3,2,1,0:T(8,128)S(1)}, f32[2,4,8,7168]{3,2,1,0:T(8,128)S(1)}, u32[]{:S(2)}, u32[]{:S(2)}) %collective-permute-start.15) | collective-permute-done | bytes 1835040 | tf_op jit(solution)/shard_map/ppermute | solution.py:40
  68.2 10.2 %collective-permute-done.21 = bf16[4,8,7168]{2,1,0:T(8,128)(2,1)S(1)} collective-permute-done((bf16[4,8,7168]{2,1,0:T(8,128)(2,1)S(1)}, bf16[4,8,7168]{2,1,0:T(8,128)(2,1)S(1)}, u32[]{:S(2)}, u32[]{:S(2)}) %collective-permute-start.21) | collective-permute-done | bytes 458784 | tf_op jit(solution)/shard_map/ppermute | solution.py:40
  78.6 2.1 %collective-permute-start.24 = (bf16[8,7168]{1,0:T(8,128)(2,1)S(1)}, bf16[8,7168]{1,0:T(8,128)(2,1)S(1)}, u32[]{:S(2)}, u32[]{:S(2)}) collective-permute-start(bf16[8,7168]{1,0:T(8,128)(2,1)S(1)} %get-tuple-element.19), channel_id=1, source_target_pairs={{0,20},{4,24},{8,28},{12,0},{16,4},{20,8},{24,12},{28,16},{1,21},{... | collective-permute-start | bytes 344072 | tf_op jit(solution)/shard_map/ppermute | solution.py:93
  81.6 3.3 %collective-permute-start.22 = (bf16[8,7168]{1,0:T(8,128)(2,1)S(1)}, bf16[8,7168]{1,0:T(8,128)(2,1)S(1)}, u32[]{:S(2)}, u32[]{:S(2)}) collective-permute-start(bf16[8,7168]{1,0:T(8,128)(2,1)S(1)} %get-tuple-element.17), channel_id=1, source_target_pairs={{0,24},{4,28},{8,0},{12,4},{16,8},{20,12},{24,16},{28,20},{1,25},{... | collective-permute-start | bytes 344072 | tf_op jit(solution)/shard_map/ppermute | solution.py:93
  84.9 2.6 %collective-permute-done.16 = bf16[4,8,7168]{2,1,0:T(8,128)(2,1)S(1)} collective-permute-done((bf16[4,8,7168]{2,1,0:T(8,128)(2,1)S(1)}, bf16[4,8,7168]{2,1,0:T(8,128)(2,1)S(1)}, u32[]{:S(2)}, u32[]{:S(2)}) %collective-permute-start.16) | collective-permute-done | bytes 458784 | tf_op jit(solution)/shard_map/ppermute | solution.py:40
  87.7 1.7 %collective-permute-done.25 = bf16[8,7168]{1,0:T(8,128)(2,1)S(1)} collective-permute-done((bf16[8,7168]{1,0:T(8,128)(2,1)S(1)}, bf16[8,7168]{1,0:T(8,128)(2,1)S(1)}, u32[]{:S(2)}, u32[]{:S(2)}) %collective-permute-start.25) | collective-permute-done | bytes 114720 | tf_op jit(solution)/shard_map/ppermute | solution.py:93
  89.5 4.9 %collective-permute-start.18 = (bf16[8,7168]{1,0:T(8,128)(2,1)S(1)}, bf16[8,7168]{1,0:T(8,128)(2,1)S(1)}, u32[]{:S(2)}, u32[]{:S(2)}) collective-permute-start(bf16[8,7168]{1,0:T(8,128)(2,1)S(1)} %get-tuple-element.16), channel_id=1, source_target_pairs={{0,28},{4,0},{8,4},{12,8},{16,12},{20,16},{24,20},{28,24},{1,29},{... | collective-permute-start | bytes 344072 | tf_op jit(solution)/shard_map/ppermute | solution.py:93
  95.3 1.3 %collective-permute-done.22 = bf16[8,7168]{1,0:T(8,128)(2,1)S(1)} collective-permute-done((bf16[8,7168]{1,0:T(8,128)(2,1)S(1)}, bf16[8,7168]{1,0:T(8,128)(2,1)S(1)}, u32[]{:S(2)}, u32[]{:S(2)}) %collective-permute-start.22) | collective-permute-done | bytes 114720 | tf_op jit(solution)/shard_map/ppermute | solution.py:93
  96.7 5.1 %collective-permute-done.17 = bf16[8,7168]{1,0:T(8,128)(2,1)S(1)} collective-permute-done((bf16[8,7168]{1,0:T(8,128)(2,1)S(1)}, bf16[8,7168]{1,0:T(8,128)(2,1)S(1)}, u32[]{:S(2)}, u32[]{:S(2)}) %collective-permute-start.17) | collective-permute-done | bytes 114720 | tf_op jit(solution)/shard_map/ppermute | solution.py:93
  (85 shorter events, 13.3 us)
Async XLA Ops:
  0.6 9.5 %copy-start = (bf16[2,1024,512]{2,1,0:T(8,128)(2,1)S(1)}, bf16[2,1024,512]{2,1,0:T(8,128)(2,1)}, u32[]{:S(2)}) copy-start(bf16[2,1024,512]{2,1,0:T(8,128)(2,1)} %param.13) | copy-start | bytes 6291460
  0.6 11.3 %copy-start.7 = (s32[2]{0:T(128)S(1)}, s32[2]{0:T(128)}, u32[]{:S(2)}) copy-start(s32[2]{0:T(128)} %param.15) | copy-start | bytes 28
  0.7 11.4 %copy-start.2 = (bf16[2,64,1024]{2,1,0:T(8,128)(2,1)S(1)}, bf16[2,64,1024]{2,1,0:T(8,128)(2,1)}, u32[]{:S(2)}) copy-start(bf16[2,64,1024]{2,1,0:T(8,128)(2,1)} %param.14) | copy-start | bytes 786436
  0.7 21.7 %collective-permute-start.12 = (bf16[8,7168]{1,0:T(8,128)(2,1)}, bf16[8,7168]{1,0:T(8,128)(2,1)}, u32[]{:S(2)}, u32[]{:S(2)}) collective-permute-start(bf16[8,7168]{1,0:T(8,128)(2,1)} %param.16), channel_id=1, source_target_pairs={{0,16},{4,20},{8,24},{12,28},{16,0},{20,4},{24,8},{28,12},{1,17},{... | collective-permute-start | bytes 344072 | tf_op jit(solution)/shard_map/ppermute | solution.py:61
  4.8 20.1 %collective-permute-start.11 = (bf16[8,7168]{1,0:T(8,128)(2,1)}, bf16[8,7168]{1,0:T(8,128)(2,1)}, u32[]{:S(2)}, u32[]{:S(2)}) collective-permute-start(bf16[8,7168]{1,0:T(8,128)(2,1)} %param.16), channel_id=1, source_target_pairs={{0,12},{4,16},{8,20},{12,24},{16,28},{20,0},{24,4},{28,8},{1,13},{... | collective-permute-start | bytes 344072 | tf_op jit(solution)/shard_map/ppermute | solution.py:61
  7.3 19.9 %collective-permute-start.10 = (bf16[8,7168]{1,0:T(8,128)(2,1)}, bf16[8,7168]{1,0:T(8,128)(2,1)}, u32[]{:S(2)}, u32[]{:S(2)}) collective-permute-start(bf16[8,7168]{1,0:T(8,128)(2,1)} %param.16), channel_id=1, source_target_pairs={{0,20},{4,24},{8,28},{12,0},{16,4},{20,8},{24,12},{28,16},{1,21},{... | collective-permute-start | bytes 344072 | tf_op jit(solution)/shard_map/ppermute | solution.py:61
  8.6 18.6 %collective-permute-start.9 = (bf16[8,7168]{1,0:T(8,128)(2,1)}, bf16[8,7168]{1,0:T(8,128)(2,1)}, u32[]{:S(2)}, u32[]{:S(2)}) collective-permute-start(bf16[8,7168]{1,0:T(8,128)(2,1)} %param.16), channel_id=1, source_target_pairs={{0,8},{4,12},{8,16},{12,20},{16,24},{20,28},{24,0},{28,4},{1,9},{5... | collective-permute-start | bytes 344072 | tf_op jit(solution)/shard_map/ppermute | solution.py:61
  12.0 5.5 %copy-start.3 = (bf16[8,7168]{1,0:T(8,128)(2,1)S(1)}, bf16[8,7168]{1,0:T(8,128)(2,1)}, u32[]{:S(2)}) copy-start(bf16[8,7168]{1,0:T(8,128)(2,1)} %param.16) | copy-start | bytes 344068
  12.5 1.3 %collective-permute-start = (f32[2,128]{1,0:T(2,128)S(1)}, f32[2,128]{1,0:T(2,128)S(1)}, u32[]{:S(2)}, u32[]{:S(2)}) collective-permute-start(f32[2,128]{1,0:T(2,128)S(1)} %get-tuple-element.33), channel_id=1, source_target_pairs={{0,1},{1,0},{2,3},{3,2},{4,5},{5,4},{6,7},{7,6},{8,9},{9,8},{10,11... | collective-permute-start | bytes 3080 | tf_op jit(solution)/shard_map/ppermute | solution.py:137
  13.8 3.6 %collective-permute-start.1 = (f32[2,128]{1,0:T(2,128)S(1)}, f32[2,128]{1,0:T(2,128)S(1)}, u32[]{:S(2)}, u32[]{:S(2)}) collective-permute-start(f32[2,128]{1,0:T(2,128)S(1)} %max.6), channel_id=1, source_target_pairs={{0,2},{1,3},{2,0},{3,1},{4,6},{5,7},{6,4},{7,5},{8,10},{9,11},{10,... | collective-permute-start | bytes 3080 | tf_op jit(solution)/shard_map/ppermute | solution.py:137
  17.4 12.4 %collective-permute-start.6 = (bf16[8,7168]{1,0:T(8,128)(2,1)S(1)}, bf16[8,7168]{1,0:T(8,128)(2,1)S(1)}, u32[]{:S(2)}, u32[]{:S(2)}) collective-permute-start(bf16[8,7168]{1,0:T(8,128)(2,1)S(1)} %copy-done.3), channel_id=1, source_target_pairs={{0,24},{4,28},{8,0},{12,4},{16,8},{20,12},{24,16},{28,20},{1,25},{... | collective-permute-start | bytes 344072 | tf_op jit(solution)/shard_map/ppermute | solution.py:61
  22.4 7.7 %collective-permute-start.5 = (bf16[8,7168]{1,0:T(8,128)(2,1)S(1)}, bf16[8,7168]{1,0:T(8,128)(2,1)S(1)}, u32[]{:S(2)}, u32[]{:S(2)}) collective-permute-start(bf16[8,7168]{1,0:T(8,128)(2,1)S(1)} %copy-done.3), channel_id=1, source_target_pairs={{0,4},{4,8},{8,12},{12,16},{16,20},{20,24},{24,28},{28,0},{1,5},{5... | collective-permute-start | bytes 344072 | tf_op jit(solution)/shard_map/ppermute | solution.py:61
  24.9 6.7 %collective-permute-start.4 = (bf16[8,7168]{1,0:T(8,128)(2,1)S(1)}, bf16[8,7168]{1,0:T(8,128)(2,1)S(1)}, u32[]{:S(2)}, u32[]{:S(2)}) collective-permute-start(bf16[8,7168]{1,0:T(8,128)(2,1)S(1)} %copy-done.3), channel_id=1, source_target_pairs={{0,28},{4,0},{8,4},{12,8},{16,12},{20,16},{24,20},{28,24},{1,29},{... | collective-permute-start | bytes 344072 | tf_op jit(solution)/shard_map/ppermute | solution.py:61
  27.2 6.0 %collective-permute-start.2 = (f32[2,2,32,513]{3,2,0,1:T(8,128)S(1)}, f32[2,2,32,513]{3,2,0,1:T(8,128)S(1)}, u32[]{:S(2)}, u32[]{:S(2)}) collective-permute-start(f32[2,2,32,513]{3,2,0,1:T(8,128)S(1)} %bitcast.120), channel_id=1, source_target_pairs={{0,1},{1,0},{2,3},{3,2},{4,5},{5,4},{6,7},{7,6},{8,9},{9,8},{10,11... | collective-permute-start | bytes 787976 | tf_op jit(solution)/shard_map/ppermute | solution.py:150
  28.3 13.4 %collective-permute-start.13 = (bf16[4,8,7168]{2,1,0:T(8,128)(2,1)S(1)}, bf16[4,8,7168]{2,1,0:T(8,128)(2,1)S(1)}, u32[]{:S(2)}, u32[]{:S(2)}) collective-permute-start(bf16[4,8,7168]{2,1,0:T(8,128)(2,1)S(1)} %get-tuple-element.24), channel_id=1, source_target_pairs={{0,2},{1,3},{2,0},{3,1},{4,6},{5,7},{6,4},{7,5},{8,10},{9,11},{10,... | collective-permute-start | bytes 1376264 | tf_op jit(solution)/shard_map/ppermute | solution.py:34
  31.6 19.5 %collective-permute-start.7 = (bf16[4,8,7168]{2,1,0:T(8,128)(2,1)S(1)}, bf16[4,8,7168]{2,1,0:T(8,128)(2,1)S(1)}, u32[]{:S(2)}, u32[]{:S(2)}) collective-permute-start(bf16[4,8,7168]{2,1,0:T(8,128)(2,1)S(1)} %get-tuple-element.22), channel_id=1, source_target_pairs={{0,2},{1,3},{2,0},{3,1},{4,6},{5,7},{6,4},{7,5},{8,10},{9,11},{10,... | collective-permute-start | bytes 1376264 | tf_op jit(solution)/shard_map/ppermute | solution.py:34
  41.8 11.1 %collective-permute-start.14 = (bf16[2,4,8,7168]{3,2,1,0:T(8,128)(2,1)S(1)}, bf16[2,4,8,7168]{3,2,1,0:T(8,128)(2,1)S(1)}, u32[]{:S(2)}, u32[]{:S(2)}) collective-permute-start(bf16[2,4,8,7168]{3,2,1,0:T(8,128)(2,1)S(1)} %get-tuple-element.11), channel_id=1, source_target_pairs={{0,1},{1,0},{2,3},{3,2},{4,5},{5,4},{6,7},{7,6},{8,9},{9,8},{10,11... | collective-permute-start | bytes 2752520 | tf_op jit(solution)/shard_map/ppermute | solution.py:34
  51.3 2.5 %collective-permute-start.8 = (bf16[2,4,8,7168]{3,2,1,0:T(8,128)(2,1)S(1)}, bf16[2,4,8,7168]{3,2,1,0:T(8,128)(2,1)S(1)}, u32[]{:S(2)}, u32[]{:S(2)}) collective-permute-start(bf16[2,4,8,7168]{3,2,1,0:T(8,128)(2,1)S(1)} %get-tuple-element.9), channel_id=1, source_target_pairs={{0,1},{1,0},{2,3},{3,2},{4,5},{5,4},{6,7},{7,6},{8,9},{9,8},{10,11... | collective-permute-start | bytes 2752520 | tf_op jit(solution)/shard_map/ppermute | solution.py:34
  51.4 10.5 %collective-permute-start.3 = (f32[2,1,32,513]{3,2,0,1:T(8,128)S(1)}, f32[2,1,32,513]{3,2,0,1:T(8,128)S(1)}, u32[]{:S(2)}, u32[]{:S(2)}) collective-permute-start(f32[2,1,32,513]{3,2,0,1:T(8,128)S(1)} %constant_dynamic-slice_fusion), channel_id=1, source_target_pairs={{0,2},{1,3},{2,0},{3,1},{4,6},{5,7},{6,4},{7,5},{8,10},{9,11},{10,... | collective-permute-start | bytes 393992 | tf_op jit(solution)/shard_map/ppermute | solution.py:150
  53.1 2.0 %copy-start.8 = (bf16[1,7168,256]{2,1,0:T(8,128)(2,1)S(1)}, bf16[1,7168,256]{2,1,0:T(8,128)(2,1)}, u32[]{:S(2)}) copy-start(bf16[1,7168,256]{2,1,0:T(8,128)(2,1)} %param.19) | copy-start | bytes 11010052
  55.2 2.0 %copy-start.9 = (bf16[1,7168,256]{2,1,0:T(8,128)(2,1)S(1)}, bf16[1,7168,256]{2,1,0:T(8,128)(2,1)}, u32[]{:S(2)}) copy-start(bf16[1,7168,256]{2,1,0:T(8,128)(2,1)} %param.20) | copy-start | bytes 11010052
  60.9 3.9 %collective-permute-start.20 = (f32[2,4,8,7168]{3,2,1,0:T(8,128)S(1)}, f32[2,4,8,7168]{3,2,1,0:T(8,128)S(1)}, u32[]{:S(2)}, u32[]{:S(2)}) collective-permute-start(f32[2,4,8,7168]{3,2,1,0:T(8,128)S(1)} %bitcast.111), channel_id=1, source_target_pairs={{0,1},{1,0},{2,3},{3,2},{4,5},{5,4},{6,7},{7,6},{8,9},{9,8},{10,11... | collective-permute-start | bytes 5505032 | tf_op jit(solution)/shard_map/ppermute | solution.py:40
  61.5 5.9 %collective-permute-start.15 = (f32[2,4,8,7168]{3,2,1,0:T(8,128)S(1)}, f32[2,4,8,7168]{3,2,1,0:T(8,128)S(1)}, u32[]{:S(2)}, u32[]{:S(2)}) collective-permute-start(f32[2,4,8,7168]{3,2,1,0:T(8,128)S(1)} %bitcast.110), channel_id=1, source_target_pairs={{0,1},{1,0},{2,3},{3,2},{4,5},{5,4},{6,7},{7,6},{8,9},{9,8},{10,11... | collective-permute-start | bytes 5505032 | tf_op jit(solution)/shard_map/ppermute | solution.py:40
  65.0 13.4 %collective-permute-start.21 = (bf16[4,8,7168]{2,1,0:T(8,128)(2,1)S(1)}, bf16[4,8,7168]{2,1,0:T(8,128)(2,1)S(1)}, u32[]{:S(2)}, u32[]{:S(2)}) collective-permute-start(bf16[4,8,7168]{2,1,0:T(8,128)(2,1)S(1)} %fusion.22), channel_id=1, source_target_pairs={{0,2},{1,3},{2,0},{3,1},{4,6},{5,7},{6,4},{7,5},{8,10},{9,11},{10,... | collective-permute-start | bytes 1376264 | tf_op jit(solution)/shard_map/ppermute | solution.py:40
  67.6 19.9 %collective-permute-start.16 = (bf16[4,8,7168]{2,1,0:T(8,128)(2,1)S(1)}, bf16[4,8,7168]{2,1,0:T(8,128)(2,1)S(1)}, u32[]{:S(2)}, u32[]{:S(2)}) collective-permute-start(bf16[4,8,7168]{2,1,0:T(8,128)(2,1)S(1)} %fusion.21), channel_id=1, source_target_pairs={{0,2},{1,3},{2,0},{3,1},{4,6},{5,7},{6,4},{7,5},{8,10},{9,11},{10,... | collective-permute-start | bytes 1376264 | tf_op jit(solution)/shard_map/ppermute | solution.py:40
  78.5 10.9 %collective-permute-start.25 = (bf16[8,7168]{1,0:T(8,128)(2,1)S(1)}, bf16[8,7168]{1,0:T(8,128)(2,1)S(1)}, u32[]{:S(2)}, u32[]{:S(2)}) collective-permute-start(bf16[8,7168]{1,0:T(8,128)(2,1)S(1)} %get-tuple-element.18), channel_id=1, source_target_pairs={{0,16},{4,20},{8,24},{12,28},{16,0},{20,4},{24,8},{28,12},{1,17},{... | collective-permute-start | bytes 344072 | tf_op jit(solution)/shard_map/ppermute | solution.py:93
  78.6 15.7 %collective-permute-start.24 = (bf16[8,7168]{1,0:T(8,128)(2,1)S(1)}, bf16[8,7168]{1,0:T(8,128)(2,1)S(1)}, u32[]{:S(2)}, u32[]{:S(2)}) collective-permute-start(bf16[8,7168]{1,0:T(8,128)(2,1)S(1)} %get-tuple-element.19), channel_id=1, source_target_pairs={{0,20},{4,24},{8,28},{12,0},{16,4},{20,8},{24,12},{28,16},{1,21},{... | collective-permute-start | bytes 344072 | tf_op jit(solution)/shard_map/ppermute | solution.py:93
  80.7 14.6 %collective-permute-start.23 = (bf16[8,7168]{1,0:T(8,128)(2,1)S(1)}, bf16[8,7168]{1,0:T(8,128)(2,1)S(1)}, u32[]{:S(2)}, u32[]{:S(2)}) collective-permute-start(bf16[8,7168]{1,0:T(8,128)(2,1)S(1)} %get-tuple-element.20), channel_id=1, source_target_pairs={{0,12},{4,16},{8,20},{12,24},{16,28},{20,0},{24,4},{28,8},{1,13},{... | collective-permute-start | bytes 344072 | tf_op jit(solution)/shard_map/ppermute | solution.py:93
  81.6 14.9 %collective-permute-start.22 = (bf16[8,7168]{1,0:T(8,128)(2,1)S(1)}, bf16[8,7168]{1,0:T(8,128)(2,1)S(1)}, u32[]{:S(2)}, u32[]{:S(2)}) collective-permute-start(bf16[8,7168]{1,0:T(8,128)(2,1)S(1)} %get-tuple-element.17), channel_id=1, source_target_pairs={{0,24},{4,28},{8,0},{12,4},{16,8},{20,12},{24,16},{28,20},{1,25},{... | collective-permute-start | bytes 344072 | tf_op jit(solution)/shard_map/ppermute | solution.py:93
  87.7 8.9 %collective-permute-start.19 = (bf16[8,7168]{1,0:T(8,128)(2,1)S(1)}, bf16[8,7168]{1,0:T(8,128)(2,1)S(1)}, u32[]{:S(2)}, u32[]{:S(2)}) collective-permute-start(bf16[8,7168]{1,0:T(8,128)(2,1)S(1)} %get-tuple-element.15), channel_id=1, source_target_pairs={{0,8},{4,12},{8,16},{12,20},{16,24},{20,28},{24,0},{28,4},{1,9},{5... | collective-permute-start | bytes 344072 | tf_op jit(solution)/shard_map/ppermute | solution.py:93
  89.5 7.3 %collective-permute-start.18 = (bf16[8,7168]{1,0:T(8,128)(2,1)S(1)}, bf16[8,7168]{1,0:T(8,128)(2,1)S(1)}, u32[]{:S(2)}, u32[]{:S(2)}) collective-permute-start(bf16[8,7168]{1,0:T(8,128)(2,1)S(1)} %get-tuple-element.16), channel_id=1, source_target_pairs={{0,28},{4,0},{8,4},{12,8},{16,12},{20,16},{24,20},{28,24},{1,29},{... | collective-permute-start | bytes 344072 | tf_op jit(solution)/shard_map/ppermute | solution.py:93
  94.4 7.5 %collective-permute-start.17 = (bf16[8,7168]{1,0:T(8,128)(2,1)S(1)}, bf16[8,7168]{1,0:T(8,128)(2,1)S(1)}, u32[]{:S(2)}, u32[]{:S(2)}) collective-permute-start(bf16[8,7168]{1,0:T(8,128)(2,1)S(1)} %get-tuple-element.14), channel_id=1, source_target_pairs={{0,4},{4,8},{8,12},{12,16},{16,20},{20,24},{24,28},{28,0},{1,5},{5... | collective-permute-start | bytes 344072 | tf_op jit(solution)/shard_map/ppermute | solution.py:93
  (4 other events, 6.0 us)
